TPU v7x, 256 devices: a whole 4x4x8 slice. The times are simulated.
256 devices in a mesh: grp: 8 (over z_lo, y), tile: 32 (over z_hi, x, core).
Axes of the slice: x: 4, y: 4, z: 8 (z_hi: 4, z_lo: 2; z = z_hi * 2 + z_lo), core: 2. Of those that a mesh axis runs over, the one named last changes fastest.
Arguments:
- parent_state: float32 [3, 8, 2048, 2048], P(None, None, ('grp', 'tile')), may hold values from -6 to 6
- terrain: int32 [2048, 2048], P(('grp', 'tile')), may hold values from 0 to 4000
- nest_state: float32 [3, 8, 8, 384, 768], P(None, None, 'grp', 'tile'), may hold values from -6 to 6
- nest_offsets: int32 [8, 2], P('grp'), may hold values from 1 to 1791, as said below
Outputs:
- new_parent: float32 [3, 8, 2048, 2048], P(None, None, ('grp', 'tile'))
- new_nest: float32 [3, 8, 8, 384, 768], P(None, None, 'grp', 'tile')
Inputs may be any that keep to these rules, and one draw needn't show every extreme that they name: `nest_offsets`: row g holds nest g's first footprint row counted within group g's band of 256 parent rows, from 1 to 127, and its first footprint column, from 1 to 1791. In every draw one nest has the largest row offset and column offset 1, and another nest has the largest column offset.
All inputs are finite; a program needn't handle non-finite values.
Results may differ from a plain program's by a relative error of at most 0.0001.
Values sent between devices are 32-bit elements; how exact they have to be, the bound alone decides.
No kernel may reach another device: no remote copies, remote signals or barrier semaphores. Data moves between devices by JAX's collectives and lax.ppermute only.
A program may use at most 128 MiB of HBM per device.

v0:
```python
import jax
import jax.numpy as jnp
from jax import lax
from jax.sharding import PartitionSpec as P

SUBSTEPS = 3


parent_courant = 0.35
nest_courant = 0.35
nudge_rate = 0.2
terrain_scale = 6000.0


def extended_2(value, sides, width):
    for axis, dim in sides:
        devices, length = (lax.axis_size(axis), value.shape[dim])
        up = [(i, (i + 1) % devices) for i in range(devices - 1)]
        down = [(j, i) for i, j in up]
        last = lax.slice_in_dim(value, length - width, length, axis=dim)
        first = lax.slice_in_dim(value, 0, width, axis=dim)
        before = lax.ppermute(last, axis, up)
        after = lax.ppermute(first, axis, down)
        value = jnp.concatenate([before, value, after], axis=dim)
    return value


def substep(fields, sound_factor, courant, east_edge, west_edge):
    pressure = fields[0]
    zonal_wind = fields[1]
    merid_wind = fields[2]
    east_side = jnp.concatenate([pressure[..., 1:], east_edge[..., None]], axis=-1)
    zonal_next = zonal_wind - courant * (east_side - pressure)
    below_side = jnp.concatenate(
        [pressure[..., 1:, :], jnp.zeros_like(pressure[..., :1, :])], axis=-2
    )
    merid_next = merid_wind - courant * (below_side - pressure)
    west_side = jnp.concatenate([west_edge[..., None], zonal_next[..., :-1]], axis=-1)
    above_side = jnp.concatenate(
        [jnp.zeros_like(merid_next[..., :1, :]), merid_next[..., :-1, :]], axis=-2
    )
    pressure_next = pressure - courant * sound_factor * (
        zonal_next - west_side + (merid_next - above_side)
    )
    return jnp.stack([pressure_next, zonal_next, merid_next])


def local(parent_state, terrain, nest_state, nest_offsets):
    tile_count = lax.axis_size("tile")
    tile_index = lax.axis_index("tile")
    levels = parent_state.shape[1]
    parent_rows = parent_state.shape[2]
    nest_rows = nest_state.shape[3]
    nest_cols = nest_state.shape[4]
    coarse_rows = nest_rows // 3
    coarse_cols = nest_cols // 3
    foot_rows = coarse_rows + 2
    row_offset = nest_offsets[0, 0]
    col_offset = nest_offsets[0, 1]
    sound_factor = 1.0 - terrain.astype(jnp.float32) / terrain_scale
    halo_fields = parent_state[0:3:2]
    padded = extended_2(halo_fields, ((("grp", "tile"), 2),), 1)
    zonal_ext = jnp.pad(parent_state[1], ((0, 0), (1, 1), (0, 0)))
    extended = jnp.stack([padded[0], zonal_ext, padded[1]])
    factor_ext = jnp.pad(sound_factor, ((1, 1), (0, 0)))
    edge_zeros = jnp.zeros((levels, parent_rows + 2), jnp.float32)
    advanced = substep(extended, factor_ext, parent_courant, edge_zeros, edge_zeros)[:, :, 1:-1]
    window = lax.dynamic_slice_in_dim(advanced, col_offset - 1, coarse_cols + 2, axis=3)
    factor_window = lax.dynamic_slice_in_dim(sound_factor, col_offset - 1, coarse_cols + 2, axis=1)[
        None, None
    ]
    highest = lax.Precision.HIGHEST
    needed = row_offset + coarse_rows * tile_index - 1 + jnp.arange(foot_rows, dtype=jnp.int32)
    portions = (
        lax.all_gather(window, "tile", axis=2, tiled=True),
        lax.all_gather(factor_window, "tile", axis=2, tiled=True),
    )
    count = portions[0].shape[2]
    picker = (needed[:, None] == jnp.arange(count, dtype=jnp.int32)[None, :]).astype(jnp.float32)
    footprint = jnp.einsum("kj,vljc->vlkc", picker, portions[0], precision=highest)
    foot_factor = jnp.einsum("kj,abjc->abkc", picker, portions[1], precision=highest)
    foot_factor = foot_factor[0, 0]
    injected = jnp.repeat(jnp.repeat(footprint[..., 1:-1], 3, axis=3), 3, axis=2)
    west_rows = jnp.repeat(footprint[1, :, :, 0], 3, axis=1)
    east_rows = jnp.repeat(footprint[0, :, :, -1], 3, axis=1)
    factor_rows = jnp.repeat(jnp.repeat(foot_factor[:, 1:-1], 3, axis=1), 3, axis=0)
    local_rows = jnp.arange(nest_rows + 6, dtype=jnp.int32) - 3
    global_rows = nest_rows * tile_index + local_rows
    outside = (global_rows < 0) | (global_rows >= nest_rows * tile_count)
    nest_fields = nest_state[:, :, 0]
    for _ in range(SUBSTEPS):
        fields = extended_2(nest_fields, (("tile", 2),), 1)
        advance_fields = fields
        high_row = nest_rows + 4
        boundary = injected[:, :, 2:high_row]
        advance_fields = jnp.where(
            outside[2:high_row][None, None, :, None], boundary, advance_fields
        )
        stepped = substep(
            advance_fields,
            factor_rows[2:high_row],
            nest_courant,
            east_rows[:, 2:high_row],
            west_rows[:, 2:high_row],
        )
        nest_fields = (stepped + nudge_rate * (boundary - stepped))[:, :, 1:-1]
    block_means = nest_fields.reshape(3, levels, coarse_rows, 3, coarse_cols, 3).mean(axis=(3, 5))
    owned_rows = parent_rows * tile_index + jnp.arange(parent_rows, dtype=jnp.int32) - row_offset
    portion = lax.all_gather(block_means, "tile", axis=2, tiled=True)
    count = portion.shape[2]
    picker = (owned_rows[:, None] == jnp.arange(count, dtype=jnp.int32)[None, :]).astype(
        jnp.float32
    )
    placed = jnp.einsum("ij,vljc->vlic", picker, portion, precision=highest)
    covered = jnp.sum(picker, axis=1)
    previous = lax.dynamic_slice_in_dim(advanced, col_offset, coarse_cols, axis=3)
    merged = jnp.where(covered[None, None, :, None] > 0.5, placed, previous)
    new_parent = lax.dynamic_update_slice_in_dim(advanced, merged, col_offset, axis=3)
    return (new_parent, nest_fields[:, :, None])


def solution(mesh):
    placed = (
        P(None, None, ("grp", "tile"), None),
        P(("grp", "tile"), None),
        P(None, None, "grp", "tile", None),
        P("grp", None),
    )
    return jax.shard_map(
        local,
        mesh=mesh,
        in_specs=placed,
        out_specs=(P(None, None, ("grp", "tile"), None), P(None, None, "grp", "tile", None)),
        check_vma=False,
    )
```

profile of v0, /device:TPU:1, one launch (start us, length us, event | category | flops | bytes accessed | tf_op | source)
XLA Modules:
  0.0 293.5 jit_solution(1897532774218277156)
XLA Ops:
  8.7 4.5 %collective-permute-start = (f32[2,8,1,2048]{3,2,1,0:T(1,128)S(1)}, f32[2,8,1,2048]{3,2,1,0:T(1,128)S(1)}, u32[]{:S(2)}, u32[]{:S(2)}) collective-permute-start(f32[2,8,1,2048]{3,2,1,0:T(1,128)S(1)} %get-tuple-element.12), channel_id=1, source_target_pairs={{0,1},{1,2},{2,3},{3,4},{4,5},{5,6},{6,7},{7,8},{8,9},{9,10},{10,1... | collective-permute-start | bytes 393224 | tf_op jit(solution)/shard_map/ppermute | solution.py:22
  13.2 1.9 collective-permute-start.1
  24.7 2.4 collective-permute-start.2
  27.1 2.6 collective-permute-start.3
  30.5 56.2 %all-gather = f32[256,258]{1,0:T(8,128)S(1)} all-gather(f32[8,258]{1,0:T(8,128)S(1)} %constant_dynamic-slice_fusion), channel_id=2, replica_groups=mesh['grp'=8,'tile'=32] {'tile'}, dimensions={0}, use_global_device_ids=true | all-gather | bytes 272448 | tf_op jit(solution)/shard_map/all_gather | solution.py:76
  88.4 26.9 %all-gather.4.cloned.1.call-done = f32[3,8,256,258]{3,2,1,0:T(8,128)} async-done(((f32[3,8,8,258]{3,2,1,0:T(8,128)}), f32[3,8,256,258]{3,2,1,0:T(8,128)}) %all-gather.4.cloned.1.call-update) | async-done | bytes 6340624 | tf_op jit(solution)/shard_map/all_gather | solution.py:75
  115.3 6.7 %convolution_bitcast_fusion = f32[3,8,6,258]{3,2,1,0:T(8,128)S(1)} fusion(f32[3,8,256,258]{3,2,1,0:T(8,128)} %all-gather.4.cloned.1.call-done, s32[6]{0:T(128)S(1)} %iota_add_fusion), kind=kOutput, calls=%fused_computation.5 | convolution fusion | flops 114132480 | bytes 6489240 | tf_op jit(solution)/shard_map/kj,vljc->vlkc/dot_general | solution.py:80
  122.9 5.4 %broadcast_in_dim.70 = f32[3,8,6,256,3]{1,4,3,2,0:T(4,128)} broadcast(f32[3,8,6,256]{1,3,2,0:T(8,128)S(1)} %copy.55), dimensions={0,1,2,3} | broadcast | bytes 589824 | tf_op jit(solution)/shard_map/broadcast_in_dim | solution.py:83
  128.3 11.8 %reshape.54 = f32[3,8,6,768]{1,3,2,0:T(8,128)} reshape(f32[3,8,6,256,3]{1,4,3,2,0:T(4,128)} %broadcast_in_dim.70) | data formatting | bytes 884736 | tf_op jit(solution)/shard_map/reshape | solution.py:83
  140.1 4.6 %copy.56 = f32[3,8,6,768]{3,1,2,0:T(8,128)S(1)} copy(f32[3,8,6,768]{1,3,2,0:T(8,128)} %reshape.54) | data formatting | bytes 884736 | tf_op jit(solution)/shard_map/reshape | solution.py:83
  148.3 1.9 collective-permute-start.4
  150.2 2.6 collective-permute-start.5
  152.9 3.0 %collective-permute-done.5 = f32[3,8,1,768]{3,1,2,0:T(8,128)S(1)} collective-permute-done((f32[3,8,1,768]{3,1,2,0:T(8,128)S(1)}, f32[3,8,1,768]{3,1,2,0:T(8,128)S(1)}, u32[]{:S(2)}, u32[]{:S(2)}) %collective-permute-start.5) | collective-permute-done | bytes 73760 | tf_op jit(solution)/shard_map/ppermute | solution.py:23
  157.0 1.9 collective-permute-start.6
  158.9 2.4 collective-permute-start.7
  161.4 3.2 %collective-permute-done.7 = f32[3,8,1,768]{3,1,2,0:T(8,128)S(1)} collective-permute-done((f32[3,8,1,768]{3,1,2,0:T(8,128)S(1)}, f32[3,8,1,768]{3,1,2,0:T(8,128)S(1)}, u32[]{:S(2)}, u32[]{:S(2)}) %collective-permute-start.7) | collective-permute-done | bytes 73760 | tf_op jit(solution)/shard_map/ppermute | solution.py:23
  165.6 7.1 %copy.72 = f32[3,8,12,768]{1,3,2,0:T(8,128)} copy(f32[3,8,12,768]{3,1,2,0:T(8,128)S(1)} %fusion.10) | data formatting | bytes 1769472 | tf_op jit(solution)/shard_map/slice | solution.py:106
  172.7 21.8 %reshape.61 = f32[3,8,4,3,256,3]{1,5,4,3,2,0:T(4,128)} reshape(f32[3,8,12,768]{1,3,2,0:T(8,128)} %copy.72) | data formatting | bytes 1769472 | tf_op jit(solution)/shard_map/reshape | solution.py:107
  194.5 15.7 %reduce_sum.19 = f32[3,8,4,256]{1,3,2,0:T(8,128)} reduce(f32[3,8,4,3,256,3]{1,5,4,3,2,0:T(4,128)} %reshape.61, f32[]{:T(128)} %constant.19.clone.1), dimensions={3,5}, to_apply=%region_1.2 | reduce | flops 196608 | bytes 983044 | tf_op jit(solution)/shard_map/reduce_sum | solution.py:107
  210.2 1.8 copy.73
  215.6 1.8 copy.76
  217.5 60.4 %all-gather.6.cloned.1.call-done = f32[3,8,128,256]{3,1,0,2:T(8,128)} async-done(((f32[3,8,4,256]{3,1,0,2:T(8,128)}), f32[3,8,128,256]{3,1,0,2:T(8,128)}) %all-gather.6.cloned.1.call-update) | async-done | bytes 3145744 | tf_op jit(solution)/shard_map/all_gather | solution.py:109
  277.8 3.8 %fusion.5 = f32[3,8,8,256]{3,2,1,0:T(8,128)S(1)} fusion(f32[3,8,128,256]{3,1,0,2:T(8,128)} %all-gather.6.cloned.1.call-done, f32[3,8,8,2048]{3,2,1,0:T(8,128)} %copy-done, s32[]{:T(128)S(6)} %select_n.26, pred[8]{0:T(512)(128)(4,1)S(1)} %broadcast_compare_fusion, s32[8]{0:T(128)S(1)} %add_subtract_fusion), kind=kOutput, calls=%fused_computation.7 | convolution fusion | flops 75547648 | bytes 3538988 | tf_op jit(solution)/shard_map/ij,vljc->vlic/dot_general | solution.py:114
  281.6 5.1 %dynamic_update_slice.3 = f32[3,8,8,2048]{3,2,1,0:T(8,128)} dynamic-update-slice(f32[3,8,8,2048]{3,2,1,0:T(8,128)} %copy-done, f32[3,8,8,256]{3,2,1,0:T(8,128)S(1)} %fusion.5, s32[]{:T(128)} %constant.10.clone.1, s32[]{:T(128)} %constant.10.clone.1, s32[]{:T(128)} %constant.10.clone.1, s32[]{:T(128)S(6)} %select_n.26) | dynamic-update-slice | bytes 393220 | tf_op jit(solution)/shard_map/dynamic_update_slice | solution.py:118
  (101 shorter events, 19.6 us)
Async XLA Ops:
  7.2 9.1 %copy-start.4 = (s32[1,2]{1,0:T(1,128)S(1)}, s32[1,2]{1,0:T(1,128)}, u32[]{:S(2)}) copy-start(s32[1,2]{1,0:T(1,128)} %param.7) | copy-start | bytes 28
  7.2 11.0 %copy-start.3 = (s32[8,2048]{1,0:T(8,128)S(1)}, s32[8,2048]{1,0:T(8,128)}, u32[]{:S(2)}) copy-start(s32[8,2048]{1,0:T(8,128)} %param.5) | copy-start | bytes 196612
  7.2 108.1 %all-gather.4.cloned.1.call-start = ((), (), s32[]{:S(2)}) async-start(), calls=%async_computation | async-start | bytes 9732096 | tf_op jit(solution)/shard_map/all_gather | solution.py:75
  8.7 9.5 %collective-permute-start = (f32[2,8,1,2048]{3,2,1,0:T(1,128)S(1)}, f32[2,8,1,2048]{3,2,1,0:T(1,128)S(1)}, u32[]{:S(2)}, u32[]{:S(2)}) collective-permute-start(f32[2,8,1,2048]{3,2,1,0:T(1,128)S(1)} %get-tuple-element.12), channel_id=1, source_target_pairs={{0,1},{1,2},{2,3},{3,4},{4,5},{5,6},{6,7},{7,8},{8,9},{9,10},{10,1... | collective-permute-start | bytes 393224 | tf_op jit(solution)/shard_map/ppermute | solution.py:22
  13.2 6.3 %collective-permute-start.1 = (f32[2,8,1,2048]{3,2,1,0:T(1,128)S(1)}, f32[2,8,1,2048]{3,2,1,0:T(1,128)S(1)}, u32[]{:S(2)}, u32[]{:S(2)}) collective-permute-start(f32[2,8,1,2048]{3,2,1,0:T(1,128)S(1)} %get-tuple-element.13), channel_id=1, source_target_pairs={{1,0},{2,1},{3,2},{4,3},{5,4},{6,5},{7,6},{8,7},{9,8},{10,9},{11,1... | collective-permute-start | bytes 393224 | tf_op jit(solution)/shard_map/ppermute | solution.py:23
  21.5 2.3 copy-start.1
  21.8 1.1 copy-start
  23.8 254.0 %all-gather.6.cloned.1.call-start = ((), (), s32[]{:S(2)}) async-start(), calls=%async_computation.1 | async-start | bytes 3244032 | tf_op jit(solution)/shard_map/all_gather | solution.py:109
  24.7 120.1 %collective-permute-start.2 = (f32[3,8,1,768]{3,1,2,0:T(8,128)}, f32[3,8,1,768]{3,1,2,0:T(8,128)}, u32[]{:S(2)}, u32[]{:S(2)}) collective-permute-start(f32[3,8,1,768]{3,1,2,0:T(8,128)} %get-tuple-element.24), channel_id=1, source_target_pairs={{0,1},{1,2},{2,3},{3,4},{4,5},{5,6},{6,7},{7,8},{8,9},{9,10},{10,1... | collective-permute-start | bytes 221192 | tf_op jit(solution)/shard_map/ppermute | solution.py:22
  27.1 117.7 %collective-permute-start.3 = (f32[3,8,1,768]{3,1,2,0:T(8,128)}, f32[3,8,1,768]{3,1,2,0:T(8,128)}, u32[]{:S(2)}, u32[]{:S(2)}) collective-permute-start(f32[3,8,1,768]{3,1,2,0:T(8,128)} %get-tuple-element.25), channel_id=1, source_target_pairs={{1,0},{2,1},{3,2},{4,3},{5,4},{6,5},{7,6},{8,7},{9,8},{10,9},{11,1... | collective-permute-start | bytes 221192 | tf_op jit(solution)/shard_map/ppermute | solution.py:23
  147.1 0.8 copy-start.2
  148.3 4.6 %collective-permute-start.4 = (f32[3,8,1,768]{3,1,2,0:T(8,128)S(1)}, f32[3,8,1,768]{3,1,2,0:T(8,128)S(1)}, u32[]{:S(2)}, u32[]{:S(2)}) collective-permute-start(f32[3,8,1,768]{3,1,2,0:T(8,128)S(1)} %get-tuple-element.20), channel_id=1, source_target_pairs={{0,1},{1,2},{2,3},{3,4},{4,5},{5,6},{6,7},{7,8},{8,9},{9,10},{10,1... | collective-permute-start | bytes 221192 | tf_op jit(solution)/shard_map/ppermute | solution.py:22
  150.2 5.7 %collective-permute-start.5 = (f32[3,8,1,768]{3,1,2,0:T(8,128)S(1)}, f32[3,8,1,768]{3,1,2,0:T(8,128)S(1)}, u32[]{:S(2)}, u32[]{:S(2)}) collective-permute-start(f32[3,8,1,768]{3,1,2,0:T(8,128)S(1)} %get-tuple-element.21), channel_id=1, source_target_pairs={{1,0},{2,1},{3,2},{4,3},{5,4},{6,5},{7,6},{8,7},{9,8},{10,9},{11,1... | collective-permute-start | bytes 221192 | tf_op jit(solution)/shard_map/ppermute | solution.py:23
  157.0 4.4 %collective-permute-start.6 = (f32[3,8,1,768]{3,1,2,0:T(8,128)S(1)}, f32[3,8,1,768]{3,1,2,0:T(8,128)S(1)}, u32[]{:S(2)}, u32[]{:S(2)}) collective-permute-start(f32[3,8,1,768]{3,1,2,0:T(8,128)S(1)} %get-tuple-element.16), channel_id=1, source_target_pairs={{0,1},{1,2},{2,3},{3,4},{4,5},{5,6},{6,7},{7,8},{8,9},{9,10},{10,1... | collective-permute-start | bytes 221192 | tf_op jit(solution)/shard_map/ppermute | solution.py:22
  158.9 5.7 %collective-permute-start.7 = (f32[3,8,1,768]{3,1,2,0:T(8,128)S(1)}, f32[3,8,1,768]{3,1,2,0:T(8,128)S(1)}, u32[]{:S(2)}, u32[]{:S(2)}) collective-permute-start(f32[3,8,1,768]{3,1,2,0:T(8,128)S(1)} %get-tuple-element.17), channel_id=1, source_target_pairs={{1,0},{2,1},{3,2},{4,3},{5,4},{6,5},{7,6},{8,7},{9,8},{10,9},{11,1... | collective-permute-start | bytes 221192 | tf_op jit(solution)/shard_map/ppermute | solution.py:23
Sparse Core Ops, SparseCore 0:
  23.9 91.3 all-gather.3
  212.9 64.9 all-gather.5
where the time goes:
time: 295 us; the launch traced here: 294 us
  waiting for transfers between devices  94.8 us (32%)
  local copies, waits for them, and re-layouts  70.8 us (24%)
  blocking collectives  56.2 us (19%)
  other arithmetic  22.3 us (8%)
  starting transfers between devices  20.3 us (7%)
  between operations  18.5 us (6%)
  matrix products  10.8 us (4%)
    all_gather x1, waiting for transfers between devices, local(): portion = lax.all_gather(block_means, 'tile', axis=2, tiled=True)  60.4 us
    all_gather x1, blocking collectives, local(): lax.all_gather(factor_window, 'tile', axis=2, tiled=True)  56.2 us
    all_gather x1, waiting for transfers between devices, local(): lax.all_gather(window, 'tile', axis=2, tiled=True)  26.9 us
    reshape x1, local copies, waits for them, and re-layouts, local(): nest_fields.reshape(3, levels, coarse_rows, 3, coarse_cols, 3)  21.8 us
    reshape x2, local copies, waits for them, and re-layouts, local(): jnp.repeat(footprint[..., 1:-1], 3, axis=3)  16.4 us
    reduce_sum x1, other arithmetic, local(): nest_fields.reshape(3, levels, coarse_rows, 3, coarse_cols, 3)  15.7 us
    ppermute x4, starting transfers between devices, extended_2(): before = lax.ppermute(last, axis, up)  10.7 us
    ppermute x4, starting transfers between devices, extended_2(): after = lax.ppermute(first, axis, down)  9.47 us
  transfers between devices with their start and end apart: 10, of which 5 were waited for; matrix products, arithmetic and copies ran while one was open for 13% of the time, Pallas kernels for 0%

commit v1 on v0

v1 whole, which is shorter than its diff:
```python
import jax
import jax.numpy as jnp
from jax import lax
from jax.sharding import PartitionSpec as P

SUBSTEPS = 3


parent_courant = 0.35
nest_courant = 0.35
nudge_rate = 0.2
terrain_scale = 6000.0

HIGHEST = lax.Precision.HIGHEST


def shift_from(value, axis, offset, devices):
    pairs = [(d + offset, d) for d in range(devices) if 0 <= d + offset < devices]
    return lax.ppermute(value, axis, pairs)


def extended_2(value, sides, width):
    for axis, dim in sides:
        devices, length = (lax.axis_size(axis), value.shape[dim])
        up = [(i, (i + 1) % devices) for i in range(devices - 1)]
        down = [(j, i) for i, j in up]
        last = lax.slice_in_dim(value, length - width, length, axis=dim)
        first = lax.slice_in_dim(value, 0, width, axis=dim)
        before = lax.ppermute(last, axis, up)
        after = lax.ppermute(first, axis, down)
        value = jnp.concatenate([before, value, after], axis=dim)
    return value


def substep(fields, sound_factor, courant, east_edge, west_edge):
    pressure = fields[0]
    zonal_wind = fields[1]
    merid_wind = fields[2]
    east_side = jnp.concatenate([pressure[..., 1:], east_edge[..., None]], axis=-1)
    zonal_next = zonal_wind - courant * (east_side - pressure)
    below_side = jnp.concatenate(
        [pressure[..., 1:, :], jnp.zeros_like(pressure[..., :1, :])], axis=-2
    )
    merid_next = merid_wind - courant * (below_side - pressure)
    west_side = jnp.concatenate([west_edge[..., None], zonal_next[..., :-1]], axis=-1)
    above_side = jnp.concatenate(
        [jnp.zeros_like(merid_next[..., :1, :]), merid_next[..., :-1, :]], axis=-2
    )
    pressure_next = pressure - courant * sound_factor * (
        zonal_next - west_side + (merid_next - above_side)
    )
    return jnp.stack([pressure_next, zonal_next, merid_next])


def repeat_matrix(small, factor):
    rows = jnp.arange(small, dtype=jnp.int32)[:, None]
    cols = jnp.arange(small * factor, dtype=jnp.int32)[None, :] // factor
    return (rows == cols).astype(jnp.float32)


def local(parent_state, terrain, nest_state, nest_offsets):
    tiles = lax.axis_size("tile")
    tile_index = lax.axis_index("tile")
    levels = parent_state.shape[1]
    parent_rows = parent_state.shape[2]
    nest_rows = nest_state.shape[3]
    nest_cols = nest_state.shape[4]
    coarse_rows = nest_rows // 3
    coarse_cols = nest_cols // 3
    foot_rows = coarse_rows + 2
    assert parent_rows == 2 * coarse_rows
    band_rows = parent_rows * tiles
    nest_total = nest_rows * tiles
    coarse_total = nest_total // 3
    largest_offset = band_rows - coarse_total - 1
    largest_q = largest_offset // parent_rows
    bits = max(1, int(largest_q).bit_length())
    planes = 3 * levels

    row_offset = nest_offsets[0, 0]
    col_offset = nest_offsets[0, 1]
    q = row_offset // parent_rows
    r = row_offset - q * parent_rows

    nest_fields = nest_state[:, :, 0]
    above3 = shift_from(nest_fields[:, :, nest_rows - 3 :], "tile", -1, tiles)
    below3 = shift_from(nest_fields[:, :, :3], "tile", 1, tiles)

    sound_factor = 1.0 - terrain.astype(jnp.float32) / terrain_scale
    halo_fields = parent_state[0:3:2]
    padded = extended_2(halo_fields, ((("grp", "tile"), 2),), 1)
    zonal_ext = jnp.pad(parent_state[1], ((0, 0), (1, 1), (0, 0)))
    extended = jnp.stack([padded[0], zonal_ext, padded[1]])
    factor_ext = jnp.pad(sound_factor, ((1, 1), (0, 0)))
    edge_zeros = jnp.zeros((levels, parent_rows + 2), jnp.float32)
    advanced = substep(extended, factor_ext, parent_courant, edge_zeros, edge_zeros)[:, :, 1:-1]

    window = lax.dynamic_slice_in_dim(advanced, col_offset - 1, coarse_cols + 2, axis=3)
    factor_window = lax.dynamic_slice_in_dim(sound_factor, col_offset - 1, coarse_cols + 2, axis=1)
    rows_here = jnp.concatenate(
        [window.reshape(planes, parent_rows, coarse_cols + 2), factor_window[None]], axis=0
    )
    last_before = shift_from(rows_here[:, parent_rows - 1 :], "tile", -1, tiles)
    rows_after = shift_from(rows_here, "tile", 1, tiles)
    joined = jnp.concatenate([last_before, rows_here, rows_after], axis=1)
    block = lax.dynamic_slice_in_dim(joined, r, parent_rows + 2, axis=1)
    for k in range(bits):
        moved = shift_from(block, "tile", 1 << k, tiles)
        block = jnp.where(((q >> k) & 1) == 1, moved, block)
    half = tiles // 2
    to_even = lax.ppermute(block[:, 0:foot_rows], "tile", [(m, 2 * m) for m in range(half)])
    to_odd = lax.ppermute(
        block[:, coarse_rows : coarse_rows + foot_rows], "tile", [(m, 2 * m + 1) for m in range(half)]
    )
    footprint = jnp.where(tile_index % 2 == 0, to_even, to_odd)

    widen = repeat_matrix(coarse_cols, 3)
    heighten = repeat_matrix(foot_rows, 3).T
    inner = jnp.einsum("pic,cj->pij", footprint[:, :, 1:-1], widen, precision=HIGHEST)
    expanded = jnp.einsum("ri,pij->prj", heighten, inner, precision=HIGHEST)
    injected = expanded[:planes].reshape(3, levels, 3 * foot_rows, nest_cols)
    nest_factor = expanded[planes]
    west_rows = jnp.repeat(footprint[levels : 2 * levels, :, 0], 3, axis=1)
    east_rows = jnp.repeat(footprint[0:levels, :, -1], 3, axis=1)

    local_rows = jnp.arange(3 * foot_rows, dtype=jnp.int32) - 3
    global_rows = nest_rows * tile_index + local_rows
    outside = ((global_rows < 0) | (global_rows >= nest_total))[None, None, :, None]
    fields = jnp.concatenate([above3, nest_fields, below3], axis=2)
    for _ in range(SUBSTEPS):
        fields = jnp.where(outside, injected, fields)
        stepped = substep(fields, nest_factor, nest_courant, east_rows, west_rows)
        fields = stepped + nudge_rate * (injected - stepped)
    new_nest = fields[:, :, 3 : 3 + nest_rows]

    narrow = repeat_matrix(coarse_cols, 3).T
    shorten = repeat_matrix(coarse_rows, 3)
    col_sums = jnp.einsum("plrj,jc->plrc", new_nest, narrow, precision=HIGHEST)
    sums = jnp.einsum("kr,plrc->plkc", shorten, col_sums, precision=HIGHEST)
    means = (sums / 9.0).reshape(planes, coarse_rows, coarse_cols)

    from_even = lax.ppermute(means, "tile", [(2 * m, m) for m in range(half)])
    from_odd = lax.ppermute(means, "tile", [(2 * m + 1, m) for m in range(half)])
    back = jnp.concatenate([from_even, from_odd], axis=1)
    for k in range(bits):
        moved = shift_from(back, "tile", -(1 << k), tiles)
        back = jnp.where(((q >> k) & 1) == 1, moved, back)
    back_before = shift_from(back, "tile", -1, tiles)
    both = jnp.concatenate([back_before, back], axis=1)
    placed = lax.dynamic_slice_in_dim(both, parent_rows - r, parent_rows, axis=1)
    placed = placed.reshape(3, levels, parent_rows, coarse_cols)
    band_row = parent_rows * tile_index + jnp.arange(parent_rows, dtype=jnp.int32) - row_offset
    covered = ((band_row >= 0) & (band_row < coarse_total))[None, None, :, None]
    previous = lax.dynamic_slice_in_dim(advanced, col_offset, coarse_cols, axis=3)
    merged = jnp.where(covered, placed, previous)
    new_parent = lax.dynamic_update_slice_in_dim(advanced, merged, col_offset, axis=3)
    return (new_parent, new_nest[:, :, None])


def solution(mesh):
    placed = (
        P(None, None, ("grp", "tile"), None),
        P(("grp", "tile"), None),
        P(None, None, "grp", "tile", None),
        P("grp", None),
    )
    return jax.shard_map(
        local,
        mesh=mesh,
        in_specs=placed,
        out_specs=(P(None, None, ("grp", "tile"), None), P(None, None, "grp", "tile", None)),
        check_vma=False,
    )
```

time: 295 us -> 251 us (0.85)
  the two profiles are of different devices: /device:TPU:1 before, /device:TPU:96 now
where the time goes in v1:
time: 251 us; the launch traced here: 250 us
  waiting for transfers between devices  152 us (61%)
  starting transfers between devices  55.8 us (22%)
  local copies, waits for them, and re-layouts  22 us (9%)
  other arithmetic  10.4 us (4%)
  between operations  7.6 us (3%)
    ppermute x13, waiting for transfers between devices, shift_from(): return lax.ppermute(value, axis, pairs)  112 us
    ppermute x13, starting transfers between devices, shift_from(): return lax.ppermute(value, axis, pairs)  35.6 us
    ppermute x1, waiting for transfers between devices, local(): lax.ppermute(block[:, 0:foot_rows], 'tile', [(m, 2 * m) for m in range(ha...  26.4 us
    ppermute x1, waiting for transfers between devices, local(): lax.ppermute(means, 'tile', [(2 * m + 1, m) for m in range(half)])  7.15 us
    ppermute x1, starting transfers between devices, extended_2(): after = lax.ppermute(first, axis, down)  6.65 us
    ppermute x1, starting transfers between devices, local(): lax.ppermute(block[:, coarse_rows:coarse_rows + foot_rows], 'tile', [(m,...  6.33 us
    unnamed x28, local copies, waits for them, and re-layouts  5.27 us
    ppermute x1, waiting for transfers between devices, local(): lax.ppermute(block[:, coarse_rows:coarse_rows + foot_rows], 'tile', [(m,...  5.2 us
  transfers between devices with their start and end apart: 19, of which 14 were waited for; matrix products, arithmetic and copies ran while one was open for 4% of the time, Pallas kernels for 0%

profile of v1, /device:TPU:96, one launch (start us, length us, event | category | flops | bytes accessed | tf_op | source)
XLA Modules:
  0.0 249.9 jit_solution(5489087046833316981)
XLA Ops:
  2.2 1.9 collective-permute-start
  4.1 6.7 %collective-permute-start.1 = (f32[2,8,1,2048]{3,2,1,0:T(1,128)S(1)}, f32[2,8,1,2048]{3,2,1,0:T(1,128)S(1)}, u32[]{:S(2)}, u32[]{:S(2)}) collective-permute-start(f32[2,8,1,2048]{3,2,1,0:T(1,128)S(1)} %get-tuple-element.15), channel_id=1, source_target_pairs={{1,0},{2,1},{3,2},{4,3},{5,4},{6,5},{7,6},{8,7},{9,8},{10,9},{11,1... | collective-permute-start | bytes 393224 | tf_op jit(solution)/shard_map/ppermute | solution.py:30
  17.4 6.3 %collective-permute-start.3 = (f32[25,8,258]{2,1,0:T(8,128)S(1)}, f32[25,8,258]{2,1,0:T(8,128)S(1)}, u32[]{:S(2)}, u32[]{:S(2)}) collective-permute-start(f32[25,8,258]{2,1,0:T(8,128)S(1)} %pad_maximum_fusion.15), channel_id=1, source_target_pairs={{1,0},{2,1},{3,2},{4,3},{5,4},{6,5},{7,6},{8,7},{9,8},{10,9},{11,1... | collective-permute-start | bytes 619208 | tf_op jit(solution)/shard_map/ppermute | solution.py:19
  28.9 3.2 %collective-permute-done.2 = f32[25,1,258]{2,1,0:T(1,128)S(1)} collective-permute-done((f32[25,1,258]{2,1,0:T(1,128)S(1)}, f32[25,1,258]{2,1,0:T(1,128)S(1)}, u32[]{:S(2)}, u32[]{:S(2)}) %collective-permute-start.2) | collective-permute-done | bytes 25832 | tf_op jit(solution)/shard_map/ppermute | solution.py:19
  32.2 3.5 %collective-permute-start.4 = (f32[25,10,258]{2,0,1:T(8,128)S(1)}, f32[25,10,258]{2,0,1:T(8,128)S(1)}, u32[]{:S(2)}, u32[]{:S(2)}) collective-permute-start(f32[25,10,258]{2,0,1:T(8,128)S(1)} %fusion.9), channel_id=1, source_target_pairs={{1,0},{2,1},{3,2},{4,3},{5,4},{6,5},{7,6},{8,7},{9,8},{10,9},{11,1... | collective-permute-start | bytes 774008 | tf_op jit(solution)/shard_map/ppermute | solution.py:19
  35.8 6.4 %collective-permute-done.4 = f32[25,10,258]{2,0,1:T(8,128)S(1)} collective-permute-done((f32[25,10,258]{2,0,1:T(8,128)S(1)}, f32[25,10,258]{2,0,1:T(8,128)S(1)}, u32[]{:S(2)}, u32[]{:S(2)}) %collective-permute-start.4) | collective-permute-done | bytes 258032 | tf_op jit(solution)/shard_map/ppermute | solution.py:19
  42.2 1.9 collective-permute-start.5
  44.1 16.4 %collective-permute-done.5 = f32[25,10,258]{2,0,1:T(8,128)S(1)} collective-permute-done((f32[25,10,258]{2,0,1:T(8,128)S(1)}, f32[25,10,258]{2,0,1:T(8,128)S(1)}, u32[]{:S(2)}, u32[]{:S(2)}) %collective-permute-start.5) | collective-permute-done | bytes 258032 | tf_op jit(solution)/shard_map/ppermute | solution.py:19
  60.5 1.9 collective-permute-start.6
  62.6 21.5 %collective-permute-done.6 = f32[25,10,258]{2,0,1:T(8,128)S(1)} collective-permute-done((f32[25,10,258]{2,0,1:T(8,128)S(1)}, f32[25,10,258]{2,0,1:T(8,128)S(1)}, u32[]{:S(2)}, u32[]{:S(2)}) %collective-permute-start.6) | collective-permute-done | bytes 258032 | tf_op jit(solution)/shard_map/ppermute | solution.py:19
  88.1 6.7 %collective-permute-start.11 = (f32[3,8,3,768]{3,1,2,0:T(8,128)S(1)}, f32[3,8,3,768]{3,1,2,0:T(8,128)S(1)}, u32[]{:S(2)}, u32[]{:S(2)}) collective-permute-start(f32[3,8,3,768]{3,1,2,0:T(8,128)S(1)} %get-tuple-element.17), channel_id=1, source_target_pairs={{1,0},{2,1},{3,2},{4,3},{5,4},{6,5},{7,6},{8,7},{9,8},{10,9},{11,1... | collective-permute-start | bytes 663560 | tf_op jit(solution)/shard_map/ppermute | solution.py:19
  95.4 18.4 %collective-permute-done.7 = f32[25,10,258]{2,0,1:T(8,128)S(1)} collective-permute-done((f32[25,10,258]{2,0,1:T(8,128)S(1)}, f32[25,10,258]{2,0,1:T(8,128)S(1)}, u32[]{:S(2)}, u32[]{:S(2)}) %collective-permute-start.7) | collective-permute-done | bytes 258032 | tf_op jit(solution)/shard_map/ppermute | solution.py:19
  113.9 6.3 %collective-permute-start.9 = (f32[25,6,258]{2,0,1:T(8,128)S(1)}, f32[25,6,258]{2,0,1:T(8,128)S(1)}, u32[]{:S(2)}, u32[]{:S(2)}) collective-permute-start(f32[25,6,258]{2,0,1:T(8,128)S(1)} %get-tuple-element.18), channel_id=1, source_target_pairs={{0,1},{1,3},{2,5},{3,7},{4,9},{5,11},{6,13},{7,15},{8,17},{9,19},{... | collective-permute-start | bytes 464408 | tf_op jit(solution)/shard_map/ppermute | solution.py:112
  120.2 2.1 collective-permute-start.8
  122.4 5.2 %collective-permute-done.9 = f32[25,6,258]{2,0,1:T(8,128)S(1)} collective-permute-done((f32[25,6,258]{2,0,1:T(8,128)S(1)}, f32[25,6,258]{2,0,1:T(8,128)S(1)}, u32[]{:S(2)}, u32[]{:S(2)}) %collective-permute-start.9) | collective-permute-done | bytes 154832 | tf_op jit(solution)/shard_map/ppermute | solution.py:112
  127.6 26.4 %collective-permute-done.8 = f32[25,6,258]{2,0,1:T(8,128)S(1)} collective-permute-done((f32[25,6,258]{2,0,1:T(8,128)S(1)}, f32[25,6,258]{2,0,1:T(8,128)S(1)}, u32[]{:S(2)}, u32[]{:S(2)}) %collective-permute-start.8) | collective-permute-done | bytes 154832 | tf_op jit(solution)/shard_map/ppermute | solution.py:111
  173.3 1.9 collective-permute-start.12
  175.2 7.2 %collective-permute-done.13 = f32[24,4,256]{2,1,0:T(4,128)S(1)} collective-permute-done((f32[24,4,256]{2,1,0:T(4,128)S(1)}, f32[24,4,256]{2,1,0:T(4,128)S(1)}, u32[]{:S(2)}, u32[]{:S(2)}) %collective-permute-start.13) | collective-permute-done | bytes 98336 | tf_op jit(solution)/shard_map/ppermute | solution.py:143
  185.2 10.2 %collective-permute-done.14 = f32[24,8,256]{2,1,0:T(8,128)S(1)} collective-permute-done((f32[24,8,256]{2,1,0:T(8,128)S(1)}, f32[24,8,256]{2,1,0:T(8,128)S(1)}, u32[]{:S(2)}, u32[]{:S(2)}) %collective-permute-start.14) | collective-permute-done | bytes 196640 | tf_op jit(solution)/shard_map/ppermute | solution.py:19
  197.3 16.8 %collective-permute-done.15 = f32[24,8,256]{2,1,0:T(8,128)S(1)} collective-permute-done((f32[24,8,256]{2,1,0:T(8,128)S(1)}, f32[24,8,256]{2,1,0:T(8,128)S(1)}, u32[]{:S(2)}, u32[]{:S(2)}) %collective-permute-start.15) | collective-permute-done | bytes 196640 | tf_op jit(solution)/shard_map/ppermute | solution.py:19
  216.0 9.0 %collective-permute-done.16 = f32[24,8,256]{2,1,0:T(8,128)S(1)} collective-permute-done((f32[24,8,256]{2,1,0:T(8,128)S(1)}, f32[24,8,256]{2,1,0:T(8,128)S(1)}, u32[]{:S(2)}, u32[]{:S(2)}) %collective-permute-start.16) | collective-permute-done | bytes 196640 | tf_op jit(solution)/shard_map/ppermute | solution.py:19
  229.5 4.0 %collective-permute-done.17 = f32[24,8,256]{2,1,0:T(8,128)S(1)} collective-permute-done((f32[24,8,256]{2,1,0:T(8,128)S(1)}, f32[24,8,256]{2,1,0:T(8,128)S(1)}, u32[]{:S(2)}, u32[]{:S(2)}) %collective-permute-start.17) | collective-permute-done | bytes 196640 | tf_op jit(solution)/shard_map/ppermute | solution.py:19
  237.4 6.2 %collective-permute-done.18 = f32[24,8,256]{2,1,0:T(8,128)S(1)} collective-permute-done((f32[24,8,256]{2,1,0:T(8,128)S(1)}, f32[24,8,256]{2,1,0:T(8,128)S(1)}, u32[]{:S(2)}, u32[]{:S(2)}) %collective-permute-start.18) | collective-permute-done | bytes 196640 | tf_op jit(solution)/shard_map/ppermute | solution.py:19
  244.8 5.1 %dynamic_update_slice.3 = f32[3,8,8,2048]{3,2,1,0:T(8,128)} dynamic-update-slice(f32[3,8,8,2048]{3,2,1,0:T(8,128)} %copy-done.2, f32[3,8,8,256]{3,2,1,0:T(8,128)S(1)} %dynamic-slice_select_fusion, s32[]{:T(128)} %constant.78.clone.1, s32[]{:T(128)} %constant.78.clone.1, s32[]{:T(128)} %constant.78.clone.1, s32[]{:T(128)S(6)} %select_n.161) | dynamic-update-slice | bytes 393220 | tf_op jit(solution)/shard_map/dynamic_update_slice | solution.py:156
  (123 shorter events, 47.3 us)
Async XLA Ops:
  0.6 11.2 %copy-start.8 = (s32[8,2048]{1,0:T(8,128)S(1)}, s32[8,2048]{1,0:T(8,128)}, u32[]{:S(2)}) copy-start(s32[8,2048]{1,0:T(8,128)} %param.5) | copy-start | bytes 196612
  2.0 9.9 %copy-start.11 = (s32[1,2]{1,0:T(1,128)S(1)}, s32[1,2]{1,0:T(1,128)}, u32[]{:S(2)}) copy-start(s32[1,2]{1,0:T(1,128)} %param.7) | copy-start | bytes 28
  2.2 11.7 %collective-permute-start = (f32[2,8,1,2048]{3,2,1,0:T(1,128)S(1)}, f32[2,8,1,2048]{3,2,1,0:T(1,128)S(1)}, u32[]{:S(2)}, u32[]{:S(2)}) collective-permute-start(f32[2,8,1,2048]{3,2,1,0:T(1,128)S(1)} %get-tuple-element.14), channel_id=1, source_target_pairs={{0,1},{1,2},{2,3},{3,4},{4,5},{5,6},{6,7},{7,8},{8,9},{9,10},{10,1... | collective-permute-start | bytes 393224 | tf_op jit(solution)/shard_map/ppermute | solution.py:29
  4.1 9.7 %collective-permute-start.1 = (f32[2,8,1,2048]{3,2,1,0:T(1,128)S(1)}, f32[2,8,1,2048]{3,2,1,0:T(1,128)S(1)}, u32[]{:S(2)}, u32[]{:S(2)}) collective-permute-start(f32[2,8,1,2048]{3,2,1,0:T(1,128)S(1)} %get-tuple-element.15), channel_id=1, source_target_pairs={{1,0},{2,1},{3,2},{4,3},{5,4},{6,5},{7,6},{8,7},{9,8},{10,9},{11,1... | collective-permute-start | bytes 393224 | tf_op jit(solution)/shard_map/ppermute | solution.py:30
  17.4 14.6 %collective-permute-start.3 = (f32[25,8,258]{2,1,0:T(8,128)S(1)}, f32[25,8,258]{2,1,0:T(8,128)S(1)}, u32[]{:S(2)}, u32[]{:S(2)}) collective-permute-start(f32[25,8,258]{2,1,0:T(8,128)S(1)} %pad_maximum_fusion.15), channel_id=1, source_target_pairs={{1,0},{2,1},{3,2},{4,3},{5,4},{6,5},{7,6},{8,7},{9,8},{10,9},{11,1... | collective-permute-start | bytes 619208 | tf_op jit(solution)/shard_map/ppermute | solution.py:19
  23.7 8.3 %collective-permute-start.2 = (f32[25,1,258]{2,1,0:T(1,128)S(1)}, f32[25,1,258]{2,1,0:T(1,128)S(1)}, u32[]{:S(2)}, u32[]{:S(2)}) collective-permute-start(f32[25,1,258]{2,1,0:T(1,128)S(1)} %fusion.52), channel_id=1, source_target_pairs={{0,1},{1,2},{2,3},{3,4},{4,5},{5,6},{6,7},{7,8},{8,9},{9,10},{10,1... | collective-permute-start | bytes 77408 | tf_op jit(solution)/shard_map/ppermute | solution.py:19
  32.2 9.9 %collective-permute-start.4 = (f32[25,10,258]{2,0,1:T(8,128)S(1)}, f32[25,10,258]{2,0,1:T(8,128)S(1)}, u32[]{:S(2)}, u32[]{:S(2)}) collective-permute-start(f32[25,10,258]{2,0,1:T(8,128)S(1)} %fusion.9), channel_id=1, source_target_pairs={{1,0},{2,1},{3,2},{4,3},{5,4},{6,5},{7,6},{8,7},{9,8},{10,9},{11,1... | collective-permute-start | bytes 774008 | tf_op jit(solution)/shard_map/ppermute | solution.py:19
  35.8 26.7 %copy-start.7 = (f32[3,8,1,12,768]{4,2,3,1,0:T(1,128)S(1)}, f32[3,8,1,12,768]{4,2,3,1,0:T(1,128)}, u32[]{:S(2)}) copy-start(f32[3,8,1,12,768]{4,2,3,1,0:T(1,128)} %param.6) | copy-start | bytes 2654212
  42.2 18.3 %collective-permute-start.5 = (f32[25,10,258]{2,0,1:T(8,128)S(1)}, f32[25,10,258]{2,0,1:T(8,128)S(1)}, u32[]{:S(2)}, u32[]{:S(2)}) collective-permute-start(f32[25,10,258]{2,0,1:T(8,128)S(1)} %broadcast_select_fusion), channel_id=1, source_target_pairs={{2,0},{3,1},{4,2},{5,3},{6,4},{7,5},{8,6},{9,7},{10,8},{11,9},{12,... | collective-permute-start | bytes 774008 | tf_op jit(solution)/shard_map/ppermute | solution.py:19
  60.5 23.6 %collective-permute-start.6 = (f32[25,10,258]{2,0,1:T(8,128)S(1)}, f32[25,10,258]{2,0,1:T(8,128)S(1)}, u32[]{:S(2)}, u32[]{:S(2)}) collective-permute-start(f32[25,10,258]{2,0,1:T(8,128)S(1)} %broadcast_select_fusion.1), channel_id=1, source_target_pairs={{4,0},{5,1},{6,2},{7,3},{8,4},{9,5},{10,6},{11,7},{12,8},{13,9},{1... | collective-permute-start | bytes 774008 | tf_op jit(solution)/shard_map/ppermute | solution.py:19
  62.6 23.5 %copy-start = (f32[3,8,1,12,768]{4,1,3,2,0:T(8,128)}, f32[3,8,1,12,768]{4,1,3,2,0:T(8,128)S(1)}, u32[]{:S(2)}) copy-start(f32[3,8,1,12,768]{4,1,3,2,0:T(8,128)S(1)} %copy.68) | copy-start | bytes 2654212
  84.2 29.6 %collective-permute-start.7 = (f32[25,10,258]{2,0,1:T(8,128)S(1)}, f32[25,10,258]{2,0,1:T(8,128)S(1)}, u32[]{:S(2)}, u32[]{:S(2)}) collective-permute-start(f32[25,10,258]{2,0,1:T(8,128)S(1)} %broadcast_select_fusion.2), channel_id=1, source_target_pairs={{8,0},{9,1},{10,2},{11,3},{12,4},{13,5},{14,6},{15,7},{16,8},{17,9... | collective-permute-start | bytes 774008 | tf_op jit(solution)/shard_map/ppermute | solution.py:19
  86.2 72.3 %collective-permute-start.10 = (f32[3,8,3,768]{3,1,2,0:T(8,128)S(1)}, f32[3,8,3,768]{3,1,2,0:T(8,128)S(1)}, u32[]{:S(2)}, u32[]{:S(2)}) collective-permute-start(f32[3,8,3,768]{3,1,2,0:T(8,128)S(1)} %get-tuple-element.16), channel_id=1, source_target_pairs={{0,1},{1,2},{2,3},{3,4},{4,5},{5,6},{6,7},{7,8},{8,9},{9,10},{10,1... | collective-permute-start | bytes 663560 | tf_op jit(solution)/shard_map/ppermute | solution.py:19
  88.1 70.3 %collective-permute-start.11 = (f32[3,8,3,768]{3,1,2,0:T(8,128)S(1)}, f32[3,8,3,768]{3,1,2,0:T(8,128)S(1)}, u32[]{:S(2)}, u32[]{:S(2)}) collective-permute-start(f32[3,8,3,768]{3,1,2,0:T(8,128)S(1)} %get-tuple-element.17), channel_id=1, source_target_pairs={{1,0},{2,1},{3,2},{4,3},{5,4},{6,5},{7,6},{8,7},{9,8},{10,9},{11,1... | collective-permute-start | bytes 663560 | tf_op jit(solution)/shard_map/ppermute | solution.py:19
  113.9 13.7 %collective-permute-start.9 = (f32[25,6,258]{2,0,1:T(8,128)S(1)}, f32[25,6,258]{2,0,1:T(8,128)S(1)}, u32[]{:S(2)}, u32[]{:S(2)}) collective-permute-start(f32[25,6,258]{2,0,1:T(8,128)S(1)} %get-tuple-element.18), channel_id=1, source_target_pairs={{0,1},{1,3},{2,5},{3,7},{4,9},{5,11},{6,13},{7,15},{8,17},{9,19},{... | collective-permute-start | bytes 464408 | tf_op jit(solution)/shard_map/ppermute | solution.py:112
  120.2 33.7 %collective-permute-start.8 = (f32[25,6,258]{2,0,1:T(8,128)S(1)}, f32[25,6,258]{2,0,1:T(8,128)S(1)}, u32[]{:S(2)}, u32[]{:S(2)}) collective-permute-start(f32[25,6,258]{2,0,1:T(8,128)S(1)} %get-tuple-element.19), channel_id=1, source_target_pairs={{0,0},{1,2},{2,4},{3,6},{4,8},{5,10},{6,12},{7,14},{8,16},{9,18},{... | collective-permute-start | bytes 464408 | tf_op jit(solution)/shard_map/ppermute | solution.py:111
  122.4 36.1 %copy-start.9 = (pred[18]{0:T(512)(128)(4,1)}, pred[18]{0:T(512)(128)(4,1)S(1)}, u32[]{:S(2)}) copy-start(pred[18]{0:T(512)(128)(4,1)S(1)} %compare_or_fusion) | copy-start | bytes 58
  172.0 10.4 %collective-permute-start.13 = (f32[24,4,256]{2,1,0:T(4,128)S(1)}, f32[24,4,256]{2,1,0:T(4,128)S(1)}, u32[]{:S(2)}, u32[]{:S(2)}) collective-permute-start(f32[24,4,256]{2,1,0:T(4,128)S(1)} %bitcast.145), channel_id=1, source_target_pairs={{1,0},{3,1},{5,2},{7,3},{9,4},{11,5},{13,6},{15,7},{17,8},{19,9},{... | collective-permute-start | bytes 294920 | tf_op jit(solution)/shard_map/ppermute | solution.py:143
  173.3 9.9 %collective-permute-start.12 = (f32[24,4,256]{2,1,0:T(4,128)S(1)}, f32[24,4,256]{2,1,0:T(4,128)S(1)}, u32[]{:S(2)}, u32[]{:S(2)}) collective-permute-start(f32[24,4,256]{2,1,0:T(4,128)S(1)} %bitcast.146), channel_id=1, source_target_pairs={{0,0},{2,1},{4,2},{6,3},{8,4},{10,5},{12,6},{14,7},{16,8},{18,9},{... | collective-permute-start | bytes 294920 | tf_op jit(solution)/shard_map/ppermute | solution.py:142
  183.2 12.1 %collective-permute-start.14 = (f32[24,8,256]{2,1,0:T(8,128)S(1)}, f32[24,8,256]{2,1,0:T(8,128)S(1)}, u32[]{:S(2)}, u32[]{:S(2)}) collective-permute-start(f32[24,8,256]{2,1,0:T(8,128)S(1)} %pad_maximum_fusion.16), channel_id=1, source_target_pairs={{0,1},{1,2},{2,3},{3,4},{4,5},{5,6},{6,7},{7,8},{8,9},{9,10},{10,1... | collective-permute-start | bytes 589832 | tf_op jit(solution)/shard_map/ppermute | solution.py:19
  195.4 18.7 %collective-permute-start.15 = (f32[24,8,256]{2,1,0:T(8,128)S(1)}, f32[24,8,256]{2,1,0:T(8,128)S(1)}, u32[]{:S(2)}, u32[]{:S(2)}) collective-permute-start(f32[24,8,256]{2,1,0:T(8,128)S(1)} %broadcast_select_fusion.5), channel_id=1, source_target_pairs={{0,2},{1,3},{2,4},{3,5},{4,6},{5,7},{6,8},{7,9},{8,10},{9,11},{10,... | collective-permute-start | bytes 589832 | tf_op jit(solution)/shard_map/ppermute | solution.py:19
  214.1 11.0 %collective-permute-start.16 = (f32[24,8,256]{2,1,0:T(8,128)S(1)}, f32[24,8,256]{2,1,0:T(8,128)S(1)}, u32[]{:S(2)}, u32[]{:S(2)}) collective-permute-start(f32[24,8,256]{2,1,0:T(8,128)S(1)} %broadcast_select_fusion.6), channel_id=1, source_target_pairs={{0,4},{1,5},{2,6},{3,7},{4,8},{5,9},{6,10},{7,11},{8,12},{9,13},{1... | collective-permute-start | bytes 589832 | tf_op jit(solution)/shard_map/ppermute | solution.py:19
  225.1 8.5 %collective-permute-start.17 = (f32[24,8,256]{2,1,0:T(8,128)S(1)}, f32[24,8,256]{2,1,0:T(8,128)S(1)}, u32[]{:S(2)}, u32[]{:S(2)}) collective-permute-start(f32[24,8,256]{2,1,0:T(8,128)S(1)} %broadcast_select_fusion.7), channel_id=1, source_target_pairs={{0,8},{1,9},{2,10},{3,11},{4,12},{5,13},{6,14},{7,15},{8,16},{9,17... | collective-permute-start | bytes 589832 | tf_op jit(solution)/shard_map/ppermute | solution.py:19
  233.6 10.0 %collective-permute-start.18 = (f32[24,8,256]{2,1,0:T(8,128)S(1)}, f32[24,8,256]{2,1,0:T(8,128)S(1)}, u32[]{:S(2)}, u32[]{:S(2)}) collective-permute-start(f32[24,8,256]{2,1,0:T(8,128)S(1)} %broadcast_select_fusion.8), channel_id=1, source_target_pairs={{0,1},{1,2},{2,3},{3,4},{4,5},{5,6},{6,7},{7,8},{8,9},{9,10},{10,1... | collective-permute-start | bytes 589832 | tf_op jit(solution)/shard_map/ppermute | solution.py:19
  (8 other events, 8.3 us)

commit v2 on v1

--- a/solution.py
+++ b/solution.py
@@ -58,6 +58,17 @@
     return (rows == cols).astype(jnp.float32)
 
 
+def barrel(value, amount, digits, direction, tiles):
+    for j in range(digits):
+        digit = (amount >> (2 * j)) & 3
+        step = 4**j
+        moved = [shift_from(value, "tile", direction * k * step, tiles) for k in (1, 2, 3)]
+        value = jnp.where(
+            digit == 0, value, jnp.where(digit == 1, moved[0], jnp.where(digit == 2, moved[1], moved[2]))
+        )
+    return value
+
+
 def local(parent_state, terrain, nest_state, nest_offsets):
     tiles = lax.axis_size("tile")
     tile_index = lax.axis_index("tile")
@@ -68,14 +79,15 @@
     coarse_rows = nest_rows // 3
     coarse_cols = nest_cols // 3
     foot_rows = coarse_rows + 2
-    assert parent_rows == 2 * coarse_rows
+    assert parent_rows == 2 * coarse_rows and 2 * levels <= coarse_cols
     band_rows = parent_rows * tiles
     nest_total = nest_rows * tiles
     coarse_total = nest_total // 3
     largest_offset = band_rows - coarse_total - 1
     largest_q = largest_offset // parent_rows
-    bits = max(1, int(largest_q).bit_length())
+    digits = max(1, (int(largest_q).bit_length() + 1) // 2)
     planes = 3 * levels
+    half = tiles // 2
 
     row_offset = nest_offsets[0, 0]
     col_offset = nest_offsets[0, 1]
@@ -96,32 +108,40 @@
     advanced = substep(extended, factor_ext, parent_courant, edge_zeros, edge_zeros)[:, :, 1:-1]
 
     window = lax.dynamic_slice_in_dim(advanced, col_offset - 1, coarse_cols + 2, axis=3)
-    factor_window = lax.dynamic_slice_in_dim(sound_factor, col_offset - 1, coarse_cols + 2, axis=1)
+    factor_window = lax.dynamic_slice_in_dim(sound_factor, col_offset, coarse_cols, axis=1)
+    east_col = window[0, :, :, -1].T
+    west_col = window[1, :, :, 0].T
+    edge_plane = jnp.concatenate(
+        [east_col, west_col, jnp.zeros((parent_rows, coarse_cols - 2 * levels), jnp.float32)], axis=1
+    )
     rows_here = jnp.concatenate(
-        [window.reshape(planes, parent_rows, coarse_cols + 2), factor_window[None]], axis=0
+        [
+            window[..., 1:-1].reshape(planes, parent_rows, coarse_cols),
+            factor_window[None],
+            edge_plane[None],
+        ],
+        axis=0,
     )
-    last_before = shift_from(rows_here[:, parent_rows - 1 :], "tile", -1, tiles)
+    above3, below3, rows_here = lax.optimization_barrier((above3, below3, rows_here))
+    last_before = shift_from(rows_here[:, parent_rows - 1], "tile", -1, tiles)
     rows_after = shift_from(rows_here, "tile", 1, tiles)
-    joined = jnp.concatenate([last_before, rows_here, rows_after], axis=1)
-    block = lax.dynamic_slice_in_dim(joined, r, parent_rows + 2, axis=1)
-    for k in range(bits):
-        moved = shift_from(block, "tile", 1 << k, tiles)
-        block = jnp.where(((q >> k) & 1) == 1, moved, block)
-    half = tiles // 2
-    to_even = lax.ppermute(block[:, 0:foot_rows], "tile", [(m, 2 * m) for m in range(half)])
-    to_odd = lax.ppermute(
-        block[:, coarse_rows : coarse_rows + foot_rows], "tile", [(m, 2 * m + 1) for m in range(half)]
-    )
-    footprint = jnp.where(tile_index % 2 == 0, to_even, to_odd)
+    joined = jnp.concatenate([last_before[:, None], rows_here, rows_after], axis=1)
+    block = lax.dynamic_slice_in_dim(joined, r, parent_rows, axis=1)
+    block = barrel(block, q, digits, 1, tiles)
+    to_even = lax.ppermute(block, "tile", [(m, 2 * m) for m in range(half)])
+    to_odd = lax.ppermute(block, "tile", [(m, 2 * m + 1) for m in range(half)])
+    next_odd = lax.ppermute(block, "tile", [(m + 1, 2 * m + 1) for m in range(half)])
+    odd_rows = jnp.concatenate([to_odd[:, coarse_rows:], next_odd[:, : foot_rows - coarse_rows]], axis=1)
+    footprint = jnp.where(tile_index % 2 == 0, to_even[:, :foot_rows], odd_rows)
 
     widen = repeat_matrix(coarse_cols, 3)
     heighten = repeat_matrix(foot_rows, 3).T
-    inner = jnp.einsum("pic,cj->pij", footprint[:, :, 1:-1], widen, precision=HIGHEST)
+    inner = jnp.einsum("pic,cj->pij", footprint[: planes + 1], widen, precision=HIGHEST)
     expanded = jnp.einsum("ri,pij->prj", heighten, inner, precision=HIGHEST)
     injected = expanded[:planes].reshape(3, levels, 3 * foot_rows, nest_cols)
     nest_factor = expanded[planes]
-    west_rows = jnp.repeat(footprint[levels : 2 * levels, :, 0], 3, axis=1)
-    east_rows = jnp.repeat(footprint[0:levels, :, -1], 3, axis=1)
+    east_rows = jnp.repeat(footprint[planes + 1, :, 0:levels].T, 3, axis=1)
+    west_rows = jnp.repeat(footprint[planes + 1, :, levels : 2 * levels].T, 3, axis=1)
 
     local_rows = jnp.arange(3 * foot_rows, dtype=jnp.int32) - 3
     global_rows = nest_rows * tile_index + local_rows
@@ -136,19 +156,17 @@
     narrow = repeat_matrix(coarse_cols, 3).T
     shorten = repeat_matrix(coarse_rows, 3)
     col_sums = jnp.einsum("plrj,jc->plrc", new_nest, narrow, precision=HIGHEST)
-    sums = jnp.einsum("kr,plrc->plkc", shorten, col_sums, precision=HIGHEST)
-    means = (sums / 9.0).reshape(planes, coarse_rows, coarse_cols)
+    sums = jnp.einsum("kr,plrc->kplc", shorten, col_sums, precision=HIGHEST)
+    means = (sums / 9.0).reshape(coarse_rows, planes, coarse_cols)
 
-    from_even = lax.ppermute(means, "tile", [(2 * m, m) for m in range(half)])
-    from_odd = lax.ppermute(means, "tile", [(2 * m + 1, m) for m in range(half)])
-    back = jnp.concatenate([from_even, from_odd], axis=1)
-    for k in range(bits):
-        moved = shift_from(back, "tile", -(1 << k), tiles)
-        back = jnp.where(((q >> k) & 1) == 1, moved, back)
-    back_before = shift_from(back, "tile", -1, tiles)
-    both = jnp.concatenate([back_before, back], axis=1)
-    placed = lax.dynamic_slice_in_dim(both, parent_rows - r, parent_rows, axis=1)
-    placed = placed.reshape(3, levels, parent_rows, coarse_cols)
+    gathered = [
+        lax.ppermute(means, "tile", [(2 * m + k, m) for m in range(half + 1) if 0 <= 2 * m + k < tiles])
+        for k in (-2, -1, 0, 1)
+    ]
+    both = jnp.concatenate(gathered, axis=0)
+    back = lax.dynamic_slice_in_dim(both, parent_rows - r, parent_rows, axis=0)
+    back = barrel(back, q, digits, -1, tiles)
+    placed = jnp.transpose(back, (1, 0, 2)).reshape(3, levels, parent_rows, coarse_cols)
     band_row = parent_rows * tile_index + jnp.arange(parent_rows, dtype=jnp.int32) - row_offset
     covered = ((band_row >= 0) & (band_row < coarse_total))[None, None, :, None]
     previous = lax.dynamic_slice_in_dim(advanced, col_offset, coarse_cols, axis=3)

time: 251 us -> 240 us (0.956)
  the two profiles are of different devices: /device:TPU:96 before, /device:TPU:36 now
where the time goes in v2:
time: 240 us; the launch traced here: 239 us
  starting transfers between devices  107 us (45%)
  waiting for transfers between devices  91.4 us (38%)
  local copies, waits for them, and re-layouts  19.5 us (8%)
  other arithmetic  10.8 us (4%)
  between operations  7.87 us (3%)
  matrix products  2.42 us (1%)
    ppermute x16, starting transfers between devices, shift_from(): return lax.ppermute(value, axis, pairs)  83.9 us
    ppermute x16, waiting for transfers between devices, shift_from(): return lax.ppermute(value, axis, pairs)  64.9 us
    ppermute x4, waiting for transfers between devices, local(): lax.ppermute(means, 'tile', [(2 * m + k, m) for m in range(half + 1) if 0...  14.1 us
    ppermute x1, waiting for transfers between devices, local(): to_odd = lax.ppermute(block, 'tile', [(m, 2 * m + 1) for m in range(half)])  9.53 us
    unnamed x30, local copies, waits for them, and re-layouts  6.89 us
    ppermute x4, starting transfers between devices, local(): lax.ppermute(means, 'tile', [(2 * m + k, m) for m in range(half + 1) if 0...  6.43 us
    dynamic_update_slice x1, local copies, waits for them, and re-layouts, local(): lax.dynamic_update_slice_in_dim(advanced, merged, col_offset, axis=3)  5.09 us
  transfers between devices with their start and end apart: 25, of which 12 were waited for; matrix products, arithmetic and copies ran while one was open for 3% of the time, Pallas kernels for 0%

profile of v2, /device:TPU:36, one launch (start us, length us, event | category | flops | bytes accessed | tf_op | source)
XLA Modules:
  0.0 238.9 jit_solution(5493085096886807613)
XLA Ops:
  7.7 3.0 %collective-permute-start = (f32[2,8,1,2048]{3,2,1,0:T(1,128)S(1)}, f32[2,8,1,2048]{3,2,1,0:T(1,128)S(1)}, u32[]{:S(2)}, u32[]{:S(2)}) collective-permute-start(f32[2,8,1,2048]{3,2,1,0:T(1,128)S(1)} %get-tuple-element.24), channel_id=1, source_target_pairs={{0,1},{1,2},{2,3},{3,4},{4,5},{5,6},{6,7},{7,8},{8,9},{9,10},{10,1... | collective-permute-start | bytes 393224 | tf_op jit(solution)/shard_map/ppermute | solution.py:29
  10.7 2.6 %collective-permute-start.1 = (f32[2,8,1,2048]{3,2,1,0:T(1,128)S(1)}, f32[2,8,1,2048]{3,2,1,0:T(1,128)S(1)}, u32[]{:S(2)}, u32[]{:S(2)}) collective-permute-start(f32[2,8,1,2048]{3,2,1,0:T(1,128)S(1)} %get-tuple-element.25), channel_id=1, source_target_pairs={{1,0},{2,1},{3,2},{4,3},{5,4},{6,5},{7,6},{8,7},{9,8},{10,9},{11,1... | collective-permute-start | bytes 393224 | tf_op jit(solution)/shard_map/ppermute | solution.py:30
  22.5 3.8 %collective-permute-start.4 = (f32[26,256]{1,0:T(8,128)S(1)}, f32[26,256]{1,0:T(8,128)S(1)}, u32[]{:S(2)}, u32[]{:S(2)}) collective-permute-start(f32[26,256]{1,0:T(8,128)S(1)} %slice_bitcast_fusion.10), channel_id=1, source_target_pairs={{0,1},{1,2},{2,3},{3,4},{4,5},{5,6},{6,7},{7,8},{8,9},{9,10},{10,1... | collective-permute-start | bytes 79880 | tf_op jit(solution)/shard_map/ppermute | solution.py:19
  29.7 8.1 %collective-permute-start.8 = (f32[26,8,256]{2,0,1:T(8,128)S(1)}, f32[26,8,256]{2,0,1:T(8,128)S(1)}, u32[]{:S(2)}, u32[]{:S(2)}) collective-permute-start(f32[26,8,256]{2,0,1:T(8,128)S(1)} %fusion.48), channel_id=1, source_target_pairs={{3,0},{4,1},{5,2},{6,3},{7,4},{8,5},{9,6},{10,7},{11,8},{12,9},{13... | collective-permute-start | bytes 638984 | tf_op jit(solution)/shard_map/ppermute | solution.py:19
  39.7 2.6 %collective-permute-start.6 = (f32[26,8,256]{2,0,1:T(8,128)S(1)}, f32[26,8,256]{2,0,1:T(8,128)S(1)}, u32[]{:S(2)}, u32[]{:S(2)}) collective-permute-start(f32[26,8,256]{2,0,1:T(8,128)S(1)} %fusion.48), channel_id=1, source_target_pairs={{1,0},{2,1},{3,2},{4,3},{5,4},{6,5},{7,6},{8,7},{9,8},{10,9},{11,1... | collective-permute-start | bytes 638984 | tf_op jit(solution)/shard_map/ppermute | solution.py:19
  42.3 3.7 %collective-permute-done.8 = f32[26,8,256]{2,0,1:T(8,128)S(1)} collective-permute-done((f32[26,8,256]{2,0,1:T(8,128)S(1)}, f32[26,8,256]{2,0,1:T(8,128)S(1)}, u32[]{:S(2)}, u32[]{:S(2)}) %collective-permute-start.8) | collective-permute-done | bytes 213024 | tf_op jit(solution)/shard_map/ppermute | solution.py:19
  46.1 2.8 %collective-permute-done.7 = f32[26,8,256]{2,0,1:T(8,128)S(1)} collective-permute-done((f32[26,8,256]{2,0,1:T(8,128)S(1)}, f32[26,8,256]{2,0,1:T(8,128)S(1)}, u32[]{:S(2)}, u32[]{:S(2)}) %collective-permute-start.7) | collective-permute-done | bytes 213024 | tf_op jit(solution)/shard_map/ppermute | solution.py:19
  53.5 2.5 %collective-permute-start.9 = (f32[26,8,256]{2,0,1:T(8,128)S(1)}, f32[26,8,256]{2,0,1:T(8,128)S(1)}, u32[]{:S(2)}, u32[]{:S(2)}) collective-permute-start(f32[26,8,256]{2,0,1:T(8,128)S(1)} %select_select_fusion.1), channel_id=1, source_target_pairs={{4,0},{5,1},{6,2},{7,3},{8,4},{9,5},{10,6},{11,7},{12,8},{13,9},{1... | collective-permute-start | bytes 638984 | tf_op jit(solution)/shard_map/ppermute | solution.py:19
  56.6 46.5 %collective-permute-done.11 = f32[26,8,256]{2,0,1:T(8,128)S(1)} collective-permute-done((f32[26,8,256]{2,0,1:T(8,128)S(1)}, f32[26,8,256]{2,0,1:T(8,128)S(1)}, u32[]{:S(2)}, u32[]{:S(2)}) %collective-permute-start.11) | collective-permute-done | bytes 213024 | tf_op jit(solution)/shard_map/ppermute | solution.py:19
  103.2 4.2 %collective-permute-start.14 = (f32[26,8,256]{2,0,1:T(8,128)S(1)}, f32[26,8,256]{2,0,1:T(8,128)S(1)}, u32[]{:S(2)}, u32[]{:S(2)}) collective-permute-start(f32[26,8,256]{2,0,1:T(8,128)S(1)} %select_select_fusion), channel_id=1, source_target_pairs={{1,1},{2,3},{3,5},{4,7},{5,9},{6,11},{7,13},{8,15},{9,17},{10,19},... | collective-permute-start | bytes 638984 | tf_op jit(solution)/shard_map/ppermute | solution.py:133
  107.4 4.8 %collective-permute-start.13 = (f32[26,8,256]{2,0,1:T(8,128)S(1)}, f32[26,8,256]{2,0,1:T(8,128)S(1)}, u32[]{:S(2)}, u32[]{:S(2)}) collective-permute-start(f32[26,8,256]{2,0,1:T(8,128)S(1)} %select_select_fusion), channel_id=1, source_target_pairs={{0,1},{1,3},{2,5},{3,7},{4,9},{5,11},{6,13},{7,15},{8,17},{9,19},{... | collective-permute-start | bytes 638984 | tf_op jit(solution)/shard_map/ppermute | solution.py:132
  114.8 9.5 %collective-permute-done.13 = f32[26,8,256]{2,0,1:T(8,128)S(1)} collective-permute-done((f32[26,8,256]{2,0,1:T(8,128)S(1)}, f32[26,8,256]{2,0,1:T(8,128)S(1)}, u32[]{:S(2)}, u32[]{:S(2)}) %collective-permute-start.13) | collective-permute-done | bytes 213024 | tf_op jit(solution)/shard_map/ppermute | solution.py:132
  124.4 2.8 %collective-permute-done.12 = f32[26,8,256]{2,0,1:T(8,128)S(1)} collective-permute-done((f32[26,8,256]{2,0,1:T(8,128)S(1)}, f32[26,8,256]{2,0,1:T(8,128)S(1)}, u32[]{:S(2)}, u32[]{:S(2)}) %collective-permute-start.12) | collective-permute-done | bytes 213024 | tf_op jit(solution)/shard_map/ppermute | solution.py:131
  150.0 7.0 %collective-permute-done.18 = f32[4,24,256]{2,0,1:T(4,128)S(1)} collective-permute-done((f32[4,24,256]{2,0,1:T(4,128)S(1)}, f32[4,24,256]{2,0,1:T(4,128)S(1)}, u32[]{:S(2)}, u32[]{:S(2)}) %collective-permute-start.18) | collective-permute-done | bytes 98336 | tf_op jit(solution)/shard_map/ppermute | solution.py:163
  157.0 2.8 %collective-permute-done.17 = f32[4,24,256]{2,0,1:T(4,128)S(1)} collective-permute-done((f32[4,24,256]{2,0,1:T(4,128)S(1)}, f32[4,24,256]{2,0,1:T(4,128)S(1)}, u32[]{:S(2)}, u32[]{:S(2)}) %collective-permute-start.17) | collective-permute-done | bytes 98336 | tf_op jit(solution)/shard_map/ppermute | solution.py:163
  159.7 4.3 %collective-permute-done.16 = f32[4,24,256]{2,0,1:T(4,128)S(1)} collective-permute-done((f32[4,24,256]{2,0,1:T(4,128)S(1)}, f32[4,24,256]{2,0,1:T(4,128)S(1)}, u32[]{:S(2)}, u32[]{:S(2)}) %collective-permute-start.16) | collective-permute-done | bytes 98336 | tf_op jit(solution)/shard_map/ppermute | solution.py:163
  164.3 6.4 %collective-permute-start.21 = (f32[8,24,256]{2,0,1:T(8,128)S(1)}, f32[8,24,256]{2,0,1:T(8,128)S(1)}, u32[]{:S(2)}, u32[]{:S(2)}) collective-permute-start(f32[8,24,256]{2,0,1:T(8,128)S(1)} %fusion.51), channel_id=1, source_target_pairs={{0,3},{1,4},{2,5},{3,6},{4,7},{5,8},{6,9},{7,10},{8,11},{9,12},{10... | collective-permute-start | bytes 589832 | tf_op jit(solution)/shard_map/ppermute | solution.py:19
  172.6 3.4 %collective-permute-start.19 = (f32[8,24,256]{2,0,1:T(8,128)S(1)}, f32[8,24,256]{2,0,1:T(8,128)S(1)}, u32[]{:S(2)}, u32[]{:S(2)}) collective-permute-start(f32[8,24,256]{2,0,1:T(8,128)S(1)} %fusion.51), channel_id=1, source_target_pairs={{0,1},{1,2},{2,3},{3,4},{4,5},{5,6},{6,7},{7,8},{8,9},{9,10},{10,1... | collective-permute-start | bytes 589832 | tf_op jit(solution)/shard_map/ppermute | solution.py:19
  176.7 3.2 %collective-permute-done.20 = f32[8,24,256]{2,0,1:T(8,128)S(1)} collective-permute-done((f32[8,24,256]{2,0,1:T(8,128)S(1)}, f32[8,24,256]{2,0,1:T(8,128)S(1)}, u32[]{:S(2)}, u32[]{:S(2)}) %collective-permute-start.20) | collective-permute-done | bytes 196640 | tf_op jit(solution)/shard_map/ppermute | solution.py:19
  179.9 2.6 %collective-permute-done.19 = f32[8,24,256]{2,0,1:T(8,128)S(1)} collective-permute-done((f32[8,24,256]{2,0,1:T(8,128)S(1)}, f32[8,24,256]{2,0,1:T(8,128)S(1)}, u32[]{:S(2)}, u32[]{:S(2)}) %collective-permute-start.19) | collective-permute-done | bytes 196640 | tf_op jit(solution)/shard_map/ppermute | solution.py:19
  182.5 39.8 %collective-permute-start.24 = (f32[8,24,256]{2,0,1:T(8,128)S(1)}, f32[8,24,256]{2,0,1:T(8,128)S(1)}, u32[]{:S(2)}, u32[]{:S(2)}) collective-permute-start(f32[8,24,256]{2,0,1:T(8,128)S(1)} %select_select_fusion.3), channel_id=1, source_target_pairs={{0,12},{1,13},{2,14},{3,15},{4,16},{5,17},{6,18},{7,19},{8,20},{9,... | collective-permute-start | bytes 589832 | tf_op jit(solution)/shard_map/ppermute | solution.py:19
  223.6 3.1 %collective-permute-start.22 = (f32[8,24,256]{2,0,1:T(8,128)S(1)}, f32[8,24,256]{2,0,1:T(8,128)S(1)}, u32[]{:S(2)}, u32[]{:S(2)}) collective-permute-start(f32[8,24,256]{2,0,1:T(8,128)S(1)} %select_select_fusion.3), channel_id=1, source_target_pairs={{0,4},{1,5},{2,6},{3,7},{4,8},{5,9},{6,10},{7,11},{8,12},{9,13},{1... | collective-permute-start | bytes 589832 | tf_op jit(solution)/shard_map/ppermute | solution.py:19
  228.6 4.1 %collective-permute-done.22 = f32[8,24,256]{2,0,1:T(8,128)S(1)} collective-permute-done((f32[8,24,256]{2,0,1:T(8,128)S(1)}, f32[8,24,256]{2,0,1:T(8,128)S(1)}, u32[]{:S(2)}, u32[]{:S(2)}) %collective-permute-start.22) | collective-permute-done | bytes 196640 | tf_op jit(solution)/shard_map/ppermute | solution.py:19
  233.8 5.1 %dynamic_update_slice.3 = f32[3,8,8,2048]{3,2,1,0:T(8,128)} dynamic-update-slice(f32[3,8,8,2048]{3,2,1,0:T(8,128)} %copy-done.2, f32[3,8,8,256]{3,2,1,0:T(8,128)S(1)} %dynamic-slice_select_fusion, s32[]{:T(128)} %constant.79.clone.1, s32[]{:T(128)} %constant.79.clone.1, s32[]{:T(128)} %constant.79.clone.1, s32[]{:T(128)S(6)} %select_n.165) | dynamic-update-slice | bytes 393220 | tf_op jit(solution)/shard_map/dynamic_update_slice | solution.py:174
  (138 shorter events, 52.4 us)
Async XLA Ops:
  3.0 17.3 %collective-permute-start.3 = (f32[3,8,3,768]{3,1,2,0:T(8,128)S(1)}, f32[3,8,3,768]{3,1,2,0:T(8,128)S(1)}, u32[]{:S(2)}, u32[]{:S(2)}) collective-permute-start(f32[3,8,3,768]{3,1,2,0:T(8,128)S(1)} %get-tuple-element.26), channel_id=1, source_target_pairs={{1,0},{2,1},{3,2},{4,3},{5,4},{6,5},{7,6},{8,7},{9,8},{10,9},{11,1... | collective-permute-start | bytes 663560 | tf_op jit(solution)/shard_map/ppermute | solution.py:19
  5.0 15.4 %collective-permute-start.2 = (f32[3,8,3,768]{3,1,2,0:T(8,128)S(1)}, f32[3,8,3,768]{3,1,2,0:T(8,128)S(1)}, u32[]{:S(2)}, u32[]{:S(2)}) collective-permute-start(f32[3,8,3,768]{3,1,2,0:T(8,128)S(1)} %get-tuple-element.27), channel_id=1, source_target_pairs={{0,1},{1,2},{2,3},{3,4},{4,5},{5,6},{6,7},{7,8},{8,9},{9,10},{10,1... | collective-permute-start | bytes 663560 | tf_op jit(solution)/shard_map/ppermute | solution.py:19
  7.7 9.7 %collective-permute-start = (f32[2,8,1,2048]{3,2,1,0:T(1,128)S(1)}, f32[2,8,1,2048]{3,2,1,0:T(1,128)S(1)}, u32[]{:S(2)}, u32[]{:S(2)}) collective-permute-start(f32[2,8,1,2048]{3,2,1,0:T(1,128)S(1)} %get-tuple-element.24), channel_id=1, source_target_pairs={{0,1},{1,2},{2,3},{3,4},{4,5},{5,6},{6,7},{7,8},{8,9},{9,10},{10,1... | collective-permute-start | bytes 393224 | tf_op jit(solution)/shard_map/ppermute | solution.py:29
  10.7 6.7 %collective-permute-start.1 = (f32[2,8,1,2048]{3,2,1,0:T(1,128)S(1)}, f32[2,8,1,2048]{3,2,1,0:T(1,128)S(1)}, u32[]{:S(2)}, u32[]{:S(2)}) collective-permute-start(f32[2,8,1,2048]{3,2,1,0:T(1,128)S(1)} %get-tuple-element.25), channel_id=1, source_target_pairs={{1,0},{2,1},{3,2},{4,3},{5,4},{6,5},{7,6},{8,7},{9,8},{10,9},{11,1... | collective-permute-start | bytes 393224 | tf_op jit(solution)/shard_map/ppermute | solution.py:30
  20.4 9.2 %collective-permute-start.5 = (f32[26,8,256]{2,0,1:T(8,128)S(1)}, f32[26,8,256]{2,0,1:T(8,128)S(1)}, u32[]{:S(2)}, u32[]{:S(2)}) collective-permute-start(f32[26,8,256]{2,0,1:T(8,128)S(1)} %pad_maximum_fusion.15), channel_id=1, source_target_pairs={{1,0},{2,1},{3,2},{4,3},{5,4},{6,5},{7,6},{8,7},{9,8},{10,9},{11,1... | collective-permute-start | bytes 638984 | tf_op jit(solution)/shard_map/ppermute | solution.py:19
  22.5 7.0 %collective-permute-start.4 = (f32[26,256]{1,0:T(8,128)S(1)}, f32[26,256]{1,0:T(8,128)S(1)}, u32[]{:S(2)}, u32[]{:S(2)}) collective-permute-start(f32[26,256]{1,0:T(8,128)S(1)} %slice_bitcast_fusion.10), channel_id=1, source_target_pairs={{0,1},{1,2},{2,3},{3,4},{4,5},{5,6},{6,7},{7,8},{8,9},{9,10},{10,1... | collective-permute-start | bytes 79880 | tf_op jit(solution)/shard_map/ppermute | solution.py:19
  29.7 16.4 %collective-permute-start.8 = (f32[26,8,256]{2,0,1:T(8,128)S(1)}, f32[26,8,256]{2,0,1:T(8,128)S(1)}, u32[]{:S(2)}, u32[]{:S(2)}) collective-permute-start(f32[26,8,256]{2,0,1:T(8,128)S(1)} %fusion.48), channel_id=1, source_target_pairs={{3,0},{4,1},{5,2},{6,3},{7,4},{8,5},{9,6},{10,7},{11,8},{12,9},{13... | collective-permute-start | bytes 638984 | tf_op jit(solution)/shard_map/ppermute | solution.py:19
  37.8 11.1 %collective-permute-start.7 = (f32[26,8,256]{2,0,1:T(8,128)S(1)}, f32[26,8,256]{2,0,1:T(8,128)S(1)}, u32[]{:S(2)}, u32[]{:S(2)}) collective-permute-start(f32[26,8,256]{2,0,1:T(8,128)S(1)} %fusion.48), channel_id=1, source_target_pairs={{2,0},{3,1},{4,2},{5,3},{6,4},{7,5},{8,6},{9,7},{10,8},{11,9},{12,... | collective-permute-start | bytes 638984 | tf_op jit(solution)/shard_map/ppermute | solution.py:19
  39.7 11.1 %collective-permute-start.6 = (f32[26,8,256]{2,0,1:T(8,128)S(1)}, f32[26,8,256]{2,0,1:T(8,128)S(1)}, u32[]{:S(2)}, u32[]{:S(2)}) collective-permute-start(f32[26,8,256]{2,0,1:T(8,128)S(1)} %fusion.48), channel_id=1, source_target_pairs={{1,0},{2,1},{3,2},{4,3},{5,4},{6,5},{7,6},{8,7},{9,8},{10,9},{11,1... | collective-permute-start | bytes 638984 | tf_op jit(solution)/shard_map/ppermute | solution.py:19
  50.9 52.2 %collective-permute-start.11 = (f32[26,8,256]{2,0,1:T(8,128)S(1)}, f32[26,8,256]{2,0,1:T(8,128)S(1)}, u32[]{:S(2)}, u32[]{:S(2)}) collective-permute-start(f32[26,8,256]{2,0,1:T(8,128)S(1)} %select_select_fusion.1), channel_id=1, source_target_pairs={{12,0},{13,1},{14,2},{15,3},{16,4},{17,5},{18,6},{19,7},{20,8},{21... | collective-permute-start | bytes 638984 | tf_op jit(solution)/shard_map/ppermute | solution.py:19
  52.2 50.9 %collective-permute-start.10 = (f32[26,8,256]{2,0,1:T(8,128)S(1)}, f32[26,8,256]{2,0,1:T(8,128)S(1)}, u32[]{:S(2)}, u32[]{:S(2)}) collective-permute-start(f32[26,8,256]{2,0,1:T(8,128)S(1)} %select_select_fusion.1), channel_id=1, source_target_pairs={{8,0},{9,1},{10,2},{11,3},{12,4},{13,5},{14,6},{15,7},{16,8},{17,9... | collective-permute-start | bytes 638984 | tf_op jit(solution)/shard_map/ppermute | solution.py:19
  53.5 49.7 %collective-permute-start.9 = (f32[26,8,256]{2,0,1:T(8,128)S(1)}, f32[26,8,256]{2,0,1:T(8,128)S(1)}, u32[]{:S(2)}, u32[]{:S(2)}) collective-permute-start(f32[26,8,256]{2,0,1:T(8,128)S(1)} %select_select_fusion.1), channel_id=1, source_target_pairs={{4,0},{5,1},{6,2},{7,3},{8,4},{9,5},{10,6},{11,7},{12,8},{13,9},{1... | collective-permute-start | bytes 638984 | tf_op jit(solution)/shard_map/ppermute | solution.py:19
  103.2 11.6 %collective-permute-start.14 = (f32[26,8,256]{2,0,1:T(8,128)S(1)}, f32[26,8,256]{2,0,1:T(8,128)S(1)}, u32[]{:S(2)}, u32[]{:S(2)}) collective-permute-start(f32[26,8,256]{2,0,1:T(8,128)S(1)} %select_select_fusion), channel_id=1, source_target_pairs={{1,1},{2,3},{3,5},{4,7},{5,9},{6,11},{7,13},{8,15},{9,17},{10,19},... | collective-permute-start | bytes 638984 | tf_op jit(solution)/shard_map/ppermute | solution.py:133
  107.4 16.9 %collective-permute-start.13 = (f32[26,8,256]{2,0,1:T(8,128)S(1)}, f32[26,8,256]{2,0,1:T(8,128)S(1)}, u32[]{:S(2)}, u32[]{:S(2)}) collective-permute-start(f32[26,8,256]{2,0,1:T(8,128)S(1)} %select_select_fusion), channel_id=1, source_target_pairs={{0,1},{1,3},{2,5},{3,7},{4,9},{5,11},{6,13},{7,15},{8,17},{9,19},{... | collective-permute-start | bytes 638984 | tf_op jit(solution)/shard_map/ppermute | solution.py:132
  112.2 15.0 %collective-permute-start.12 = (f32[26,8,256]{2,0,1:T(8,128)S(1)}, f32[26,8,256]{2,0,1:T(8,128)S(1)}, u32[]{:S(2)}, u32[]{:S(2)}) collective-permute-start(f32[26,8,256]{2,0,1:T(8,128)S(1)} %select_select_fusion), channel_id=1, source_target_pairs={{0,0},{1,2},{2,4},{3,6},{4,8},{5,10},{6,12},{7,14},{8,16},{9,18},{... | collective-permute-start | bytes 638984 | tf_op jit(solution)/shard_map/ppermute | solution.py:131
  143.5 13.5 %collective-permute-start.18 = (f32[4,24,256]{2,0,1:T(4,128)S(1)}, f32[4,24,256]{2,0,1:T(4,128)S(1)}, u32[]{:S(2)}, u32[]{:S(2)}) collective-permute-start(f32[4,24,256]{2,0,1:T(4,128)S(1)} %bitcast.155), channel_id=1, source_target_pairs={{1,0},{3,1},{5,2},{7,3},{9,4},{11,5},{13,6},{15,7},{17,8},{19,9},{... | collective-permute-start | bytes 294920 | tf_op jit(solution)/shard_map/ppermute | solution.py:163
  144.8 14.9 %collective-permute-start.17 = (f32[4,24,256]{2,0,1:T(4,128)S(1)}, f32[4,24,256]{2,0,1:T(4,128)S(1)}, u32[]{:S(2)}, u32[]{:S(2)}) collective-permute-start(f32[4,24,256]{2,0,1:T(4,128)S(1)} %bitcast.156), channel_id=1, source_target_pairs={{0,0},{2,1},{4,2},{6,3},{8,4},{10,5},{12,6},{14,7},{16,8},{18,9},{... | collective-permute-start | bytes 294920 | tf_op jit(solution)/shard_map/ppermute | solution.py:163
  146.7 17.4 %collective-permute-start.16 = (f32[4,24,256]{2,0,1:T(4,128)S(1)}, f32[4,24,256]{2,0,1:T(4,128)S(1)}, u32[]{:S(2)}, u32[]{:S(2)}) collective-permute-start(f32[4,24,256]{2,0,1:T(4,128)S(1)} %bitcast.157), channel_id=1, source_target_pairs={{1,1},{3,2},{5,3},{7,4},{9,5},{11,6},{13,7},{15,8},{17,9},{19,10},... | collective-permute-start | bytes 294920 | tf_op jit(solution)/shard_map/ppermute | solution.py:163
  148.0 16.1 %collective-permute-start.15 = (f32[4,24,256]{2,0,1:T(4,128)S(1)}, f32[4,24,256]{2,0,1:T(4,128)S(1)}, u32[]{:S(2)}, u32[]{:S(2)}) collective-permute-start(f32[4,24,256]{2,0,1:T(4,128)S(1)} %bitcast.158), channel_id=1, source_target_pairs={{0,1},{2,2},{4,3},{6,4},{8,5},{10,6},{12,7},{14,8},{16,9},{18,10},... | collective-permute-start | bytes 294920 | tf_op jit(solution)/shard_map/ppermute | solution.py:163
  164.3 12.4 %collective-permute-start.21 = (f32[8,24,256]{2,0,1:T(8,128)S(1)}, f32[8,24,256]{2,0,1:T(8,128)S(1)}, u32[]{:S(2)}, u32[]{:S(2)}) collective-permute-start(f32[8,24,256]{2,0,1:T(8,128)S(1)} %fusion.51), channel_id=1, source_target_pairs={{0,3},{1,4},{2,5},{3,6},{4,7},{5,8},{6,9},{7,10},{8,11},{9,12},{10... | collective-permute-start | bytes 589832 | tf_op jit(solution)/shard_map/ppermute | solution.py:19
  170.7 9.2 %collective-permute-start.20 = (f32[8,24,256]{2,0,1:T(8,128)S(1)}, f32[8,24,256]{2,0,1:T(8,128)S(1)}, u32[]{:S(2)}, u32[]{:S(2)}) collective-permute-start(f32[8,24,256]{2,0,1:T(8,128)S(1)} %fusion.51), channel_id=1, source_target_pairs={{0,2},{1,3},{2,4},{3,5},{4,6},{5,7},{6,8},{7,9},{8,10},{9,11},{10,... | collective-permute-start | bytes 589832 | tf_op jit(solution)/shard_map/ppermute | solution.py:19
  172.6 9.8 %collective-permute-start.19 = (f32[8,24,256]{2,0,1:T(8,128)S(1)}, f32[8,24,256]{2,0,1:T(8,128)S(1)}, u32[]{:S(2)}, u32[]{:S(2)}) collective-permute-start(f32[8,24,256]{2,0,1:T(8,128)S(1)} %fusion.51), channel_id=1, source_target_pairs={{0,1},{1,2},{2,3},{3,4},{4,5},{5,6},{6,7},{7,8},{8,9},{9,10},{10,1... | collective-permute-start | bytes 589832 | tf_op jit(solution)/shard_map/ppermute | solution.py:19
  182.5 46.1 %collective-permute-start.24 = (f32[8,24,256]{2,0,1:T(8,128)S(1)}, f32[8,24,256]{2,0,1:T(8,128)S(1)}, u32[]{:S(2)}, u32[]{:S(2)}) collective-permute-start(f32[8,24,256]{2,0,1:T(8,128)S(1)} %select_select_fusion.3), channel_id=1, source_target_pairs={{0,12},{1,13},{2,14},{3,15},{4,16},{5,17},{6,18},{7,19},{8,20},{9,... | collective-permute-start | bytes 589832 | tf_op jit(solution)/shard_map/ppermute | solution.py:19
  223.6 9.1 %collective-permute-start.22 = (f32[8,24,256]{2,0,1:T(8,128)S(1)}, f32[8,24,256]{2,0,1:T(8,128)S(1)}, u32[]{:S(2)}, u32[]{:S(2)}) collective-permute-start(f32[8,24,256]{2,0,1:T(8,128)S(1)} %select_select_fusion.3), channel_id=1, source_target_pairs={{0,4},{1,5},{2,6},{3,7},{4,8},{5,9},{6,10},{7,11},{8,12},{9,13},{1... | collective-permute-start | bytes 589832 | tf_op jit(solution)/shard_map/ppermute | solution.py:19
  (15 other events, 152.4 us)

commit v3 on v2

--- a/solution.py
+++ b/solution.py
@@ -58,15 +58,11 @@
     return (rows == cols).astype(jnp.float32)
 
 
-def barrel(value, amount, digits, direction, tiles):
-    for j in range(digits):
-        digit = (amount >> (2 * j)) & 3
-        step = 4**j
-        moved = [shift_from(value, "tile", direction * k * step, tiles) for k in (1, 2, 3)]
-        value = jnp.where(
-            digit == 0, value, jnp.where(digit == 1, moved[0], jnp.where(digit == 2, moved[1], moved[2]))
-        )
-    return value
+def pick(value, options, tiles):
+    out = value
+    for offset, predicate in options:
+        out = jnp.where(predicate, shift_from(value, "tile", offset, tiles), out)
+    return out
 
 
 def local(parent_state, terrain, nest_state, nest_offsets):
@@ -85,7 +81,8 @@
     coarse_total = nest_total // 3
     largest_offset = band_rows - coarse_total - 1
     largest_q = largest_offset // parent_rows
-    digits = max(1, (int(largest_q).bit_length() + 1) // 2)
+    assert largest_q < 16 and tiles >= 2 * 16
+    center = 8
     planes = 3 * levels
     half = tiles // 2
 
@@ -127,10 +124,15 @@
     rows_after = shift_from(rows_here, "tile", 1, tiles)
     joined = jnp.concatenate([last_before[:, None], rows_here, rows_after], axis=1)
     block = lax.dynamic_slice_in_dim(joined, r, parent_rows, axis=1)
-    block = barrel(block, q, digits, 1, tiles)
-    to_even = lax.ppermute(block, "tile", [(m, 2 * m) for m in range(half)])
-    to_odd = lax.ppermute(block, "tile", [(m, 2 * m + 1) for m in range(half)])
-    next_odd = lax.ppermute(block, "tile", [(m + 1, 2 * m + 1) for m in range(half)])
+    low = q & 3
+    bit2 = ((q >> 2) & 1) == 1
+    bit3 = ((q >> 3) & 1) == 1
+    block = pick(block, [(1, low == 1), (2, low == 2), (3, low == 3)], tiles)
+    block = pick(block, [(4, bit2)], tiles)
+    block = pick(block, [(-center, jnp.logical_not(bit3))], tiles)
+    to_even = lax.ppermute(block, "tile", [(m + center, 2 * m) for m in range(half)])
+    to_odd = lax.ppermute(block, "tile", [(m + center, 2 * m + 1) for m in range(half)])
+    next_odd = lax.ppermute(block, "tile", [(m + center + 1, 2 * m + 1) for m in range(half)])
     odd_rows = jnp.concatenate([to_odd[:, coarse_rows:], next_odd[:, : foot_rows - coarse_rows]], axis=1)
     footprint = jnp.where(tile_index % 2 == 0, to_even[:, :foot_rows], odd_rows)
 
@@ -160,12 +162,16 @@
     means = (sums / 9.0).reshape(coarse_rows, planes, coarse_cols)
 
     gathered = [
-        lax.ppermute(means, "tile", [(2 * m + k, m) for m in range(half + 1) if 0 <= 2 * m + k < tiles])
+        lax.ppermute(
+            means, "tile", [(2 * m + k, m + center) for m in range(half + 1) if 0 <= 2 * m + k < tiles]
+        )
         for k in (-2, -1, 0, 1)
     ]
     both = jnp.concatenate(gathered, axis=0)
     back = lax.dynamic_slice_in_dim(both, parent_rows - r, parent_rows, axis=0)
-    back = barrel(back, q, digits, -1, tiles)
+    back = pick(back, [(center, jnp.logical_not(bit3))], tiles)
+    back = pick(back, [(-1, low == 1), (-2, low == 2), (-3, low == 3)], tiles)
+    back = pick(back, [(-4, bit2)], tiles)
     placed = jnp.transpose(back, (1, 0, 2)).reshape(3, levels, parent_rows, coarse_cols)
     band_row = parent_rows * tile_index + jnp.arange(parent_rows, dtype=jnp.int32) - row_offset
     covered = ((band_row >= 0) & (band_row < coarse_total))[None, None, :, None]

time: 240 us -> 217 us (0.904)
  the two profiles are of different devices: /device:TPU:36 before, /device:TPU:170 now
where the time goes in v3:
time: 217 us; the launch traced here: 216 us
  starting transfers between devices  90.3 us (42%)
  waiting for transfers between devices  85.6 us (39%)
  local copies, waits for them, and re-layouts  19.5 us (9%)
  other arithmetic  10.9 us (5%)
  between operations  7.7 us (4%)
  matrix products  2.42 us (1%)
    ppermute x14, starting transfers between devices, shift_from(): return lax.ppermute(value, axis, pairs)  64.8 us
    ppermute x14, waiting for transfers between devices, shift_from(): return lax.ppermute(value, axis, pairs)  63.8 us
    ppermute x4, waiting for transfers between devices, local(): lax.ppermute(means, 'tile', [(2 * m + k, m + center) for m in range(half...  16.2 us
    ppermute x1, starting transfers between devices, local(): lax.ppermute(block, 'tile', [(m + center, 2 * m + 1) for m in range(half)])  11.3 us
    unnamed x30, local copies, waits for them, and re-layouts  6.93 us
    ppermute x4, starting transfers between devices, local(): lax.ppermute(means, 'tile', [(2 * m + k, m + center) for m in range(half...  5.17 us
    dynamic_update_slice x1, local copies, waits for them, and re-layouts, local(): lax.dynamic_update_slice_in_dim(advanced, merged, col_offset, axis=3)  5.09 us
  transfers between devices with their start and end apart: 23, of which 12 were waited for; matrix products, arithmetic and copies ran while one was open for 4% of the time, Pallas kernels for 0%

profile of v3, /device:TPU:170, one launch (start us, length us, event | category | flops | bytes accessed | tf_op | source)
XLA Modules:
  0.0 216.3 jit_solution(3785277105244404117)
XLA Ops:
  5.0 2.4 %collective-permute-start.2 = (f32[3,8,3,768]{3,1,2,0:T(8,128)S(1)}, f32[3,8,3,768]{3,1,2,0:T(8,128)S(1)}, u32[]{:S(2)}, u32[]{:S(2)}) collective-permute-start(f32[3,8,3,768]{3,1,2,0:T(8,128)S(1)} %get-tuple-element.27), channel_id=1, source_target_pairs={{0,1},{1,2},{2,3},{3,4},{4,5},{5,6},{6,7},{7,8},{8,9},{9,10},{10,1... | collective-permute-start | bytes 663560 | tf_op jit(solution)/shard_map/ppermute | solution.py:19
  7.7 3.0 %collective-permute-start = (f32[2,8,1,2048]{3,2,1,0:T(1,128)S(1)}, f32[2,8,1,2048]{3,2,1,0:T(1,128)S(1)}, u32[]{:S(2)}, u32[]{:S(2)}) collective-permute-start(f32[2,8,1,2048]{3,2,1,0:T(1,128)S(1)} %get-tuple-element.24), channel_id=1, source_target_pairs={{0,1},{1,2},{2,3},{3,4},{4,5},{5,6},{6,7},{7,8},{8,9},{9,10},{10,1... | collective-permute-start | bytes 393224 | tf_op jit(solution)/shard_map/ppermute | solution.py:29
  10.7 2.5 %collective-permute-start.1 = (f32[2,8,1,2048]{3,2,1,0:T(1,128)S(1)}, f32[2,8,1,2048]{3,2,1,0:T(1,128)S(1)}, u32[]{:S(2)}, u32[]{:S(2)}) collective-permute-start(f32[2,8,1,2048]{3,2,1,0:T(1,128)S(1)} %get-tuple-element.25), channel_id=1, source_target_pairs={{1,0},{2,1},{3,2},{4,3},{5,4},{6,5},{7,6},{8,7},{9,8},{10,9},{11,1... | collective-permute-start | bytes 393224 | tf_op jit(solution)/shard_map/ppermute | solution.py:30
  20.4 2.5 %collective-permute-start.5 = (f32[26,8,256]{2,0,1:T(8,128)S(1)}, f32[26,8,256]{2,0,1:T(8,128)S(1)}, u32[]{:S(2)}, u32[]{:S(2)}) collective-permute-start(f32[26,8,256]{2,0,1:T(8,128)S(1)} %pad_maximum_fusion.15), channel_id=1, source_target_pairs={{1,0},{2,1},{3,2},{4,3},{5,4},{6,5},{7,6},{8,7},{9,8},{10,9},{11,1... | collective-permute-start | bytes 638984 | tf_op jit(solution)/shard_map/ppermute | solution.py:19
  27.9 4.5 %collective-permute-done.4 = f32[26,256]{1,0:T(8,128)S(1)} collective-permute-done((f32[26,256]{1,0:T(8,128)S(1)}, f32[26,256]{1,0:T(8,128)S(1)}, u32[]{:S(2)}, u32[]{:S(2)}) %collective-permute-start.4) | collective-permute-done | bytes 26656 | tf_op jit(solution)/shard_map/ppermute | solution.py:19
  32.4 6.0 %collective-permute-start.8 = (f32[26,8,256]{2,0,1:T(8,128)S(1)}, f32[26,8,256]{2,0,1:T(8,128)S(1)}, u32[]{:S(2)}, u32[]{:S(2)}) collective-permute-start(f32[26,8,256]{2,0,1:T(8,128)S(1)} %fusion.48), channel_id=1, source_target_pairs={{1,0},{2,1},{3,2},{4,3},{5,4},{6,5},{7,6},{8,7},{9,8},{10,9},{11,1... | collective-permute-start | bytes 638984 | tf_op jit(solution)/shard_map/ppermute | solution.py:19
  38.5 12.0 %collective-permute-start.7 = (f32[26,8,256]{2,0,1:T(8,128)S(1)}, f32[26,8,256]{2,0,1:T(8,128)S(1)}, u32[]{:S(2)}, u32[]{:S(2)}) collective-permute-start(f32[26,8,256]{2,0,1:T(8,128)S(1)} %fusion.48), channel_id=1, source_target_pairs={{2,0},{3,1},{4,2},{5,3},{6,4},{7,5},{8,6},{9,7},{10,8},{11,9},{12,... | collective-permute-start | bytes 638984 | tf_op jit(solution)/shard_map/ppermute | solution.py:19
  52.4 6.0 %collective-permute-done.7 = f32[26,8,256]{2,0,1:T(8,128)S(1)} collective-permute-done((f32[26,8,256]{2,0,1:T(8,128)S(1)}, f32[26,8,256]{2,0,1:T(8,128)S(1)}, u32[]{:S(2)}, u32[]{:S(2)}) %collective-permute-start.7) | collective-permute-done | bytes 213024 | tf_op jit(solution)/shard_map/ppermute | solution.py:19
  59.6 18.9 %collective-permute-start.9 = (f32[26,8,256]{2,0,1:T(8,128)S(1)}, f32[26,8,256]{2,0,1:T(8,128)S(1)}, u32[]{:S(2)}, u32[]{:S(2)}) collective-permute-start(f32[26,8,256]{2,0,1:T(8,128)S(1)} %select_select_fusion), channel_id=1, source_target_pairs={{4,0},{5,1},{6,2},{7,3},{8,4},{9,5},{10,6},{11,7},{12,8},{13,9},{1... | collective-permute-start | bytes 638984 | tf_op jit(solution)/shard_map/ppermute | solution.py:19
  78.6 3.8 %collective-permute-done.9 = f32[26,8,256]{2,0,1:T(8,128)S(1)} collective-permute-done((f32[26,8,256]{2,0,1:T(8,128)S(1)}, f32[26,8,256]{2,0,1:T(8,128)S(1)}, u32[]{:S(2)}, u32[]{:S(2)}) %collective-permute-start.9) | collective-permute-done | bytes 213024 | tf_op jit(solution)/shard_map/ppermute | solution.py:19
  82.4 1.9 collective-permute-start.10
  85.0 7.8 %collective-permute-done.10 = f32[26,8,256]{2,0,1:T(8,128)S(1)} collective-permute-done((f32[26,8,256]{2,0,1:T(8,128)S(1)}, f32[26,8,256]{2,0,1:T(8,128)S(1)}, u32[]{:S(2)}, u32[]{:S(2)}) %collective-permute-start.10) | collective-permute-done | bytes 213024 | tf_op jit(solution)/shard_map/ppermute | solution.py:19
  94.2 11.3 %collective-permute-start.12 = (f32[26,8,256]{2,0,1:T(8,128)S(1)}, f32[26,8,256]{2,0,1:T(8,128)S(1)}, u32[]{:S(2)}, u32[]{:S(2)}) collective-permute-start(f32[26,8,256]{2,0,1:T(8,128)S(1)} %broadcast_select_fusion.1), channel_id=1, source_target_pairs={{8,1},{9,3},{10,5},{11,7},{12,9},{13,11},{14,13},{15,15},{16,17},{... | collective-permute-start | bytes 638984 | tf_op jit(solution)/shard_map/ppermute | solution.py:134
  105.5 2.1 collective-permute-start.11
  109.7 4.1 %collective-permute-done.11 = f32[26,8,256]{2,0,1:T(8,128)S(1)} collective-permute-done((f32[26,8,256]{2,0,1:T(8,128)S(1)}, f32[26,8,256]{2,0,1:T(8,128)S(1)}, u32[]{:S(2)}, u32[]{:S(2)}) %collective-permute-start.11) | collective-permute-done | bytes 213024 | tf_op jit(solution)/shard_map/ppermute | solution.py:133
  135.4 16.2 %collective-permute-done.17 = f32[4,24,256]{2,0,1:T(4,128)S(1)} collective-permute-done((f32[4,24,256]{2,0,1:T(4,128)S(1)}, f32[4,24,256]{2,0,1:T(4,128)S(1)}, u32[]{:S(2)}, u32[]{:S(2)}) %collective-permute-start.17) | collective-permute-done | bytes 98336 | tf_op jit(solution)/shard_map/ppermute | solution.py:165
  151.7 1.9 collective-permute-start.18
  153.7 10.8 %collective-permute-done.18 = f32[8,24,256]{2,0,1:T(8,128)S(1)} collective-permute-done((f32[8,24,256]{2,0,1:T(8,128)S(1)}, f32[8,24,256]{2,0,1:T(8,128)S(1)}, u32[]{:S(2)}, u32[]{:S(2)}) %collective-permute-start.18) | collective-permute-done | bytes 196640 | tf_op jit(solution)/shard_map/ppermute | solution.py:19
  166.4 7.6 %collective-permute-start.20 = (f32[8,24,256]{2,0,1:T(8,128)S(1)}, f32[8,24,256]{2,0,1:T(8,128)S(1)}, u32[]{:S(2)}, u32[]{:S(2)}) collective-permute-start(f32[8,24,256]{2,0,1:T(8,128)S(1)} %broadcast_select_fusion.2), channel_id=1, source_target_pairs={{0,2},{1,3},{2,4},{3,5},{4,6},{5,7},{6,8},{7,9},{8,10},{9,11},{10,... | collective-permute-start | bytes 589832 | tf_op jit(solution)/shard_map/ppermute | solution.py:19
  174.0 1.9 collective-permute-start.19
  176.6 2.3 %collective-permute-done.20 = f32[8,24,256]{2,0,1:T(8,128)S(1)} collective-permute-done((f32[8,24,256]{2,0,1:T(8,128)S(1)}, f32[8,24,256]{2,0,1:T(8,128)S(1)}, u32[]{:S(2)}, u32[]{:S(2)}) %collective-permute-start.20) | collective-permute-done | bytes 196640 | tf_op jit(solution)/shard_map/ppermute | solution.py:19
  178.9 19.1 %collective-permute-done.19 = f32[8,24,256]{2,0,1:T(8,128)S(1)} collective-permute-done((f32[8,24,256]{2,0,1:T(8,128)S(1)}, f32[8,24,256]{2,0,1:T(8,128)S(1)}, u32[]{:S(2)}, u32[]{:S(2)}) %collective-permute-start.19) | collective-permute-done | bytes 196640 | tf_op jit(solution)/shard_map/ppermute | solution.py:19
  201.9 8.2 %collective-permute-done.22 = f32[8,24,256]{2,0,1:T(8,128)S(1)} collective-permute-done((f32[8,24,256]{2,0,1:T(8,128)S(1)}, f32[8,24,256]{2,0,1:T(8,128)S(1)}, u32[]{:S(2)}, u32[]{:S(2)}) %collective-permute-start.22) | collective-permute-done | bytes 196640 | tf_op jit(solution)/shard_map/ppermute | solution.py:19
  211.2 5.1 %dynamic_update_slice.3 = f32[3,8,8,2048]{3,2,1,0:T(8,128)} dynamic-update-slice(f32[3,8,8,2048]{3,2,1,0:T(8,128)} %copy-done.2, f32[3,8,8,256]{3,2,1,0:T(8,128)S(1)} %dynamic-slice_select_fusion, s32[]{:T(128)} %constant.79.clone.1, s32[]{:T(128)} %constant.79.clone.1, s32[]{:T(128)} %constant.79.clone.1, s32[]{:T(128)S(6)} %select_n.155) | dynamic-update-slice | bytes 393220 | tf_op jit(solution)/shard_map/dynamic_update_slice | solution.py:180
  (136 shorter events, 46.5 us)
Async XLA Ops:
  3.0 17.3 %collective-permute-start.3 = (f32[3,8,3,768]{3,1,2,0:T(8,128)S(1)}, f32[3,8,3,768]{3,1,2,0:T(8,128)S(1)}, u32[]{:S(2)}, u32[]{:S(2)}) collective-permute-start(f32[3,8,3,768]{3,1,2,0:T(8,128)S(1)} %get-tuple-element.26), channel_id=1, source_target_pairs={{1,0},{2,1},{3,2},{4,3},{5,4},{6,5},{7,6},{8,7},{9,8},{10,9},{11,1... | collective-permute-start | bytes 663560 | tf_op jit(solution)/shard_map/ppermute | solution.py:19
  5.0 15.4 %collective-permute-start.2 = (f32[3,8,3,768]{3,1,2,0:T(8,128)S(1)}, f32[3,8,3,768]{3,1,2,0:T(8,128)S(1)}, u32[]{:S(2)}, u32[]{:S(2)}) collective-permute-start(f32[3,8,3,768]{3,1,2,0:T(8,128)S(1)} %get-tuple-element.27), channel_id=1, source_target_pairs={{0,1},{1,2},{2,3},{3,4},{4,5},{5,6},{6,7},{7,8},{8,9},{9,10},{10,1... | collective-permute-start | bytes 663560 | tf_op jit(solution)/shard_map/ppermute | solution.py:19
  7.7 9.7 %collective-permute-start = (f32[2,8,1,2048]{3,2,1,0:T(1,128)S(1)}, f32[2,8,1,2048]{3,2,1,0:T(1,128)S(1)}, u32[]{:S(2)}, u32[]{:S(2)}) collective-permute-start(f32[2,8,1,2048]{3,2,1,0:T(1,128)S(1)} %get-tuple-element.24), channel_id=1, source_target_pairs={{0,1},{1,2},{2,3},{3,4},{4,5},{5,6},{6,7},{7,8},{8,9},{9,10},{10,1... | collective-permute-start | bytes 393224 | tf_op jit(solution)/shard_map/ppermute | solution.py:29
  10.7 6.7 %collective-permute-start.1 = (f32[2,8,1,2048]{3,2,1,0:T(1,128)S(1)}, f32[2,8,1,2048]{3,2,1,0:T(1,128)S(1)}, u32[]{:S(2)}, u32[]{:S(2)}) collective-permute-start(f32[2,8,1,2048]{3,2,1,0:T(1,128)S(1)} %get-tuple-element.25), channel_id=1, source_target_pairs={{1,0},{2,1},{3,2},{4,3},{5,4},{6,5},{7,6},{8,7},{9,8},{10,9},{11,1... | collective-permute-start | bytes 393224 | tf_op jit(solution)/shard_map/ppermute | solution.py:30
  19.6 97.8 %copy-start.2 = (f32[3,8,8,2048]{3,2,1,0:T(8,128)}, f32[3,8,8,2048]{3,2,1,0:T(8,128)S(1)}, u32[]{:S(2)}) copy-start(f32[3,8,8,2048]{3,2,1,0:T(8,128)S(1)} %pad_maximum_fusion.1) | copy-start | bytes 4718596
  20.4 12.0 %collective-permute-start.5 = (f32[26,8,256]{2,0,1:T(8,128)S(1)}, f32[26,8,256]{2,0,1:T(8,128)S(1)}, u32[]{:S(2)}, u32[]{:S(2)}) collective-permute-start(f32[26,8,256]{2,0,1:T(8,128)S(1)} %pad_maximum_fusion.15), channel_id=1, source_target_pairs={{1,0},{2,1},{3,2},{4,3},{5,4},{6,5},{7,6},{8,7},{9,8},{10,9},{11,1... | collective-permute-start | bytes 638984 | tf_op jit(solution)/shard_map/ppermute | solution.py:19
  22.9 9.5 %collective-permute-start.4 = (f32[26,256]{1,0:T(8,128)S(1)}, f32[26,256]{1,0:T(8,128)S(1)}, u32[]{:S(2)}, u32[]{:S(2)}) collective-permute-start(f32[26,256]{1,0:T(8,128)S(1)} %slice_bitcast_fusion.10), channel_id=1, source_target_pairs={{0,1},{1,2},{2,3},{3,4},{4,5},{5,6},{6,7},{7,8},{8,9},{9,10},{10,1... | collective-permute-start | bytes 79880 | tf_op jit(solution)/shard_map/ppermute | solution.py:19
  32.4 20.0 %collective-permute-start.8 = (f32[26,8,256]{2,0,1:T(8,128)S(1)}, f32[26,8,256]{2,0,1:T(8,128)S(1)}, u32[]{:S(2)}, u32[]{:S(2)}) collective-permute-start(f32[26,8,256]{2,0,1:T(8,128)S(1)} %fusion.48), channel_id=1, source_target_pairs={{1,0},{2,1},{3,2},{4,3},{5,4},{6,5},{7,6},{8,7},{9,8},{10,9},{11,1... | collective-permute-start | bytes 638984 | tf_op jit(solution)/shard_map/ppermute | solution.py:19
  38.5 19.9 %collective-permute-start.7 = (f32[26,8,256]{2,0,1:T(8,128)S(1)}, f32[26,8,256]{2,0,1:T(8,128)S(1)}, u32[]{:S(2)}, u32[]{:S(2)}) collective-permute-start(f32[26,8,256]{2,0,1:T(8,128)S(1)} %fusion.48), channel_id=1, source_target_pairs={{2,0},{3,1},{4,2},{5,3},{6,4},{7,5},{8,6},{9,7},{10,8},{11,9},{12,... | collective-permute-start | bytes 638984 | tf_op jit(solution)/shard_map/ppermute | solution.py:19
  50.4 9.1 %collective-permute-start.6 = (f32[26,8,256]{2,0,1:T(8,128)S(1)}, f32[26,8,256]{2,0,1:T(8,128)S(1)}, u32[]{:S(2)}, u32[]{:S(2)}) collective-permute-start(f32[26,8,256]{2,0,1:T(8,128)S(1)} %fusion.48), channel_id=1, source_target_pairs={{3,0},{4,1},{5,2},{6,3},{7,4},{8,5},{9,6},{10,7},{11,8},{12,9},{13... | collective-permute-start | bytes 638984 | tf_op jit(solution)/shard_map/ppermute | solution.py:19
  59.6 22.8 %collective-permute-start.9 = (f32[26,8,256]{2,0,1:T(8,128)S(1)}, f32[26,8,256]{2,0,1:T(8,128)S(1)}, u32[]{:S(2)}, u32[]{:S(2)}) collective-permute-start(f32[26,8,256]{2,0,1:T(8,128)S(1)} %select_select_fusion), channel_id=1, source_target_pairs={{4,0},{5,1},{6,2},{7,3},{8,4},{9,5},{10,6},{11,7},{12,8},{13,9},{1... | collective-permute-start | bytes 638984 | tf_op jit(solution)/shard_map/ppermute | solution.py:19
  82.4 10.4 %collective-permute-start.10 = (f32[26,8,256]{2,0,1:T(8,128)S(1)}, f32[26,8,256]{2,0,1:T(8,128)S(1)}, u32[]{:S(2)}, u32[]{:S(2)}) collective-permute-start(f32[26,8,256]{2,0,1:T(8,128)S(1)} %broadcast_select_fusion), channel_id=1, source_target_pairs={{0,8},{1,9},{2,10},{3,11},{4,12},{5,13},{6,14},{7,15},{8,16},{9,17... | collective-permute-start | bytes 638984 | tf_op jit(solution)/shard_map/ppermute | solution.py:19
  92.9 15.3 %collective-permute-start.13 = (f32[26,8,256]{2,0,1:T(8,128)S(1)}, f32[26,8,256]{2,0,1:T(8,128)S(1)}, u32[]{:S(2)}, u32[]{:S(2)}) collective-permute-start(f32[26,8,256]{2,0,1:T(8,128)S(1)} %broadcast_select_fusion.1), channel_id=1, source_target_pairs={{9,1},{10,3},{11,5},{12,7},{13,9},{14,11},{15,13},{16,15},{17,17},... | collective-permute-start | bytes 638984 | tf_op jit(solution)/shard_map/ppermute | solution.py:135
  94.2 15.5 %collective-permute-start.12 = (f32[26,8,256]{2,0,1:T(8,128)S(1)}, f32[26,8,256]{2,0,1:T(8,128)S(1)}, u32[]{:S(2)}, u32[]{:S(2)}) collective-permute-start(f32[26,8,256]{2,0,1:T(8,128)S(1)} %broadcast_select_fusion.1), channel_id=1, source_target_pairs={{8,1},{9,3},{10,5},{11,7},{12,9},{13,11},{14,13},{15,15},{16,17},{... | collective-permute-start | bytes 638984 | tf_op jit(solution)/shard_map/ppermute | solution.py:134
  105.5 8.3 %collective-permute-start.11 = (f32[26,8,256]{2,0,1:T(8,128)S(1)}, f32[26,8,256]{2,0,1:T(8,128)S(1)}, u32[]{:S(2)}, u32[]{:S(2)}) collective-permute-start(f32[26,8,256]{2,0,1:T(8,128)S(1)} %broadcast_select_fusion.1), channel_id=1, source_target_pairs={{8,0},{9,2},{10,4},{11,6},{12,8},{13,10},{14,12},{15,14},{16,16},{... | collective-permute-start | bytes 638984 | tf_op jit(solution)/shard_map/ppermute | solution.py:133
  130.2 21.4 %collective-permute-start.17 = (f32[4,24,256]{2,0,1:T(4,128)S(1)}, f32[4,24,256]{2,0,1:T(4,128)S(1)}, u32[]{:S(2)}, u32[]{:S(2)}) collective-permute-start(f32[4,24,256]{2,0,1:T(4,128)S(1)} %bitcast.155), channel_id=1, source_target_pairs={{1,8},{3,9},{5,10},{7,11},{9,12},{11,13},{13,14},{15,15},{17,16},{... | collective-permute-start | bytes 294920 | tf_op jit(solution)/shard_map/ppermute | solution.py:165
  131.5 20.1 %collective-permute-start.16 = (f32[4,24,256]{2,0,1:T(4,128)S(1)}, f32[4,24,256]{2,0,1:T(4,128)S(1)}, u32[]{:S(2)}, u32[]{:S(2)}) collective-permute-start(f32[4,24,256]{2,0,1:T(4,128)S(1)} %bitcast.156), channel_id=1, source_target_pairs={{0,8},{2,9},{4,10},{6,11},{8,12},{10,13},{12,14},{14,15},{16,16},{... | collective-permute-start | bytes 294920 | tf_op jit(solution)/shard_map/ppermute | solution.py:165
  133.4 18.2 %collective-permute-start.15 = (f32[4,24,256]{2,0,1:T(4,128)S(1)}, f32[4,24,256]{2,0,1:T(4,128)S(1)}, u32[]{:S(2)}, u32[]{:S(2)}) collective-permute-start(f32[4,24,256]{2,0,1:T(4,128)S(1)} %bitcast.157), channel_id=1, source_target_pairs={{1,9},{3,10},{5,11},{7,12},{9,13},{11,14},{13,15},{15,16},{17,17},... | collective-permute-start | bytes 294920 | tf_op jit(solution)/shard_map/ppermute | solution.py:165
  134.7 16.9 %collective-permute-start.14 = (f32[4,24,256]{2,0,1:T(4,128)S(1)}, f32[4,24,256]{2,0,1:T(4,128)S(1)}, u32[]{:S(2)}, u32[]{:S(2)}) collective-permute-start(f32[4,24,256]{2,0,1:T(4,128)S(1)} %bitcast.158), channel_id=1, source_target_pairs={{0,9},{2,10},{4,11},{6,12},{8,13},{10,14},{12,15},{14,16},{16,17},... | collective-permute-start | bytes 294920 | tf_op jit(solution)/shard_map/ppermute | solution.py:165
  151.7 12.7 %collective-permute-start.18 = (f32[8,24,256]{2,0,1:T(8,128)S(1)}, f32[8,24,256]{2,0,1:T(8,128)S(1)}, u32[]{:S(2)}, u32[]{:S(2)}) collective-permute-start(f32[8,24,256]{2,0,1:T(8,128)S(1)} %fusion.51), channel_id=1, source_target_pairs={{8,0},{9,1},{10,2},{11,3},{12,4},{13,5},{14,6},{15,7},{16,8},{17,9... | collective-permute-start | bytes 589832 | tf_op jit(solution)/shard_map/ppermute | solution.py:19
  164.5 12.1 %collective-permute-start.21 = (f32[8,24,256]{2,0,1:T(8,128)S(1)}, f32[8,24,256]{2,0,1:T(8,128)S(1)}, u32[]{:S(2)}, u32[]{:S(2)}) collective-permute-start(f32[8,24,256]{2,0,1:T(8,128)S(1)} %broadcast_select_fusion.2), channel_id=1, source_target_pairs={{0,1},{1,2},{2,3},{3,4},{4,5},{5,6},{6,7},{7,8},{8,9},{9,10},{10,1... | collective-permute-start | bytes 589832 | tf_op jit(solution)/shard_map/ppermute | solution.py:19
  166.4 12.5 %collective-permute-start.20 = (f32[8,24,256]{2,0,1:T(8,128)S(1)}, f32[8,24,256]{2,0,1:T(8,128)S(1)}, u32[]{:S(2)}, u32[]{:S(2)}) collective-permute-start(f32[8,24,256]{2,0,1:T(8,128)S(1)} %broadcast_select_fusion.2), channel_id=1, source_target_pairs={{0,2},{1,3},{2,4},{3,5},{4,6},{5,7},{6,8},{7,9},{8,10},{9,11},{10,... | collective-permute-start | bytes 589832 | tf_op jit(solution)/shard_map/ppermute | solution.py:19
  174.0 24.0 %collective-permute-start.19 = (f32[8,24,256]{2,0,1:T(8,128)S(1)}, f32[8,24,256]{2,0,1:T(8,128)S(1)}, u32[]{:S(2)}, u32[]{:S(2)}) collective-permute-start(f32[8,24,256]{2,0,1:T(8,128)S(1)} %broadcast_select_fusion.2), channel_id=1, source_target_pairs={{0,3},{1,4},{2,5},{3,6},{4,7},{5,8},{6,9},{7,10},{8,11},{9,12},{10... | collective-permute-start | bytes 589832 | tf_op jit(solution)/shard_map/ppermute | solution.py:19
  198.0 12.1 %collective-permute-start.22 = (f32[8,24,256]{2,0,1:T(8,128)S(1)}, f32[8,24,256]{2,0,1:T(8,128)S(1)}, u32[]{:S(2)}, u32[]{:S(2)}) collective-permute-start(f32[8,24,256]{2,0,1:T(8,128)S(1)} %select_select_fusion.1), channel_id=1, source_target_pairs={{0,4},{1,5},{2,6},{3,7},{4,8},{5,9},{6,10},{7,11},{8,12},{9,13},{1... | collective-permute-start | bytes 589832 | tf_op jit(solution)/shard_map/ppermute | solution.py:19
  (13 other events, 35.0 us)

commit v4 on v3

--- a/solution.py
+++ b/solution.py
@@ -127,13 +127,14 @@
     low = q & 3
     bit2 = ((q >> 2) & 1) == 1
     bit3 = ((q >> 3) & 1) == 1
+    block = pick(block, [(-center, jnp.logical_not(bit3))], tiles)
     block = pick(block, [(1, low == 1), (2, low == 2), (3, low == 3)], tiles)
     block = pick(block, [(4, bit2)], tiles)
-    block = pick(block, [(-center, jnp.logical_not(bit3))], tiles)
     to_even = lax.ppermute(block, "tile", [(m + center, 2 * m) for m in range(half)])
     to_odd = lax.ppermute(block, "tile", [(m + center, 2 * m + 1) for m in range(half)])
-    next_odd = lax.ppermute(block, "tile", [(m + center + 1, 2 * m + 1) for m in range(half)])
-    odd_rows = jnp.concatenate([to_odd[:, coarse_rows:], next_odd[:, : foot_rows - coarse_rows]], axis=1)
+    next_rows = jnp.transpose(block[:, : foot_rows - coarse_rows], (1, 0, 2))
+    next_odd = lax.ppermute(next_rows, "tile", [(m + center + 1, 2 * m + 1) for m in range(half)])
+    odd_rows = jnp.concatenate([to_odd[:, coarse_rows:], jnp.transpose(next_odd, (1, 0, 2))], axis=1)
     footprint = jnp.where(tile_index % 2 == 0, to_even[:, :foot_rows], odd_rows)
 
     widen = repeat_matrix(coarse_cols, 3)

time: 217 us -> 202 us (0.931)
  the two profiles are of different devices: /device:TPU:170 before, /device:TPU:153 now
where the time goes in v4:
time: 202 us; the launch traced here: 201 us
  starting transfers between devices  90.5 us (45%)
  waiting for transfers between devices  70.2 us (35%)
  local copies, waits for them, and re-layouts  19.5 us (10%)
  other arithmetic  10.8 us (5%)
  between operations  7.69 us (4%)
  matrix products  2.43 us (1%)
    ppermute x14, starting transfers between devices, shift_from(): return lax.ppermute(value, axis, pairs)  69.4 us
    ppermute x14, waiting for transfers between devices, shift_from(): return lax.ppermute(value, axis, pairs)  65.2 us
    ppermute x4, starting transfers between devices, local(): lax.ppermute(means, 'tile', [(2 * m + k, m + center) for m in range(half...  7.32 us
    unnamed x30, local copies, waits for them, and re-layouts  6.93 us
    ppermute x1, starting transfers between devices, local(): lax.ppermute(block, 'tile', [(m + center, 2 * m) for m in range(half)])  6.63 us
    dynamic_update_slice x1, local copies, waits for them, and re-layouts, local(): lax.dynamic_update_slice_in_dim(advanced, merged, col_offset, axis=3)  5.09 us
  transfers between devices with their start and end apart: 23, of which 12 were waited for; matrix products, arithmetic and copies ran while one was open for 4% of the time, Pallas kernels for 0%

profile of v4, /device:TPU:153, one launch (start us, length us, event | category | flops | bytes accessed | tf_op | source)
XLA Modules:
  0.0 201.2 jit_solution(57860066313483831)
XLA Ops:
  3.0 2.6 %collective-permute-start.3 = (f32[3,8,3,768]{3,1,2,0:T(8,128)S(1)}, f32[3,8,3,768]{3,1,2,0:T(8,128)S(1)}, u32[]{:S(2)}, u32[]{:S(2)}) collective-permute-start(f32[3,8,3,768]{3,1,2,0:T(8,128)S(1)} %get-tuple-element.26), channel_id=1, source_target_pairs={{1,0},{2,1},{3,2},{4,3},{5,4},{6,5},{7,6},{8,7},{9,8},{10,9},{11,1... | collective-permute-start | bytes 663560 | tf_op jit(solution)/shard_map/ppermute | solution.py:19
  5.6 3.0 %collective-permute-start.2 = (f32[3,8,3,768]{3,1,2,0:T(8,128)S(1)}, f32[3,8,3,768]{3,1,2,0:T(8,128)S(1)}, u32[]{:S(2)}, u32[]{:S(2)}) collective-permute-start(f32[3,8,3,768]{3,1,2,0:T(8,128)S(1)} %get-tuple-element.27), channel_id=1, source_target_pairs={{0,1},{1,2},{2,3},{3,4},{4,5},{5,6},{6,7},{7,8},{8,9},{9,10},{10,1... | collective-permute-start | bytes 663560 | tf_op jit(solution)/shard_map/ppermute | solution.py:19
  8.9 2.4 %collective-permute-start = (f32[2,8,1,2048]{3,2,1,0:T(1,128)S(1)}, f32[2,8,1,2048]{3,2,1,0:T(1,128)S(1)}, u32[]{:S(2)}, u32[]{:S(2)}) collective-permute-start(f32[2,8,1,2048]{3,2,1,0:T(1,128)S(1)} %get-tuple-element.24), channel_id=1, source_target_pairs={{0,1},{1,2},{2,3},{3,4},{4,5},{5,6},{6,7},{7,8},{8,9},{9,10},{10,1... | collective-permute-start | bytes 393224 | tf_op jit(solution)/shard_map/ppermute | solution.py:29
  20.9 7.5 %collective-permute-start.5 = (f32[26,8,256]{2,0,1:T(8,128)S(1)}, f32[26,8,256]{2,0,1:T(8,128)S(1)}, u32[]{:S(2)}, u32[]{:S(2)}) collective-permute-start(f32[26,8,256]{2,0,1:T(8,128)S(1)} %pad_maximum_fusion.15), channel_id=1, source_target_pairs={{1,0},{2,1},{3,2},{4,3},{5,4},{6,5},{7,6},{8,7},{9,8},{10,9},{11,1... | collective-permute-start | bytes 638984 | tf_op jit(solution)/shard_map/ppermute | solution.py:19
  35.1 3.9 %collective-permute-start.6 = (f32[26,8,256]{2,0,1:T(8,128)S(1)}, f32[26,8,256]{2,0,1:T(8,128)S(1)}, u32[]{:S(2)}, u32[]{:S(2)}) collective-permute-start(f32[26,8,256]{2,0,1:T(8,128)S(1)} %fusion.48), channel_id=1, source_target_pairs={{0,8},{1,9},{2,10},{3,11},{4,12},{5,13},{6,14},{7,15},{8,16},{9,17... | collective-permute-start | bytes 638984 | tf_op jit(solution)/shard_map/ppermute | solution.py:19
  39.0 6.6 %collective-permute-done.6 = f32[26,8,256]{2,0,1:T(8,128)S(1)} collective-permute-done((f32[26,8,256]{2,0,1:T(8,128)S(1)}, f32[26,8,256]{2,0,1:T(8,128)S(1)}, u32[]{:S(2)}, u32[]{:S(2)}) %collective-permute-start.6) | collective-permute-done | bytes 213024 | tf_op jit(solution)/shard_map/ppermute | solution.py:19
  45.7 8.7 %collective-permute-start.9 = (f32[26,8,256]{2,0,1:T(8,128)S(1)}, f32[26,8,256]{2,0,1:T(8,128)S(1)}, u32[]{:S(2)}, u32[]{:S(2)}) collective-permute-start(f32[26,8,256]{2,0,1:T(8,128)S(1)} %broadcast_select_fusion), channel_id=1, source_target_pairs={{1,0},{2,1},{3,2},{4,3},{5,4},{6,5},{7,6},{8,7},{9,8},{10,9},{11,1... | collective-permute-start | bytes 638984 | tf_op jit(solution)/shard_map/ppermute | solution.py:19
  54.4 4.4 %collective-permute-start.8 = (f32[26,8,256]{2,0,1:T(8,128)S(1)}, f32[26,8,256]{2,0,1:T(8,128)S(1)}, u32[]{:S(2)}, u32[]{:S(2)}) collective-permute-start(f32[26,8,256]{2,0,1:T(8,128)S(1)} %broadcast_select_fusion), channel_id=1, source_target_pairs={{2,0},{3,1},{4,2},{5,3},{6,4},{7,5},{8,6},{9,7},{10,8},{11,9},{12,... | collective-permute-start | bytes 638984 | tf_op jit(solution)/shard_map/ppermute | solution.py:19
  61.4 17.2 %collective-permute-done.8 = f32[26,8,256]{2,0,1:T(8,128)S(1)} collective-permute-done((f32[26,8,256]{2,0,1:T(8,128)S(1)}, f32[26,8,256]{2,0,1:T(8,128)S(1)}, u32[]{:S(2)}, u32[]{:S(2)}) %collective-permute-start.8) | collective-permute-done | bytes 213024 | tf_op jit(solution)/shard_map/ppermute | solution.py:19
  78.6 11.2 %collective-permute-done.7 = f32[26,8,256]{2,0,1:T(8,128)S(1)} collective-permute-done((f32[26,8,256]{2,0,1:T(8,128)S(1)}, f32[26,8,256]{2,0,1:T(8,128)S(1)}, u32[]{:S(2)}, u32[]{:S(2)}) %collective-permute-start.7) | collective-permute-done | bytes 213024 | tf_op jit(solution)/shard_map/ppermute | solution.py:19
  89.9 10.3 %collective-permute-start.10 = (f32[26,8,256]{2,0,1:T(8,128)S(1)}, f32[26,8,256]{2,0,1:T(8,128)S(1)}, u32[]{:S(2)}, u32[]{:S(2)}) collective-permute-start(f32[26,8,256]{2,0,1:T(8,128)S(1)} %select_select_fusion), channel_id=1, source_target_pairs={{4,0},{5,1},{6,2},{7,3},{8,4},{9,5},{10,6},{11,7},{12,8},{13,9},{1... | collective-permute-start | bytes 638984 | tf_op jit(solution)/shard_map/ppermute | solution.py:19
  100.2 5.2 %collective-permute-done.10 = f32[26,8,256]{2,0,1:T(8,128)S(1)} collective-permute-done((f32[26,8,256]{2,0,1:T(8,128)S(1)}, f32[26,8,256]{2,0,1:T(8,128)S(1)}, u32[]{:S(2)}, u32[]{:S(2)}) %collective-permute-start.10) | collective-permute-done | bytes 213024 | tf_op jit(solution)/shard_map/ppermute | solution.py:19
  107.4 6.6 %collective-permute-start.11 = (f32[26,8,256]{2,0,1:T(8,128)S(1)}, f32[26,8,256]{2,0,1:T(8,128)S(1)}, u32[]{:S(2)}, u32[]{:S(2)}) collective-permute-start(f32[26,8,256]{2,0,1:T(8,128)S(1)} %broadcast_select_fusion.1), channel_id=1, source_target_pairs={{8,0},{9,2},{10,4},{11,6},{12,8},{13,10},{14,12},{15,14},{16,16},{... | collective-permute-start | bytes 638984 | tf_op jit(solution)/shard_map/ppermute | solution.py:133
  133.7 4.1 %collective-permute-start.17 = (f32[4,24,256]{2,0,1:T(4,128)S(1)}, f32[4,24,256]{2,0,1:T(4,128)S(1)}, u32[]{:S(2)}, u32[]{:S(2)}) collective-permute-start(f32[4,24,256]{2,0,1:T(4,128)S(1)} %bitcast.158), channel_id=1, source_target_pairs={{1,8},{3,9},{5,10},{7,11},{9,12},{11,13},{13,14},{15,15},{17,16},{... | collective-permute-start | bytes 294920 | tf_op jit(solution)/shard_map/ppermute | solution.py:166
  141.1 2.6 %collective-permute-done.16 = f32[4,24,256]{2,0,1:T(4,128)S(1)} collective-permute-done((f32[4,24,256]{2,0,1:T(4,128)S(1)}, f32[4,24,256]{2,0,1:T(4,128)S(1)}, u32[]{:S(2)}, u32[]{:S(2)}) %collective-permute-start.16) | collective-permute-done | bytes 98336 | tf_op jit(solution)/shard_map/ppermute | solution.py:166
  143.9 9.3 %collective-permute-start.18 = (f32[8,24,256]{2,0,1:T(8,128)S(1)}, f32[8,24,256]{2,0,1:T(8,128)S(1)}, u32[]{:S(2)}, u32[]{:S(2)}) collective-permute-start(f32[8,24,256]{2,0,1:T(8,128)S(1)} %fusion.51), channel_id=1, source_target_pairs={{8,0},{9,1},{10,2},{11,3},{12,4},{13,5},{14,6},{15,7},{16,8},{17,9... | collective-permute-start | bytes 589832 | tf_op jit(solution)/shard_map/ppermute | solution.py:19
  153.3 4.1 %collective-permute-done.18 = f32[8,24,256]{2,0,1:T(8,128)S(1)} collective-permute-done((f32[8,24,256]{2,0,1:T(8,128)S(1)}, f32[8,24,256]{2,0,1:T(8,128)S(1)}, u32[]{:S(2)}, u32[]{:S(2)}) %collective-permute-start.18) | collective-permute-done | bytes 196640 | tf_op jit(solution)/shard_map/ppermute | solution.py:19
  157.3 2.0 collective-permute-start.21
  159.4 5.4 %collective-permute-start.20 = (f32[8,24,256]{2,0,1:T(8,128)S(1)}, f32[8,24,256]{2,0,1:T(8,128)S(1)}, u32[]{:S(2)}, u32[]{:S(2)}) collective-permute-start(f32[8,24,256]{2,0,1:T(8,128)S(1)} %broadcast_select_fusion.2), channel_id=1, source_target_pairs={{0,2},{1,3},{2,4},{3,5},{4,6},{5,7},{6,8},{7,9},{8,10},{9,11},{10,... | collective-permute-start | bytes 589832 | tf_op jit(solution)/shard_map/ppermute | solution.py:19
  164.8 6.4 %collective-permute-start.19 = (f32[8,24,256]{2,0,1:T(8,128)S(1)}, f32[8,24,256]{2,0,1:T(8,128)S(1)}, u32[]{:S(2)}, u32[]{:S(2)}) collective-permute-start(f32[8,24,256]{2,0,1:T(8,128)S(1)} %broadcast_select_fusion.2), channel_id=1, source_target_pairs={{0,3},{1,4},{2,5},{3,6},{4,7},{5,8},{6,9},{7,10},{8,11},{9,12},{10... | collective-permute-start | bytes 589832 | tf_op jit(solution)/shard_map/ppermute | solution.py:19
  171.9 6.0 %collective-permute-done.20 = f32[8,24,256]{2,0,1:T(8,128)S(1)} collective-permute-done((f32[8,24,256]{2,0,1:T(8,128)S(1)}, f32[8,24,256]{2,0,1:T(8,128)S(1)}, u32[]{:S(2)}, u32[]{:S(2)}) %collective-permute-start.20) | collective-permute-done | bytes 196640 | tf_op jit(solution)/shard_map/ppermute | solution.py:19
  177.8 2.4 %collective-permute-done.19 = f32[8,24,256]{2,0,1:T(8,128)S(1)} collective-permute-done((f32[8,24,256]{2,0,1:T(8,128)S(1)}, f32[8,24,256]{2,0,1:T(8,128)S(1)}, u32[]{:S(2)}, u32[]{:S(2)}) %collective-permute-start.19) | collective-permute-done | bytes 196640 | tf_op jit(solution)/shard_map/ppermute | solution.py:19
  184.1 10.8 %collective-permute-done.22 = f32[8,24,256]{2,0,1:T(8,128)S(1)} collective-permute-done((f32[8,24,256]{2,0,1:T(8,128)S(1)}, f32[8,24,256]{2,0,1:T(8,128)S(1)}, u32[]{:S(2)}, u32[]{:S(2)}) %collective-permute-start.22) | collective-permute-done | bytes 196640 | tf_op jit(solution)/shard_map/ppermute | solution.py:19
  196.1 5.1 %dynamic_update_slice.3 = f32[3,8,8,2048]{3,2,1,0:T(8,128)} dynamic-update-slice(f32[3,8,8,2048]{3,2,1,0:T(8,128)} %copy-done.2, f32[3,8,8,256]{3,2,1,0:T(8,128)S(1)} %dynamic-slice_select_fusion, s32[]{:T(128)} %constant.79.clone.1, s32[]{:T(128)} %constant.79.clone.1, s32[]{:T(128)} %constant.79.clone.1, s32[]{:T(128)S(6)} %select_n.155) | dynamic-update-slice | bytes 393220 | tf_op jit(solution)/shard_map/dynamic_update_slice | solution.py:181
  (136 shorter events, 45.4 us)
Async XLA Ops:
  3.0 17.9 %collective-permute-start.3 = (f32[3,8,3,768]{3,1,2,0:T(8,128)S(1)}, f32[3,8,3,768]{3,1,2,0:T(8,128)S(1)}, u32[]{:S(2)}, u32[]{:S(2)}) collective-permute-start(f32[3,8,3,768]{3,1,2,0:T(8,128)S(1)} %get-tuple-element.26), channel_id=1, source_target_pairs={{1,0},{2,1},{3,2},{4,3},{5,4},{6,5},{7,6},{8,7},{9,8},{10,9},{11,1... | collective-permute-start | bytes 663560 | tf_op jit(solution)/shard_map/ppermute | solution.py:19
  5.6 15.3 %collective-permute-start.2 = (f32[3,8,3,768]{3,1,2,0:T(8,128)S(1)}, f32[3,8,3,768]{3,1,2,0:T(8,128)S(1)}, u32[]{:S(2)}, u32[]{:S(2)}) collective-permute-start(f32[3,8,3,768]{3,1,2,0:T(8,128)S(1)} %get-tuple-element.27), channel_id=1, source_target_pairs={{0,1},{1,2},{2,3},{3,4},{4,5},{5,6},{6,7},{7,8},{8,9},{9,10},{10,1... | collective-permute-start | bytes 663560 | tf_op jit(solution)/shard_map/ppermute | solution.py:19
  8.9 8.4 %collective-permute-start = (f32[2,8,1,2048]{3,2,1,0:T(1,128)S(1)}, f32[2,8,1,2048]{3,2,1,0:T(1,128)S(1)}, u32[]{:S(2)}, u32[]{:S(2)}) collective-permute-start(f32[2,8,1,2048]{3,2,1,0:T(1,128)S(1)} %get-tuple-element.24), channel_id=1, source_target_pairs={{0,1},{1,2},{2,3},{3,4},{4,5},{5,6},{6,7},{7,8},{8,9},{9,10},{10,1... | collective-permute-start | bytes 393224 | tf_op jit(solution)/shard_map/ppermute | solution.py:29
  11.4 6.6 %collective-permute-start.1 = (f32[2,8,1,2048]{3,2,1,0:T(1,128)S(1)}, f32[2,8,1,2048]{3,2,1,0:T(1,128)S(1)}, u32[]{:S(2)}, u32[]{:S(2)}) collective-permute-start(f32[2,8,1,2048]{3,2,1,0:T(1,128)S(1)} %get-tuple-element.25), channel_id=1, source_target_pairs={{1,0},{2,1},{3,2},{4,3},{5,4},{6,5},{7,6},{8,7},{9,8},{10,9},{11,1... | collective-permute-start | bytes 393224 | tf_op jit(solution)/shard_map/ppermute | solution.py:30
  20.2 100.7 %copy-start.2 = (f32[3,8,8,2048]{3,2,1,0:T(8,128)}, f32[3,8,8,2048]{3,2,1,0:T(8,128)S(1)}, u32[]{:S(2)}) copy-start(f32[3,8,8,2048]{3,2,1,0:T(8,128)S(1)} %pad_maximum_fusion.1) | copy-start | bytes 4718596
  20.9 14.1 %collective-permute-start.5 = (f32[26,8,256]{2,0,1:T(8,128)S(1)}, f32[26,8,256]{2,0,1:T(8,128)S(1)}, u32[]{:S(2)}, u32[]{:S(2)}) collective-permute-start(f32[26,8,256]{2,0,1:T(8,128)S(1)} %pad_maximum_fusion.15), channel_id=1, source_target_pairs={{1,0},{2,1},{3,2},{4,3},{5,4},{6,5},{7,6},{8,7},{9,8},{10,9},{11,1... | collective-permute-start | bytes 638984 | tf_op jit(solution)/shard_map/ppermute | solution.py:19
  28.5 6.6 %collective-permute-start.4 = (f32[26,256]{1,0:T(8,128)S(1)}, f32[26,256]{1,0:T(8,128)S(1)}, u32[]{:S(2)}, u32[]{:S(2)}) collective-permute-start(f32[26,256]{1,0:T(8,128)S(1)} %slice_bitcast_fusion.11), channel_id=1, source_target_pairs={{0,1},{1,2},{2,3},{3,4},{4,5},{5,6},{6,7},{7,8},{8,9},{9,10},{10,1... | collective-permute-start | bytes 79880 | tf_op jit(solution)/shard_map/ppermute | solution.py:19
  35.1 10.5 %collective-permute-start.6 = (f32[26,8,256]{2,0,1:T(8,128)S(1)}, f32[26,8,256]{2,0,1:T(8,128)S(1)}, u32[]{:S(2)}, u32[]{:S(2)}) collective-permute-start(f32[26,8,256]{2,0,1:T(8,128)S(1)} %fusion.48), channel_id=1, source_target_pairs={{0,8},{1,9},{2,10},{3,11},{4,12},{5,13},{6,14},{7,15},{8,16},{9,17... | collective-permute-start | bytes 638984 | tf_op jit(solution)/shard_map/ppermute | solution.py:19
  45.7 15.7 %collective-permute-start.9 = (f32[26,8,256]{2,0,1:T(8,128)S(1)}, f32[26,8,256]{2,0,1:T(8,128)S(1)}, u32[]{:S(2)}, u32[]{:S(2)}) collective-permute-start(f32[26,8,256]{2,0,1:T(8,128)S(1)} %broadcast_select_fusion), channel_id=1, source_target_pairs={{1,0},{2,1},{3,2},{4,3},{5,4},{6,5},{7,6},{8,7},{9,8},{10,9},{11,1... | collective-permute-start | bytes 638984 | tf_op jit(solution)/shard_map/ppermute | solution.py:19
  54.4 24.2 %collective-permute-start.8 = (f32[26,8,256]{2,0,1:T(8,128)S(1)}, f32[26,8,256]{2,0,1:T(8,128)S(1)}, u32[]{:S(2)}, u32[]{:S(2)}) collective-permute-start(f32[26,8,256]{2,0,1:T(8,128)S(1)} %broadcast_select_fusion), channel_id=1, source_target_pairs={{2,0},{3,1},{4,2},{5,3},{6,4},{7,5},{8,6},{9,7},{10,8},{11,9},{12,... | collective-permute-start | bytes 638984 | tf_op jit(solution)/shard_map/ppermute | solution.py:19
  58.8 31.0 %collective-permute-start.7 = (f32[26,8,256]{2,0,1:T(8,128)S(1)}, f32[26,8,256]{2,0,1:T(8,128)S(1)}, u32[]{:S(2)}, u32[]{:S(2)}) collective-permute-start(f32[26,8,256]{2,0,1:T(8,128)S(1)} %broadcast_select_fusion), channel_id=1, source_target_pairs={{3,0},{4,1},{5,2},{6,3},{7,4},{8,5},{9,6},{10,7},{11,8},{12,9},{13... | collective-permute-start | bytes 638984 | tf_op jit(solution)/shard_map/ppermute | solution.py:19
  89.9 15.6 %collective-permute-start.10 = (f32[26,8,256]{2,0,1:T(8,128)S(1)}, f32[26,8,256]{2,0,1:T(8,128)S(1)}, u32[]{:S(2)}, u32[]{:S(2)}) collective-permute-start(f32[26,8,256]{2,0,1:T(8,128)S(1)} %select_select_fusion), channel_id=1, source_target_pairs={{4,0},{5,1},{6,2},{7,3},{8,4},{9,5},{10,6},{11,7},{12,8},{13,9},{1... | collective-permute-start | bytes 638984 | tf_op jit(solution)/shard_map/ppermute | solution.py:19
  105.5 10.0 %collective-permute-start.12 = (f32[26,8,256]{2,0,1:T(8,128)S(1)}, f32[26,8,256]{2,0,1:T(8,128)S(1)}, u32[]{:S(2)}, u32[]{:S(2)}) collective-permute-start(f32[26,8,256]{2,0,1:T(8,128)S(1)} %broadcast_select_fusion.1), channel_id=1, source_target_pairs={{8,1},{9,3},{10,5},{11,7},{12,9},{13,11},{14,13},{15,15},{16,17},{... | collective-permute-start | bytes 638984 | tf_op jit(solution)/shard_map/ppermute | solution.py:134
  107.4 9.9 %collective-permute-start.11 = (f32[26,8,256]{2,0,1:T(8,128)S(1)}, f32[26,8,256]{2,0,1:T(8,128)S(1)}, u32[]{:S(2)}, u32[]{:S(2)}) collective-permute-start(f32[26,8,256]{2,0,1:T(8,128)S(1)} %broadcast_select_fusion.1), channel_id=1, source_target_pairs={{8,0},{9,2},{10,4},{11,6},{12,8},{13,10},{14,12},{15,14},{16,16},{... | collective-permute-start | bytes 638984 | tf_op jit(solution)/shard_map/ppermute | solution.py:133
  114.0 1.4 collective-permute-start.13
  133.7 7.4 %collective-permute-start.17 = (f32[4,24,256]{2,0,1:T(4,128)S(1)}, f32[4,24,256]{2,0,1:T(4,128)S(1)}, u32[]{:S(2)}, u32[]{:S(2)}) collective-permute-start(f32[4,24,256]{2,0,1:T(4,128)S(1)} %bitcast.158), channel_id=1, source_target_pairs={{1,8},{3,9},{5,10},{7,11},{9,12},{11,13},{13,14},{15,15},{17,16},{... | collective-permute-start | bytes 294920 | tf_op jit(solution)/shard_map/ppermute | solution.py:166
  137.8 5.9 %collective-permute-start.16 = (f32[4,24,256]{2,0,1:T(4,128)S(1)}, f32[4,24,256]{2,0,1:T(4,128)S(1)}, u32[]{:S(2)}, u32[]{:S(2)}) collective-permute-start(f32[4,24,256]{2,0,1:T(4,128)S(1)} %bitcast.159), channel_id=1, source_target_pairs={{0,8},{2,9},{4,10},{6,11},{8,12},{10,13},{12,14},{14,15},{16,16},{... | collective-permute-start | bytes 294920 | tf_op jit(solution)/shard_map/ppermute | solution.py:166
  139.1 4.6 %collective-permute-start.15 = (f32[4,24,256]{2,0,1:T(4,128)S(1)}, f32[4,24,256]{2,0,1:T(4,128)S(1)}, u32[]{:S(2)}, u32[]{:S(2)}) collective-permute-start(f32[4,24,256]{2,0,1:T(4,128)S(1)} %bitcast.160), channel_id=1, source_target_pairs={{1,9},{3,10},{5,11},{7,12},{9,13},{11,14},{13,15},{15,16},{17,17},... | collective-permute-start | bytes 294920 | tf_op jit(solution)/shard_map/ppermute | solution.py:166
  139.8 4.0 %collective-permute-start.14 = (f32[4,24,256]{2,0,1:T(4,128)S(1)}, f32[4,24,256]{2,0,1:T(4,128)S(1)}, u32[]{:S(2)}, u32[]{:S(2)}) collective-permute-start(f32[4,24,256]{2,0,1:T(4,128)S(1)} %bitcast.161), channel_id=1, source_target_pairs={{0,9},{2,10},{4,11},{6,12},{8,13},{10,14},{12,15},{14,16},{16,17},... | collective-permute-start | bytes 294920 | tf_op jit(solution)/shard_map/ppermute | solution.py:166
  143.9 13.4 %collective-permute-start.18 = (f32[8,24,256]{2,0,1:T(8,128)S(1)}, f32[8,24,256]{2,0,1:T(8,128)S(1)}, u32[]{:S(2)}, u32[]{:S(2)}) collective-permute-start(f32[8,24,256]{2,0,1:T(8,128)S(1)} %fusion.51), channel_id=1, source_target_pairs={{8,0},{9,1},{10,2},{11,3},{12,4},{13,5},{14,6},{15,7},{16,8},{17,9... | collective-permute-start | bytes 589832 | tf_op jit(solution)/shard_map/ppermute | solution.py:19
  157.3 14.5 %collective-permute-start.21 = (f32[8,24,256]{2,0,1:T(8,128)S(1)}, f32[8,24,256]{2,0,1:T(8,128)S(1)}, u32[]{:S(2)}, u32[]{:S(2)}) collective-permute-start(f32[8,24,256]{2,0,1:T(8,128)S(1)} %broadcast_select_fusion.2), channel_id=1, source_target_pairs={{0,1},{1,2},{2,3},{3,4},{4,5},{5,6},{6,7},{7,8},{8,9},{9,10},{10,1... | collective-permute-start | bytes 589832 | tf_op jit(solution)/shard_map/ppermute | solution.py:19
  159.4 18.5 %collective-permute-start.20 = (f32[8,24,256]{2,0,1:T(8,128)S(1)}, f32[8,24,256]{2,0,1:T(8,128)S(1)}, u32[]{:S(2)}, u32[]{:S(2)}) collective-permute-start(f32[8,24,256]{2,0,1:T(8,128)S(1)} %broadcast_select_fusion.2), channel_id=1, source_target_pairs={{0,2},{1,3},{2,4},{3,5},{4,6},{5,7},{6,8},{7,9},{8,10},{9,11},{10,... | collective-permute-start | bytes 589832 | tf_op jit(solution)/shard_map/ppermute | solution.py:19
  164.8 15.5 %collective-permute-start.19 = (f32[8,24,256]{2,0,1:T(8,128)S(1)}, f32[8,24,256]{2,0,1:T(8,128)S(1)}, u32[]{:S(2)}, u32[]{:S(2)}) collective-permute-start(f32[8,24,256]{2,0,1:T(8,128)S(1)} %broadcast_select_fusion.2), channel_id=1, source_target_pairs={{0,3},{1,4},{2,5},{3,6},{4,7},{5,8},{6,9},{7,10},{8,11},{9,12},{10... | collective-permute-start | bytes 589832 | tf_op jit(solution)/shard_map/ppermute | solution.py:19
  180.3 14.6 %collective-permute-start.22 = (f32[8,24,256]{2,0,1:T(8,128)S(1)}, f32[8,24,256]{2,0,1:T(8,128)S(1)}, u32[]{:S(2)}, u32[]{:S(2)}) collective-permute-start(f32[8,24,256]{2,0,1:T(8,128)S(1)} %select_select_fusion.1), channel_id=1, source_target_pairs={{0,4},{1,5},{2,6},{3,7},{4,8},{5,9},{6,10},{7,11},{8,12},{9,13},{1... | collective-permute-start | bytes 589832 | tf_op jit(solution)/shard_map/ppermute | solution.py:19
  (13 other events, 34.4 us)

commit v5 on v4

--- a/solution.py
+++ b/solution.py
@@ -56,6 +56,14 @@
     rows = jnp.arange(small, dtype=jnp.int32)[:, None]
     cols = jnp.arange(small * factor, dtype=jnp.int32)[None, :] // factor
     return (rows == cols).astype(jnp.float32)
+
+
+def rotate(value, options, slab, tiles):
+    out = value
+    for offset, predicate in options:
+        pairs = [(s + (w + offset) % slab, s + w) for s in range(0, tiles, slab) for w in range(slab)]
+        out = jnp.where(predicate, lax.ppermute(value, "tile", pairs), out)
+    return out
 
 
 def pick(value, options, tiles):
@@ -81,7 +89,7 @@
     coarse_total = nest_total // 3
     largest_offset = band_rows - coarse_total - 1
     largest_q = largest_offset // parent_rows
-    assert largest_q < 16 and tiles >= 2 * 16
+    assert largest_q < 16 and tiles % 8 == 0 and tiles >= 32
     center = 8
     planes = 3 * levels
     half = tiles // 2
@@ -127,9 +135,13 @@
     low = q & 3
     bit2 = ((q >> 2) & 1) == 1
     bit3 = ((q >> 3) & 1) == 1
-    block = pick(block, [(-center, jnp.logical_not(bit3))], tiles)
-    block = pick(block, [(1, low == 1), (2, low == 2), (3, low == 3)], tiles)
-    block = pick(block, [(4, bit2)], tiles)
+    low3 = q & (center - 1)
+    slab_pos = tile_index % center
+    block = rotate(block, [(1, low == 1), (2, low == 2), (3, low == 3)], center, tiles)
+    block = rotate(block, [(4, bit2)], center, tiles)
+    carry = (slab_pos + low3 >= center).astype(jnp.int32)
+    slab_shift = bit3.astype(jnp.int32) + carry - 1
+    block = pick(block, [(-center, slab_shift == -1), (center, slab_shift == 1)], tiles)
     to_even = lax.ppermute(block, "tile", [(m + center, 2 * m) for m in range(half)])
     to_odd = lax.ppermute(block, "tile", [(m + center, 2 * m + 1) for m in range(half)])
     next_rows = jnp.transpose(block[:, : foot_rows - coarse_rows], (1, 0, 2))

time: 202 us -> 197 us (0.975)
  the two profiles are of different devices: /device:TPU:153 before, /device:TPU:170 now
where the time goes in v5:
time: 197 us; the launch traced here: 196 us
  waiting for transfers between devices  82.5 us (42%)
  starting transfers between devices  72.6 us (37%)
  local copies, waits for them, and re-layouts  19.6 us (10%)
  other arithmetic  10.9 us (6%)
  between operations  7.82 us (4%)
  matrix products  2.43 us (1%)
    ppermute x11, waiting for transfers between devices, shift_from(): return lax.ppermute(value, axis, pairs)  52.7 us
    ppermute x11, starting transfers between devices, shift_from(): return lax.ppermute(value, axis, pairs)  32.1 us
    ppermute x4, starting transfers between devices, rotate(): out = jnp.where(predicate, lax.ppermute(value, 'tile', pairs), out)  16.7 us
    ppermute x4, waiting for transfers between devices, rotate(): out = jnp.where(predicate, lax.ppermute(value, 'tile', pairs), out)  16 us
    ppermute x4, waiting for transfers between devices, local(): lax.ppermute(means, 'tile', [(2 * m + k, m + center) for m in range(half...  11.5 us
    ppermute x4, starting transfers between devices, local(): lax.ppermute(means, 'tile', [(2 * m + k, m + center) for m in range(half...  9.97 us
    unnamed x30, local copies, waits for them, and re-layouts  6.98 us
    dynamic_update_slice x1, local copies, waits for them, and re-layouts, local(): lax.dynamic_update_slice_in_dim(advanced, merged, col_offset, axis=3)  5.06 us
  transfers between devices with their start and end apart: 24, of which 13 were waited for; matrix products, arithmetic and copies ran while one was open for 4% of the time, Pallas kernels for 0%

profile of v5, /device:TPU:170, one launch (start us, length us, event | category | flops | bytes accessed | tf_op | source)
XLA Modules:
  0.0 195.7 jit_solution(5005849910074686144)
XLA Ops:
  5.0 2.4 %collective-permute-start.2 = (f32[3,8,3,768]{3,1,2,0:T(8,128)S(1)}, f32[3,8,3,768]{3,1,2,0:T(8,128)S(1)}, u32[]{:S(2)}, u32[]{:S(2)}) collective-permute-start(f32[3,8,3,768]{3,1,2,0:T(8,128)S(1)} %get-tuple-element.27), channel_id=1, source_target_pairs={{0,1},{1,2},{2,3},{3,4},{4,5},{5,6},{6,7},{7,8},{8,9},{9,10},{10,1... | collective-permute-start | bytes 663560 | tf_op jit(solution)/shard_map/ppermute | solution.py:19
  7.7 3.0 %collective-permute-start = (f32[2,8,1,2048]{3,2,1,0:T(1,128)S(1)}, f32[2,8,1,2048]{3,2,1,0:T(1,128)S(1)}, u32[]{:S(2)}, u32[]{:S(2)}) collective-permute-start(f32[2,8,1,2048]{3,2,1,0:T(1,128)S(1)} %get-tuple-element.24), channel_id=1, source_target_pairs={{0,1},{1,2},{2,3},{3,4},{4,5},{5,6},{6,7},{7,8},{8,9},{9,10},{10,1... | collective-permute-start | bytes 393224 | tf_op jit(solution)/shard_map/ppermute | solution.py:29
  10.7 2.5 %collective-permute-start.1 = (f32[2,8,1,2048]{3,2,1,0:T(1,128)S(1)}, f32[2,8,1,2048]{3,2,1,0:T(1,128)S(1)}, u32[]{:S(2)}, u32[]{:S(2)}) collective-permute-start(f32[2,8,1,2048]{3,2,1,0:T(1,128)S(1)} %get-tuple-element.25), channel_id=1, source_target_pairs={{1,0},{2,1},{3,2},{4,3},{5,4},{6,5},{7,6},{8,7},{9,8},{10,9},{11,1... | collective-permute-start | bytes 393224 | tf_op jit(solution)/shard_map/ppermute | solution.py:30
  20.4 2.5 %collective-permute-start.5 = (f32[26,8,256]{2,0,1:T(8,128)S(1)}, f32[26,8,256]{2,0,1:T(8,128)S(1)}, u32[]{:S(2)}, u32[]{:S(2)}) collective-permute-start(f32[26,8,256]{2,0,1:T(8,128)S(1)} %pad_maximum_fusion.15), channel_id=1, source_target_pairs={{1,0},{2,1},{3,2},{4,3},{5,4},{6,5},{7,6},{8,7},{9,8},{10,9},{11,1... | collective-permute-start | bytes 638984 | tf_op jit(solution)/shard_map/ppermute | solution.py:19
  28.0 4.3 %collective-permute-done.4 = f32[26,256]{1,0:T(8,128)S(1)} collective-permute-done((f32[26,256]{1,0:T(8,128)S(1)}, f32[26,256]{1,0:T(8,128)S(1)}, u32[]{:S(2)}, u32[]{:S(2)}) %collective-permute-start.4) | collective-permute-done | bytes 26656 | tf_op jit(solution)/shard_map/ppermute | solution.py:19
  32.4 4.1 %collective-permute-start.8 = (f32[26,8,256]{2,0,1:T(8,128)S(1)}, f32[26,8,256]{2,0,1:T(8,128)S(1)}, u32[]{:S(2)}, u32[]{:S(2)}) collective-permute-start(f32[26,8,256]{2,0,1:T(8,128)S(1)} %fusion.48), channel_id=1, source_target_pairs={{1,0},{2,1},{3,2},{4,3},{5,4},{6,5},{7,6},{0,7},{9,8},{10,9},{11,1... | collective-permute-start | bytes 638984 | tf_op jit(solution)/shard_map/ppermute | solution.py:65
  36.6 6.8 %collective-permute-start.7 = (f32[26,8,256]{2,0,1:T(8,128)S(1)}, f32[26,8,256]{2,0,1:T(8,128)S(1)}, u32[]{:S(2)}, u32[]{:S(2)}) collective-permute-start(f32[26,8,256]{2,0,1:T(8,128)S(1)} %fusion.48), channel_id=1, source_target_pairs={{2,0},{3,1},{4,2},{5,3},{6,4},{7,5},{0,6},{1,7},{10,8},{11,9},{12,... | collective-permute-start | bytes 638984 | tf_op jit(solution)/shard_map/ppermute | solution.py:65
  43.4 6.7 %collective-permute-done.7 = f32[26,8,256]{2,0,1:T(8,128)S(1)} collective-permute-done((f32[26,8,256]{2,0,1:T(8,128)S(1)}, f32[26,8,256]{2,0,1:T(8,128)S(1)}, u32[]{:S(2)}, u32[]{:S(2)}) %collective-permute-start.7) | collective-permute-done | bytes 213024 | tf_op jit(solution)/shard_map/ppermute | solution.py:65
  50.1 5.1 %collective-permute-done.6 = f32[26,8,256]{2,0,1:T(8,128)S(1)} collective-permute-done((f32[26,8,256]{2,0,1:T(8,128)S(1)}, f32[26,8,256]{2,0,1:T(8,128)S(1)}, u32[]{:S(2)}, u32[]{:S(2)}) %collective-permute-start.6) | collective-permute-done | bytes 213024 | tf_op jit(solution)/shard_map/ppermute | solution.py:65
  55.2 5.7 %collective-permute-start.9 = (f32[26,8,256]{2,0,1:T(8,128)S(1)}, f32[26,8,256]{2,0,1:T(8,128)S(1)}, u32[]{:S(2)}, u32[]{:S(2)}) collective-permute-start(f32[26,8,256]{2,0,1:T(8,128)S(1)} %select_select_fusion.1), channel_id=1, source_target_pairs={{4,0},{5,1},{6,2},{7,3},{0,4},{1,5},{2,6},{3,7},{12,8},{13,9},{14,... | collective-permute-start | bytes 638984 | tf_op jit(solution)/shard_map/ppermute | solution.py:65
  61.5 4.2 %collective-permute-done.9 = f32[26,8,256]{2,0,1:T(8,128)S(1)} collective-permute-done((f32[26,8,256]{2,0,1:T(8,128)S(1)}, f32[26,8,256]{2,0,1:T(8,128)S(1)}, u32[]{:S(2)}, u32[]{:S(2)}) %collective-permute-start.9) | collective-permute-done | bytes 213024 | tf_op jit(solution)/shard_map/ppermute | solution.py:65
  67.6 6.0 %collective-permute-start.10 = (f32[26,8,256]{2,0,1:T(8,128)S(1)}, f32[26,8,256]{2,0,1:T(8,128)S(1)}, u32[]{:S(2)}, u32[]{:S(2)}) collective-permute-start(f32[26,8,256]{2,0,1:T(8,128)S(1)} %broadcast_select_fusion), channel_id=1, source_target_pairs={{8,0},{9,1},{10,2},{11,3},{12,4},{13,5},{14,6},{15,7},{16,8},{17,9... | collective-permute-start | bytes 638984 | tf_op jit(solution)/shard_map/ppermute | solution.py:19
  73.7 6.4 %collective-permute-done.11 = f32[26,8,256]{2,0,1:T(8,128)S(1)} collective-permute-done((f32[26,8,256]{2,0,1:T(8,128)S(1)}, f32[26,8,256]{2,0,1:T(8,128)S(1)}, u32[]{:S(2)}, u32[]{:S(2)}) %collective-permute-start.11) | collective-permute-done | bytes 213024 | tf_op jit(solution)/shard_map/ppermute | solution.py:19
  81.6 2.8 %collective-permute-start.13 = (f32[26,8,256]{2,0,1:T(8,128)S(1)}, f32[26,8,256]{2,0,1:T(8,128)S(1)}, u32[]{:S(2)}, u32[]{:S(2)}) collective-permute-start(f32[26,8,256]{2,0,1:T(8,128)S(1)} %select_select_fusion), channel_id=1, source_target_pairs={{8,1},{9,3},{10,5},{11,7},{12,9},{13,11},{14,13},{15,15},{16,17},{... | collective-permute-start | bytes 638984 | tf_op jit(solution)/shard_map/ppermute | solution.py:146
  84.4 3.5 %collective-permute-start.12 = (f32[26,8,256]{2,0,1:T(8,128)S(1)}, f32[26,8,256]{2,0,1:T(8,128)S(1)}, u32[]{:S(2)}, u32[]{:S(2)}) collective-permute-start(f32[26,8,256]{2,0,1:T(8,128)S(1)} %select_select_fusion), channel_id=1, source_target_pairs={{8,0},{9,2},{10,4},{11,6},{12,8},{13,10},{14,12},{15,14},{16,16},{... | collective-permute-start | bytes 638984 | tf_op jit(solution)/shard_map/ppermute | solution.py:145
  90.6 2.1 %collective-permute-done.12 = f32[26,8,256]{2,0,1:T(8,128)S(1)} collective-permute-done((f32[26,8,256]{2,0,1:T(8,128)S(1)}, f32[26,8,256]{2,0,1:T(8,128)S(1)}, u32[]{:S(2)}, u32[]{:S(2)}) %collective-permute-start.12) | collective-permute-done | bytes 213024 | tf_op jit(solution)/shard_map/ppermute | solution.py:145
  110.5 6.7 %collective-permute-start.17 = (f32[4,24,256]{2,0,1:T(4,128)S(1)}, f32[4,24,256]{2,0,1:T(4,128)S(1)}, u32[]{:S(2)}, u32[]{:S(2)}) collective-permute-start(f32[4,24,256]{2,0,1:T(4,128)S(1)} %bitcast.159), channel_id=1, source_target_pairs={{0,8},{2,9},{4,10},{6,11},{8,12},{10,13},{12,14},{14,15},{16,16},{... | collective-permute-start | bytes 294920 | tf_op jit(solution)/shard_map/ppermute | solution.py:178
  119.2 10.8 %collective-permute-done.18 = f32[4,24,256]{2,0,1:T(4,128)S(1)} collective-permute-done((f32[4,24,256]{2,0,1:T(4,128)S(1)}, f32[4,24,256]{2,0,1:T(4,128)S(1)}, u32[]{:S(2)}, u32[]{:S(2)}) %collective-permute-start.18) | collective-permute-done | bytes 98336 | tf_op jit(solution)/shard_map/ppermute | solution.py:178
  132.8 10.9 %collective-permute-done.19 = f32[8,24,256]{2,0,1:T(8,128)S(1)} collective-permute-done((f32[8,24,256]{2,0,1:T(8,128)S(1)}, f32[8,24,256]{2,0,1:T(8,128)S(1)}, u32[]{:S(2)}, u32[]{:S(2)}) %collective-permute-start.19) | collective-permute-done | bytes 196640 | tf_op jit(solution)/shard_map/ppermute | solution.py:19
  145.7 5.9 %collective-permute-start.21 = (f32[8,24,256]{2,0,1:T(8,128)S(1)}, f32[8,24,256]{2,0,1:T(8,128)S(1)}, u32[]{:S(2)}, u32[]{:S(2)}) collective-permute-start(f32[8,24,256]{2,0,1:T(8,128)S(1)} %broadcast_select_fusion.1), channel_id=1, source_target_pairs={{0,2},{1,3},{2,4},{3,5},{4,6},{5,7},{6,8},{7,9},{8,10},{9,11},{10,... | collective-permute-start | bytes 589832 | tf_op jit(solution)/shard_map/ppermute | solution.py:19
  151.6 3.6 %collective-permute-start.20 = (f32[8,24,256]{2,0,1:T(8,128)S(1)}, f32[8,24,256]{2,0,1:T(8,128)S(1)}, u32[]{:S(2)}, u32[]{:S(2)}) collective-permute-start(f32[8,24,256]{2,0,1:T(8,128)S(1)} %broadcast_select_fusion.1), channel_id=1, source_target_pairs={{0,3},{1,4},{2,5},{3,6},{4,7},{5,8},{6,9},{7,10},{8,11},{9,12},{10... | collective-permute-start | bytes 589832 | tf_op jit(solution)/shard_map/ppermute | solution.py:19
  155.9 21.4 %collective-permute-done.20 = f32[8,24,256]{2,0,1:T(8,128)S(1)} collective-permute-done((f32[8,24,256]{2,0,1:T(8,128)S(1)}, f32[8,24,256]{2,0,1:T(8,128)S(1)}, u32[]{:S(2)}, u32[]{:S(2)}) %collective-permute-start.20) | collective-permute-done | bytes 196640 | tf_op jit(solution)/shard_map/ppermute | solution.py:19
  181.3 8.2 %collective-permute-done.23 = f32[8,24,256]{2,0,1:T(8,128)S(1)} collective-permute-done((f32[8,24,256]{2,0,1:T(8,128)S(1)}, f32[8,24,256]{2,0,1:T(8,128)S(1)}, u32[]{:S(2)}, u32[]{:S(2)}) %collective-permute-start.23) | collective-permute-done | bytes 196640 | tf_op jit(solution)/shard_map/ppermute | solution.py:19
  190.6 5.1 %dynamic_update_slice.3 = f32[3,8,8,2048]{3,2,1,0:T(8,128)} dynamic-update-slice(f32[3,8,8,2048]{3,2,1,0:T(8,128)} %copy-done.2, f32[3,8,8,256]{3,2,1,0:T(8,128)S(1)} %dynamic-slice_select_fusion, s32[]{:T(128)} %constant.89.clone.1, s32[]{:T(128)} %constant.89.clone.1, s32[]{:T(128)} %constant.89.clone.1, s32[]{:T(128)S(6)} %select_n.166) | dynamic-update-slice | bytes 393220 | tf_op jit(solution)/shard_map/dynamic_update_slice | solution.py:193
  (138 shorter events, 46.8 us)
Async XLA Ops:
  3.0 17.3 %collective-permute-start.3 = (f32[3,8,3,768]{3,1,2,0:T(8,128)S(1)}, f32[3,8,3,768]{3,1,2,0:T(8,128)S(1)}, u32[]{:S(2)}, u32[]{:S(2)}) collective-permute-start(f32[3,8,3,768]{3,1,2,0:T(8,128)S(1)} %get-tuple-element.26), channel_id=1, source_target_pairs={{1,0},{2,1},{3,2},{4,3},{5,4},{6,5},{7,6},{8,7},{9,8},{10,9},{11,1... | collective-permute-start | bytes 663560 | tf_op jit(solution)/shard_map/ppermute | solution.py:19
  5.0 15.4 %collective-permute-start.2 = (f32[3,8,3,768]{3,1,2,0:T(8,128)S(1)}, f32[3,8,3,768]{3,1,2,0:T(8,128)S(1)}, u32[]{:S(2)}, u32[]{:S(2)}) collective-permute-start(f32[3,8,3,768]{3,1,2,0:T(8,128)S(1)} %get-tuple-element.27), channel_id=1, source_target_pairs={{0,1},{1,2},{2,3},{3,4},{4,5},{5,6},{6,7},{7,8},{8,9},{9,10},{10,1... | collective-permute-start | bytes 663560 | tf_op jit(solution)/shard_map/ppermute | solution.py:19
  7.7 9.7 %collective-permute-start = (f32[2,8,1,2048]{3,2,1,0:T(1,128)S(1)}, f32[2,8,1,2048]{3,2,1,0:T(1,128)S(1)}, u32[]{:S(2)}, u32[]{:S(2)}) collective-permute-start(f32[2,8,1,2048]{3,2,1,0:T(1,128)S(1)} %get-tuple-element.24), channel_id=1, source_target_pairs={{0,1},{1,2},{2,3},{3,4},{4,5},{5,6},{6,7},{7,8},{8,9},{9,10},{10,1... | collective-permute-start | bytes 393224 | tf_op jit(solution)/shard_map/ppermute | solution.py:29
  10.7 6.7 %collective-permute-start.1 = (f32[2,8,1,2048]{3,2,1,0:T(1,128)S(1)}, f32[2,8,1,2048]{3,2,1,0:T(1,128)S(1)}, u32[]{:S(2)}, u32[]{:S(2)}) collective-permute-start(f32[2,8,1,2048]{3,2,1,0:T(1,128)S(1)} %get-tuple-element.25), channel_id=1, source_target_pairs={{1,0},{2,1},{3,2},{4,3},{5,4},{6,5},{7,6},{8,7},{9,8},{10,9},{11,1... | collective-permute-start | bytes 393224 | tf_op jit(solution)/shard_map/ppermute | solution.py:30
  20.4 12.0 %collective-permute-start.5 = (f32[26,8,256]{2,0,1:T(8,128)S(1)}, f32[26,8,256]{2,0,1:T(8,128)S(1)}, u32[]{:S(2)}, u32[]{:S(2)}) collective-permute-start(f32[26,8,256]{2,0,1:T(8,128)S(1)} %pad_maximum_fusion.15), channel_id=1, source_target_pairs={{1,0},{2,1},{3,2},{4,3},{5,4},{6,5},{7,6},{8,7},{9,8},{10,9},{11,1... | collective-permute-start | bytes 638984 | tf_op jit(solution)/shard_map/ppermute | solution.py:19
  22.9 9.5 %collective-permute-start.4 = (f32[26,256]{1,0:T(8,128)S(1)}, f32[26,256]{1,0:T(8,128)S(1)}, u32[]{:S(2)}, u32[]{:S(2)}) collective-permute-start(f32[26,256]{1,0:T(8,128)S(1)} %slice_bitcast_fusion.11), channel_id=1, source_target_pairs={{0,1},{1,2},{2,3},{3,4},{4,5},{5,6},{6,7},{7,8},{8,9},{9,10},{10,1... | collective-permute-start | bytes 79880 | tf_op jit(solution)/shard_map/ppermute | solution.py:19
  32.4 11.0 %collective-permute-start.8 = (f32[26,8,256]{2,0,1:T(8,128)S(1)}, f32[26,8,256]{2,0,1:T(8,128)S(1)}, u32[]{:S(2)}, u32[]{:S(2)}) collective-permute-start(f32[26,8,256]{2,0,1:T(8,128)S(1)} %fusion.48), channel_id=1, source_target_pairs={{1,0},{2,1},{3,2},{4,3},{5,4},{6,5},{7,6},{0,7},{9,8},{10,9},{11,1... | collective-permute-start | bytes 638984 | tf_op jit(solution)/shard_map/ppermute | solution.py:65
  36.6 13.5 %collective-permute-start.7 = (f32[26,8,256]{2,0,1:T(8,128)S(1)}, f32[26,8,256]{2,0,1:T(8,128)S(1)}, u32[]{:S(2)}, u32[]{:S(2)}) collective-permute-start(f32[26,8,256]{2,0,1:T(8,128)S(1)} %fusion.48), channel_id=1, source_target_pairs={{2,0},{3,1},{4,2},{5,3},{6,4},{7,5},{0,6},{1,7},{10,8},{11,9},{12,... | collective-permute-start | bytes 638984 | tf_op jit(solution)/shard_map/ppermute | solution.py:65
  43.4 11.8 %collective-permute-start.6 = (f32[26,8,256]{2,0,1:T(8,128)S(1)}, f32[26,8,256]{2,0,1:T(8,128)S(1)}, u32[]{:S(2)}, u32[]{:S(2)}) collective-permute-start(f32[26,8,256]{2,0,1:T(8,128)S(1)} %fusion.48), channel_id=1, source_target_pairs={{3,0},{4,1},{5,2},{6,3},{7,4},{0,5},{1,6},{2,7},{11,8},{12,9},{13,... | collective-permute-start | bytes 638984 | tf_op jit(solution)/shard_map/ppermute | solution.py:65
  55.2 10.5 %collective-permute-start.9 = (f32[26,8,256]{2,0,1:T(8,128)S(1)}, f32[26,8,256]{2,0,1:T(8,128)S(1)}, u32[]{:S(2)}, u32[]{:S(2)}) collective-permute-start(f32[26,8,256]{2,0,1:T(8,128)S(1)} %select_select_fusion.1), channel_id=1, source_target_pairs={{4,0},{5,1},{6,2},{7,3},{0,4},{1,5},{2,6},{3,7},{12,8},{13,9},{14,... | collective-permute-start | bytes 638984 | tf_op jit(solution)/shard_map/ppermute | solution.py:65
  65.7 14.4 %collective-permute-start.11 = (f32[26,8,256]{2,0,1:T(8,128)S(1)}, f32[26,8,256]{2,0,1:T(8,128)S(1)}, u32[]{:S(2)}, u32[]{:S(2)}) collective-permute-start(f32[26,8,256]{2,0,1:T(8,128)S(1)} %broadcast_select_fusion), channel_id=1, source_target_pairs={{0,8},{1,9},{2,10},{3,11},{4,12},{5,13},{6,14},{7,15},{8,16},{9,17... | collective-permute-start | bytes 638984 | tf_op jit(solution)/shard_map/ppermute | solution.py:19
  67.6 13.9 %collective-permute-start.10 = (f32[26,8,256]{2,0,1:T(8,128)S(1)}, f32[26,8,256]{2,0,1:T(8,128)S(1)}, u32[]{:S(2)}, u32[]{:S(2)}) collective-permute-start(f32[26,8,256]{2,0,1:T(8,128)S(1)} %broadcast_select_fusion), channel_id=1, source_target_pairs={{8,0},{9,1},{10,2},{11,3},{12,4},{13,5},{14,6},{15,7},{16,8},{17,9... | collective-permute-start | bytes 638984 | tf_op jit(solution)/shard_map/ppermute | solution.py:19
  81.6 8.9 %collective-permute-start.13 = (f32[26,8,256]{2,0,1:T(8,128)S(1)}, f32[26,8,256]{2,0,1:T(8,128)S(1)}, u32[]{:S(2)}, u32[]{:S(2)}) collective-permute-start(f32[26,8,256]{2,0,1:T(8,128)S(1)} %select_select_fusion), channel_id=1, source_target_pairs={{8,1},{9,3},{10,5},{11,7},{12,9},{13,11},{14,13},{15,15},{16,17},{... | collective-permute-start | bytes 638984 | tf_op jit(solution)/shard_map/ppermute | solution.py:146
  84.4 8.3 %collective-permute-start.12 = (f32[26,8,256]{2,0,1:T(8,128)S(1)}, f32[26,8,256]{2,0,1:T(8,128)S(1)}, u32[]{:S(2)}, u32[]{:S(2)}) collective-permute-start(f32[26,8,256]{2,0,1:T(8,128)S(1)} %select_select_fusion), channel_id=1, source_target_pairs={{8,0},{9,2},{10,4},{11,6},{12,8},{13,10},{14,12},{15,14},{16,16},{... | collective-permute-start | bytes 638984 | tf_op jit(solution)/shard_map/ppermute | solution.py:145
  88.0 2.7 %collective-permute-start.14 = (f32[2,26,256]{2,1,0:T(8,128)S(1)}, f32[2,26,256]{2,1,0:T(8,128)S(1)}, u32[]{:S(2)}, u32[]{:S(2)}) collective-permute-start(f32[2,26,256]{2,1,0:T(8,128)S(1)} %slice_bitcast_fusion.10), channel_id=1, source_target_pairs={{9,1},{10,3},{11,5},{12,7},{13,9},{14,11},{15,13},{16,15},{17,17},... | collective-permute-start | bytes 159752 | tf_op jit(solution)/shard_map/ppermute | solution.py:148
  109.2 20.8 %collective-permute-start.18 = (f32[4,24,256]{2,0,1:T(4,128)S(1)}, f32[4,24,256]{2,0,1:T(4,128)S(1)}, u32[]{:S(2)}, u32[]{:S(2)}) collective-permute-start(f32[4,24,256]{2,0,1:T(4,128)S(1)} %bitcast.158), channel_id=1, source_target_pairs={{1,8},{3,9},{5,10},{7,11},{9,12},{11,13},{13,14},{15,15},{17,16},{... | collective-permute-start | bytes 294920 | tf_op jit(solution)/shard_map/ppermute | solution.py:178
  110.5 20.2 %collective-permute-start.17 = (f32[4,24,256]{2,0,1:T(4,128)S(1)}, f32[4,24,256]{2,0,1:T(4,128)S(1)}, u32[]{:S(2)}, u32[]{:S(2)}) collective-permute-start(f32[4,24,256]{2,0,1:T(4,128)S(1)} %bitcast.159), channel_id=1, source_target_pairs={{0,8},{2,9},{4,10},{6,11},{8,12},{10,13},{12,14},{14,15},{16,16},{... | collective-permute-start | bytes 294920 | tf_op jit(solution)/shard_map/ppermute | solution.py:178
  117.2 13.5 %collective-permute-start.16 = (f32[4,24,256]{2,0,1:T(4,128)S(1)}, f32[4,24,256]{2,0,1:T(4,128)S(1)}, u32[]{:S(2)}, u32[]{:S(2)}) collective-permute-start(f32[4,24,256]{2,0,1:T(4,128)S(1)} %bitcast.160), channel_id=1, source_target_pairs={{1,9},{3,10},{5,11},{7,12},{9,13},{11,14},{13,15},{15,16},{17,17},... | collective-permute-start | bytes 294920 | tf_op jit(solution)/shard_map/ppermute | solution.py:178
  118.5 12.2 %collective-permute-start.15 = (f32[4,24,256]{2,0,1:T(4,128)S(1)}, f32[4,24,256]{2,0,1:T(4,128)S(1)}, u32[]{:S(2)}, u32[]{:S(2)}) collective-permute-start(f32[4,24,256]{2,0,1:T(4,128)S(1)} %bitcast.161), channel_id=1, source_target_pairs={{0,9},{2,10},{4,11},{6,12},{8,13},{10,14},{12,15},{14,16},{16,17},... | collective-permute-start | bytes 294920 | tf_op jit(solution)/shard_map/ppermute | solution.py:178
  130.9 12.8 %collective-permute-start.19 = (f32[8,24,256]{2,0,1:T(8,128)S(1)}, f32[8,24,256]{2,0,1:T(8,128)S(1)}, u32[]{:S(2)}, u32[]{:S(2)}) collective-permute-start(f32[8,24,256]{2,0,1:T(8,128)S(1)} %fusion.51), channel_id=1, source_target_pairs={{8,0},{9,1},{10,2},{11,3},{12,4},{13,5},{14,6},{15,7},{16,8},{17,9... | collective-permute-start | bytes 589832 | tf_op jit(solution)/shard_map/ppermute | solution.py:19
  143.7 12.2 %collective-permute-start.22 = (f32[8,24,256]{2,0,1:T(8,128)S(1)}, f32[8,24,256]{2,0,1:T(8,128)S(1)}, u32[]{:S(2)}, u32[]{:S(2)}) collective-permute-start(f32[8,24,256]{2,0,1:T(8,128)S(1)} %broadcast_select_fusion.1), channel_id=1, source_target_pairs={{0,1},{1,2},{2,3},{3,4},{4,5},{5,6},{6,7},{7,8},{8,9},{9,10},{10,1... | collective-permute-start | bytes 589832 | tf_op jit(solution)/shard_map/ppermute | solution.py:19
  145.7 10.3 %collective-permute-start.21 = (f32[8,24,256]{2,0,1:T(8,128)S(1)}, f32[8,24,256]{2,0,1:T(8,128)S(1)}, u32[]{:S(2)}, u32[]{:S(2)}) collective-permute-start(f32[8,24,256]{2,0,1:T(8,128)S(1)} %broadcast_select_fusion.1), channel_id=1, source_target_pairs={{0,2},{1,3},{2,4},{3,5},{4,6},{5,7},{6,8},{7,9},{8,10},{9,11},{10,... | collective-permute-start | bytes 589832 | tf_op jit(solution)/shard_map/ppermute | solution.py:19
  151.6 25.8 %collective-permute-start.20 = (f32[8,24,256]{2,0,1:T(8,128)S(1)}, f32[8,24,256]{2,0,1:T(8,128)S(1)}, u32[]{:S(2)}, u32[]{:S(2)}) collective-permute-start(f32[8,24,256]{2,0,1:T(8,128)S(1)} %broadcast_select_fusion.1), channel_id=1, source_target_pairs={{0,3},{1,4},{2,5},{3,6},{4,7},{5,8},{6,9},{7,10},{8,11},{9,12},{10... | collective-permute-start | bytes 589832 | tf_op jit(solution)/shard_map/ppermute | solution.py:19
  177.4 12.1 %collective-permute-start.23 = (f32[8,24,256]{2,0,1:T(8,128)S(1)}, f32[8,24,256]{2,0,1:T(8,128)S(1)}, u32[]{:S(2)}, u32[]{:S(2)}) collective-permute-start(f32[8,24,256]{2,0,1:T(8,128)S(1)} %select_select_fusion.2), channel_id=1, source_target_pairs={{0,4},{1,5},{2,6},{3,7},{4,8},{5,9},{6,10},{7,11},{8,12},{9,13},{1... | collective-permute-start | bytes 589832 | tf_op jit(solution)/shard_map/ppermute | solution.py:19
  (14 other events, 111.9 us)

commit v6 on v5

--- a/solution.py
+++ b/solution.py
@@ -127,11 +127,7 @@
         ],
         axis=0,
     )
-    above3, below3, rows_here = lax.optimization_barrier((above3, below3, rows_here))
-    last_before = shift_from(rows_here[:, parent_rows - 1], "tile", -1, tiles)
-    rows_after = shift_from(rows_here, "tile", 1, tiles)
-    joined = jnp.concatenate([last_before[:, None], rows_here, rows_after], axis=1)
-    block = lax.dynamic_slice_in_dim(joined, r, parent_rows, axis=1)
+    above3, below3, block = lax.optimization_barrier((above3, below3, rows_here))
     low = q & 3
     bit2 = ((q >> 2) & 1) == 1
     bit3 = ((q >> 3) & 1) == 1
@@ -142,12 +138,24 @@
     carry = (slab_pos + low3 >= center).astype(jnp.int32)
     slab_shift = bit3.astype(jnp.int32) + carry - 1
     block = pick(block, [(-center, slab_shift == -1), (center, slab_shift == 1)], tiles)
-    to_even = lax.ppermute(block, "tile", [(m + center, 2 * m) for m in range(half)])
-    to_odd = lax.ppermute(block, "tile", [(m + center, 2 * m + 1) for m in range(half)])
-    next_rows = jnp.transpose(block[:, : foot_rows - coarse_rows], (1, 0, 2))
-    next_odd = lax.ppermute(next_rows, "tile", [(m + center + 1, 2 * m + 1) for m in range(half)])
-    odd_rows = jnp.concatenate([to_odd[:, coarse_rows:], jnp.transpose(next_odd, (1, 0, 2))], axis=1)
-    footprint = jnp.where(tile_index % 2 == 0, to_even[:, :foot_rows], odd_rows)
+    extra = foot_rows - 2
+    own_even = lax.ppermute(block, "tile", [(m + center, 2 * m) for m in range(half)])
+    last_even = lax.ppermute(
+        block[:, parent_rows - 1], "tile", [(m + center - 1, 2 * m) for m in range(half)]
+    )
+    first_rows = jnp.transpose(block[:, :extra], (1, 0, 2))
+    next_even = lax.ppermute(first_rows, "tile", [(m + center + 1, 2 * m) for m in range(half)])
+    own_odd = lax.ppermute(block, "tile", [(m + center, 2 * m + 1) for m in range(half)])
+    next_odd = lax.ppermute(block, "tile", [(m + center + 1, 2 * m + 1) for m in range(half)])
+    even_rows = jnp.concatenate(
+        [last_even[:, None], own_even, jnp.transpose(next_even, (1, 0, 2))], axis=1
+    )
+    odd_rows = jnp.concatenate([own_odd, next_odd], axis=1)
+    footprint = jnp.where(
+        tile_index % 2 == 0,
+        lax.dynamic_slice_in_dim(even_rows, r, foot_rows, axis=1),
+        lax.dynamic_slice_in_dim(odd_rows, r + coarse_rows - 1, foot_rows, axis=1),
+    )
 
     widen = repeat_matrix(coarse_cols, 3)
     heighten = repeat_matrix(foot_rows, 3).T

time: 197 us -> 195 us (0.990)
  the two profiles are of different devices: /device:TPU:170 before, /device:TPU:154 now
where the time goes in v6:
time: 195 us; the launch traced here: 194 us
  starting transfers between devices  98.5 us (51%)
  waiting for transfers between devices  54.6 us (28%)
  local copies, waits for them, and re-layouts  19.6 us (10%)
  other arithmetic  10.9 us (6%)
  between operations  7.86 us (4%)
  matrix products  2.43 us (1%)
    ppermute x9, starting transfers between devices, shift_from(): return lax.ppermute(value, axis, pairs)  49.9 us
    ppermute x9, waiting for transfers between devices, shift_from(): return lax.ppermute(value, axis, pairs)  41 us
    ppermute x4, starting transfers between devices, rotate(): out = jnp.where(predicate, lax.ppermute(value, 'tile', pairs), out)  18.2 us
    ppermute x4, starting transfers between devices, local(): lax.ppermute(means, 'tile', [(2 * m + k, m + center) for m in range(half...  11.9 us
    ppermute x4, waiting for transfers between devices, rotate(): out = jnp.where(predicate, lax.ppermute(value, 'tile', pairs), out)  10.2 us
    unnamed x30, local copies, waits for them, and re-layouts  6.98 us
    ppermute x1, starting transfers between devices, local(): lax.ppermute(block, 'tile', [(m + center, 2 * m + 1) for m in range(half)])  6.95 us
    dynamic_update_slice x1, local copies, waits for them, and re-layouts, local(): lax.dynamic_update_slice_in_dim(advanced, merged, col_offset, axis=3)  5.09 us
  transfers between devices with their start and end apart: 24, of which 12 were waited for; matrix products, arithmetic and copies ran while one was open for 4% of the time, Pallas kernels for 0%

profile of v6, /device:TPU:154, one launch (start us, length us, event | category | flops | bytes accessed | tf_op | source)
XLA Modules:
  0.0 193.8 jit_solution(3537609468421836148)
XLA Ops:
  3.0 1.9 collective-permute-start.3
  5.0 2.4 %collective-permute-start.2 = (f32[3,8,3,768]{3,1,2,0:T(8,128)S(1)}, f32[3,8,3,768]{3,1,2,0:T(8,128)S(1)}, u32[]{:S(2)}, u32[]{:S(2)}) collective-permute-start(f32[3,8,3,768]{3,1,2,0:T(8,128)S(1)} %get-tuple-element.27), channel_id=1, source_target_pairs={{0,1},{1,2},{2,3},{3,4},{4,5},{5,6},{6,7},{7,8},{8,9},{9,10},{10,1... | collective-permute-start | bytes 663560 | tf_op jit(solution)/shard_map/ppermute | solution.py:19
  7.7 3.0 %collective-permute-start = (f32[2,8,1,2048]{3,2,1,0:T(1,128)S(1)}, f32[2,8,1,2048]{3,2,1,0:T(1,128)S(1)}, u32[]{:S(2)}, u32[]{:S(2)}) collective-permute-start(f32[2,8,1,2048]{3,2,1,0:T(1,128)S(1)} %get-tuple-element.24), channel_id=1, source_target_pairs={{0,1},{1,2},{2,3},{3,4},{4,5},{5,6},{6,7},{7,8},{8,9},{9,10},{10,1... | collective-permute-start | bytes 393224 | tf_op jit(solution)/shard_map/ppermute | solution.py:29
  10.7 2.5 %collective-permute-start.1 = (f32[2,8,1,2048]{3,2,1,0:T(1,128)S(1)}, f32[2,8,1,2048]{3,2,1,0:T(1,128)S(1)}, u32[]{:S(2)}, u32[]{:S(2)}) collective-permute-start(f32[2,8,1,2048]{3,2,1,0:T(1,128)S(1)} %get-tuple-element.25), channel_id=1, source_target_pairs={{1,0},{2,1},{3,2},{4,3},{5,4},{6,5},{7,6},{8,7},{9,8},{10,9},{11,1... | collective-permute-start | bytes 393224 | tf_op jit(solution)/shard_map/ppermute | solution.py:30
  20.9 9.4 %collective-permute-start.5 = (f32[26,8,256]{2,0,1:T(8,128)S(1)}, f32[26,8,256]{2,0,1:T(8,128)S(1)}, u32[]{:S(2)}, u32[]{:S(2)}) collective-permute-start(f32[26,8,256]{2,0,1:T(8,128)S(1)} %pad_maximum_fusion.15), channel_id=1, source_target_pairs={{2,0},{3,1},{4,2},{5,3},{6,4},{7,5},{0,6},{1,7},{10,8},{11,9},{12,... | collective-permute-start | bytes 638984 | tf_op jit(solution)/shard_map/ppermute | solution.py:65
  32.9 3.5 %collective-permute-done.5 = f32[26,8,256]{2,0,1:T(8,128)S(1)} collective-permute-done((f32[26,8,256]{2,0,1:T(8,128)S(1)}, f32[26,8,256]{2,0,1:T(8,128)S(1)}, u32[]{:S(2)}, u32[]{:S(2)}) %collective-permute-start.5) | collective-permute-done | bytes 213024 | tf_op jit(solution)/shard_map/ppermute | solution.py:65
  36.4 2.9 %collective-permute-done.4 = f32[26,8,256]{2,0,1:T(8,128)S(1)} collective-permute-done((f32[26,8,256]{2,0,1:T(8,128)S(1)}, f32[26,8,256]{2,0,1:T(8,128)S(1)}, u32[]{:S(2)}, u32[]{:S(2)}) %collective-permute-start.4) | collective-permute-done | bytes 213024 | tf_op jit(solution)/shard_map/ppermute | solution.py:65
  39.3 8.3 %collective-permute-start.7 = (f32[26,8,256]{2,0,1:T(8,128)S(1)}, f32[26,8,256]{2,0,1:T(8,128)S(1)}, u32[]{:S(2)}, u32[]{:S(2)}) collective-permute-start(f32[26,8,256]{2,0,1:T(8,128)S(1)} %select_select_fusion.1), channel_id=1, source_target_pairs={{4,0},{5,1},{6,2},{7,3},{0,4},{1,5},{2,6},{3,7},{12,8},{13,9},{14,... | collective-permute-start | bytes 638984 | tf_op jit(solution)/shard_map/ppermute | solution.py:65
  48.2 3.8 %collective-permute-done.7 = f32[26,8,256]{2,0,1:T(8,128)S(1)} collective-permute-done((f32[26,8,256]{2,0,1:T(8,128)S(1)}, f32[26,8,256]{2,0,1:T(8,128)S(1)}, u32[]{:S(2)}, u32[]{:S(2)}) %collective-permute-start.7) | collective-permute-done | bytes 213024 | tf_op jit(solution)/shard_map/ppermute | solution.py:65
  52.0 1.9 collective-permute-start.9
  53.9 6.0 %collective-permute-start.8 = (f32[26,8,256]{2,0,1:T(8,128)S(1)}, f32[26,8,256]{2,0,1:T(8,128)S(1)}, u32[]{:S(2)}, u32[]{:S(2)}) collective-permute-start(f32[26,8,256]{2,0,1:T(8,128)S(1)} %broadcast_select_fusion), channel_id=1, source_target_pairs={{8,0},{9,1},{10,2},{11,3},{12,4},{13,5},{14,6},{15,7},{16,8},{17,9... | collective-permute-start | bytes 638984 | tf_op jit(solution)/shard_map/ppermute | solution.py:19
  60.0 5.2 %collective-permute-done.9 = f32[26,8,256]{2,0,1:T(8,128)S(1)} collective-permute-done((f32[26,8,256]{2,0,1:T(8,128)S(1)}, f32[26,8,256]{2,0,1:T(8,128)S(1)}, u32[]{:S(2)}, u32[]{:S(2)}) %collective-permute-start.9) | collective-permute-done | bytes 213024 | tf_op jit(solution)/shard_map/ppermute | solution.py:19
  67.7 7.0 %collective-permute-start.13 = (f32[26,8,256]{2,0,1:T(8,128)S(1)}, f32[26,8,256]{2,0,1:T(8,128)S(1)}, u32[]{:S(2)}, u32[]{:S(2)}) collective-permute-start(f32[26,8,256]{2,0,1:T(8,128)S(1)} %select_select_fusion), channel_id=1, source_target_pairs={{8,1},{9,3},{10,5},{11,7},{12,9},{13,11},{14,13},{15,15},{16,17},{... | collective-permute-start | bytes 638984 | tf_op jit(solution)/shard_map/ppermute | solution.py:148
  76.6 1.9 collective-permute-start.10
  80.6 2.1 %collective-permute-done.10 = f32[26,256]{1,0:T(8,128)S(1)} collective-permute-done((f32[26,256]{1,0:T(8,128)S(1)}, f32[26,256]{1,0:T(8,128)S(1)}, u32[]{:S(2)}, u32[]{:S(2)}) %collective-permute-start.10) | collective-permute-done | bytes 26656 | tf_op jit(solution)/shard_map/ppermute | solution.py:143
  100.6 8.6 %collective-permute-start.17 = (f32[4,24,256]{2,0,1:T(4,128)S(1)}, f32[4,24,256]{2,0,1:T(4,128)S(1)}, u32[]{:S(2)}, u32[]{:S(2)}) collective-permute-start(f32[4,24,256]{2,0,1:T(4,128)S(1)} %bitcast.160), channel_id=1, source_target_pairs={{0,8},{2,9},{4,10},{6,11},{8,12},{10,13},{12,14},{14,15},{16,16},{... | collective-permute-start | bytes 294920 | tf_op jit(solution)/shard_map/ppermute | solution.py:186
  112.6 29.0 %collective-permute-start.19 = (f32[8,24,256]{2,0,1:T(8,128)S(1)}, f32[8,24,256]{2,0,1:T(8,128)S(1)}, u32[]{:S(2)}, u32[]{:S(2)}) collective-permute-start(f32[8,24,256]{2,0,1:T(8,128)S(1)} %fusion.49), channel_id=1, source_target_pairs={{8,0},{9,1},{10,2},{11,3},{12,4},{13,5},{14,6},{15,7},{16,8},{17,9... | collective-permute-start | bytes 589832 | tf_op jit(solution)/shard_map/ppermute | solution.py:19
  141.6 5.2 %collective-permute-done.19 = f32[8,24,256]{2,0,1:T(8,128)S(1)} collective-permute-done((f32[8,24,256]{2,0,1:T(8,128)S(1)}, f32[8,24,256]{2,0,1:T(8,128)S(1)}, u32[]{:S(2)}, u32[]{:S(2)}) %collective-permute-start.19) | collective-permute-done | bytes 196640 | tf_op jit(solution)/shard_map/ppermute | solution.py:19
  146.8 1.9 collective-permute-start.22
  150.7 2.9 %collective-permute-start.20 = (f32[8,24,256]{2,0,1:T(8,128)S(1)}, f32[8,24,256]{2,0,1:T(8,128)S(1)}, u32[]{:S(2)}, u32[]{:S(2)}) collective-permute-start(f32[8,24,256]{2,0,1:T(8,128)S(1)} %broadcast_select_fusion.1), channel_id=1, source_target_pairs={{0,3},{1,4},{2,5},{3,6},{4,7},{5,8},{6,9},{7,10},{8,11},{9,12},{10... | collective-permute-start | bytes 589832 | tf_op jit(solution)/shard_map/ppermute | solution.py:19
  154.2 4.2 %collective-permute-done.21 = f32[8,24,256]{2,0,1:T(8,128)S(1)} collective-permute-done((f32[8,24,256]{2,0,1:T(8,128)S(1)}, f32[8,24,256]{2,0,1:T(8,128)S(1)}, u32[]{:S(2)}, u32[]{:S(2)}) %collective-permute-start.21) | collective-permute-done | bytes 196640 | tf_op jit(solution)/shard_map/ppermute | solution.py:19
  158.4 17.1 %collective-permute-done.20 = f32[8,24,256]{2,0,1:T(8,128)S(1)} collective-permute-done((f32[8,24,256]{2,0,1:T(8,128)S(1)}, f32[8,24,256]{2,0,1:T(8,128)S(1)}, u32[]{:S(2)}, u32[]{:S(2)}) %collective-permute-start.20) | collective-permute-done | bytes 196640 | tf_op jit(solution)/shard_map/ppermute | solution.py:19
  179.4 8.2 %collective-permute-done.23 = f32[8,24,256]{2,0,1:T(8,128)S(1)} collective-permute-done((f32[8,24,256]{2,0,1:T(8,128)S(1)}, f32[8,24,256]{2,0,1:T(8,128)S(1)}, u32[]{:S(2)}, u32[]{:S(2)}) %collective-permute-start.23) | collective-permute-done | bytes 196640 | tf_op jit(solution)/shard_map/ppermute | solution.py:19
  188.7 5.1 %dynamic_update_slice.3 = f32[3,8,8,2048]{3,2,1,0:T(8,128)} dynamic-update-slice(f32[3,8,8,2048]{3,2,1,0:T(8,128)} %copy-done.2, f32[3,8,8,256]{3,2,1,0:T(8,128)S(1)} %dynamic-slice_select_fusion, s32[]{:T(128)} %constant.93.clone.1, s32[]{:T(128)} %constant.93.clone.1, s32[]{:T(128)} %constant.93.clone.1, s32[]{:T(128)S(6)} %select_n.169) | dynamic-update-slice | bytes 393220 | tf_op jit(solution)/shard_map/dynamic_update_slice | solution.py:201
  (136 shorter events, 41.9 us)
Async XLA Ops:
  3.0 17.3 %collective-permute-start.3 = (f32[3,8,3,768]{3,1,2,0:T(8,128)S(1)}, f32[3,8,3,768]{3,1,2,0:T(8,128)S(1)}, u32[]{:S(2)}, u32[]{:S(2)}) collective-permute-start(f32[3,8,3,768]{3,1,2,0:T(8,128)S(1)} %get-tuple-element.26), channel_id=1, source_target_pairs={{1,0},{2,1},{3,2},{4,3},{5,4},{6,5},{7,6},{8,7},{9,8},{10,9},{11,1... | collective-permute-start | bytes 663560 | tf_op jit(solution)/shard_map/ppermute | solution.py:19
  5.0 15.4 %collective-permute-start.2 = (f32[3,8,3,768]{3,1,2,0:T(8,128)S(1)}, f32[3,8,3,768]{3,1,2,0:T(8,128)S(1)}, u32[]{:S(2)}, u32[]{:S(2)}) collective-permute-start(f32[3,8,3,768]{3,1,2,0:T(8,128)S(1)} %get-tuple-element.27), channel_id=1, source_target_pairs={{0,1},{1,2},{2,3},{3,4},{4,5},{5,6},{6,7},{7,8},{8,9},{9,10},{10,1... | collective-permute-start | bytes 663560 | tf_op jit(solution)/shard_map/ppermute | solution.py:19
  7.7 9.7 %collective-permute-start = (f32[2,8,1,2048]{3,2,1,0:T(1,128)S(1)}, f32[2,8,1,2048]{3,2,1,0:T(1,128)S(1)}, u32[]{:S(2)}, u32[]{:S(2)}) collective-permute-start(f32[2,8,1,2048]{3,2,1,0:T(1,128)S(1)} %get-tuple-element.24), channel_id=1, source_target_pairs={{0,1},{1,2},{2,3},{3,4},{4,5},{5,6},{6,7},{7,8},{8,9},{9,10},{10,1... | collective-permute-start | bytes 393224 | tf_op jit(solution)/shard_map/ppermute | solution.py:29
  10.7 6.7 %collective-permute-start.1 = (f32[2,8,1,2048]{3,2,1,0:T(1,128)S(1)}, f32[2,8,1,2048]{3,2,1,0:T(1,128)S(1)}, u32[]{:S(2)}, u32[]{:S(2)}) collective-permute-start(f32[2,8,1,2048]{3,2,1,0:T(1,128)S(1)} %get-tuple-element.25), channel_id=1, source_target_pairs={{1,0},{2,1},{3,2},{4,3},{5,4},{6,5},{7,6},{8,7},{9,8},{10,9},{11,1... | collective-permute-start | bytes 393224 | tf_op jit(solution)/shard_map/ppermute | solution.py:30
  20.4 12.5 %collective-permute-start.6 = (f32[26,8,256]{2,0,1:T(8,128)S(1)}, f32[26,8,256]{2,0,1:T(8,128)S(1)}, u32[]{:S(2)}, u32[]{:S(2)}) collective-permute-start(f32[26,8,256]{2,0,1:T(8,128)S(1)} %pad_maximum_fusion.15), channel_id=1, source_target_pairs={{1,0},{2,1},{3,2},{4,3},{5,4},{6,5},{7,6},{0,7},{9,8},{10,9},{11,1... | collective-permute-start | bytes 638984 | tf_op jit(solution)/shard_map/ppermute | solution.py:65
  20.9 15.5 %collective-permute-start.5 = (f32[26,8,256]{2,0,1:T(8,128)S(1)}, f32[26,8,256]{2,0,1:T(8,128)S(1)}, u32[]{:S(2)}, u32[]{:S(2)}) collective-permute-start(f32[26,8,256]{2,0,1:T(8,128)S(1)} %pad_maximum_fusion.15), channel_id=1, source_target_pairs={{2,0},{3,1},{4,2},{5,3},{6,4},{7,5},{0,6},{1,7},{10,8},{11,9},{12,... | collective-permute-start | bytes 638984 | tf_op jit(solution)/shard_map/ppermute | solution.py:65
  30.3 9.0 %collective-permute-start.4 = (f32[26,8,256]{2,0,1:T(8,128)S(1)}, f32[26,8,256]{2,0,1:T(8,128)S(1)}, u32[]{:S(2)}, u32[]{:S(2)}) collective-permute-start(f32[26,8,256]{2,0,1:T(8,128)S(1)} %pad_maximum_fusion.15), channel_id=1, source_target_pairs={{3,0},{4,1},{5,2},{6,3},{7,4},{0,5},{1,6},{2,7},{11,8},{12,9},{13,... | collective-permute-start | bytes 638984 | tf_op jit(solution)/shard_map/ppermute | solution.py:65
  39.3 12.6 %collective-permute-start.7 = (f32[26,8,256]{2,0,1:T(8,128)S(1)}, f32[26,8,256]{2,0,1:T(8,128)S(1)}, u32[]{:S(2)}, u32[]{:S(2)}) collective-permute-start(f32[26,8,256]{2,0,1:T(8,128)S(1)} %select_select_fusion.1), channel_id=1, source_target_pairs={{4,0},{5,1},{6,2},{7,3},{0,4},{1,5},{2,6},{3,7},{12,8},{13,9},{14,... | collective-permute-start | bytes 638984 | tf_op jit(solution)/shard_map/ppermute | solution.py:65
  52.0 13.2 %collective-permute-start.9 = (f32[26,8,256]{2,0,1:T(8,128)S(1)}, f32[26,8,256]{2,0,1:T(8,128)S(1)}, u32[]{:S(2)}, u32[]{:S(2)}) collective-permute-start(f32[26,8,256]{2,0,1:T(8,128)S(1)} %broadcast_select_fusion), channel_id=1, source_target_pairs={{0,8},{1,9},{2,10},{3,11},{4,12},{5,13},{6,14},{7,15},{8,16},{9,17... | collective-permute-start | bytes 638984 | tf_op jit(solution)/shard_map/ppermute | solution.py:19
  53.9 12.4 %collective-permute-start.8 = (f32[26,8,256]{2,0,1:T(8,128)S(1)}, f32[26,8,256]{2,0,1:T(8,128)S(1)}, u32[]{:S(2)}, u32[]{:S(2)}) collective-permute-start(f32[26,8,256]{2,0,1:T(8,128)S(1)} %broadcast_select_fusion), channel_id=1, source_target_pairs={{8,0},{9,1},{10,2},{11,3},{12,4},{13,5},{14,6},{15,7},{16,8},{17,9... | collective-permute-start | bytes 638984 | tf_op jit(solution)/shard_map/ppermute | solution.py:19
  66.4 16.4 %collective-permute-start.14 = (f32[26,8,256]{2,0,1:T(8,128)S(1)}, f32[26,8,256]{2,0,1:T(8,128)S(1)}, u32[]{:S(2)}, u32[]{:S(2)}) collective-permute-start(f32[26,8,256]{2,0,1:T(8,128)S(1)} %select_select_fusion), channel_id=1, source_target_pairs={{9,1},{10,3},{11,5},{12,7},{13,9},{14,11},{15,13},{16,15},{17,17},... | collective-permute-start | bytes 638984 | tf_op jit(solution)/shard_map/ppermute | solution.py:149
  67.7 15.1 %collective-permute-start.13 = (f32[26,8,256]{2,0,1:T(8,128)S(1)}, f32[26,8,256]{2,0,1:T(8,128)S(1)}, u32[]{:S(2)}, u32[]{:S(2)}) collective-permute-start(f32[26,8,256]{2,0,1:T(8,128)S(1)} %select_select_fusion), channel_id=1, source_target_pairs={{8,1},{9,3},{10,5},{11,7},{12,9},{13,11},{14,13},{15,15},{16,17},{... | collective-permute-start | bytes 638984 | tf_op jit(solution)/shard_map/ppermute | solution.py:148
  74.7 8.1 %collective-permute-start.11 = (f32[26,8,256]{2,0,1:T(8,128)S(1)}, f32[26,8,256]{2,0,1:T(8,128)S(1)}, u32[]{:S(2)}, u32[]{:S(2)}) collective-permute-start(f32[26,8,256]{2,0,1:T(8,128)S(1)} %select_select_fusion), channel_id=1, source_target_pairs={{8,0},{9,2},{10,4},{11,6},{12,8},{13,10},{14,12},{15,14},{16,16},{... | collective-permute-start | bytes 638984 | tf_op jit(solution)/shard_map/ppermute | solution.py:142
  76.6 6.2 %collective-permute-start.10 = (f32[26,256]{1,0:T(8,128)S(1)}, f32[26,256]{1,0:T(8,128)S(1)}, u32[]{:S(2)}, u32[]{:S(2)}) collective-permute-start(f32[26,256]{1,0:T(8,128)S(1)} %slice_bitcast_fusion.11), channel_id=1, source_target_pairs={{7,0},{8,2},{9,4},{10,6},{11,8},{12,10},{13,12},{14,14},{15,16},{1... | collective-permute-start | bytes 79880 | tf_op jit(solution)/shard_map/ppermute | solution.py:143
  78.5 4.2 %collective-permute-start.12 = (f32[4,26,256]{2,1,0:T(8,128)S(1)}, f32[4,26,256]{2,1,0:T(8,128)S(1)}, u32[]{:S(2)}, u32[]{:S(2)}) collective-permute-start(f32[4,26,256]{2,1,0:T(8,128)S(1)} %slice_bitcast_fusion.10), channel_id=1, source_target_pairs={{9,0},{10,2},{11,4},{12,6},{13,8},{14,10},{15,12},{16,14},{17,16},... | collective-permute-start | bytes 319496 | tf_op jit(solution)/shard_map/ppermute | solution.py:147
  99.3 11.9 %collective-permute-start.18 = (f32[4,24,256]{2,0,1:T(4,128)S(1)}, f32[4,24,256]{2,0,1:T(4,128)S(1)}, u32[]{:S(2)}, u32[]{:S(2)}) collective-permute-start(f32[4,24,256]{2,0,1:T(4,128)S(1)} %bitcast.159), channel_id=1, source_target_pairs={{1,8},{3,9},{5,10},{7,11},{9,12},{11,13},{13,14},{15,15},{17,16},{... | collective-permute-start | bytes 294920 | tf_op jit(solution)/shard_map/ppermute | solution.py:186
  100.6 10.8 %collective-permute-start.17 = (f32[4,24,256]{2,0,1:T(4,128)S(1)}, f32[4,24,256]{2,0,1:T(4,128)S(1)}, u32[]{:S(2)}, u32[]{:S(2)}) collective-permute-start(f32[4,24,256]{2,0,1:T(4,128)S(1)} %bitcast.160), channel_id=1, source_target_pairs={{0,8},{2,9},{4,10},{6,11},{8,12},{10,13},{12,14},{14,15},{16,16},{... | collective-permute-start | bytes 294920 | tf_op jit(solution)/shard_map/ppermute | solution.py:186
  109.2 3.2 %collective-permute-start.16 = (f32[4,24,256]{2,0,1:T(4,128)S(1)}, f32[4,24,256]{2,0,1:T(4,128)S(1)}, u32[]{:S(2)}, u32[]{:S(2)}) collective-permute-start(f32[4,24,256]{2,0,1:T(4,128)S(1)} %bitcast.161), channel_id=1, source_target_pairs={{1,9},{3,10},{5,11},{7,12},{9,13},{11,14},{13,15},{15,16},{17,17},... | collective-permute-start | bytes 294920 | tf_op jit(solution)/shard_map/ppermute | solution.py:186
  110.5 1.9 collective-permute-start.15
  112.6 34.2 %collective-permute-start.19 = (f32[8,24,256]{2,0,1:T(8,128)S(1)}, f32[8,24,256]{2,0,1:T(8,128)S(1)}, u32[]{:S(2)}, u32[]{:S(2)}) collective-permute-start(f32[8,24,256]{2,0,1:T(8,128)S(1)} %fusion.49), channel_id=1, source_target_pairs={{8,0},{9,1},{10,2},{11,3},{12,4},{13,5},{14,6},{15,7},{16,8},{17,9... | collective-permute-start | bytes 589832 | tf_op jit(solution)/shard_map/ppermute | solution.py:19
  146.8 7.4 %collective-permute-start.22 = (f32[8,24,256]{2,0,1:T(8,128)S(1)}, f32[8,24,256]{2,0,1:T(8,128)S(1)}, u32[]{:S(2)}, u32[]{:S(2)}) collective-permute-start(f32[8,24,256]{2,0,1:T(8,128)S(1)} %broadcast_select_fusion.1), channel_id=1, source_target_pairs={{0,1},{1,2},{2,3},{3,4},{4,5},{5,6},{6,7},{7,8},{8,9},{9,10},{10,1... | collective-permute-start | bytes 589832 | tf_op jit(solution)/shard_map/ppermute | solution.py:19
  148.8 9.7 %collective-permute-start.21 = (f32[8,24,256]{2,0,1:T(8,128)S(1)}, f32[8,24,256]{2,0,1:T(8,128)S(1)}, u32[]{:S(2)}, u32[]{:S(2)}) collective-permute-start(f32[8,24,256]{2,0,1:T(8,128)S(1)} %broadcast_select_fusion.1), channel_id=1, source_target_pairs={{0,2},{1,3},{2,4},{3,5},{4,6},{5,7},{6,8},{7,9},{8,10},{9,11},{10,... | collective-permute-start | bytes 589832 | tf_op jit(solution)/shard_map/ppermute | solution.py:19
  150.7 24.8 %collective-permute-start.20 = (f32[8,24,256]{2,0,1:T(8,128)S(1)}, f32[8,24,256]{2,0,1:T(8,128)S(1)}, u32[]{:S(2)}, u32[]{:S(2)}) collective-permute-start(f32[8,24,256]{2,0,1:T(8,128)S(1)} %broadcast_select_fusion.1), channel_id=1, source_target_pairs={{0,3},{1,4},{2,5},{3,6},{4,7},{5,8},{6,9},{7,10},{8,11},{9,12},{10... | collective-permute-start | bytes 589832 | tf_op jit(solution)/shard_map/ppermute | solution.py:19
  175.5 12.1 %collective-permute-start.23 = (f32[8,24,256]{2,0,1:T(8,128)S(1)}, f32[8,24,256]{2,0,1:T(8,128)S(1)}, u32[]{:S(2)}, u32[]{:S(2)}) collective-permute-start(f32[8,24,256]{2,0,1:T(8,128)S(1)} %select_select_fusion.2), channel_id=1, source_target_pairs={{0,4},{1,5},{2,6},{3,7},{4,8},{5,9},{6,10},{7,11},{8,12},{9,13},{1... | collective-permute-start | bytes 589832 | tf_op jit(solution)/shard_map/ppermute | solution.py:19
  (14 other events, 101.9 us)

commit v7 on v6

--- a/solution.py
+++ b/solution.py
@@ -100,12 +100,16 @@
     r = row_offset - q * parent_rows
 
     nest_fields = nest_state[:, :, 0]
-    above3 = shift_from(nest_fields[:, :, nest_rows - 3 :], "tile", -1, tiles)
-    below3 = shift_from(nest_fields[:, :, :3], "tile", 1, tiles)
+    above3 = shift_from(jnp.moveaxis(nest_fields[:, :, nest_rows - 3 :], 2, 0), "tile", -1, tiles)
+    below3 = shift_from(jnp.moveaxis(nest_fields[:, :, :3], 2, 0), "tile", 1, tiles)
 
     sound_factor = 1.0 - terrain.astype(jnp.float32) / terrain_scale
     halo_fields = parent_state[0:3:2]
-    padded = extended_2(halo_fields, ((("grp", "tile"), 2),), 1)
+    line = ("grp", "tile")
+    lines = lax.axis_size(line)
+    row_above = shift_from(halo_fields[:, :, parent_rows - 1], line, -1, lines)
+    row_below = shift_from(halo_fields[:, :, 0], line, 1, lines)
+    padded = jnp.concatenate([row_above[:, :, None], halo_fields, row_below[:, :, None]], axis=2)
     zonal_ext = jnp.pad(parent_state[1], ((0, 0), (1, 1), (0, 0)))
     extended = jnp.stack([padded[0], zonal_ext, padded[1]])
     factor_ext = jnp.pad(sound_factor, ((1, 1), (0, 0)))
@@ -169,7 +173,9 @@
     local_rows = jnp.arange(3 * foot_rows, dtype=jnp.int32) - 3
     global_rows = nest_rows * tile_index + local_rows
     outside = ((global_rows < 0) | (global_rows >= nest_total))[None, None, :, None]
-    fields = jnp.concatenate([above3, nest_fields, below3], axis=2)
+    fields = jnp.concatenate(
+        [jnp.moveaxis(above3, 0, 2), nest_fields, jnp.moveaxis(below3, 0, 2)], axis=2
+    )
     for _ in range(SUBSTEPS):
         fields = jnp.where(outside, injected, fields)
         stepped = substep(fields, nest_factor, nest_courant, east_rows, west_rows)
@@ -190,9 +196,11 @@
     ]
     both = jnp.concatenate(gathered, axis=0)
     back = lax.dynamic_slice_in_dim(both, parent_rows - r, parent_rows, axis=0)
-    back = pick(back, [(center, jnp.logical_not(bit3))], tiles)
-    back = pick(back, [(-1, low == 1), (-2, low == 2), (-3, low == 3)], tiles)
-    back = pick(back, [(-4, bit2)], tiles)
+    back_carry = carry
+    back_shift = bit3.astype(jnp.int32) + back_carry - 1
+    back = pick(back, [(-center, back_shift == 1), (center, back_shift == -1)], tiles)
+    back = rotate(back, [(-1, low == 1), (-2, low == 2), (-3, low == 3)], center, tiles)
+    back = rotate(back, [(-4, bit2)], center, tiles)
     placed = jnp.transpose(back, (1, 0, 2)).reshape(3, levels, parent_rows, coarse_cols)
     band_row = parent_rows * tile_index + jnp.arange(parent_rows, dtype=jnp.int32) - row_offset
     covered = ((band_row >= 0) & (band_row < coarse_total))[None, None, :, None]

time: 195 us -> 172 us (0.88)
  the two profiles are of different devices: /device:TPU:154 before, /device:TPU:1 now
where the time goes in v7:
time: 172 us; the launch traced here: 170 us
  waiting for transfers between devices  67 us (39%)
  starting transfers between devices  63.1 us (37%)
  local copies, waits for them, and re-layouts  20.7 us (12%)
  other arithmetic  8.47 us (5%)
  between operations  7.82 us (5%)
  matrix products  2.45 us (1%)
    ppermute x8, starting transfers between devices, shift_from(): return lax.ppermute(value, axis, pairs)  28.4 us
    ppermute x8, waiting for transfers between devices, rotate(): out = jnp.where(predicate, lax.ppermute(value, 'tile', pairs), out)  27.3 us
    ppermute x8, starting transfers between devices, rotate(): out = jnp.where(predicate, lax.ppermute(value, 'tile', pairs), out)  18 us
    ppermute x1, waiting for transfers between devices, local(): lax.ppermute(block, 'tile', [(m + center, 2 * m + 1) for m in range(half)])  17.6 us
    ppermute x8, waiting for transfers between devices, shift_from(): return lax.ppermute(value, axis, pairs)  14.1 us
    ppermute x4, starting transfers between devices, local(): lax.ppermute(means, 'tile', [(2 * m + k, m + center) for m in range(half...  11.9 us
    unnamed x36, local copies, waits for them, and re-layouts  9.08 us
    ppermute x1, waiting for transfers between devices, local(): lax.ppermute(block, 'tile', [(m + center + 1, 2 * m + 1) for m in range(h...  7.18 us
  transfers between devices with their start and end apart: 25, of which 14 were waited for; matrix products, arithmetic and copies ran while one was open for 4% of the time, Pallas kernels for 0%

profile of v7, /device:TPU:1, one launch (start us, length us, event | category | flops | bytes accessed | tf_op | source)
XLA Modules:
  0.0 169.6 jit_solution(3086758455051872995)
XLA Ops:
  2.1 5.1 %collective-permute-start.3 = (f32[3,3,8,768]{3,2,0,1:T(8,128)S(1)}, f32[3,3,8,768]{3,2,0,1:T(8,128)S(1)}, u32[]{:S(2)}, u32[]{:S(2)}) collective-permute-start(f32[3,3,8,768]{3,2,0,1:T(8,128)S(1)} %get-tuple-element.24), channel_id=1, source_target_pairs={{1,0},{2,1},{3,2},{4,3},{5,4},{6,5},{7,6},{8,7},{9,8},{10,9},{11,1... | collective-permute-start | bytes 663560 | tf_op jit(solution)/shard_map/ppermute | solution.py:19
  7.2 1.9 %collective-permute-start.2 = (f32[3,3,8,768]{3,2,0,1:T(8,128)S(1)}, f32[3,3,8,768]{3,2,0,1:T(8,128)S(1)}, u32[]{:S(2)}, u32[]{:S(2)}) collective-permute-start(f32[3,3,8,768]{3,2,0,1:T(8,128)S(1)} %get-tuple-element.25), channel_id=1, source_target_pairs={{0,1},{1,2},{2,3},{3,4},{4,5},{5,6},{6,7},{7,8},{8,9},{9,10},{10,1... | collective-permute-start | bytes 663560 | tf_op jit(solution)/shard_map/ppermute | solution.py:19
  10.6 1.9 %collective-permute-start = (f32[2,8,2048]{2,1,0:T(8,128)}, f32[2,8,2048]{2,1,0:T(8,128)S(1)}, u32[]{:S(2)}, u32[]{:S(2)}) collective-permute-start(f32[2,8,2048]{2,1,0:T(8,128)} %get-tuple-element.22), channel_id=1, source_target_pairs={{0,1},{1,2},{2,3},{3,4},{4,5},{5,6},{6,7},{7,8},{8,9},{9,10},{10,1... | collective-permute-start | bytes 393224 | tf_op jit(solution)/shard_map/ppermute | solution.py:19
  12.5 2.4 %collective-permute-start.1 = (f32[2,8,2048]{2,1,0:T(8,128)S(1)}, f32[2,8,2048]{2,1,0:T(8,128)S(1)}, u32[]{:S(2)}, u32[]{:S(2)}) collective-permute-start(f32[2,8,2048]{2,1,0:T(8,128)S(1)} %get-tuple-element.23), channel_id=1, source_target_pairs={{1,0},{2,1},{3,2},{4,3},{5,4},{6,5},{7,6},{8,7},{9,8},{10,9},{11,1... | collective-permute-start | bytes 393224 | tf_op jit(solution)/shard_map/ppermute | solution.py:19
  21.2 7.5 %collective-permute-start.5 = (f32[26,8,256]{2,1,0:T(8,128)S(1)}, f32[26,8,256]{2,1,0:T(8,128)S(1)}, u32[]{:S(2)}, u32[]{:S(2)}) collective-permute-start(f32[26,8,256]{2,1,0:T(8,128)S(1)} %pad_maximum_fusion.15), channel_id=1, source_target_pairs={{2,0},{3,1},{4,2},{5,3},{6,4},{7,5},{0,6},{1,7},{10,8},{11,9},{12,... | collective-permute-start | bytes 638984 | tf_op jit(solution)/shard_map/ppermute | solution.py:65
  31.2 2.0 %collective-permute-done.5 = f32[26,8,256]{2,1,0:T(8,128)S(1)} collective-permute-done((f32[26,8,256]{2,1,0:T(8,128)S(1)}, f32[26,8,256]{2,1,0:T(8,128)S(1)}, u32[]{:S(2)}, u32[]{:S(2)}) %collective-permute-start.5) | collective-permute-done | bytes 213024 | tf_op jit(solution)/shard_map/ppermute | solution.py:65
  33.3 6.8 %collective-permute-done.4 = f32[26,8,256]{2,1,0:T(8,128)S(1)} collective-permute-done((f32[26,8,256]{2,1,0:T(8,128)S(1)}, f32[26,8,256]{2,1,0:T(8,128)S(1)}, u32[]{:S(2)}, u32[]{:S(2)}) %collective-permute-start.4) | collective-permute-done | bytes 213024 | tf_op jit(solution)/shard_map/ppermute | solution.py:65
  40.8 6.9 %collective-permute-done.7 = f32[26,8,256]{2,1,0:T(8,128)S(1)} collective-permute-done((f32[26,8,256]{2,1,0:T(8,128)S(1)}, f32[26,8,256]{2,1,0:T(8,128)S(1)}, u32[]{:S(2)}, u32[]{:S(2)}) %collective-permute-start.7) | collective-permute-done | bytes 213024 | tf_op jit(solution)/shard_map/ppermute | solution.py:65
  47.7 7.3 %collective-permute-start.9 = (f32[26,8,256]{2,1,0:T(8,128)S(1)}, f32[26,8,256]{2,1,0:T(8,128)S(1)}, u32[]{:S(2)}, u32[]{:S(2)}) collective-permute-start(f32[26,8,256]{2,1,0:T(8,128)S(1)} %broadcast_select_fusion), channel_id=1, source_target_pairs={{0,8},{1,9},{2,10},{3,11},{4,12},{5,13},{6,14},{7,15},{8,16},{9,17... | collective-permute-start | bytes 638984 | tf_op jit(solution)/shard_map/ppermute | solution.py:19
  57.8 4.7 %collective-permute-done.8 = f32[26,8,256]{2,1,0:T(8,128)S(1)} collective-permute-done((f32[26,8,256]{2,1,0:T(8,128)S(1)}, f32[26,8,256]{2,1,0:T(8,128)S(1)}, u32[]{:S(2)}, u32[]{:S(2)}) %collective-permute-start.8) | collective-permute-done | bytes 213024 | tf_op jit(solution)/shard_map/ppermute | solution.py:19
  68.2 7.2 %collective-permute-done.14 = f32[26,8,256]{2,1,0:T(8,128)S(1)} collective-permute-done((f32[26,8,256]{2,1,0:T(8,128)S(1)}, f32[26,8,256]{2,1,0:T(8,128)S(1)}, u32[]{:S(2)}, u32[]{:S(2)}) %collective-permute-start.14) | collective-permute-done | bytes 213024 | tf_op jit(solution)/shard_map/ppermute | solution.py:153
  75.4 17.6 %collective-permute-done.13 = f32[26,8,256]{2,1,0:T(8,128)S(1)} collective-permute-done((f32[26,8,256]{2,1,0:T(8,128)S(1)}, f32[26,8,256]{2,1,0:T(8,128)S(1)}, u32[]{:S(2)}, u32[]{:S(2)}) %collective-permute-start.13) | collective-permute-done | bytes 213024 | tf_op jit(solution)/shard_map/ppermute | solution.py:152
  109.6 7.1 %collective-permute-start.18 = (f32[4,24,256]{2,0,1:T(4,128)S(1)}, f32[4,24,256]{2,0,1:T(4,128)S(1)}, u32[]{:S(2)}, u32[]{:S(2)}) collective-permute-start(f32[4,24,256]{2,0,1:T(4,128)S(1)} %bitcast.183), channel_id=1, source_target_pairs={{1,8},{3,9},{5,10},{7,11},{9,12},{11,13},{13,14},{15,15},{17,16},{... | collective-permute-start | bytes 294920 | tf_op jit(solution)/shard_map/ppermute | solution.py:192
  117.3 3.5 %collective-permute-start.16 = (f32[4,24,256]{2,0,1:T(4,128)S(1)}, f32[4,24,256]{2,0,1:T(4,128)S(1)}, u32[]{:S(2)}, u32[]{:S(2)}) collective-permute-start(f32[4,24,256]{2,0,1:T(4,128)S(1)} %bitcast.185), channel_id=1, source_target_pairs={{1,9},{3,10},{5,11},{7,12},{9,13},{11,14},{13,15},{15,16},{17,17},... | collective-permute-start | bytes 294920 | tf_op jit(solution)/shard_map/ppermute | solution.py:192
  122.6 7.2 %collective-permute-start.20 = (f32[8,24,256]{2,0,1:T(8,128)S(1)}, f32[8,24,256]{2,0,1:T(8,128)S(1)}, u32[]{:S(2)}, u32[]{:S(2)}) collective-permute-start(f32[8,24,256]{2,0,1:T(8,128)S(1)} %fusion.53), channel_id=1, source_target_pairs={{0,8},{1,9},{2,10},{3,11},{4,12},{5,13},{6,14},{7,15},{8,16},{9,17... | collective-permute-start | bytes 589832 | tf_op jit(solution)/shard_map/ppermute | solution.py:19
  132.4 6.6 %collective-permute-done.19 = f32[8,24,256]{2,0,1:T(8,128)S(1)} collective-permute-done((f32[8,24,256]{2,0,1:T(8,128)S(1)}, f32[8,24,256]{2,0,1:T(8,128)S(1)}, u32[]{:S(2)}, u32[]{:S(2)}) %collective-permute-start.19) | collective-permute-done | bytes 196640 | tf_op jit(solution)/shard_map/ppermute | solution.py:19
  139.0 4.6 %collective-permute-start.23 = (f32[8,24,256]{2,0,1:T(8,128)S(1)}, f32[8,24,256]{2,0,1:T(8,128)S(1)}, u32[]{:S(2)}, u32[]{:S(2)}) collective-permute-start(f32[8,24,256]{2,0,1:T(8,128)S(1)} %select_select_fusion.3), channel_id=1, source_target_pairs={{7,0},{0,1},{1,2},{2,3},{3,4},{4,5},{5,6},{6,7},{15,8},{8,9},{9,10... | collective-permute-start | bytes 589832 | tf_op jit(solution)/shard_map/ppermute | solution.py:65
  147.6 4.2 %collective-permute-done.22 = f32[8,24,256]{2,0,1:T(8,128)S(1)} collective-permute-done((f32[8,24,256]{2,0,1:T(8,128)S(1)}, f32[8,24,256]{2,0,1:T(8,128)S(1)}, u32[]{:S(2)}, u32[]{:S(2)}) %collective-permute-start.22) | collective-permute-done | bytes 196640 | tf_op jit(solution)/shard_map/ppermute | solution.py:65
  151.9 2.8 %collective-permute-done.21 = f32[8,24,256]{2,0,1:T(8,128)S(1)} collective-permute-done((f32[8,24,256]{2,0,1:T(8,128)S(1)}, f32[8,24,256]{2,0,1:T(8,128)S(1)}, u32[]{:S(2)}, u32[]{:S(2)}) %collective-permute-start.21) | collective-permute-done | bytes 196640 | tf_op jit(solution)/shard_map/ppermute | solution.py:65
  154.7 4.0 %collective-permute-start.24 = (f32[8,24,256]{2,0,1:T(8,128)S(1)}, f32[8,24,256]{2,0,1:T(8,128)S(1)}, u32[]{:S(2)}, u32[]{:S(2)}) collective-permute-start(f32[8,24,256]{2,0,1:T(8,128)S(1)} %select_select_fusion.2), channel_id=1, source_target_pairs={{4,0},{5,1},{6,2},{7,3},{0,4},{1,5},{2,6},{3,7},{12,8},{13,9},{14,... | collective-permute-start | bytes 589832 | tf_op jit(solution)/shard_map/ppermute | solution.py:65
  158.8 1.8 %copy.44 = f32[3,8,1,12,768]{4,2,3,1,0:T(1,128)} copy(f32[3,8,1,12,768]{4,1,3,2,0:T(8,128)S(1)} %slice_bitcast_fusion) | data formatting | bytes 1769472
  160.7 2.9 %collective-permute-done.24 = f32[8,24,256]{2,0,1:T(8,128)S(1)} collective-permute-done((f32[8,24,256]{2,0,1:T(8,128)S(1)}, f32[8,24,256]{2,0,1:T(8,128)S(1)}, u32[]{:S(2)}, u32[]{:S(2)}) %collective-permute-start.24) | collective-permute-done | bytes 196640 | tf_op jit(solution)/shard_map/ppermute | solution.py:65
  163.8 3.8 %dynamic_update_slice.3 = f32[3,8,8,2048]{3,1,2,0:T(8,128)S(1)} dynamic-update-slice(f32[3,8,8,2048]{3,1,2,0:T(8,128)S(1)} %copy-done.1, f32[3,8,8,256]{3,1,2,0:T(8,128)S(1)} %copy_select_fusion, s32[]{:T(128)} %constant.93.clone.1, s32[]{:T(128)} %constant.93.clone.1, s32[]{:T(128)} %constant.93.clone.1, s32[]{:T(128)S(6)} %select_n.175) | dynamic-update-slice | bytes 393220 | tf_op jit(solution)/shard_map/dynamic_update_slice | solution.py:209
  167.6 2.1 %copy.43 = f32[3,8,8,2048]{3,2,1,0:T(8,128)} copy(f32[3,8,8,2048]{3,1,2,0:T(8,128)S(1)} %dynamic_update_slice.3) | data formatting | bytes 3145728
  (143 shorter events, 39.9 us)
Async XLA Ops:
  2.1 19.0 %collective-permute-start.3 = (f32[3,3,8,768]{3,2,0,1:T(8,128)S(1)}, f32[3,3,8,768]{3,2,0,1:T(8,128)S(1)}, u32[]{:S(2)}, u32[]{:S(2)}) collective-permute-start(f32[3,3,8,768]{3,2,0,1:T(8,128)S(1)} %get-tuple-element.24), channel_id=1, source_target_pairs={{1,0},{2,1},{3,2},{4,3},{5,4},{6,5},{7,6},{8,7},{9,8},{10,9},{11,1... | collective-permute-start | bytes 663560 | tf_op jit(solution)/shard_map/ppermute | solution.py:19
  7.2 13.9 %collective-permute-start.2 = (f32[3,3,8,768]{3,2,0,1:T(8,128)S(1)}, f32[3,3,8,768]{3,2,0,1:T(8,128)S(1)}, u32[]{:S(2)}, u32[]{:S(2)}) collective-permute-start(f32[3,3,8,768]{3,2,0,1:T(8,128)S(1)} %get-tuple-element.25), channel_id=1, source_target_pairs={{0,1},{1,2},{2,3},{3,4},{4,5},{5,6},{6,7},{7,8},{8,9},{9,10},{10,1... | collective-permute-start | bytes 663560 | tf_op jit(solution)/shard_map/ppermute | solution.py:19
  10.6 8.6 %collective-permute-start = (f32[2,8,2048]{2,1,0:T(8,128)}, f32[2,8,2048]{2,1,0:T(8,128)S(1)}, u32[]{:S(2)}, u32[]{:S(2)}) collective-permute-start(f32[2,8,2048]{2,1,0:T(8,128)} %get-tuple-element.22), channel_id=1, source_target_pairs={{0,1},{1,2},{2,3},{3,4},{4,5},{5,6},{6,7},{7,8},{8,9},{9,10},{10,1... | collective-permute-start | bytes 393224 | tf_op jit(solution)/shard_map/ppermute | solution.py:19
  12.5 6.7 %collective-permute-start.1 = (f32[2,8,2048]{2,1,0:T(8,128)S(1)}, f32[2,8,2048]{2,1,0:T(8,128)S(1)}, u32[]{:S(2)}, u32[]{:S(2)}) collective-permute-start(f32[2,8,2048]{2,1,0:T(8,128)S(1)} %get-tuple-element.23), channel_id=1, source_target_pairs={{1,0},{2,1},{3,2},{4,3},{5,4},{6,5},{7,6},{8,7},{9,8},{10,9},{11,1... | collective-permute-start | bytes 393224 | tf_op jit(solution)/shard_map/ppermute | solution.py:19
  21.1 10.1 %collective-permute-start.6 = (f32[26,8,256]{2,1,0:T(8,128)S(1)}, f32[26,8,256]{2,1,0:T(8,128)S(1)}, u32[]{:S(2)}, u32[]{:S(2)}) collective-permute-start(f32[26,8,256]{2,1,0:T(8,128)S(1)} %pad_maximum_fusion.15), channel_id=1, source_target_pairs={{1,0},{2,1},{3,2},{4,3},{5,4},{6,5},{7,6},{0,7},{9,8},{10,9},{11,1... | collective-permute-start | bytes 638984 | tf_op jit(solution)/shard_map/ppermute | solution.py:65
  21.2 12.1 %collective-permute-start.5 = (f32[26,8,256]{2,1,0:T(8,128)S(1)}, f32[26,8,256]{2,1,0:T(8,128)S(1)}, u32[]{:S(2)}, u32[]{:S(2)}) collective-permute-start(f32[26,8,256]{2,1,0:T(8,128)S(1)} %pad_maximum_fusion.15), channel_id=1, source_target_pairs={{2,0},{3,1},{4,2},{5,3},{6,4},{7,5},{0,6},{1,7},{10,8},{11,9},{12,... | collective-permute-start | bytes 638984 | tf_op jit(solution)/shard_map/ppermute | solution.py:65
  28.7 11.4 %collective-permute-start.4 = (f32[26,8,256]{2,1,0:T(8,128)S(1)}, f32[26,8,256]{2,1,0:T(8,128)S(1)}, u32[]{:S(2)}, u32[]{:S(2)}) collective-permute-start(f32[26,8,256]{2,1,0:T(8,128)S(1)} %pad_maximum_fusion.15), channel_id=1, source_target_pairs={{3,0},{4,1},{5,2},{6,3},{7,4},{0,5},{1,6},{2,7},{11,8},{12,9},{13,... | collective-permute-start | bytes 638984 | tf_op jit(solution)/shard_map/ppermute | solution.py:65
  40.2 7.5 %collective-permute-start.7 = (f32[26,8,256]{2,1,0:T(8,128)S(1)}, f32[26,8,256]{2,1,0:T(8,128)S(1)}, u32[]{:S(2)}, u32[]{:S(2)}) collective-permute-start(f32[26,8,256]{2,1,0:T(8,128)S(1)} %select_select_fusion.1), channel_id=1, source_target_pairs={{4,0},{5,1},{6,2},{7,3},{0,4},{1,5},{2,6},{3,7},{12,8},{13,9},{14,... | collective-permute-start | bytes 638984 | tf_op jit(solution)/shard_map/ppermute | solution.py:65
  47.7 10.1 %collective-permute-start.9 = (f32[26,8,256]{2,1,0:T(8,128)S(1)}, f32[26,8,256]{2,1,0:T(8,128)S(1)}, u32[]{:S(2)}, u32[]{:S(2)}) collective-permute-start(f32[26,8,256]{2,1,0:T(8,128)S(1)} %broadcast_select_fusion), channel_id=1, source_target_pairs={{0,8},{1,9},{2,10},{3,11},{4,12},{5,13},{6,14},{7,15},{8,16},{9,17... | collective-permute-start | bytes 638984 | tf_op jit(solution)/shard_map/ppermute | solution.py:19
  55.1 7.5 %collective-permute-start.8 = (f32[26,8,256]{2,1,0:T(8,128)S(1)}, f32[26,8,256]{2,1,0:T(8,128)S(1)}, u32[]{:S(2)}, u32[]{:S(2)}) collective-permute-start(f32[26,8,256]{2,1,0:T(8,128)S(1)} %broadcast_select_fusion), channel_id=1, source_target_pairs={{8,0},{9,1},{10,2},{11,3},{12,4},{13,5},{14,6},{15,7},{16,8},{17,9... | collective-permute-start | bytes 638984 | tf_op jit(solution)/shard_map/ppermute | solution.py:19
  62.6 12.8 %collective-permute-start.14 = (f32[26,8,256]{2,1,0:T(8,128)S(1)}, f32[26,8,256]{2,1,0:T(8,128)S(1)}, u32[]{:S(2)}, u32[]{:S(2)}) collective-permute-start(f32[26,8,256]{2,1,0:T(8,128)S(1)} %select_select_fusion), channel_id=1, source_target_pairs={{9,1},{10,3},{11,5},{12,7},{13,9},{14,11},{15,13},{16,15},{17,17},... | collective-permute-start | bytes 638984 | tf_op jit(solution)/shard_map/ppermute | solution.py:153
  63.9 29.1 %collective-permute-start.13 = (f32[26,8,256]{2,1,0:T(8,128)S(1)}, f32[26,8,256]{2,1,0:T(8,128)S(1)}, u32[]{:S(2)}, u32[]{:S(2)}) collective-permute-start(f32[26,8,256]{2,1,0:T(8,128)S(1)} %select_select_fusion), channel_id=1, source_target_pairs={{8,1},{9,3},{10,5},{11,7},{12,9},{13,11},{14,13},{15,15},{16,17},{... | collective-permute-start | bytes 638984 | tf_op jit(solution)/shard_map/ppermute | solution.py:152
  65.2 27.8 %collective-permute-start.11 = (f32[26,8,256]{2,1,0:T(8,128)S(1)}, f32[26,8,256]{2,1,0:T(8,128)S(1)}, u32[]{:S(2)}, u32[]{:S(2)}) collective-permute-start(f32[26,8,256]{2,1,0:T(8,128)S(1)} %select_select_fusion), channel_id=1, source_target_pairs={{8,0},{9,2},{10,4},{11,6},{12,8},{13,10},{14,12},{15,14},{16,16},{... | collective-permute-start | bytes 638984 | tf_op jit(solution)/shard_map/ppermute | solution.py:146
  65.9 2.2 %collective-permute-start.10 = (f32[26,256]{1,0:T(8,128)S(1)}, f32[26,256]{1,0:T(8,128)S(1)}, u32[]{:S(2)}, u32[]{:S(2)}) collective-permute-start(f32[26,256]{1,0:T(8,128)S(1)} %bitcast.187), channel_id=1, source_target_pairs={{7,0},{8,2},{9,4},{10,6},{11,8},{12,10},{13,12},{14,14},{15,16},{1... | collective-permute-start | bytes 79880 | tf_op jit(solution)/shard_map/ppermute | solution.py:147
  109.6 11.9 %collective-permute-start.18 = (f32[4,24,256]{2,0,1:T(4,128)S(1)}, f32[4,24,256]{2,0,1:T(4,128)S(1)}, u32[]{:S(2)}, u32[]{:S(2)}) collective-permute-start(f32[4,24,256]{2,0,1:T(4,128)S(1)} %bitcast.183), channel_id=1, source_target_pairs={{1,8},{3,9},{5,10},{7,11},{9,12},{11,13},{13,14},{15,15},{17,16},{... | collective-permute-start | bytes 294920 | tf_op jit(solution)/shard_map/ppermute | solution.py:192
  116.7 4.9 %collective-permute-start.17 = (f32[4,24,256]{2,0,1:T(4,128)S(1)}, f32[4,24,256]{2,0,1:T(4,128)S(1)}, u32[]{:S(2)}, u32[]{:S(2)}) collective-permute-start(f32[4,24,256]{2,0,1:T(4,128)S(1)} %bitcast.184), channel_id=1, source_target_pairs={{0,8},{2,9},{4,10},{6,11},{8,12},{10,13},{12,14},{14,15},{16,16},{... | collective-permute-start | bytes 294920 | tf_op jit(solution)/shard_map/ppermute | solution.py:192
  117.3 5.1 %collective-permute-start.16 = (f32[4,24,256]{2,0,1:T(4,128)S(1)}, f32[4,24,256]{2,0,1:T(4,128)S(1)}, u32[]{:S(2)}, u32[]{:S(2)}) collective-permute-start(f32[4,24,256]{2,0,1:T(4,128)S(1)} %bitcast.185), channel_id=1, source_target_pairs={{1,9},{3,10},{5,11},{7,12},{9,13},{11,14},{13,15},{15,16},{17,17},... | collective-permute-start | bytes 294920 | tf_op jit(solution)/shard_map/ppermute | solution.py:192
  120.8 1.6 collective-permute-start.15
  122.6 9.8 %collective-permute-start.20 = (f32[8,24,256]{2,0,1:T(8,128)S(1)}, f32[8,24,256]{2,0,1:T(8,128)S(1)}, u32[]{:S(2)}, u32[]{:S(2)}) collective-permute-start(f32[8,24,256]{2,0,1:T(8,128)S(1)} %fusion.53), channel_id=1, source_target_pairs={{0,8},{1,9},{2,10},{3,11},{4,12},{5,13},{6,14},{7,15},{8,16},{9,17... | collective-permute-start | bytes 589832 | tf_op jit(solution)/shard_map/ppermute | solution.py:19
  129.8 9.2 %collective-permute-start.19 = (f32[8,24,256]{2,0,1:T(8,128)S(1)}, f32[8,24,256]{2,0,1:T(8,128)S(1)}, u32[]{:S(2)}, u32[]{:S(2)}) collective-permute-start(f32[8,24,256]{2,0,1:T(8,128)S(1)} %fusion.53), channel_id=1, source_target_pairs={{8,0},{9,1},{10,2},{11,3},{12,4},{13,5},{14,6},{15,7},{16,8},{17,9... | collective-permute-start | bytes 589832 | tf_op jit(solution)/shard_map/ppermute | solution.py:19
  139.0 8.6 %collective-permute-start.23 = (f32[8,24,256]{2,0,1:T(8,128)S(1)}, f32[8,24,256]{2,0,1:T(8,128)S(1)}, u32[]{:S(2)}, u32[]{:S(2)}) collective-permute-start(f32[8,24,256]{2,0,1:T(8,128)S(1)} %select_select_fusion.3), channel_id=1, source_target_pairs={{7,0},{0,1},{1,2},{2,3},{3,4},{4,5},{5,6},{6,7},{15,8},{8,9},{9,10... | collective-permute-start | bytes 589832 | tf_op jit(solution)/shard_map/ppermute | solution.py:65
  143.6 8.3 %collective-permute-start.22 = (f32[8,24,256]{2,0,1:T(8,128)S(1)}, f32[8,24,256]{2,0,1:T(8,128)S(1)}, u32[]{:S(2)}, u32[]{:S(2)}) collective-permute-start(f32[8,24,256]{2,0,1:T(8,128)S(1)} %select_select_fusion.3), channel_id=1, source_target_pairs={{6,0},{7,1},{0,2},{1,3},{2,4},{3,5},{4,6},{5,7},{14,8},{15,9},{8,1... | collective-permute-start | bytes 589832 | tf_op jit(solution)/shard_map/ppermute | solution.py:65
  144.9 9.8 %collective-permute-start.21 = (f32[8,24,256]{2,0,1:T(8,128)S(1)}, f32[8,24,256]{2,0,1:T(8,128)S(1)}, u32[]{:S(2)}, u32[]{:S(2)}) collective-permute-start(f32[8,24,256]{2,0,1:T(8,128)S(1)} %select_select_fusion.3), channel_id=1, source_target_pairs={{5,0},{6,1},{7,2},{0,3},{1,4},{2,5},{3,6},{4,7},{13,8},{14,9},{15,... | collective-permute-start | bytes 589832 | tf_op jit(solution)/shard_map/ppermute | solution.py:65
  154.7 8.8 %collective-permute-start.24 = (f32[8,24,256]{2,0,1:T(8,128)S(1)}, f32[8,24,256]{2,0,1:T(8,128)S(1)}, u32[]{:S(2)}, u32[]{:S(2)}) collective-permute-start(f32[8,24,256]{2,0,1:T(8,128)S(1)} %select_select_fusion.2), channel_id=1, source_target_pairs={{4,0},{5,1},{6,2},{7,3},{0,4},{1,5},{2,6},{3,7},{12,8},{13,9},{14,... | collective-permute-start | bytes 589832 | tf_op jit(solution)/shard_map/ppermute | solution.py:65
  (16 other events, 102.3 us)

commit v8 on v7

--- a/solution.py
+++ b/solution.py
@@ -147,10 +147,10 @@
     last_even = lax.ppermute(
         block[:, parent_rows - 1], "tile", [(m + center - 1, 2 * m) for m in range(half)]
     )
-    first_rows = jnp.transpose(block[:, :extra], (1, 0, 2))
-    next_even = lax.ppermute(first_rows, "tile", [(m + center + 1, 2 * m) for m in range(half)])
-    own_odd = lax.ppermute(block, "tile", [(m + center, 2 * m + 1) for m in range(half)])
     next_odd = lax.ppermute(block, "tile", [(m + center + 1, 2 * m + 1) for m in range(half)])
+    own_odd = lax.ppermute(own_even, "tile", [(2 * m, 2 * m + 1) for m in range(half)])
+    first_rows = jnp.transpose(next_odd[:, :extra], (1, 0, 2))
+    next_even = lax.ppermute(first_rows, "tile", [(2 * m + 1, 2 * m) for m in range(half)])
     even_rows = jnp.concatenate(
         [last_even[:, None], own_even, jnp.transpose(next_even, (1, 0, 2))], axis=1
     )

time: 172 us -> 164 us (0.953)
  waiting for transfers between devices: 67 us -> 51.8 us
  starting transfers between devices: 63.1 us -> 71.7 us
    ppermute x2, waiting for transfers between devices: 17.6 us -> 0.03 us  [the longest x1 0.03 us: local(): lax.ppermute(first_rows, 'tile', [(2 * m + 1, 2 * m) for m in range(half)])]
    ppermute x2, starting transfers between devices: 2.14 us -> 17.9 us  [the longest x1 16.6 us: local(): lax.ppermute(first_rows, 'tile', [(2 * m + 1, 2 * m) for m in range(half)])]
    ppermute x4, starting transfers between devices: 11.9 us -> 5.05 us  [local(): lax.ppermute(means, 'tile', [(2 * m + k, m + center) for m in range(half...]
  transfers between devices with their start and end apart: 25 -> 25, of which waited for: 14 -> 13; matrix products, arithmetic and copies ran while one was open for 4% -> 5% of each run, Pallas kernels for 0% -> 0%
where the time goes in v8:
time: 164 us; the launch traced here: 163 us
  starting transfers between devices  71.7 us (44%)
  waiting for transfers between devices  51.8 us (32%)
  local copies, waits for them, and re-layouts  20.7 us (13%)
  other arithmetic  8.47 us (5%)
  between operations  7.82 us (5%)
  matrix products  2.45 us (1%)
    ppermute x8, starting transfers between devices, shift_from(): return lax.ppermute(value, axis, pairs)  28.4 us
    ppermute x8, waiting for transfers between devices, rotate(): out = jnp.where(predicate, lax.ppermute(value, 'tile', pairs), out)  27.6 us
    ppermute x8, starting transfers between devices, rotate(): out = jnp.where(predicate, lax.ppermute(value, 'tile', pairs), out)  17.8 us
    ppermute x1, starting transfers between devices, local(): lax.ppermute(first_rows, 'tile', [(2 * m + 1, 2 * m) for m in range(half)])  16.6 us
    ppermute x8, waiting for transfers between devices, shift_from(): return lax.ppermute(value, axis, pairs)  14.6 us
    unnamed x36, local copies, waits for them, and re-layouts  9.08 us
    ppermute x1, waiting for transfers between devices, local(): lax.ppermute(block, 'tile', [(m + center + 1, 2 * m + 1) for m in range(h...  8.64 us
    ppermute x4, starting transfers between devices, local(): lax.ppermute(means, 'tile', [(2 * m + k, m + center) for m in range(half...  5.05 us
  transfers between devices with their start and end apart: 25, of which 13 were waited for; matrix products, arithmetic and copies ran while one was open for 5% of the time, Pallas kernels for 0%

profile of v8, /device:TPU:1, one launch (start us, length us, event | category | flops | bytes accessed | tf_op | source)
XLA Modules:
  0.0 162.9 jit_solution(16448814122237677720)
XLA Ops:
  2.1 5.1 %collective-permute-start.3 = (f32[3,3,8,768]{3,2,0,1:T(8,128)S(1)}, f32[3,3,8,768]{3,2,0,1:T(8,128)S(1)}, u32[]{:S(2)}, u32[]{:S(2)}) collective-permute-start(f32[3,3,8,768]{3,2,0,1:T(8,128)S(1)} %get-tuple-element.24), channel_id=1, source_target_pairs={{1,0},{2,1},{3,2},{4,3},{5,4},{6,5},{7,6},{8,7},{9,8},{10,9},{11,1... | collective-permute-start | bytes 663560 | tf_op jit(solution)/shard_map/ppermute | solution.py:19
  7.2 1.9 %collective-permute-start.2 = (f32[3,3,8,768]{3,2,0,1:T(8,128)S(1)}, f32[3,3,8,768]{3,2,0,1:T(8,128)S(1)}, u32[]{:S(2)}, u32[]{:S(2)}) collective-permute-start(f32[3,3,8,768]{3,2,0,1:T(8,128)S(1)} %get-tuple-element.25), channel_id=1, source_target_pairs={{0,1},{1,2},{2,3},{3,4},{4,5},{5,6},{6,7},{7,8},{8,9},{9,10},{10,1... | collective-permute-start | bytes 663560 | tf_op jit(solution)/shard_map/ppermute | solution.py:19
  10.6 1.9 %collective-permute-start = (f32[2,8,2048]{2,1,0:T(8,128)}, f32[2,8,2048]{2,1,0:T(8,128)S(1)}, u32[]{:S(2)}, u32[]{:S(2)}) collective-permute-start(f32[2,8,2048]{2,1,0:T(8,128)} %get-tuple-element.22), channel_id=1, source_target_pairs={{0,1},{1,2},{2,3},{3,4},{4,5},{5,6},{6,7},{7,8},{8,9},{9,10},{10,1... | collective-permute-start | bytes 393224 | tf_op jit(solution)/shard_map/ppermute | solution.py:19
  12.5 2.4 %collective-permute-start.1 = (f32[2,8,2048]{2,1,0:T(8,128)S(1)}, f32[2,8,2048]{2,1,0:T(8,128)S(1)}, u32[]{:S(2)}, u32[]{:S(2)}) collective-permute-start(f32[2,8,2048]{2,1,0:T(8,128)S(1)} %get-tuple-element.23), channel_id=1, source_target_pairs={{1,0},{2,1},{3,2},{4,3},{5,4},{6,5},{7,6},{8,7},{9,8},{10,9},{11,1... | collective-permute-start | bytes 393224 | tf_op jit(solution)/shard_map/ppermute | solution.py:19
  21.2 7.5 %collective-permute-start.5 = (f32[26,8,256]{2,1,0:T(8,128)S(1)}, f32[26,8,256]{2,1,0:T(8,128)S(1)}, u32[]{:S(2)}, u32[]{:S(2)}) collective-permute-start(f32[26,8,256]{2,1,0:T(8,128)S(1)} %pad_maximum_fusion.15), channel_id=1, source_target_pairs={{2,0},{3,1},{4,2},{5,3},{6,4},{7,5},{0,6},{1,7},{10,8},{11,9},{12,... | collective-permute-start | bytes 638984 | tf_op jit(solution)/shard_map/ppermute | solution.py:65
  31.2 2.0 %collective-permute-done.5 = f32[26,8,256]{2,1,0:T(8,128)S(1)} collective-permute-done((f32[26,8,256]{2,1,0:T(8,128)S(1)}, f32[26,8,256]{2,1,0:T(8,128)S(1)}, u32[]{:S(2)}, u32[]{:S(2)}) %collective-permute-start.5) | collective-permute-done | bytes 213024 | tf_op jit(solution)/shard_map/ppermute | solution.py:65
  33.3 6.8 %collective-permute-done.4 = f32[26,8,256]{2,1,0:T(8,128)S(1)} collective-permute-done((f32[26,8,256]{2,1,0:T(8,128)S(1)}, f32[26,8,256]{2,1,0:T(8,128)S(1)}, u32[]{:S(2)}, u32[]{:S(2)}) %collective-permute-start.4) | collective-permute-done | bytes 213024 | tf_op jit(solution)/shard_map/ppermute | solution.py:65
  40.3 7.4 %collective-permute-done.7 = f32[26,8,256]{2,1,0:T(8,128)S(1)} collective-permute-done((f32[26,8,256]{2,1,0:T(8,128)S(1)}, f32[26,8,256]{2,1,0:T(8,128)S(1)}, u32[]{:S(2)}, u32[]{:S(2)}) %collective-permute-start.7) | collective-permute-done | bytes 213024 | tf_op jit(solution)/shard_map/ppermute | solution.py:65
  47.7 7.3 %collective-permute-start.9 = (f32[26,8,256]{2,1,0:T(8,128)S(1)}, f32[26,8,256]{2,1,0:T(8,128)S(1)}, u32[]{:S(2)}, u32[]{:S(2)}) collective-permute-start(f32[26,8,256]{2,1,0:T(8,128)S(1)} %broadcast_select_fusion), channel_id=1, source_target_pairs={{0,8},{1,9},{2,10},{3,11},{4,12},{5,13},{6,14},{7,15},{8,16},{9,17... | collective-permute-start | bytes 638984 | tf_op jit(solution)/shard_map/ppermute | solution.py:19
  57.8 4.7 %collective-permute-done.8 = f32[26,8,256]{2,1,0:T(8,128)S(1)} collective-permute-done((f32[26,8,256]{2,1,0:T(8,128)S(1)}, f32[26,8,256]{2,1,0:T(8,128)S(1)}, u32[]{:S(2)}, u32[]{:S(2)}) %collective-permute-start.8) | collective-permute-done | bytes 213024 | tf_op jit(solution)/shard_map/ppermute | solution.py:19
  66.6 8.6 %collective-permute-done.12 = f32[26,8,256]{2,1,0:T(8,128)S(1)} collective-permute-done((f32[26,8,256]{2,1,0:T(8,128)S(1)}, f32[26,8,256]{2,1,0:T(8,128)S(1)}, u32[]{:S(2)}, u32[]{:S(2)}) %collective-permute-start.12) | collective-permute-done | bytes 213024 | tf_op jit(solution)/shard_map/ppermute | solution.py:150
  75.3 16.6 %collective-permute-start.13 = (f32[4,26,256]{2,0,1:T(4,128)S(1)}, f32[4,26,256]{2,0,1:T(4,128)S(1)}, u32[]{:S(2)}, u32[]{:S(2)}) collective-permute-start(f32[4,26,256]{2,0,1:T(4,128)S(1)} %slice_bitcast_fusion.13), channel_id=1, source_target_pairs={{1,0},{3,2},{5,4},{7,6},{9,8},{11,10},{13,12},{15,14},{17,16},{19,... | collective-permute-start | bytes 319496 | tf_op jit(solution)/shard_map/ppermute | solution.py:153
  111.3 2.3 %collective-permute-start.16 = (f32[4,24,256]{2,0,1:T(4,128)S(1)}, f32[4,24,256]{2,0,1:T(4,128)S(1)}, u32[]{:S(2)}, u32[]{:S(2)}) collective-permute-start(f32[4,24,256]{2,0,1:T(4,128)S(1)} %bitcast.185), channel_id=1, source_target_pairs={{1,9},{3,10},{5,11},{7,12},{9,13},{11,14},{13,15},{15,16},{17,17},... | collective-permute-start | bytes 294920 | tf_op jit(solution)/shard_map/ppermute | solution.py:192
  115.4 7.1 %collective-permute-start.20 = (f32[8,24,256]{2,0,1:T(8,128)S(1)}, f32[8,24,256]{2,0,1:T(8,128)S(1)}, u32[]{:S(2)}, u32[]{:S(2)}) collective-permute-start(f32[8,24,256]{2,0,1:T(8,128)S(1)} %fusion.53), channel_id=1, source_target_pairs={{0,8},{1,9},{2,10},{3,11},{4,12},{5,13},{6,14},{7,15},{8,16},{9,17... | collective-permute-start | bytes 589832 | tf_op jit(solution)/shard_map/ppermute | solution.py:19
  125.2 7.6 %collective-permute-done.19 = f32[8,24,256]{2,0,1:T(8,128)S(1)} collective-permute-done((f32[8,24,256]{2,0,1:T(8,128)S(1)}, f32[8,24,256]{2,0,1:T(8,128)S(1)}, u32[]{:S(2)}, u32[]{:S(2)}) %collective-permute-start.19) | collective-permute-done | bytes 196640 | tf_op jit(solution)/shard_map/ppermute | solution.py:19
  132.8 4.0 %collective-permute-start.23 = (f32[8,24,256]{2,0,1:T(8,128)S(1)}, f32[8,24,256]{2,0,1:T(8,128)S(1)}, u32[]{:S(2)}, u32[]{:S(2)}) collective-permute-start(f32[8,24,256]{2,0,1:T(8,128)S(1)} %select_select_fusion.3), channel_id=1, source_target_pairs={{7,0},{0,1},{1,2},{2,3},{3,4},{4,5},{5,6},{6,7},{15,8},{8,9},{9,10... | collective-permute-start | bytes 589832 | tf_op jit(solution)/shard_map/ppermute | solution.py:65
  136.8 1.6 collective-permute-start.22
  140.9 4.2 %collective-permute-done.22 = f32[8,24,256]{2,0,1:T(8,128)S(1)} collective-permute-done((f32[8,24,256]{2,0,1:T(8,128)S(1)}, f32[8,24,256]{2,0,1:T(8,128)S(1)}, u32[]{:S(2)}, u32[]{:S(2)}) %collective-permute-start.22) | collective-permute-done | bytes 196640 | tf_op jit(solution)/shard_map/ppermute | solution.py:65
  145.1 2.8 %collective-permute-done.21 = f32[8,24,256]{2,0,1:T(8,128)S(1)} collective-permute-done((f32[8,24,256]{2,0,1:T(8,128)S(1)}, f32[8,24,256]{2,0,1:T(8,128)S(1)}, u32[]{:S(2)}, u32[]{:S(2)}) %collective-permute-start.21) | collective-permute-done | bytes 196640 | tf_op jit(solution)/shard_map/ppermute | solution.py:65
  147.9 4.1 %collective-permute-start.24 = (f32[8,24,256]{2,0,1:T(8,128)S(1)}, f32[8,24,256]{2,0,1:T(8,128)S(1)}, u32[]{:S(2)}, u32[]{:S(2)}) collective-permute-start(f32[8,24,256]{2,0,1:T(8,128)S(1)} %select_select_fusion.2), channel_id=1, source_target_pairs={{4,0},{5,1},{6,2},{7,3},{0,4},{1,5},{2,6},{3,7},{12,8},{13,9},{14,... | collective-permute-start | bytes 589832 | tf_op jit(solution)/shard_map/ppermute | solution.py:65
  152.1 1.8 %copy.44 = f32[3,8,1,12,768]{4,2,3,1,0:T(1,128)} copy(f32[3,8,1,12,768]{4,1,3,2,0:T(8,128)S(1)} %slice_bitcast_fusion) | data formatting | bytes 1769472
  153.9 3.0 %collective-permute-done.24 = f32[8,24,256]{2,0,1:T(8,128)S(1)} collective-permute-done((f32[8,24,256]{2,0,1:T(8,128)S(1)}, f32[8,24,256]{2,0,1:T(8,128)S(1)}, u32[]{:S(2)}, u32[]{:S(2)}) %collective-permute-start.24) | collective-permute-done | bytes 196640 | tf_op jit(solution)/shard_map/ppermute | solution.py:65
  157.1 3.8 %dynamic_update_slice.3 = f32[3,8,8,2048]{3,1,2,0:T(8,128)S(1)} dynamic-update-slice(f32[3,8,8,2048]{3,1,2,0:T(8,128)S(1)} %copy-done.1, f32[3,8,8,256]{3,1,2,0:T(8,128)S(1)} %copy_select_fusion, s32[]{:T(128)} %constant.93.clone.1, s32[]{:T(128)} %constant.93.clone.1, s32[]{:T(128)} %constant.93.clone.1, s32[]{:T(128)S(6)} %select_n.175) | dynamic-update-slice | bytes 393220 | tf_op jit(solution)/shard_map/dynamic_update_slice | solution.py:209
  160.9 2.1 %copy.43 = f32[3,8,8,2048]{3,2,1,0:T(8,128)} copy(f32[3,8,8,2048]{3,1,2,0:T(8,128)S(1)} %dynamic_update_slice.3) | data formatting | bytes 3145728
  (143 shorter events, 38.3 us)
Async XLA Ops:
  2.1 19.0 %collective-permute-start.3 = (f32[3,3,8,768]{3,2,0,1:T(8,128)S(1)}, f32[3,3,8,768]{3,2,0,1:T(8,128)S(1)}, u32[]{:S(2)}, u32[]{:S(2)}) collective-permute-start(f32[3,3,8,768]{3,2,0,1:T(8,128)S(1)} %get-tuple-element.24), channel_id=1, source_target_pairs={{1,0},{2,1},{3,2},{4,3},{5,4},{6,5},{7,6},{8,7},{9,8},{10,9},{11,1... | collective-permute-start | bytes 663560 | tf_op jit(solution)/shard_map/ppermute | solution.py:19
  7.2 13.9 %collective-permute-start.2 = (f32[3,3,8,768]{3,2,0,1:T(8,128)S(1)}, f32[3,3,8,768]{3,2,0,1:T(8,128)S(1)}, u32[]{:S(2)}, u32[]{:S(2)}) collective-permute-start(f32[3,3,8,768]{3,2,0,1:T(8,128)S(1)} %get-tuple-element.25), channel_id=1, source_target_pairs={{0,1},{1,2},{2,3},{3,4},{4,5},{5,6},{6,7},{7,8},{8,9},{9,10},{10,1... | collective-permute-start | bytes 663560 | tf_op jit(solution)/shard_map/ppermute | solution.py:19
  10.6 8.6 %collective-permute-start = (f32[2,8,2048]{2,1,0:T(8,128)}, f32[2,8,2048]{2,1,0:T(8,128)S(1)}, u32[]{:S(2)}, u32[]{:S(2)}) collective-permute-start(f32[2,8,2048]{2,1,0:T(8,128)} %get-tuple-element.22), channel_id=1, source_target_pairs={{0,1},{1,2},{2,3},{3,4},{4,5},{5,6},{6,7},{7,8},{8,9},{9,10},{10,1... | collective-permute-start | bytes 393224 | tf_op jit(solution)/shard_map/ppermute | solution.py:19
  12.5 6.7 %collective-permute-start.1 = (f32[2,8,2048]{2,1,0:T(8,128)S(1)}, f32[2,8,2048]{2,1,0:T(8,128)S(1)}, u32[]{:S(2)}, u32[]{:S(2)}) collective-permute-start(f32[2,8,2048]{2,1,0:T(8,128)S(1)} %get-tuple-element.23), channel_id=1, source_target_pairs={{1,0},{2,1},{3,2},{4,3},{5,4},{6,5},{7,6},{8,7},{9,8},{10,9},{11,1... | collective-permute-start | bytes 393224 | tf_op jit(solution)/shard_map/ppermute | solution.py:19
  21.1 10.1 %collective-permute-start.6 = (f32[26,8,256]{2,1,0:T(8,128)S(1)}, f32[26,8,256]{2,1,0:T(8,128)S(1)}, u32[]{:S(2)}, u32[]{:S(2)}) collective-permute-start(f32[26,8,256]{2,1,0:T(8,128)S(1)} %pad_maximum_fusion.15), channel_id=1, source_target_pairs={{1,0},{2,1},{3,2},{4,3},{5,4},{6,5},{7,6},{0,7},{9,8},{10,9},{11,1... | collective-permute-start | bytes 638984 | tf_op jit(solution)/shard_map/ppermute | solution.py:65
  21.2 12.1 %collective-permute-start.5 = (f32[26,8,256]{2,1,0:T(8,128)S(1)}, f32[26,8,256]{2,1,0:T(8,128)S(1)}, u32[]{:S(2)}, u32[]{:S(2)}) collective-permute-start(f32[26,8,256]{2,1,0:T(8,128)S(1)} %pad_maximum_fusion.15), channel_id=1, source_target_pairs={{2,0},{3,1},{4,2},{5,3},{6,4},{7,5},{0,6},{1,7},{10,8},{11,9},{12,... | collective-permute-start | bytes 638984 | tf_op jit(solution)/shard_map/ppermute | solution.py:65
  28.7 11.4 %collective-permute-start.4 = (f32[26,8,256]{2,1,0:T(8,128)S(1)}, f32[26,8,256]{2,1,0:T(8,128)S(1)}, u32[]{:S(2)}, u32[]{:S(2)}) collective-permute-start(f32[26,8,256]{2,1,0:T(8,128)S(1)} %pad_maximum_fusion.15), channel_id=1, source_target_pairs={{3,0},{4,1},{5,2},{6,3},{7,4},{0,5},{1,6},{2,7},{11,8},{12,9},{13,... | collective-permute-start | bytes 638984 | tf_op jit(solution)/shard_map/ppermute | solution.py:65
  40.2 7.5 %collective-permute-start.7 = (f32[26,8,256]{2,1,0:T(8,128)S(1)}, f32[26,8,256]{2,1,0:T(8,128)S(1)}, u32[]{:S(2)}, u32[]{:S(2)}) collective-permute-start(f32[26,8,256]{2,1,0:T(8,128)S(1)} %select_select_fusion.1), channel_id=1, source_target_pairs={{4,0},{5,1},{6,2},{7,3},{0,4},{1,5},{2,6},{3,7},{12,8},{13,9},{14,... | collective-permute-start | bytes 638984 | tf_op jit(solution)/shard_map/ppermute | solution.py:65
  47.7 10.1 %collective-permute-start.9 = (f32[26,8,256]{2,1,0:T(8,128)S(1)}, f32[26,8,256]{2,1,0:T(8,128)S(1)}, u32[]{:S(2)}, u32[]{:S(2)}) collective-permute-start(f32[26,8,256]{2,1,0:T(8,128)S(1)} %broadcast_select_fusion), channel_id=1, source_target_pairs={{0,8},{1,9},{2,10},{3,11},{4,12},{5,13},{6,14},{7,15},{8,16},{9,17... | collective-permute-start | bytes 638984 | tf_op jit(solution)/shard_map/ppermute | solution.py:19
  55.1 7.5 %collective-permute-start.8 = (f32[26,8,256]{2,1,0:T(8,128)S(1)}, f32[26,8,256]{2,1,0:T(8,128)S(1)}, u32[]{:S(2)}, u32[]{:S(2)}) collective-permute-start(f32[26,8,256]{2,1,0:T(8,128)S(1)} %broadcast_select_fusion), channel_id=1, source_target_pairs={{8,0},{9,1},{10,2},{11,3},{12,4},{13,5},{14,6},{15,7},{16,8},{17,9... | collective-permute-start | bytes 638984 | tf_op jit(solution)/shard_map/ppermute | solution.py:19
  62.6 12.7 %collective-permute-start.12 = (f32[26,8,256]{2,1,0:T(8,128)S(1)}, f32[26,8,256]{2,1,0:T(8,128)S(1)}, u32[]{:S(2)}, u32[]{:S(2)}) collective-permute-start(f32[26,8,256]{2,1,0:T(8,128)S(1)} %select_select_fusion), channel_id=1, source_target_pairs={{9,1},{10,3},{11,5},{12,7},{13,9},{14,11},{15,13},{16,15},{17,17},... | collective-permute-start | bytes 638984 | tf_op jit(solution)/shard_map/ppermute | solution.py:150
  64.6 27.9 %collective-permute-start.10 = (f32[26,256]{1,0:T(8,128)S(1)}, f32[26,256]{1,0:T(8,128)S(1)}, u32[]{:S(2)}, u32[]{:S(2)}) collective-permute-start(f32[26,256]{1,0:T(8,128)S(1)} %bitcast.187), channel_id=1, source_target_pairs={{7,0},{8,2},{9,4},{10,6},{11,8},{12,10},{13,12},{14,14},{15,16},{1... | collective-permute-start | bytes 79880 | tf_op jit(solution)/shard_map/ppermute | solution.py:147
  65.3 27.3 %collective-permute-start.14 = (f32[26,8,256]{2,1,0:T(8,128)S(1)}, f32[26,8,256]{2,1,0:T(8,128)S(1)}, u32[]{:S(2)}, u32[]{:S(2)}) collective-permute-start(f32[26,8,256]{2,1,0:T(8,128)S(1)} %collective-permute-done.11), channel_id=1, source_target_pairs={{0,1},{2,3},{4,5},{6,7},{8,9},{10,11},{12,13},{14,15},{16,17},{18,... | collective-permute-start | bytes 638984 | tf_op jit(solution)/shard_map/ppermute | solution.py:151
  75.3 17.3 %collective-permute-start.13 = (f32[4,26,256]{2,0,1:T(4,128)S(1)}, f32[4,26,256]{2,0,1:T(4,128)S(1)}, u32[]{:S(2)}, u32[]{:S(2)}) collective-permute-start(f32[4,26,256]{2,0,1:T(4,128)S(1)} %slice_bitcast_fusion.13), channel_id=1, source_target_pairs={{1,0},{3,2},{5,4},{7,6},{9,8},{11,10},{13,12},{15,14},{17,16},{19,... | collective-permute-start | bytes 319496 | tf_op jit(solution)/shard_map/ppermute | solution.py:153
  109.2 5.1 %collective-permute-start.18 = (f32[4,24,256]{2,0,1:T(4,128)S(1)}, f32[4,24,256]{2,0,1:T(4,128)S(1)}, u32[]{:S(2)}, u32[]{:S(2)}) collective-permute-start(f32[4,24,256]{2,0,1:T(4,128)S(1)} %bitcast.183), channel_id=1, source_target_pairs={{1,8},{3,9},{5,10},{7,11},{9,12},{11,13},{13,14},{15,15},{17,16},{... | collective-permute-start | bytes 294920 | tf_op jit(solution)/shard_map/ppermute | solution.py:192
  110.6 3.7 %collective-permute-start.17 = (f32[4,24,256]{2,0,1:T(4,128)S(1)}, f32[4,24,256]{2,0,1:T(4,128)S(1)}, u32[]{:S(2)}, u32[]{:S(2)}) collective-permute-start(f32[4,24,256]{2,0,1:T(4,128)S(1)} %bitcast.184), channel_id=1, source_target_pairs={{0,8},{2,9},{4,10},{6,11},{8,12},{10,13},{12,14},{14,15},{16,16},{... | collective-permute-start | bytes 294920 | tf_op jit(solution)/shard_map/ppermute | solution.py:192
  111.3 3.9 %collective-permute-start.16 = (f32[4,24,256]{2,0,1:T(4,128)S(1)}, f32[4,24,256]{2,0,1:T(4,128)S(1)}, u32[]{:S(2)}, u32[]{:S(2)}) collective-permute-start(f32[4,24,256]{2,0,1:T(4,128)S(1)} %bitcast.185), channel_id=1, source_target_pairs={{1,9},{3,10},{5,11},{7,12},{9,13},{11,14},{13,15},{15,16},{17,17},... | collective-permute-start | bytes 294920 | tf_op jit(solution)/shard_map/ppermute | solution.py:192
  113.6 1.6 collective-permute-start.15
  115.4 9.7 %collective-permute-start.20 = (f32[8,24,256]{2,0,1:T(8,128)S(1)}, f32[8,24,256]{2,0,1:T(8,128)S(1)}, u32[]{:S(2)}, u32[]{:S(2)}) collective-permute-start(f32[8,24,256]{2,0,1:T(8,128)S(1)} %fusion.53), channel_id=1, source_target_pairs={{0,8},{1,9},{2,10},{3,11},{4,12},{5,13},{6,14},{7,15},{8,16},{9,17... | collective-permute-start | bytes 589832 | tf_op jit(solution)/shard_map/ppermute | solution.py:19
  122.6 10.2 %collective-permute-start.19 = (f32[8,24,256]{2,0,1:T(8,128)S(1)}, f32[8,24,256]{2,0,1:T(8,128)S(1)}, u32[]{:S(2)}, u32[]{:S(2)}) collective-permute-start(f32[8,24,256]{2,0,1:T(8,128)S(1)} %fusion.53), channel_id=1, source_target_pairs={{8,0},{9,1},{10,2},{11,3},{12,4},{13,5},{14,6},{15,7},{16,8},{17,9... | collective-permute-start | bytes 589832 | tf_op jit(solution)/shard_map/ppermute | solution.py:19
  132.8 8.1 %collective-permute-start.23 = (f32[8,24,256]{2,0,1:T(8,128)S(1)}, f32[8,24,256]{2,0,1:T(8,128)S(1)}, u32[]{:S(2)}, u32[]{:S(2)}) collective-permute-start(f32[8,24,256]{2,0,1:T(8,128)S(1)} %select_select_fusion.3), channel_id=1, source_target_pairs={{7,0},{0,1},{1,2},{2,3},{3,4},{4,5},{5,6},{6,7},{15,8},{8,9},{9,10... | collective-permute-start | bytes 589832 | tf_op jit(solution)/shard_map/ppermute | solution.py:65
  136.8 8.3 %collective-permute-start.22 = (f32[8,24,256]{2,0,1:T(8,128)S(1)}, f32[8,24,256]{2,0,1:T(8,128)S(1)}, u32[]{:S(2)}, u32[]{:S(2)}) collective-permute-start(f32[8,24,256]{2,0,1:T(8,128)S(1)} %select_select_fusion.3), channel_id=1, source_target_pairs={{6,0},{7,1},{0,2},{1,3},{2,4},{3,5},{4,6},{5,7},{14,8},{15,9},{8,1... | collective-permute-start | bytes 589832 | tf_op jit(solution)/shard_map/ppermute | solution.py:65
  138.4 9.5 %collective-permute-start.21 = (f32[8,24,256]{2,0,1:T(8,128)S(1)}, f32[8,24,256]{2,0,1:T(8,128)S(1)}, u32[]{:S(2)}, u32[]{:S(2)}) collective-permute-start(f32[8,24,256]{2,0,1:T(8,128)S(1)} %select_select_fusion.3), channel_id=1, source_target_pairs={{5,0},{6,1},{7,2},{0,3},{1,4},{2,5},{3,6},{4,7},{13,8},{14,9},{15,... | collective-permute-start | bytes 589832 | tf_op jit(solution)/shard_map/ppermute | solution.py:65
  147.9 9.0 %collective-permute-start.24 = (f32[8,24,256]{2,0,1:T(8,128)S(1)}, f32[8,24,256]{2,0,1:T(8,128)S(1)}, u32[]{:S(2)}, u32[]{:S(2)}) collective-permute-start(f32[8,24,256]{2,0,1:T(8,128)S(1)} %select_select_fusion.2), channel_id=1, source_target_pairs={{4,0},{5,1},{6,2},{7,3},{0,4},{1,5},{2,6},{3,7},{12,8},{13,9},{14,... | collective-permute-start | bytes 589832 | tf_op jit(solution)/shard_map/ppermute | solution.py:65
  (16 other events, 77.4 us)

commit v9 on v8

--- a/solution.py
+++ b/solution.py
@@ -147,10 +147,16 @@
     last_even = lax.ppermute(
         block[:, parent_rows - 1], "tile", [(m + center - 1, 2 * m) for m in range(half)]
     )
-    next_odd = lax.ppermute(block, "tile", [(m + center + 1, 2 * m + 1) for m in range(half)])
+    tail_full = lax.ppermute(block, "tile", [(center + half, tiles - 1)])
+    tail_rows = lax.ppermute(
+        jnp.transpose(block[:, :extra], (1, 0, 2)), "tile", [(center + half, tiles - 2)]
+    )
     own_odd = lax.ppermute(own_even, "tile", [(2 * m, 2 * m + 1) for m in range(half)])
-    first_rows = jnp.transpose(next_odd[:, :extra], (1, 0, 2))
-    next_even = lax.ppermute(first_rows, "tile", [(2 * m + 1, 2 * m) for m in range(half)])
+    next_odd = lax.ppermute(own_even, "tile", [(2 * m + 2, 2 * m + 1) for m in range(half - 1)])
+    next_odd = jnp.where(tile_index == tiles - 1, tail_full, next_odd)
+    first_rows = jnp.transpose(own_even[:, :extra], (1, 0, 2))
+    next_even = lax.ppermute(first_rows, "tile", [(2 * m + 2, 2 * m) for m in range(half - 1)])
+    next_even = jnp.where(tile_index == tiles - 2, tail_rows, next_even)
     even_rows = jnp.concatenate(
         [last_even[:, None], own_even, jnp.transpose(next_even, (1, 0, 2))], axis=1
     )

time: 164 us -> 170 us (1.037)
  waiting for transfers between devices: 51.8 us -> 77 us
  starting transfers between devices: 71.7 us -> 52.2 us
    ppermute x2 -> x4, waiting for transfers between devices: 8.66 us -> 23.8 us  [the longest x1 23.8 us: local(): lax.ppermute(own_even, 'tile', [(2 * m + 2, 2 * m + 1) for m in range(hal...]
    ppermute x2 -> x4, starting transfers between devices: 17.9 us -> 3.3 us  [the longest x1 1.29 us: local(): lax.ppermute(own_even, 'tile', [(2 * m + 2, 2 * m + 1) for m in range(hal...]
    ppermute x8, starting transfers between devices: 17.8 us -> 8.89 us  [rotate(): out = jnp.where(predicate, lax.ppermute(value, 'tile', pairs), out)]
    ppermute x8, waiting for transfers between devices: 27.6 us -> 33.3 us  [rotate(): out = jnp.where(predicate, lax.ppermute(value, 'tile', pairs), out)]
    ppermute x4, starting transfers between devices: 5.05 us -> 10.2 us  [local(): lax.ppermute(means, 'tile', [(2 * m + k, m + center) for m in range(half...]
    ppermute x8, waiting for transfers between devices: 14.6 us -> 17.9 us  [shift_from(): return lax.ppermute(value, axis, pairs)]
  transfers between devices with their start and end apart: 25 -> 27, of which waited for: 13 -> 13; matrix products, arithmetic and copies ran while one was open for 5% -> 4% of each run, Pallas kernels for 0% -> 0%
where the time goes in v9:
time: 170 us
  waiting for transfers between devices  77 us (45%)
  starting transfers between devices  52.2 us (31%)
  local copies, waits for them, and re-layouts  20.7 us (12%)
  other arithmetic  8.64 us (5%)
  between operations  8.46 us (5%)
  matrix products  2.45 us (1%)
    ppermute x8, waiting for transfers between devices, rotate(): out = jnp.where(predicate, lax.ppermute(value, 'tile', pairs), out)  33.3 us
    ppermute x8, starting transfers between devices, shift_from(): return lax.ppermute(value, axis, pairs)  27 us
    ppermute x1, waiting for transfers between devices, local(): lax.ppermute(own_even, 'tile', [(2 * m + 2, 2 * m + 1) for m in range(hal...  23.8 us
    ppermute x8, waiting for transfers between devices, shift_from(): return lax.ppermute(value, axis, pairs)  17.9 us
    ppermute x4, starting transfers between devices, local(): lax.ppermute(means, 'tile', [(2 * m + k, m + center) for m in range(half...  10.2 us
    unnamed x36, local copies, waits for them, and re-layouts  9.06 us
    ppermute x8, starting transfers between devices, rotate(): out = jnp.where(predicate, lax.ppermute(value, 'tile', pairs), out)  8.89 us
    dynamic_update_slice x1, local copies, waits for them, and re-layouts, local(): lax.dynamic_update_slice_in_dim(advanced, merged, col_offset, axis=3)  3.8 us
  transfers between devices with their start and end apart: 27, of which 13 were waited for; matrix products, arithmetic and copies ran while one was open for 4% of the time, Pallas kernels for 0%

profile of v9, /device:TPU:1, one launch (start us, length us, event | category | flops | bytes accessed | tf_op | source)
XLA Modules:
  0.0 169.6 jit_solution(9098574610932051352)
XLA Ops:
  0.6 1.4 copy.70
  2.1 5.1 %collective-permute-start.3 = (f32[3,3,8,768]{3,2,0,1:T(8,128)S(1)}, f32[3,3,8,768]{3,2,0,1:T(8,128)S(1)}, u32[]{:S(2)}, u32[]{:S(2)}) collective-permute-start(f32[3,3,8,768]{3,2,0,1:T(8,128)S(1)} %get-tuple-element.24), channel_id=1, source_target_pairs={{1,0},{2,1},{3,2},{4,3},{5,4},{6,5},{7,6},{8,7},{9,8},{10,9},{11,1... | collective-permute-start | bytes 663560 | tf_op jit(solution)/shard_map/ppermute | solution.py:19
  7.2 1.9 %collective-permute-start.2 = (f32[3,3,8,768]{3,2,0,1:T(8,128)S(1)}, f32[3,3,8,768]{3,2,0,1:T(8,128)S(1)}, u32[]{:S(2)}, u32[]{:S(2)}) collective-permute-start(f32[3,3,8,768]{3,2,0,1:T(8,128)S(1)} %get-tuple-element.25), channel_id=1, source_target_pairs={{0,1},{1,2},{2,3},{3,4},{4,5},{5,6},{6,7},{7,8},{8,9},{9,10},{10,1... | collective-permute-start | bytes 663560 | tf_op jit(solution)/shard_map/ppermute | solution.py:19
  10.6 1.9 %collective-permute-start = (f32[2,8,2048]{2,1,0:T(8,128)}, f32[2,8,2048]{2,1,0:T(8,128)S(1)}, u32[]{:S(2)}, u32[]{:S(2)}) collective-permute-start(f32[2,8,2048]{2,1,0:T(8,128)} %get-tuple-element.22), channel_id=1, source_target_pairs={{0,1},{1,2},{2,3},{3,4},{4,5},{5,6},{6,7},{7,8},{8,9},{9,10},{10,1... | collective-permute-start | bytes 393224 | tf_op jit(solution)/shard_map/ppermute | solution.py:19
  12.5 2.4 %collective-permute-start.1 = (f32[2,8,2048]{2,1,0:T(8,128)S(1)}, f32[2,8,2048]{2,1,0:T(8,128)S(1)}, u32[]{:S(2)}, u32[]{:S(2)}) collective-permute-start(f32[2,8,2048]{2,1,0:T(8,128)S(1)} %get-tuple-element.23), channel_id=1, source_target_pairs={{1,0},{2,1},{3,2},{4,3},{5,4},{6,5},{7,6},{8,7},{9,8},{10,9},{11,1... | collective-permute-start | bytes 393224 | tf_op jit(solution)/shard_map/ppermute | solution.py:19
  21.4 7.2 %collective-permute-start.5 = (f32[26,8,256]{2,1,0:T(8,128)S(1)}, f32[26,8,256]{2,1,0:T(8,128)S(1)}, u32[]{:S(2)}, u32[]{:S(2)}) collective-permute-start(f32[26,8,256]{2,1,0:T(8,128)S(1)} %pad_maximum_fusion.15), channel_id=1, source_target_pairs={{2,0},{3,1},{4,2},{5,3},{6,4},{7,5},{0,6},{1,7},{10,8},{11,9},{12,... | collective-permute-start | bytes 638984 | tf_op jit(solution)/shard_map/ppermute | solution.py:65
  31.5 1.8 %collective-permute-done.5 = f32[26,8,256]{2,1,0:T(8,128)S(1)} collective-permute-done((f32[26,8,256]{2,1,0:T(8,128)S(1)}, f32[26,8,256]{2,1,0:T(8,128)S(1)}, u32[]{:S(2)}, u32[]{:S(2)}) %collective-permute-start.5) | collective-permute-done | bytes 213024 | tf_op jit(solution)/shard_map/ppermute | solution.py:65
  33.3 6.8 %collective-permute-done.4 = f32[26,8,256]{2,1,0:T(8,128)S(1)} collective-permute-done((f32[26,8,256]{2,1,0:T(8,128)S(1)}, f32[26,8,256]{2,1,0:T(8,128)S(1)}, u32[]{:S(2)}, u32[]{:S(2)}) %collective-permute-start.4) | collective-permute-done | bytes 213024 | tf_op jit(solution)/shard_map/ppermute | solution.py:65
  40.8 6.9 %collective-permute-done.7 = f32[26,8,256]{2,1,0:T(8,128)S(1)} collective-permute-done((f32[26,8,256]{2,1,0:T(8,128)S(1)}, f32[26,8,256]{2,1,0:T(8,128)S(1)}, u32[]{:S(2)}, u32[]{:S(2)}) %collective-permute-start.7) | collective-permute-done | bytes 213024 | tf_op jit(solution)/shard_map/ppermute | solution.py:65
  47.7 7.3 %collective-permute-start.9 = (f32[26,8,256]{2,1,0:T(8,128)S(1)}, f32[26,8,256]{2,1,0:T(8,128)S(1)}, u32[]{:S(2)}, u32[]{:S(2)}) collective-permute-start(f32[26,8,256]{2,1,0:T(8,128)S(1)} %broadcast_select_fusion.1), channel_id=1, source_target_pairs={{0,8},{1,9},{2,10},{3,11},{4,12},{5,13},{6,14},{7,15},{8,16},{9,17... | collective-permute-start | bytes 638984 | tf_op jit(solution)/shard_map/ppermute | solution.py:19
  57.8 4.7 %collective-permute-done.8 = f32[26,8,256]{2,1,0:T(8,128)S(1)} collective-permute-done((f32[26,8,256]{2,1,0:T(8,128)S(1)}, f32[26,8,256]{2,1,0:T(8,128)S(1)}, u32[]{:S(2)}, u32[]{:S(2)}) %collective-permute-start.8) | collective-permute-done | bytes 213024 | tf_op jit(solution)/shard_map/ppermute | solution.py:19
  68.2 1.5 collective-permute-start.14
  69.7 23.8 %collective-permute-done.16 = f32[26,8,256]{2,1,0:T(8,128)S(1)} collective-permute-done((f32[26,8,256]{2,1,0:T(8,128)S(1)}, f32[26,8,256]{2,1,0:T(8,128)S(1)}, u32[]{:S(2)}, u32[]{:S(2)}) %collective-permute-start.16) | collective-permute-done | bytes 213024 | tf_op jit(solution)/shard_map/ppermute | solution.py:155
  110.2 7.6 %collective-permute-start.20 = (f32[4,24,256]{2,0,1:T(4,128)S(1)}, f32[4,24,256]{2,0,1:T(4,128)S(1)}, u32[]{:S(2)}, u32[]{:S(2)}) collective-permute-start(f32[4,24,256]{2,0,1:T(4,128)S(1)} %bitcast.185), channel_id=1, source_target_pairs={{1,8},{3,9},{5,10},{7,11},{9,12},{11,13},{13,14},{15,15},{17,16},{... | collective-permute-start | bytes 294920 | tf_op jit(solution)/shard_map/ppermute | solution.py:198
  120.5 1.9 %collective-permute-done.18 = f32[4,24,256]{2,0,1:T(4,128)S(1)} collective-permute-done((f32[4,24,256]{2,0,1:T(4,128)S(1)}, f32[4,24,256]{2,0,1:T(4,128)S(1)}, u32[]{:S(2)}, u32[]{:S(2)}) %collective-permute-start.18) | collective-permute-done | bytes 98336 | tf_op jit(solution)/shard_map/ppermute | solution.py:198
  122.6 5.7 %collective-permute-start.22 = (f32[8,24,256]{2,0,1:T(8,128)S(1)}, f32[8,24,256]{2,0,1:T(8,128)S(1)}, u32[]{:S(2)}, u32[]{:S(2)}) collective-permute-start(f32[8,24,256]{2,0,1:T(8,128)S(1)} %fusion.53), channel_id=1, source_target_pairs={{0,8},{1,9},{2,10},{3,11},{4,12},{5,13},{6,14},{7,15},{8,16},{9,17... | collective-permute-start | bytes 589832 | tf_op jit(solution)/shard_map/ppermute | solution.py:19
  129.6 3.4 %collective-permute-done.22 = f32[8,24,256]{2,0,1:T(8,128)S(1)} collective-permute-done((f32[8,24,256]{2,0,1:T(8,128)S(1)}, f32[8,24,256]{2,0,1:T(8,128)S(1)}, u32[]{:S(2)}, u32[]{:S(2)}) %collective-permute-start.22) | collective-permute-done | bytes 196640 | tf_op jit(solution)/shard_map/ppermute | solution.py:19
  133.1 8.3 %collective-permute-done.21 = f32[8,24,256]{2,0,1:T(8,128)S(1)} collective-permute-done((f32[8,24,256]{2,0,1:T(8,128)S(1)}, f32[8,24,256]{2,0,1:T(8,128)S(1)}, u32[]{:S(2)}, u32[]{:S(2)}) %collective-permute-start.21) | collective-permute-done | bytes 196640 | tf_op jit(solution)/shard_map/ppermute | solution.py:19
  143.4 2.1 %collective-permute-done.25 = f32[8,24,256]{2,0,1:T(8,128)S(1)} collective-permute-done((f32[8,24,256]{2,0,1:T(8,128)S(1)}, f32[8,24,256]{2,0,1:T(8,128)S(1)}, u32[]{:S(2)}, u32[]{:S(2)}) %collective-permute-start.25) | collective-permute-done | bytes 196640 | tf_op jit(solution)/shard_map/ppermute | solution.py:65
  145.5 9.8 %collective-permute-done.24 = f32[8,24,256]{2,0,1:T(8,128)S(1)} collective-permute-done((f32[8,24,256]{2,0,1:T(8,128)S(1)}, f32[8,24,256]{2,0,1:T(8,128)S(1)}, u32[]{:S(2)}, u32[]{:S(2)}) %collective-permute-start.24) | collective-permute-done | bytes 196640 | tf_op jit(solution)/shard_map/ppermute | solution.py:65
  156.4 1.8 %copy.44 = f32[3,8,1,12,768]{4,2,3,1,0:T(1,128)} copy(f32[3,8,1,12,768]{4,1,3,2,0:T(8,128)S(1)} %slice_bitcast_fusion) | data formatting | bytes 1769472
  158.2 5.3 %collective-permute-done.26 = f32[8,24,256]{2,0,1:T(8,128)S(1)} collective-permute-done((f32[8,24,256]{2,0,1:T(8,128)S(1)}, f32[8,24,256]{2,0,1:T(8,128)S(1)}, u32[]{:S(2)}, u32[]{:S(2)}) %collective-permute-start.26) | collective-permute-done | bytes 196640 | tf_op jit(solution)/shard_map/ppermute | solution.py:65
  163.7 3.8 %dynamic_update_slice.3 = f32[3,8,8,2048]{3,1,2,0:T(8,128)S(1)} dynamic-update-slice(f32[3,8,8,2048]{3,1,2,0:T(8,128)S(1)} %copy-done.1, f32[3,8,8,256]{3,1,2,0:T(8,128)S(1)} %copy_select_fusion, s32[]{:T(128)} %constant.95.clone.1, s32[]{:T(128)} %constant.95.clone.1, s32[]{:T(128)} %constant.95.clone.1, s32[]{:T(128)S(6)} %select_n.189) | dynamic-update-slice | bytes 393220 | tf_op jit(solution)/shard_map/dynamic_update_slice | solution.py:215
  167.5 2.1 %copy.43 = f32[3,8,8,2048]{3,2,1,0:T(8,128)} copy(f32[3,8,8,2048]{3,1,2,0:T(8,128)S(1)} %dynamic_update_slice.3) | data formatting | bytes 3145728
  (150 shorter events, 36.4 us)
Async XLA Ops:
  2.1 19.3 %collective-permute-start.3 = (f32[3,3,8,768]{3,2,0,1:T(8,128)S(1)}, f32[3,3,8,768]{3,2,0,1:T(8,128)S(1)}, u32[]{:S(2)}, u32[]{:S(2)}) collective-permute-start(f32[3,3,8,768]{3,2,0,1:T(8,128)S(1)} %get-tuple-element.24), channel_id=1, source_target_pairs={{1,0},{2,1},{3,2},{4,3},{5,4},{6,5},{7,6},{8,7},{9,8},{10,9},{11,1... | collective-permute-start | bytes 663560 | tf_op jit(solution)/shard_map/ppermute | solution.py:19
  7.2 14.1 %collective-permute-start.2 = (f32[3,3,8,768]{3,2,0,1:T(8,128)S(1)}, f32[3,3,8,768]{3,2,0,1:T(8,128)S(1)}, u32[]{:S(2)}, u32[]{:S(2)}) collective-permute-start(f32[3,3,8,768]{3,2,0,1:T(8,128)S(1)} %get-tuple-element.25), channel_id=1, source_target_pairs={{0,1},{1,2},{2,3},{3,4},{4,5},{5,6},{6,7},{7,8},{8,9},{9,10},{10,1... | collective-permute-start | bytes 663560 | tf_op jit(solution)/shard_map/ppermute | solution.py:19
  10.6 8.9 %collective-permute-start = (f32[2,8,2048]{2,1,0:T(8,128)}, f32[2,8,2048]{2,1,0:T(8,128)S(1)}, u32[]{:S(2)}, u32[]{:S(2)}) collective-permute-start(f32[2,8,2048]{2,1,0:T(8,128)} %get-tuple-element.22), channel_id=1, source_target_pairs={{0,1},{1,2},{2,3},{3,4},{4,5},{5,6},{6,7},{7,8},{8,9},{9,10},{10,1... | collective-permute-start | bytes 393224 | tf_op jit(solution)/shard_map/ppermute | solution.py:19
  12.5 7.0 %collective-permute-start.1 = (f32[2,8,2048]{2,1,0:T(8,128)S(1)}, f32[2,8,2048]{2,1,0:T(8,128)S(1)}, u32[]{:S(2)}, u32[]{:S(2)}) collective-permute-start(f32[2,8,2048]{2,1,0:T(8,128)S(1)} %get-tuple-element.23), channel_id=1, source_target_pairs={{1,0},{2,1},{3,2},{4,3},{5,4},{6,5},{7,6},{8,7},{9,8},{10,9},{11,1... | collective-permute-start | bytes 393224 | tf_op jit(solution)/shard_map/ppermute | solution.py:19
  21.4 10.1 %collective-permute-start.6 = (f32[26,8,256]{2,1,0:T(8,128)S(1)}, f32[26,8,256]{2,1,0:T(8,128)S(1)}, u32[]{:S(2)}, u32[]{:S(2)}) collective-permute-start(f32[26,8,256]{2,1,0:T(8,128)S(1)} %pad_maximum_fusion.15), channel_id=1, source_target_pairs={{1,0},{2,1},{3,2},{4,3},{5,4},{6,5},{7,6},{0,7},{9,8},{10,9},{11,1... | collective-permute-start | bytes 638984 | tf_op jit(solution)/shard_map/ppermute | solution.py:65
  21.4 11.8 %collective-permute-start.5 = (f32[26,8,256]{2,1,0:T(8,128)S(1)}, f32[26,8,256]{2,1,0:T(8,128)S(1)}, u32[]{:S(2)}, u32[]{:S(2)}) collective-permute-start(f32[26,8,256]{2,1,0:T(8,128)S(1)} %pad_maximum_fusion.15), channel_id=1, source_target_pairs={{2,0},{3,1},{4,2},{5,3},{6,4},{7,5},{0,6},{1,7},{10,8},{11,9},{12,... | collective-permute-start | bytes 638984 | tf_op jit(solution)/shard_map/ppermute | solution.py:65
  28.7 11.4 %collective-permute-start.4 = (f32[26,8,256]{2,1,0:T(8,128)S(1)}, f32[26,8,256]{2,1,0:T(8,128)S(1)}, u32[]{:S(2)}, u32[]{:S(2)}) collective-permute-start(f32[26,8,256]{2,1,0:T(8,128)S(1)} %pad_maximum_fusion.15), channel_id=1, source_target_pairs={{3,0},{4,1},{5,2},{6,3},{7,4},{0,5},{1,6},{2,7},{11,8},{12,9},{13,... | collective-permute-start | bytes 638984 | tf_op jit(solution)/shard_map/ppermute | solution.py:65
  40.2 7.5 %collective-permute-start.7 = (f32[26,8,256]{2,1,0:T(8,128)S(1)}, f32[26,8,256]{2,1,0:T(8,128)S(1)}, u32[]{:S(2)}, u32[]{:S(2)}) collective-permute-start(f32[26,8,256]{2,1,0:T(8,128)S(1)} %select_select_fusion.1), channel_id=1, source_target_pairs={{4,0},{5,1},{6,2},{7,3},{0,4},{1,5},{2,6},{3,7},{12,8},{13,9},{14,... | collective-permute-start | bytes 638984 | tf_op jit(solution)/shard_map/ppermute | solution.py:65
  47.7 10.1 %collective-permute-start.9 = (f32[26,8,256]{2,1,0:T(8,128)S(1)}, f32[26,8,256]{2,1,0:T(8,128)S(1)}, u32[]{:S(2)}, u32[]{:S(2)}) collective-permute-start(f32[26,8,256]{2,1,0:T(8,128)S(1)} %broadcast_select_fusion.1), channel_id=1, source_target_pairs={{0,8},{1,9},{2,10},{3,11},{4,12},{5,13},{6,14},{7,15},{8,16},{9,17... | collective-permute-start | bytes 638984 | tf_op jit(solution)/shard_map/ppermute | solution.py:19
  55.1 7.5 %collective-permute-start.8 = (f32[26,8,256]{2,1,0:T(8,128)S(1)}, f32[26,8,256]{2,1,0:T(8,128)S(1)}, u32[]{:S(2)}, u32[]{:S(2)}) collective-permute-start(f32[26,8,256]{2,1,0:T(8,128)S(1)} %broadcast_select_fusion.1), channel_id=1, source_target_pairs={{8,0},{9,1},{10,2},{11,3},{12,4},{13,5},{14,6},{15,7},{16,8},{17,9... | collective-permute-start | bytes 638984 | tf_op jit(solution)/shard_map/ppermute | solution.py:19
  63.3 3.5 %collective-permute-start.10 = (f32[26,256]{1,0:T(8,128)S(1)}, f32[26,256]{1,0:T(8,128)S(1)}, u32[]{:S(2)}, u32[]{:S(2)}) collective-permute-start(f32[26,256]{1,0:T(8,128)S(1)} %bitcast.189), channel_id=1, source_target_pairs={{7,0},{8,2},{9,4},{10,6},{11,8},{12,10},{13,12},{14,14},{15,16},{1... | collective-permute-start | bytes 79880 | tf_op jit(solution)/shard_map/ppermute | solution.py:147
  64.0 5.6 %collective-permute-start.12 = (f32[4,26,256]{2,0,1:T(4,128)S(1)}, f32[4,26,256]{2,0,1:T(4,128)S(1)}, u32[]{:S(2)}, u32[]{:S(2)}) collective-permute-start(f32[4,26,256]{2,0,1:T(4,128)S(1)} %slice_bitcast_fusion.14), channel_id=1, source_target_pairs={{24,30},{56,62},{88,94},{120,126},{152,158},{184,190},{216,222},{2... | collective-permute-start | bytes 319496 | tf_op jit(solution)/shard_map/ppermute | solution.py:151
  64.7 4.9 %collective-permute-start.13 = (f32[4,26,256]{2,0,1:T(4,128)S(1)}, f32[4,26,256]{2,0,1:T(4,128)S(1)}, u32[]{:S(2)}, u32[]{:S(2)}) collective-permute-start(f32[4,26,256]{2,0,1:T(4,128)S(1)} %slice_bitcast_fusion.13), channel_id=1, source_target_pairs={{2,0},{4,2},{6,4},{8,6},{10,8},{12,10},{14,12},{16,14},{18,16},{20... | collective-permute-start | bytes 319496 | tf_op jit(solution)/shard_map/ppermute | solution.py:158
  66.1 3.6 %collective-permute-start.15 = (f32[26,8,256]{2,1,0:T(8,128)S(1)}, f32[26,8,256]{2,1,0:T(8,128)S(1)}, u32[]{:S(2)}, u32[]{:S(2)}) collective-permute-start(f32[26,8,256]{2,1,0:T(8,128)S(1)} %select_select_fusion), channel_id=1, source_target_pairs={{24,31},{56,63},{88,95},{120,127},{152,159},{184,191},{216,223},{2... | collective-permute-start | bytes 638984 | tf_op jit(solution)/shard_map/ppermute | solution.py:150
  66.9 26.7 %collective-permute-start.16 = (f32[26,8,256]{2,1,0:T(8,128)S(1)}, f32[26,8,256]{2,1,0:T(8,128)S(1)}, u32[]{:S(2)}, u32[]{:S(2)}) collective-permute-start(f32[26,8,256]{2,1,0:T(8,128)S(1)} %collective-permute-done.11), channel_id=1, source_target_pairs={{2,1},{4,3},{6,5},{8,7},{10,9},{12,11},{14,13},{16,15},{18,17},{20... | collective-permute-start | bytes 638984 | tf_op jit(solution)/shard_map/ppermute | solution.py:155
  68.2 25.4 %collective-permute-start.14 = (f32[26,8,256]{2,1,0:T(8,128)S(1)}, f32[26,8,256]{2,1,0:T(8,128)S(1)}, u32[]{:S(2)}, u32[]{:S(2)}) collective-permute-start(f32[26,8,256]{2,1,0:T(8,128)S(1)} %collective-permute-done.11), channel_id=1, source_target_pairs={{0,1},{2,3},{4,5},{6,7},{8,9},{10,11},{12,13},{14,15},{16,17},{18,... | collective-permute-start | bytes 638984 | tf_op jit(solution)/shard_map/ppermute | solution.py:154
  110.2 10.3 %collective-permute-start.20 = (f32[4,24,256]{2,0,1:T(4,128)S(1)}, f32[4,24,256]{2,0,1:T(4,128)S(1)}, u32[]{:S(2)}, u32[]{:S(2)}) collective-permute-start(f32[4,24,256]{2,0,1:T(4,128)S(1)} %bitcast.185), channel_id=1, source_target_pairs={{1,8},{3,9},{5,10},{7,11},{9,12},{11,13},{13,14},{15,15},{17,16},{... | collective-permute-start | bytes 294920 | tf_op jit(solution)/shard_map/ppermute | solution.py:198
  118.5 3.9 %collective-permute-start.18 = (f32[4,24,256]{2,0,1:T(4,128)S(1)}, f32[4,24,256]{2,0,1:T(4,128)S(1)}, u32[]{:S(2)}, u32[]{:S(2)}) collective-permute-start(f32[4,24,256]{2,0,1:T(4,128)S(1)} %bitcast.187), channel_id=1, source_target_pairs={{1,9},{3,10},{5,11},{7,12},{9,13},{11,14},{13,15},{15,16},{17,17},... | collective-permute-start | bytes 294920 | tf_op jit(solution)/shard_map/ppermute | solution.py:198
  122.6 10.5 %collective-permute-start.22 = (f32[8,24,256]{2,0,1:T(8,128)S(1)}, f32[8,24,256]{2,0,1:T(8,128)S(1)}, u32[]{:S(2)}, u32[]{:S(2)}) collective-permute-start(f32[8,24,256]{2,0,1:T(8,128)S(1)} %fusion.53), channel_id=1, source_target_pairs={{0,8},{1,9},{2,10},{3,11},{4,12},{5,13},{6,14},{7,15},{8,16},{9,17... | collective-permute-start | bytes 589832 | tf_op jit(solution)/shard_map/ppermute | solution.py:19
  128.3 13.0 %collective-permute-start.21 = (f32[8,24,256]{2,0,1:T(8,128)S(1)}, f32[8,24,256]{2,0,1:T(8,128)S(1)}, u32[]{:S(2)}, u32[]{:S(2)}) collective-permute-start(f32[8,24,256]{2,0,1:T(8,128)S(1)} %fusion.53), channel_id=1, source_target_pairs={{8,0},{9,1},{10,2},{11,3},{12,4},{13,5},{14,6},{15,7},{16,8},{17,9... | collective-permute-start | bytes 589832 | tf_op jit(solution)/shard_map/ppermute | solution.py:19
  141.4 4.0 %collective-permute-start.25 = (f32[8,24,256]{2,0,1:T(8,128)S(1)}, f32[8,24,256]{2,0,1:T(8,128)S(1)}, u32[]{:S(2)}, u32[]{:S(2)}) collective-permute-start(f32[8,24,256]{2,0,1:T(8,128)S(1)} %select_select_fusion.3), channel_id=1, source_target_pairs={{7,0},{0,1},{1,2},{2,3},{3,4},{4,5},{5,6},{6,7},{15,8},{8,9},{9,10... | collective-permute-start | bytes 589832 | tf_op jit(solution)/shard_map/ppermute | solution.py:65
  141.4 13.8 %collective-permute-start.24 = (f32[8,24,256]{2,0,1:T(8,128)S(1)}, f32[8,24,256]{2,0,1:T(8,128)S(1)}, u32[]{:S(2)}, u32[]{:S(2)}) collective-permute-start(f32[8,24,256]{2,0,1:T(8,128)S(1)} %select_select_fusion.3), channel_id=1, source_target_pairs={{6,0},{7,1},{0,2},{1,3},{2,4},{3,5},{4,6},{5,7},{14,8},{15,9},{8,1... | collective-permute-start | bytes 589832 | tf_op jit(solution)/shard_map/ppermute | solution.py:65
  141.5 14.4 %collective-permute-start.23 = (f32[8,24,256]{2,0,1:T(8,128)S(1)}, f32[8,24,256]{2,0,1:T(8,128)S(1)}, u32[]{:S(2)}, u32[]{:S(2)}) collective-permute-start(f32[8,24,256]{2,0,1:T(8,128)S(1)} %select_select_fusion.3), channel_id=1, source_target_pairs={{5,0},{6,1},{7,2},{0,3},{1,4},{2,5},{3,6},{4,7},{13,8},{14,9},{15,... | collective-permute-start | bytes 589832 | tf_op jit(solution)/shard_map/ppermute | solution.py:65
  156.0 7.6 %collective-permute-start.26 = (f32[8,24,256]{2,0,1:T(8,128)S(1)}, f32[8,24,256]{2,0,1:T(8,128)S(1)}, u32[]{:S(2)}, u32[]{:S(2)}) collective-permute-start(f32[8,24,256]{2,0,1:T(8,128)S(1)} %select_select_fusion.2), channel_id=1, source_target_pairs={{4,0},{5,1},{6,2},{7,3},{0,4},{1,5},{2,6},{3,7},{12,8},{13,9},{14,... | collective-permute-start | bytes 589832 | tf_op jit(solution)/shard_map/ppermute | solution.py:65
  (18 other events, 113.1 us)

commit v10 on v8

--- a/solution.py
+++ b/solution.py
@@ -141,13 +141,26 @@
     block = rotate(block, [(4, bit2)], center, tiles)
     carry = (slab_pos + low3 >= center).astype(jnp.int32)
     slab_shift = bit3.astype(jnp.int32) + carry - 1
-    block = pick(block, [(-center, slab_shift == -1), (center, slab_shift == 1)], tiles)
+
+    def shift_of(position):
+        return bit3.astype(jnp.int32) + (position % center + low3 >= center).astype(jnp.int32) - 1
+
+    def spread(value, first, targets):
+        own = first + tile_index // 2
+        out = jnp.zeros_like(value)
+        for s in (-1, 0, 1):
+            pairs = [
+                (first + m + center * s, targets(m))
+                for m in range(half)
+                if 0 <= first + m + center * s < tiles
+            ]
+            out = jnp.where(shift_of(own) == s, lax.ppermute(value, "tile", pairs), out)
+        return out
+
     extra = foot_rows - 2
-    own_even = lax.ppermute(block, "tile", [(m + center, 2 * m) for m in range(half)])
-    last_even = lax.ppermute(
-        block[:, parent_rows - 1], "tile", [(m + center - 1, 2 * m) for m in range(half)]
-    )
-    next_odd = lax.ppermute(block, "tile", [(m + center + 1, 2 * m + 1) for m in range(half)])
+    own_even = spread(block, center, lambda m: 2 * m)
+    last_even = spread(block[:, parent_rows - 1], center - 1, lambda m: 2 * m)
+    next_odd = spread(block, center + 1, lambda m: 2 * m + 1)
     own_odd = lax.ppermute(own_even, "tile", [(2 * m, 2 * m + 1) for m in range(half)])
     first_rows = jnp.transpose(next_odd[:, :extra], (1, 0, 2))
     next_even = lax.ppermute(first_rows, "tile", [(2 * m + 1, 2 * m) for m in range(half)])

time: 164 us -> 171 us (1.043); the launches traced: 163 us -> 168 us
  starting transfers between devices: 71.7 us -> 84.1 us
  waiting for transfers between devices: 51.8 us -> 44 us
    ppermute x4, starting transfers between devices: 5.05 us -> 19.7 us  [local(): lax.ppermute(means, 'tile', [(2 * m + k, m + center) for m in range(half...]
    ppermute x3 -> x9, starting transfers between devices: 2.63 us -> 15.9 us  [spread(): out = jnp.where(shift_of(own) == s, lax.ppermute(value, 'tile', pairs), out)]
    ppermute x8 -> x6, starting transfers between devices: 28.4 us -> 20 us  [shift_from(): return lax.ppermute(value, axis, pairs)]
    ppermute x8 -> x6, waiting for transfers between devices: 14.6 us -> 9.46 us  [shift_from(): return lax.ppermute(value, axis, pairs)]
    ppermute x8, starting transfers between devices: 17.8 us -> 13.1 us  [rotate(): out = jnp.where(predicate, lax.ppermute(value, 'tile', pairs), out)]
    ppermute x3 -> x9, waiting for transfers between devices: 8.64 us -> 4.99 us  [spread(): out = jnp.where(shift_of(own) == s, lax.ppermute(value, 'tile', pairs), out)]
    ppermute x1, starting transfers between devices: 16.6 us -> 13.8 us  [local(): lax.ppermute(first_rows, 'tile', [(2 * m + 1, 2 * m) for m in range(half)])]
    ppermute x1, waiting for transfers between devices: 0.01 us -> 1.79 us  [local(): lax.ppermute(own_even, 'tile', [(2 * m, 2 * m + 1) for m in range(half)])]
  transfers between devices with their start and end apart: 25 -> 29, of which waited for: 13 -> 12; matrix products, arithmetic and copies ran while one was open for 5% -> 4% of each run, Pallas kernels for 0% -> 0%
where the time goes in v10:
time: 171 us; the launch traced here: 168 us
  starting transfers between devices  84.1 us (49%)
  waiting for transfers between devices  44 us (26%)
  local copies, waits for them, and re-layouts  20.7 us (12%)
  other arithmetic  8.58 us (5%)
  between operations  8.21 us (5%)
  matrix products  2.45 us (1%)
    ppermute x8, waiting for transfers between devices, rotate(): out = jnp.where(predicate, lax.ppermute(value, 'tile', pairs), out)  26.8 us
    ppermute x6, starting transfers between devices, shift_from(): return lax.ppermute(value, axis, pairs)  20 us
    ppermute x4, starting transfers between devices, local(): lax.ppermute(means, 'tile', [(2 * m + k, m + center) for m in range(half...  19.7 us
    ppermute x9, starting transfers between devices, spread(): out = jnp.where(shift_of(own) == s, lax.ppermute(value, 'tile', pairs), out)  15.9 us
    ppermute x1, starting transfers between devices, local(): lax.ppermute(first_rows, 'tile', [(2 * m + 1, 2 * m) for m in range(half)])  13.8 us
    ppermute x8, starting transfers between devices, rotate(): out = jnp.where(predicate, lax.ppermute(value, 'tile', pairs), out)  13.1 us
    ppermute x6, waiting for transfers between devices, shift_from(): return lax.ppermute(value, axis, pairs)  9.46 us
    unnamed x36, local copies, waits for them, and re-layouts  9.06 us
  transfers between devices with their start and end apart: 29, of which 12 were waited for; matrix products, arithmetic and copies ran while one was open for 4% of the time, Pallas kernels for 0%

profile of v10, /device:TPU:1, one launch (start us, length us, event | category | flops | bytes accessed | tf_op | source)
XLA Modules:
  0.0 168.1 jit_solution(13964329771489176215)
XLA Ops:
  2.1 5.1 %collective-permute-start.3 = (f32[3,3,8,768]{3,2,0,1:T(8,128)S(1)}, f32[3,3,8,768]{3,2,0,1:T(8,128)S(1)}, u32[]{:S(2)}, u32[]{:S(2)}) collective-permute-start(f32[3,3,8,768]{3,2,0,1:T(8,128)S(1)} %get-tuple-element.24), channel_id=1, source_target_pairs={{1,0},{2,1},{3,2},{4,3},{5,4},{6,5},{7,6},{8,7},{9,8},{10,9},{11,1... | collective-permute-start | bytes 663560 | tf_op jit(solution)/shard_map/ppermute | solution.py:19
  7.2 1.9 %collective-permute-start.2 = (f32[3,3,8,768]{3,2,0,1:T(8,128)S(1)}, f32[3,3,8,768]{3,2,0,1:T(8,128)S(1)}, u32[]{:S(2)}, u32[]{:S(2)}) collective-permute-start(f32[3,3,8,768]{3,2,0,1:T(8,128)S(1)} %get-tuple-element.25), channel_id=1, source_target_pairs={{0,1},{1,2},{2,3},{3,4},{4,5},{5,6},{6,7},{7,8},{8,9},{9,10},{10,1... | collective-permute-start | bytes 663560 | tf_op jit(solution)/shard_map/ppermute | solution.py:19
  10.6 1.9 %collective-permute-start = (f32[2,8,2048]{2,1,0:T(8,128)}, f32[2,8,2048]{2,1,0:T(8,128)S(1)}, u32[]{:S(2)}, u32[]{:S(2)}) collective-permute-start(f32[2,8,2048]{2,1,0:T(8,128)} %get-tuple-element.22), channel_id=1, source_target_pairs={{0,1},{1,2},{2,3},{3,4},{4,5},{5,6},{6,7},{7,8},{8,9},{9,10},{10,1... | collective-permute-start | bytes 393224 | tf_op jit(solution)/shard_map/ppermute | solution.py:19
  12.5 2.4 %collective-permute-start.1 = (f32[2,8,2048]{2,1,0:T(8,128)S(1)}, f32[2,8,2048]{2,1,0:T(8,128)S(1)}, u32[]{:S(2)}, u32[]{:S(2)}) collective-permute-start(f32[2,8,2048]{2,1,0:T(8,128)S(1)} %get-tuple-element.23), channel_id=1, source_target_pairs={{1,0},{2,1},{3,2},{4,3},{5,4},{6,5},{7,6},{8,7},{9,8},{10,9},{11,1... | collective-permute-start | bytes 393224 | tf_op jit(solution)/shard_map/ppermute | solution.py:19
  21.4 7.3 %collective-permute-start.5 = (f32[26,8,256]{2,1,0:T(8,128)S(1)}, f32[26,8,256]{2,1,0:T(8,128)S(1)}, u32[]{:S(2)}, u32[]{:S(2)}) collective-permute-start(f32[26,8,256]{2,1,0:T(8,128)S(1)} %pad_maximum_fusion.15), channel_id=1, source_target_pairs={{2,0},{3,1},{4,2},{5,3},{6,4},{7,5},{0,6},{1,7},{10,8},{11,9},{12,... | collective-permute-start | bytes 638984 | tf_op jit(solution)/shard_map/ppermute | solution.py:65
  33.3 6.8 %collective-permute-done.4 = f32[26,8,256]{2,1,0:T(8,128)S(1)} collective-permute-done((f32[26,8,256]{2,1,0:T(8,128)S(1)}, f32[26,8,256]{2,1,0:T(8,128)S(1)}, u32[]{:S(2)}, u32[]{:S(2)}) %collective-permute-start.4) | collective-permute-done | bytes 213024 | tf_op jit(solution)/shard_map/ppermute | solution.py:65
  40.8 6.9 %collective-permute-done.7 = f32[26,8,256]{2,1,0:T(8,128)S(1)} collective-permute-done((f32[26,8,256]{2,1,0:T(8,128)S(1)}, f32[26,8,256]{2,1,0:T(8,128)S(1)}, u32[]{:S(2)}, u32[]{:S(2)}) %collective-permute-start.7) | collective-permute-done | bytes 213024 | tf_op jit(solution)/shard_map/ppermute | solution.py:65
  51.1 2.9 %collective-permute-start.10 = (f32[26,256]{1,0:T(8,128)S(1)}, f32[26,256]{1,0:T(8,128)S(1)}, u32[]{:S(2)}, u32[]{:S(2)}) collective-permute-start(f32[26,256]{1,0:T(8,128)S(1)} %bitcast.187), channel_id=1, source_target_pairs={{0,2},{1,4},{2,6},{3,8},{4,10},{5,12},{6,14},{7,16},{8,18},{9,20},... | collective-permute-start | bytes 79880 | tf_op jit(solution)/shard_map/ppermute | solution.py:157
  54.7 7.1 %collective-permute-start.13 = (f32[26,8,256]{2,1,0:T(8,128)S(1)}, f32[26,8,256]{2,1,0:T(8,128)S(1)}, u32[]{:S(2)}, u32[]{:S(2)}) collective-permute-start(f32[26,8,256]{2,1,0:T(8,128)S(1)} %broadcast_select_fusion), channel_id=1, source_target_pairs={{0,0},{1,2},{2,4},{3,6},{4,8},{5,10},{6,12},{7,14},{8,16},{9,18},{... | collective-permute-start | bytes 638984 | tf_op jit(solution)/shard_map/ppermute | solution.py:157
  61.8 5.0 %collective-permute-done.15 = f32[26,8,256]{2,1,0:T(8,128)S(1)} collective-permute-done((f32[26,8,256]{2,1,0:T(8,128)S(1)}, f32[26,8,256]{2,1,0:T(8,128)S(1)}, u32[]{:S(2)}, u32[]{:S(2)}) %collective-permute-start.15) | collective-permute-done | bytes 213024 | tf_op jit(solution)/shard_map/ppermute | solution.py:157
  68.9 13.8 %collective-permute-start.17 = (f32[4,26,256]{2,0,1:T(4,128)S(1)}, f32[4,26,256]{2,0,1:T(4,128)S(1)}, u32[]{:S(2)}, u32[]{:S(2)}) collective-permute-start(f32[4,26,256]{2,0,1:T(4,128)S(1)} %slice_bitcast_fusion.13), channel_id=1, source_target_pairs={{1,0},{3,2},{5,4},{7,6},{9,8},{11,10},{13,12},{15,14},{17,16},{19,... | collective-permute-start | bytes 319496 | tf_op jit(solution)/shard_map/ppermute | solution.py:166
  84.3 1.8 %collective-permute-done.18 = f32[26,8,256]{2,1,0:T(8,128)S(1)} collective-permute-done((f32[26,8,256]{2,1,0:T(8,128)S(1)}, f32[26,8,256]{2,1,0:T(8,128)S(1)}, u32[]{:S(2)}, u32[]{:S(2)}) %collective-permute-start.18) | collective-permute-done | bytes 213024 | tf_op jit(solution)/shard_map/ppermute | solution.py:164
  102.7 6.1 %collective-permute-start.22 = (f32[4,24,256]{2,0,1:T(4,128)S(1)}, f32[4,24,256]{2,0,1:T(4,128)S(1)}, u32[]{:S(2)}, u32[]{:S(2)}) collective-permute-start(f32[4,24,256]{2,0,1:T(4,128)S(1)} %bitcast.183), channel_id=1, source_target_pairs={{1,8},{3,9},{5,10},{7,11},{9,12},{11,13},{13,14},{15,15},{17,16},{... | collective-permute-start | bytes 294920 | tf_op jit(solution)/shard_map/ppermute | solution.py:205
  109.5 12.3 %collective-permute-start.20 = (f32[4,24,256]{2,0,1:T(4,128)S(1)}, f32[4,24,256]{2,0,1:T(4,128)S(1)}, u32[]{:S(2)}, u32[]{:S(2)}) collective-permute-start(f32[4,24,256]{2,0,1:T(4,128)S(1)} %bitcast.185), channel_id=1, source_target_pairs={{1,9},{3,10},{5,11},{7,12},{9,13},{11,14},{13,15},{15,16},{17,17},... | collective-permute-start | bytes 294920 | tf_op jit(solution)/shard_map/ppermute | solution.py:205
  123.6 7.4 %collective-permute-start.24 = (f32[8,24,256]{2,0,1:T(8,128)S(1)}, f32[8,24,256]{2,0,1:T(8,128)S(1)}, u32[]{:S(2)}, u32[]{:S(2)}) collective-permute-start(f32[8,24,256]{2,0,1:T(8,128)S(1)} %fusion.53), channel_id=1, source_target_pairs={{0,8},{1,9},{2,10},{3,11},{4,12},{5,13},{6,14},{7,15},{8,16},{9,17... | collective-permute-start | bytes 589832 | tf_op jit(solution)/shard_map/ppermute | solution.py:19
  133.9 7.9 %collective-permute-done.23 = f32[8,24,256]{2,0,1:T(8,128)S(1)} collective-permute-done((f32[8,24,256]{2,0,1:T(8,128)S(1)}, f32[8,24,256]{2,0,1:T(8,128)S(1)}, u32[]{:S(2)}, u32[]{:S(2)}) %collective-permute-start.23) | collective-permute-done | bytes 196640 | tf_op jit(solution)/shard_map/ppermute | solution.py:19
  141.8 2.7 %collective-permute-start.27 = (f32[8,24,256]{2,0,1:T(8,128)S(1)}, f32[8,24,256]{2,0,1:T(8,128)S(1)}, u32[]{:S(2)}, u32[]{:S(2)}) collective-permute-start(f32[8,24,256]{2,0,1:T(8,128)S(1)} %select_select_fusion.4), channel_id=1, source_target_pairs={{7,0},{0,1},{1,2},{2,3},{3,4},{4,5},{5,6},{6,7},{15,8},{8,9},{9,10... | collective-permute-start | bytes 589832 | tf_op jit(solution)/shard_map/ppermute | solution.py:65
  146.5 2.1 %collective-permute-done.27 = f32[8,24,256]{2,0,1:T(8,128)S(1)} collective-permute-done((f32[8,24,256]{2,0,1:T(8,128)S(1)}, f32[8,24,256]{2,0,1:T(8,128)S(1)}, u32[]{:S(2)}, u32[]{:S(2)}) %collective-permute-start.27) | collective-permute-done | bytes 196640 | tf_op jit(solution)/shard_map/ppermute | solution.py:65
  148.6 4.9 %collective-permute-done.26 = f32[8,24,256]{2,0,1:T(8,128)S(1)} collective-permute-done((f32[8,24,256]{2,0,1:T(8,128)S(1)}, f32[8,24,256]{2,0,1:T(8,128)S(1)}, u32[]{:S(2)}, u32[]{:S(2)}) %collective-permute-start.26) | collective-permute-done | bytes 196640 | tf_op jit(solution)/shard_map/ppermute | solution.py:65
  153.5 2.1 %collective-permute-done.25 = f32[8,24,256]{2,0,1:T(8,128)S(1)} collective-permute-done((f32[8,24,256]{2,0,1:T(8,128)S(1)}, f32[8,24,256]{2,0,1:T(8,128)S(1)}, u32[]{:S(2)}, u32[]{:S(2)}) %collective-permute-start.25) | collective-permute-done | bytes 196640 | tf_op jit(solution)/shard_map/ppermute | solution.py:65
  157.5 1.8 %copy.49 = f32[3,8,1,12,768]{4,2,3,1,0:T(1,128)} copy(f32[3,8,1,12,768]{4,1,3,2,0:T(8,128)S(1)} %slice_bitcast_fusion) | data formatting | bytes 1769472
  159.3 2.7 %collective-permute-done.28 = f32[8,24,256]{2,0,1:T(8,128)S(1)} collective-permute-done((f32[8,24,256]{2,0,1:T(8,128)S(1)}, f32[8,24,256]{2,0,1:T(8,128)S(1)}, u32[]{:S(2)}, u32[]{:S(2)}) %collective-permute-start.28) | collective-permute-done | bytes 196640 | tf_op jit(solution)/shard_map/ppermute | solution.py:65
  162.2 3.8 %dynamic_update_slice.3 = f32[3,8,8,2048]{3,1,2,0:T(8,128)S(1)} dynamic-update-slice(f32[3,8,8,2048]{3,1,2,0:T(8,128)S(1)} %copy-done.1, f32[3,8,8,256]{3,1,2,0:T(8,128)S(1)} %copy_select_fusion, s32[]{:T(128)} %constant.135.clone.1, s32[]{:T(128)} %constant.135.clone.1, s32[]{:T(128)} %constant.135.clone.1, s32[]{:T(128)S(6)} %select_n.250) | dynamic-update-slice | bytes 393220 | tf_op jit(solution)/shard_map/dynamic_update_slice | solution.py:222
  166.0 2.1 %copy.48 = f32[3,8,8,2048]{3,2,1,0:T(8,128)} copy(f32[3,8,8,2048]{3,1,2,0:T(8,128)S(1)} %dynamic_update_slice.3) | data formatting | bytes 3145728
  (153 shorter events, 41.1 us)
Async XLA Ops:
  2.1 19.2 %collective-permute-start.3 = (f32[3,3,8,768]{3,2,0,1:T(8,128)S(1)}, f32[3,3,8,768]{3,2,0,1:T(8,128)S(1)}, u32[]{:S(2)}, u32[]{:S(2)}) collective-permute-start(f32[3,3,8,768]{3,2,0,1:T(8,128)S(1)} %get-tuple-element.24), channel_id=1, source_target_pairs={{1,0},{2,1},{3,2},{4,3},{5,4},{6,5},{7,6},{8,7},{9,8},{10,9},{11,1... | collective-permute-start | bytes 663560 | tf_op jit(solution)/shard_map/ppermute | solution.py:19
  7.2 14.1 %collective-permute-start.2 = (f32[3,3,8,768]{3,2,0,1:T(8,128)S(1)}, f32[3,3,8,768]{3,2,0,1:T(8,128)S(1)}, u32[]{:S(2)}, u32[]{:S(2)}) collective-permute-start(f32[3,3,8,768]{3,2,0,1:T(8,128)S(1)} %get-tuple-element.25), channel_id=1, source_target_pairs={{0,1},{1,2},{2,3},{3,4},{4,5},{5,6},{6,7},{7,8},{8,9},{9,10},{10,1... | collective-permute-start | bytes 663560 | tf_op jit(solution)/shard_map/ppermute | solution.py:19
  10.6 8.9 %collective-permute-start = (f32[2,8,2048]{2,1,0:T(8,128)}, f32[2,8,2048]{2,1,0:T(8,128)S(1)}, u32[]{:S(2)}, u32[]{:S(2)}) collective-permute-start(f32[2,8,2048]{2,1,0:T(8,128)} %get-tuple-element.22), channel_id=1, source_target_pairs={{0,1},{1,2},{2,3},{3,4},{4,5},{5,6},{6,7},{7,8},{8,9},{9,10},{10,1... | collective-permute-start | bytes 393224 | tf_op jit(solution)/shard_map/ppermute | solution.py:19
  12.5 7.0 %collective-permute-start.1 = (f32[2,8,2048]{2,1,0:T(8,128)S(1)}, f32[2,8,2048]{2,1,0:T(8,128)S(1)}, u32[]{:S(2)}, u32[]{:S(2)}) collective-permute-start(f32[2,8,2048]{2,1,0:T(8,128)S(1)} %get-tuple-element.23), channel_id=1, source_target_pairs={{1,0},{2,1},{3,2},{4,3},{5,4},{6,5},{7,6},{8,7},{9,8},{10,9},{11,1... | collective-permute-start | bytes 393224 | tf_op jit(solution)/shard_map/ppermute | solution.py:19
  21.4 10.5 %collective-permute-start.6 = (f32[26,8,256]{2,1,0:T(8,128)S(1)}, f32[26,8,256]{2,1,0:T(8,128)S(1)}, u32[]{:S(2)}, u32[]{:S(2)}) collective-permute-start(f32[26,8,256]{2,1,0:T(8,128)S(1)} %pad_maximum_fusion.15), channel_id=1, source_target_pairs={{1,0},{2,1},{3,2},{4,3},{5,4},{6,5},{7,6},{0,7},{9,8},{10,9},{11,1... | collective-permute-start | bytes 638984 | tf_op jit(solution)/shard_map/ppermute | solution.py:65
  21.4 11.8 %collective-permute-start.5 = (f32[26,8,256]{2,1,0:T(8,128)S(1)}, f32[26,8,256]{2,1,0:T(8,128)S(1)}, u32[]{:S(2)}, u32[]{:S(2)}) collective-permute-start(f32[26,8,256]{2,1,0:T(8,128)S(1)} %pad_maximum_fusion.15), channel_id=1, source_target_pairs={{2,0},{3,1},{4,2},{5,3},{6,4},{7,5},{0,6},{1,7},{10,8},{11,9},{12,... | collective-permute-start | bytes 638984 | tf_op jit(solution)/shard_map/ppermute | solution.py:65
  28.7 11.4 %collective-permute-start.4 = (f32[26,8,256]{2,1,0:T(8,128)S(1)}, f32[26,8,256]{2,1,0:T(8,128)S(1)}, u32[]{:S(2)}, u32[]{:S(2)}) collective-permute-start(f32[26,8,256]{2,1,0:T(8,128)S(1)} %pad_maximum_fusion.15), channel_id=1, source_target_pairs={{3,0},{4,1},{5,2},{6,3},{7,4},{0,5},{1,6},{2,7},{11,8},{12,9},{13,... | collective-permute-start | bytes 638984 | tf_op jit(solution)/shard_map/ppermute | solution.py:65
  40.2 7.5 %collective-permute-start.7 = (f32[26,8,256]{2,1,0:T(8,128)S(1)}, f32[26,8,256]{2,1,0:T(8,128)S(1)}, u32[]{:S(2)}, u32[]{:S(2)}) collective-permute-start(f32[26,8,256]{2,1,0:T(8,128)S(1)} %select_select_fusion.2), channel_id=1, source_target_pairs={{4,0},{5,1},{6,2},{7,3},{0,4},{1,5},{2,6},{3,7},{12,8},{13,9},{14,... | collective-permute-start | bytes 638984 | tf_op jit(solution)/shard_map/ppermute | solution.py:65
  47.7 7.0 %collective-permute-start.16 = (f32[26,8,256]{2,1,0:T(8,128)S(1)}, f32[26,8,256]{2,1,0:T(8,128)S(1)}, u32[]{:S(2)}, u32[]{:S(2)}) collective-permute-start(f32[26,8,256]{2,1,0:T(8,128)S(1)} %broadcast_select_fusion), channel_id=1, source_target_pairs={{1,1},{2,3},{3,5},{4,7},{5,9},{6,11},{7,13},{8,15},{9,17},{10,19},... | collective-permute-start | bytes 638984 | tf_op jit(solution)/shard_map/ppermute | solution.py:157
  48.4 18.4 %collective-permute-start.15 = (f32[26,8,256]{2,1,0:T(8,128)S(1)}, f32[26,8,256]{2,1,0:T(8,128)S(1)}, u32[]{:S(2)}, u32[]{:S(2)}) collective-permute-start(f32[26,8,256]{2,1,0:T(8,128)S(1)} %broadcast_select_fusion), channel_id=1, source_target_pairs={{9,1},{10,3},{11,5},{12,7},{13,9},{14,11},{15,13},{16,15},{17,17},... | collective-permute-start | bytes 638984 | tf_op jit(solution)/shard_map/ppermute | solution.py:157
  49.7 17.8 %collective-permute-start.14 = (f32[26,8,256]{2,1,0:T(8,128)S(1)}, f32[26,8,256]{2,1,0:T(8,128)S(1)}, u32[]{:S(2)}, u32[]{:S(2)}) collective-permute-start(f32[26,8,256]{2,1,0:T(8,128)S(1)} %broadcast_select_fusion), channel_id=1, source_target_pairs={{17,1},{18,3},{19,5},{20,7},{21,9},{22,11},{23,13},{24,15},{25,17}... | collective-permute-start | bytes 638984 | tf_op jit(solution)/shard_map/ppermute | solution.py:157
  51.1 33.1 %collective-permute-start.10 = (f32[26,256]{1,0:T(8,128)S(1)}, f32[26,256]{1,0:T(8,128)S(1)}, u32[]{:S(2)}, u32[]{:S(2)}) collective-permute-start(f32[26,256]{1,0:T(8,128)S(1)} %bitcast.187), channel_id=1, source_target_pairs={{0,2},{1,4},{2,6},{3,8},{4,10},{5,12},{6,14},{7,16},{8,18},{9,20},... | collective-permute-start | bytes 79880 | tf_op jit(solution)/shard_map/ppermute | solution.py:157
  54.0 30.2 %collective-permute-start.9 = (f32[26,256]{1,0:T(8,128)S(1)}, f32[26,256]{1,0:T(8,128)S(1)}, u32[]{:S(2)}, u32[]{:S(2)}) collective-permute-start(f32[26,256]{1,0:T(8,128)S(1)} %bitcast.188), channel_id=1, source_target_pairs={{7,0},{8,2},{9,4},{10,6},{11,8},{12,10},{13,12},{14,14},{15,16},{1... | collective-permute-start | bytes 79880 | tf_op jit(solution)/shard_map/ppermute | solution.py:157
  54.7 13.5 %collective-permute-start.13 = (f32[26,8,256]{2,1,0:T(8,128)S(1)}, f32[26,8,256]{2,1,0:T(8,128)S(1)}, u32[]{:S(2)}, u32[]{:S(2)}) collective-permute-start(f32[26,8,256]{2,1,0:T(8,128)S(1)} %broadcast_select_fusion), channel_id=1, source_target_pairs={{0,0},{1,2},{2,4},{3,6},{4,8},{5,10},{6,12},{7,14},{8,16},{9,18},{... | collective-permute-start | bytes 638984 | tf_op jit(solution)/shard_map/ppermute | solution.py:157
  67.5 15.2 %collective-permute-start.11 = (f32[26,8,256]{2,1,0:T(8,128)S(1)}, f32[26,8,256]{2,1,0:T(8,128)S(1)}, u32[]{:S(2)}, u32[]{:S(2)}) collective-permute-start(f32[26,8,256]{2,1,0:T(8,128)S(1)} %broadcast_select_fusion), channel_id=1, source_target_pairs={{16,0},{17,2},{18,4},{19,6},{20,8},{21,10},{22,12},{23,14},{24,16}... | collective-permute-start | bytes 638984 | tf_op jit(solution)/shard_map/ppermute | solution.py:157
  68.2 16.0 %collective-permute-start.8 = (f32[26,256]{1,0:T(8,128)S(1)}, f32[26,256]{1,0:T(8,128)S(1)}, u32[]{:S(2)}, u32[]{:S(2)}) collective-permute-start(f32[26,256]{1,0:T(8,128)S(1)} %bitcast.189), channel_id=1, source_target_pairs={{15,0},{16,2},{17,4},{18,6},{19,8},{20,10},{21,12},{22,14},{23,16}... | collective-permute-start | bytes 79880 | tf_op jit(solution)/shard_map/ppermute | solution.py:157
  68.9 15.4 %collective-permute-start.17 = (f32[4,26,256]{2,0,1:T(4,128)S(1)}, f32[4,26,256]{2,0,1:T(4,128)S(1)}, u32[]{:S(2)}, u32[]{:S(2)}) collective-permute-start(f32[4,26,256]{2,0,1:T(4,128)S(1)} %slice_bitcast_fusion.13), channel_id=1, source_target_pairs={{1,0},{3,2},{5,4},{7,6},{9,8},{11,10},{13,12},{15,14},{17,16},{19,... | collective-permute-start | bytes 319496 | tf_op jit(solution)/shard_map/ppermute | solution.py:166
  102.7 19.8 %collective-permute-start.22 = (f32[4,24,256]{2,0,1:T(4,128)S(1)}, f32[4,24,256]{2,0,1:T(4,128)S(1)}, u32[]{:S(2)}, u32[]{:S(2)}) collective-permute-start(f32[4,24,256]{2,0,1:T(4,128)S(1)} %bitcast.183), channel_id=1, source_target_pairs={{1,8},{3,9},{5,10},{7,11},{9,12},{11,13},{13,14},{15,15},{17,16},{... | collective-permute-start | bytes 294920 | tf_op jit(solution)/shard_map/ppermute | solution.py:205
  108.8 13.7 %collective-permute-start.21 = (f32[4,24,256]{2,0,1:T(4,128)S(1)}, f32[4,24,256]{2,0,1:T(4,128)S(1)}, u32[]{:S(2)}, u32[]{:S(2)}) collective-permute-start(f32[4,24,256]{2,0,1:T(4,128)S(1)} %bitcast.184), channel_id=1, source_target_pairs={{0,8},{2,9},{4,10},{6,11},{8,12},{10,13},{12,14},{14,15},{16,16},{... | collective-permute-start | bytes 294920 | tf_op jit(solution)/shard_map/ppermute | solution.py:205
  109.5 14.0 %collective-permute-start.20 = (f32[4,24,256]{2,0,1:T(4,128)S(1)}, f32[4,24,256]{2,0,1:T(4,128)S(1)}, u32[]{:S(2)}, u32[]{:S(2)}) collective-permute-start(f32[4,24,256]{2,0,1:T(4,128)S(1)} %bitcast.185), channel_id=1, source_target_pairs={{1,9},{3,10},{5,11},{7,12},{9,13},{11,14},{13,15},{15,16},{17,17},... | collective-permute-start | bytes 294920 | tf_op jit(solution)/shard_map/ppermute | solution.py:205
  123.6 10.3 %collective-permute-start.24 = (f32[8,24,256]{2,0,1:T(8,128)S(1)}, f32[8,24,256]{2,0,1:T(8,128)S(1)}, u32[]{:S(2)}, u32[]{:S(2)}) collective-permute-start(f32[8,24,256]{2,0,1:T(8,128)S(1)} %fusion.53), channel_id=1, source_target_pairs={{0,8},{1,9},{2,10},{3,11},{4,12},{5,13},{6,14},{7,15},{8,16},{9,17... | collective-permute-start | bytes 589832 | tf_op jit(solution)/shard_map/ppermute | solution.py:19
  131.0 10.8 %collective-permute-start.23 = (f32[8,24,256]{2,0,1:T(8,128)S(1)}, f32[8,24,256]{2,0,1:T(8,128)S(1)}, u32[]{:S(2)}, u32[]{:S(2)}) collective-permute-start(f32[8,24,256]{2,0,1:T(8,128)S(1)} %fusion.53), channel_id=1, source_target_pairs={{8,0},{9,1},{10,2},{11,3},{12,4},{13,5},{14,6},{15,7},{16,8},{17,9... | collective-permute-start | bytes 589832 | tf_op jit(solution)/shard_map/ppermute | solution.py:19
  144.6 8.9 %collective-permute-start.26 = (f32[8,24,256]{2,0,1:T(8,128)S(1)}, f32[8,24,256]{2,0,1:T(8,128)S(1)}, u32[]{:S(2)}, u32[]{:S(2)}) collective-permute-start(f32[8,24,256]{2,0,1:T(8,128)S(1)} %select_select_fusion.4), channel_id=1, source_target_pairs={{6,0},{7,1},{0,2},{1,3},{2,4},{3,5},{4,6},{5,7},{14,8},{15,9},{8,1... | collective-permute-start | bytes 589832 | tf_op jit(solution)/shard_map/ppermute | solution.py:65
  145.4 10.3 %collective-permute-start.25 = (f32[8,24,256]{2,0,1:T(8,128)S(1)}, f32[8,24,256]{2,0,1:T(8,128)S(1)}, u32[]{:S(2)}, u32[]{:S(2)}) collective-permute-start(f32[8,24,256]{2,0,1:T(8,128)S(1)} %select_select_fusion.4), channel_id=1, source_target_pairs={{5,0},{6,1},{7,2},{0,3},{1,4},{2,5},{3,6},{4,7},{13,8},{14,9},{15,... | collective-permute-start | bytes 589832 | tf_op jit(solution)/shard_map/ppermute | solution.py:65
  (20 other events, 122.7 us)

commit v11 on v8

--- a/solution.py
+++ b/solution.py
@@ -199,7 +199,8 @@
     back_carry = carry
     back_shift = bit3.astype(jnp.int32) + back_carry - 1
     back = pick(back, [(-center, back_shift == 1), (center, back_shift == -1)], tiles)
-    back = rotate(back, [(-1, low == 1), (-2, low == 2), (-3, low == 3)], center, tiles)
+    back = rotate(back, [(-1, (low & 1) == 1)], center, tiles)
+    back = rotate(back, [(-2, (low & 2) == 2)], center, tiles)
     back = rotate(back, [(-4, bit2)], center, tiles)
     placed = jnp.transpose(back, (1, 0, 2)).reshape(3, levels, parent_rows, coarse_cols)
     band_row = parent_rows * tile_index + jnp.arange(parent_rows, dtype=jnp.int32) - row_offset

time: 164 us -> 162 us (0.988)
  starting transfers between devices: 71.7 us -> 67.5 us
  waiting for transfers between devices: 51.8 us -> 53.9 us
    ppermute x8 -> x7, starting transfers between devices: 17.8 us -> 13.6 us  [rotate(): out = jnp.where(predicate, lax.ppermute(value, 'tile', pairs), out)]
    ppermute x8 -> x7, waiting for transfers between devices: 27.6 us -> 29.8 us  [rotate(): out = jnp.where(predicate, lax.ppermute(value, 'tile', pairs), out)]
  transfers between devices with their start and end apart: 25 -> 24, of which waited for: 13 -> 12; matrix products, arithmetic and copies ran while one was open for 5% -> 5% of each run, Pallas kernels for 0% -> 0%
where the time goes in v11:
time: 162 us; the launch traced here: 161 us
  starting transfers between devices  67.5 us (42%)
  waiting for transfers between devices  53.9 us (33%)
  local copies, waits for them, and re-layouts  20.6 us (13%)
  other arithmetic  8.58 us (5%)
  between operations  7.93 us (5%)
  matrix products  2.45 us (2%)
    ppermute x7, waiting for transfers between devices, rotate(): out = jnp.where(predicate, lax.ppermute(value, 'tile', pairs), out)  29.8 us
    ppermute x8, starting transfers between devices, shift_from(): return lax.ppermute(value, axis, pairs)  28.4 us
    ppermute x1, starting transfers between devices, local(): lax.ppermute(first_rows, 'tile', [(2 * m + 1, 2 * m) for m in range(half)])  16.6 us
    ppermute x8, waiting for transfers between devices, shift_from(): return lax.ppermute(value, axis, pairs)  14.4 us
    ppermute x7, starting transfers between devices, rotate(): out = jnp.where(predicate, lax.ppermute(value, 'tile', pairs), out)  13.6 us
    unnamed x36, local copies, waits for them, and re-layouts  8.97 us
    ppermute x1, waiting for transfers between devices, local(): lax.ppermute(block, 'tile', [(m + center + 1, 2 * m + 1) for m in range(h...  8.64 us
    ppermute x4, starting transfers between devices, local(): lax.ppermute(means, 'tile', [(2 * m + k, m + center) for m in range(half...  5.05 us
  transfers between devices with their start and end apart: 24, of which 12 were waited for; matrix products, arithmetic and copies ran while one was open for 5% of the time, Pallas kernels for 0%

profile of v11, /device:TPU:1, one launch (start us, length us, event | category | flops | bytes accessed | tf_op | source)
XLA Modules:
  0.0 160.9 jit_solution(12764961375670525228)
XLA Ops:
  0.6 1.4 copy.70
  2.1 5.1 %collective-permute-start.3 = (f32[3,3,8,768]{3,2,0,1:T(8,128)S(1)}, f32[3,3,8,768]{3,2,0,1:T(8,128)S(1)}, u32[]{:S(2)}, u32[]{:S(2)}) collective-permute-start(f32[3,3,8,768]{3,2,0,1:T(8,128)S(1)} %get-tuple-element.24), channel_id=1, source_target_pairs={{1,0},{2,1},{3,2},{4,3},{5,4},{6,5},{7,6},{8,7},{9,8},{10,9},{11,1... | collective-permute-start | bytes 663560 | tf_op jit(solution)/shard_map/ppermute | solution.py:19
  7.2 1.9 %collective-permute-start.2 = (f32[3,3,8,768]{3,2,0,1:T(8,128)S(1)}, f32[3,3,8,768]{3,2,0,1:T(8,128)S(1)}, u32[]{:S(2)}, u32[]{:S(2)}) collective-permute-start(f32[3,3,8,768]{3,2,0,1:T(8,128)S(1)} %get-tuple-element.25), channel_id=1, source_target_pairs={{0,1},{1,2},{2,3},{3,4},{4,5},{5,6},{6,7},{7,8},{8,9},{9,10},{10,1... | collective-permute-start | bytes 663560 | tf_op jit(solution)/shard_map/ppermute | solution.py:19
  10.6 1.9 %collective-permute-start = (f32[2,8,2048]{2,1,0:T(8,128)}, f32[2,8,2048]{2,1,0:T(8,128)S(1)}, u32[]{:S(2)}, u32[]{:S(2)}) collective-permute-start(f32[2,8,2048]{2,1,0:T(8,128)} %get-tuple-element.22), channel_id=1, source_target_pairs={{0,1},{1,2},{2,3},{3,4},{4,5},{5,6},{6,7},{7,8},{8,9},{9,10},{10,1... | collective-permute-start | bytes 393224 | tf_op jit(solution)/shard_map/ppermute | solution.py:19
  12.5 2.4 %collective-permute-start.1 = (f32[2,8,2048]{2,1,0:T(8,128)S(1)}, f32[2,8,2048]{2,1,0:T(8,128)S(1)}, u32[]{:S(2)}, u32[]{:S(2)}) collective-permute-start(f32[2,8,2048]{2,1,0:T(8,128)S(1)} %get-tuple-element.23), channel_id=1, source_target_pairs={{1,0},{2,1},{3,2},{4,3},{5,4},{6,5},{7,6},{8,7},{9,8},{10,9},{11,1... | collective-permute-start | bytes 393224 | tf_op jit(solution)/shard_map/ppermute | solution.py:19
  21.2 7.5 %collective-permute-start.5 = (f32[26,8,256]{2,1,0:T(8,128)S(1)}, f32[26,8,256]{2,1,0:T(8,128)S(1)}, u32[]{:S(2)}, u32[]{:S(2)}) collective-permute-start(f32[26,8,256]{2,1,0:T(8,128)S(1)} %pad_maximum_fusion.15), channel_id=1, source_target_pairs={{2,0},{3,1},{4,2},{5,3},{6,4},{7,5},{0,6},{1,7},{10,8},{11,9},{12,... | collective-permute-start | bytes 638984 | tf_op jit(solution)/shard_map/ppermute | solution.py:65
  31.3 2.0 %collective-permute-done.5 = f32[26,8,256]{2,1,0:T(8,128)S(1)} collective-permute-done((f32[26,8,256]{2,1,0:T(8,128)S(1)}, f32[26,8,256]{2,1,0:T(8,128)S(1)}, u32[]{:S(2)}, u32[]{:S(2)}) %collective-permute-start.5) | collective-permute-done | bytes 213024 | tf_op jit(solution)/shard_map/ppermute | solution.py:65
  33.3 6.8 %collective-permute-done.4 = f32[26,8,256]{2,1,0:T(8,128)S(1)} collective-permute-done((f32[26,8,256]{2,1,0:T(8,128)S(1)}, f32[26,8,256]{2,1,0:T(8,128)S(1)}, u32[]{:S(2)}, u32[]{:S(2)}) %collective-permute-start.4) | collective-permute-done | bytes 213024 | tf_op jit(solution)/shard_map/ppermute | solution.py:65
  40.3 7.4 %collective-permute-done.7 = f32[26,8,256]{2,1,0:T(8,128)S(1)} collective-permute-done((f32[26,8,256]{2,1,0:T(8,128)S(1)}, f32[26,8,256]{2,1,0:T(8,128)S(1)}, u32[]{:S(2)}, u32[]{:S(2)}) %collective-permute-start.7) | collective-permute-done | bytes 213024 | tf_op jit(solution)/shard_map/ppermute | solution.py:65
  47.7 7.3 %collective-permute-start.9 = (f32[26,8,256]{2,1,0:T(8,128)S(1)}, f32[26,8,256]{2,1,0:T(8,128)S(1)}, u32[]{:S(2)}, u32[]{:S(2)}) collective-permute-start(f32[26,8,256]{2,1,0:T(8,128)S(1)} %broadcast_select_fusion), channel_id=1, source_target_pairs={{0,8},{1,9},{2,10},{3,11},{4,12},{5,13},{6,14},{7,15},{8,16},{9,17... | collective-permute-start | bytes 638984 | tf_op jit(solution)/shard_map/ppermute | solution.py:19
  57.8 4.7 %collective-permute-done.8 = f32[26,8,256]{2,1,0:T(8,128)S(1)} collective-permute-done((f32[26,8,256]{2,1,0:T(8,128)S(1)}, f32[26,8,256]{2,1,0:T(8,128)S(1)}, u32[]{:S(2)}, u32[]{:S(2)}) %collective-permute-start.8) | collective-permute-done | bytes 213024 | tf_op jit(solution)/shard_map/ppermute | solution.py:19
  66.6 8.6 %collective-permute-done.12 = f32[26,8,256]{2,1,0:T(8,128)S(1)} collective-permute-done((f32[26,8,256]{2,1,0:T(8,128)S(1)}, f32[26,8,256]{2,1,0:T(8,128)S(1)}, u32[]{:S(2)}, u32[]{:S(2)}) %collective-permute-start.12) | collective-permute-done | bytes 213024 | tf_op jit(solution)/shard_map/ppermute | solution.py:150
  75.3 16.6 %collective-permute-start.13 = (f32[4,26,256]{2,0,1:T(4,128)S(1)}, f32[4,26,256]{2,0,1:T(4,128)S(1)}, u32[]{:S(2)}, u32[]{:S(2)}) collective-permute-start(f32[4,26,256]{2,0,1:T(4,128)S(1)} %slice_bitcast_fusion.13), channel_id=1, source_target_pairs={{1,0},{3,2},{5,4},{7,6},{9,8},{11,10},{13,12},{15,14},{17,16},{19,... | collective-permute-start | bytes 319496 | tf_op jit(solution)/shard_map/ppermute | solution.py:153
  111.2 2.3 %collective-permute-start.16 = (f32[4,24,256]{2,0,1:T(4,128)S(1)}, f32[4,24,256]{2,0,1:T(4,128)S(1)}, u32[]{:S(2)}, u32[]{:S(2)}) collective-permute-start(f32[4,24,256]{2,0,1:T(4,128)S(1)} %bitcast.185), channel_id=1, source_target_pairs={{1,9},{3,10},{5,11},{7,12},{9,13},{11,14},{13,15},{15,16},{17,17},... | collective-permute-start | bytes 294920 | tf_op jit(solution)/shard_map/ppermute | solution.py:192
  115.3 7.1 %collective-permute-start.20 = (f32[8,24,256]{2,0,1:T(8,128)S(1)}, f32[8,24,256]{2,0,1:T(8,128)S(1)}, u32[]{:S(2)}, u32[]{:S(2)}) collective-permute-start(f32[8,24,256]{2,0,1:T(8,128)S(1)} %fusion.53), channel_id=1, source_target_pairs={{0,8},{1,9},{2,10},{3,11},{4,12},{5,13},{6,14},{7,15},{8,16},{9,17... | collective-permute-start | bytes 589832 | tf_op jit(solution)/shard_map/ppermute | solution.py:19
  125.1 7.6 %collective-permute-done.19 = f32[8,24,256]{2,0,1:T(8,128)S(1)} collective-permute-done((f32[8,24,256]{2,0,1:T(8,128)S(1)}, f32[8,24,256]{2,0,1:T(8,128)S(1)}, u32[]{:S(2)}, u32[]{:S(2)}) %collective-permute-start.19) | collective-permute-done | bytes 196640 | tf_op jit(solution)/shard_map/ppermute | solution.py:19
  132.7 4.0 %collective-permute-start.21 = (f32[8,24,256]{2,0,1:T(8,128)S(1)}, f32[8,24,256]{2,0,1:T(8,128)S(1)}, u32[]{:S(2)}, u32[]{:S(2)}) collective-permute-start(f32[8,24,256]{2,0,1:T(8,128)S(1)} %select_select_fusion.2), channel_id=1, source_target_pairs={{7,0},{0,1},{1,2},{2,3},{3,4},{4,5},{5,6},{6,7},{15,8},{8,9},{9,10... | collective-permute-start | bytes 589832 | tf_op jit(solution)/shard_map/ppermute | solution.py:65
  136.7 2.6 %collective-permute-done.21 = f32[8,24,256]{2,0,1:T(8,128)S(1)} collective-permute-done((f32[8,24,256]{2,0,1:T(8,128)S(1)}, f32[8,24,256]{2,0,1:T(8,128)S(1)}, u32[]{:S(2)}, u32[]{:S(2)}) %collective-permute-start.21) | collective-permute-done | bytes 196640 | tf_op jit(solution)/shard_map/ppermute | solution.py:65
  139.4 1.6 %collective-permute-start.22 = (f32[8,24,256]{2,0,1:T(8,128)S(1)}, f32[8,24,256]{2,0,1:T(8,128)S(1)}, u32[]{:S(2)}, u32[]{:S(2)}) collective-permute-start(f32[8,24,256]{2,0,1:T(8,128)S(1)} %broadcast_select_fusion.1), channel_id=1, source_target_pairs={{6,0},{7,1},{0,2},{1,3},{2,4},{3,5},{4,6},{5,7},{14,8},{15,9},{8,1... | collective-permute-start | bytes 589832 | tf_op jit(solution)/shard_map/ppermute | solution.py:65
  141.7 5.1 %collective-permute-done.22 = f32[8,24,256]{2,0,1:T(8,128)S(1)} collective-permute-done((f32[8,24,256]{2,0,1:T(8,128)S(1)}, f32[8,24,256]{2,0,1:T(8,128)S(1)}, u32[]{:S(2)}, u32[]{:S(2)}) %collective-permute-start.22) | collective-permute-done | bytes 196640 | tf_op jit(solution)/shard_map/ppermute | solution.py:65
  147.2 1.8 %copy.44 = f32[3,8,1,12,768]{4,2,3,1,0:T(1,128)} copy(f32[3,8,1,12,768]{4,1,3,2,0:T(8,128)S(1)} %slice_bitcast_fusion) | data formatting | bytes 1769472
  149.0 5.9 %collective-permute-done.23 = f32[8,24,256]{2,0,1:T(8,128)S(1)} collective-permute-done((f32[8,24,256]{2,0,1:T(8,128)S(1)}, f32[8,24,256]{2,0,1:T(8,128)S(1)}, u32[]{:S(2)}, u32[]{:S(2)}) %collective-permute-start.23) | collective-permute-done | bytes 196640 | tf_op jit(solution)/shard_map/ppermute | solution.py:65
  155.1 3.8 %dynamic_update_slice.3 = f32[3,8,8,2048]{3,1,2,0:T(8,128)S(1)} dynamic-update-slice(f32[3,8,8,2048]{3,1,2,0:T(8,128)S(1)} %copy-done.1, f32[3,8,8,256]{3,1,2,0:T(8,128)S(1)} %copy_select_fusion, s32[]{:T(128)} %constant.93.clone.1, s32[]{:T(128)} %constant.93.clone.1, s32[]{:T(128)} %constant.93.clone.1, s32[]{:T(128)S(6)} %select_n.170) | dynamic-update-slice | bytes 393220 | tf_op jit(solution)/shard_map/dynamic_update_slice | solution.py:210
  158.9 2.1 %copy.43 = f32[3,8,8,2048]{3,2,1,0:T(8,128)} copy(f32[3,8,8,2048]{3,1,2,0:T(8,128)S(1)} %dynamic_update_slice.3) | data formatting | bytes 3145728
  (142 shorter events, 35.3 us)
Async XLA Ops:
  2.1 19.0 %collective-permute-start.3 = (f32[3,3,8,768]{3,2,0,1:T(8,128)S(1)}, f32[3,3,8,768]{3,2,0,1:T(8,128)S(1)}, u32[]{:S(2)}, u32[]{:S(2)}) collective-permute-start(f32[3,3,8,768]{3,2,0,1:T(8,128)S(1)} %get-tuple-element.24), channel_id=1, source_target_pairs={{1,0},{2,1},{3,2},{4,3},{5,4},{6,5},{7,6},{8,7},{9,8},{10,9},{11,1... | collective-permute-start | bytes 663560 | tf_op jit(solution)/shard_map/ppermute | solution.py:19
  7.2 13.9 %collective-permute-start.2 = (f32[3,3,8,768]{3,2,0,1:T(8,128)S(1)}, f32[3,3,8,768]{3,2,0,1:T(8,128)S(1)}, u32[]{:S(2)}, u32[]{:S(2)}) collective-permute-start(f32[3,3,8,768]{3,2,0,1:T(8,128)S(1)} %get-tuple-element.25), channel_id=1, source_target_pairs={{0,1},{1,2},{2,3},{3,4},{4,5},{5,6},{6,7},{7,8},{8,9},{9,10},{10,1... | collective-permute-start | bytes 663560 | tf_op jit(solution)/shard_map/ppermute | solution.py:19
  10.6 8.6 %collective-permute-start = (f32[2,8,2048]{2,1,0:T(8,128)}, f32[2,8,2048]{2,1,0:T(8,128)S(1)}, u32[]{:S(2)}, u32[]{:S(2)}) collective-permute-start(f32[2,8,2048]{2,1,0:T(8,128)} %get-tuple-element.22), channel_id=1, source_target_pairs={{0,1},{1,2},{2,3},{3,4},{4,5},{5,6},{6,7},{7,8},{8,9},{9,10},{10,1... | collective-permute-start | bytes 393224 | tf_op jit(solution)/shard_map/ppermute | solution.py:19
  12.5 6.7 %collective-permute-start.1 = (f32[2,8,2048]{2,1,0:T(8,128)S(1)}, f32[2,8,2048]{2,1,0:T(8,128)S(1)}, u32[]{:S(2)}, u32[]{:S(2)}) collective-permute-start(f32[2,8,2048]{2,1,0:T(8,128)S(1)} %get-tuple-element.23), channel_id=1, source_target_pairs={{1,0},{2,1},{3,2},{4,3},{5,4},{6,5},{7,6},{8,7},{9,8},{10,9},{11,1... | collective-permute-start | bytes 393224 | tf_op jit(solution)/shard_map/ppermute | solution.py:19
  21.2 10.1 %collective-permute-start.6 = (f32[26,8,256]{2,1,0:T(8,128)S(1)}, f32[26,8,256]{2,1,0:T(8,128)S(1)}, u32[]{:S(2)}, u32[]{:S(2)}) collective-permute-start(f32[26,8,256]{2,1,0:T(8,128)S(1)} %pad_maximum_fusion.15), channel_id=1, source_target_pairs={{1,0},{2,1},{3,2},{4,3},{5,4},{6,5},{7,6},{0,7},{9,8},{10,9},{11,1... | collective-permute-start | bytes 638984 | tf_op jit(solution)/shard_map/ppermute | solution.py:65
  21.2 12.1 %collective-permute-start.5 = (f32[26,8,256]{2,1,0:T(8,128)S(1)}, f32[26,8,256]{2,1,0:T(8,128)S(1)}, u32[]{:S(2)}, u32[]{:S(2)}) collective-permute-start(f32[26,8,256]{2,1,0:T(8,128)S(1)} %pad_maximum_fusion.15), channel_id=1, source_target_pairs={{2,0},{3,1},{4,2},{5,3},{6,4},{7,5},{0,6},{1,7},{10,8},{11,9},{12,... | collective-permute-start | bytes 638984 | tf_op jit(solution)/shard_map/ppermute | solution.py:65
  28.7 11.4 %collective-permute-start.4 = (f32[26,8,256]{2,1,0:T(8,128)S(1)}, f32[26,8,256]{2,1,0:T(8,128)S(1)}, u32[]{:S(2)}, u32[]{:S(2)}) collective-permute-start(f32[26,8,256]{2,1,0:T(8,128)S(1)} %pad_maximum_fusion.15), channel_id=1, source_target_pairs={{3,0},{4,1},{5,2},{6,3},{7,4},{0,5},{1,6},{2,7},{11,8},{12,9},{13,... | collective-permute-start | bytes 638984 | tf_op jit(solution)/shard_map/ppermute | solution.py:65
  40.2 7.5 %collective-permute-start.7 = (f32[26,8,256]{2,1,0:T(8,128)S(1)}, f32[26,8,256]{2,1,0:T(8,128)S(1)}, u32[]{:S(2)}, u32[]{:S(2)}) collective-permute-start(f32[26,8,256]{2,1,0:T(8,128)S(1)} %select_select_fusion.1), channel_id=1, source_target_pairs={{4,0},{5,1},{6,2},{7,3},{0,4},{1,5},{2,6},{3,7},{12,8},{13,9},{14,... | collective-permute-start | bytes 638984 | tf_op jit(solution)/shard_map/ppermute | solution.py:65
  47.7 10.1 %collective-permute-start.9 = (f32[26,8,256]{2,1,0:T(8,128)S(1)}, f32[26,8,256]{2,1,0:T(8,128)S(1)}, u32[]{:S(2)}, u32[]{:S(2)}) collective-permute-start(f32[26,8,256]{2,1,0:T(8,128)S(1)} %broadcast_select_fusion), channel_id=1, source_target_pairs={{0,8},{1,9},{2,10},{3,11},{4,12},{5,13},{6,14},{7,15},{8,16},{9,17... | collective-permute-start | bytes 638984 | tf_op jit(solution)/shard_map/ppermute | solution.py:19
  55.1 7.5 %collective-permute-start.8 = (f32[26,8,256]{2,1,0:T(8,128)S(1)}, f32[26,8,256]{2,1,0:T(8,128)S(1)}, u32[]{:S(2)}, u32[]{:S(2)}) collective-permute-start(f32[26,8,256]{2,1,0:T(8,128)S(1)} %broadcast_select_fusion), channel_id=1, source_target_pairs={{8,0},{9,1},{10,2},{11,3},{12,4},{13,5},{14,6},{15,7},{16,8},{17,9... | collective-permute-start | bytes 638984 | tf_op jit(solution)/shard_map/ppermute | solution.py:19
  62.6 12.7 %collective-permute-start.12 = (f32[26,8,256]{2,1,0:T(8,128)S(1)}, f32[26,8,256]{2,1,0:T(8,128)S(1)}, u32[]{:S(2)}, u32[]{:S(2)}) collective-permute-start(f32[26,8,256]{2,1,0:T(8,128)S(1)} %select_select_fusion), channel_id=1, source_target_pairs={{9,1},{10,3},{11,5},{12,7},{13,9},{14,11},{15,13},{16,15},{17,17},... | collective-permute-start | bytes 638984 | tf_op jit(solution)/shard_map/ppermute | solution.py:150
  63.9 1.4 collective-permute-start.11
  64.6 27.9 %collective-permute-start.10 = (f32[26,256]{1,0:T(8,128)S(1)}, f32[26,256]{1,0:T(8,128)S(1)}, u32[]{:S(2)}, u32[]{:S(2)}) collective-permute-start(f32[26,256]{1,0:T(8,128)S(1)} %bitcast.187), channel_id=1, source_target_pairs={{7,0},{8,2},{9,4},{10,6},{11,8},{12,10},{13,12},{14,14},{15,16},{1... | collective-permute-start | bytes 79880 | tf_op jit(solution)/shard_map/ppermute | solution.py:147
  65.3 27.3 %collective-permute-start.14 = (f32[26,8,256]{2,1,0:T(8,128)S(1)}, f32[26,8,256]{2,1,0:T(8,128)S(1)}, u32[]{:S(2)}, u32[]{:S(2)}) collective-permute-start(f32[26,8,256]{2,1,0:T(8,128)S(1)} %collective-permute-done.11), channel_id=1, source_target_pairs={{0,1},{2,3},{4,5},{6,7},{8,9},{10,11},{12,13},{14,15},{16,17},{18,... | collective-permute-start | bytes 638984 | tf_op jit(solution)/shard_map/ppermute | solution.py:151
  75.3 17.3 %collective-permute-start.13 = (f32[4,26,256]{2,0,1:T(4,128)S(1)}, f32[4,26,256]{2,0,1:T(4,128)S(1)}, u32[]{:S(2)}, u32[]{:S(2)}) collective-permute-start(f32[4,26,256]{2,0,1:T(4,128)S(1)} %slice_bitcast_fusion.13), channel_id=1, source_target_pairs={{1,0},{3,2},{5,4},{7,6},{9,8},{11,10},{13,12},{15,14},{17,16},{19,... | collective-permute-start | bytes 319496 | tf_op jit(solution)/shard_map/ppermute | solution.py:153
  109.1 5.1 %collective-permute-start.18 = (f32[4,24,256]{2,0,1:T(4,128)S(1)}, f32[4,24,256]{2,0,1:T(4,128)S(1)}, u32[]{:S(2)}, u32[]{:S(2)}) collective-permute-start(f32[4,24,256]{2,0,1:T(4,128)S(1)} %bitcast.183), channel_id=1, source_target_pairs={{1,8},{3,9},{5,10},{7,11},{9,12},{11,13},{13,14},{15,15},{17,16},{... | collective-permute-start | bytes 294920 | tf_op jit(solution)/shard_map/ppermute | solution.py:192
  110.5 3.7 %collective-permute-start.17 = (f32[4,24,256]{2,0,1:T(4,128)S(1)}, f32[4,24,256]{2,0,1:T(4,128)S(1)}, u32[]{:S(2)}, u32[]{:S(2)}) collective-permute-start(f32[4,24,256]{2,0,1:T(4,128)S(1)} %bitcast.184), channel_id=1, source_target_pairs={{0,8},{2,9},{4,10},{6,11},{8,12},{10,13},{12,14},{14,15},{16,16},{... | collective-permute-start | bytes 294920 | tf_op jit(solution)/shard_map/ppermute | solution.py:192
  111.2 3.9 %collective-permute-start.16 = (f32[4,24,256]{2,0,1:T(4,128)S(1)}, f32[4,24,256]{2,0,1:T(4,128)S(1)}, u32[]{:S(2)}, u32[]{:S(2)}) collective-permute-start(f32[4,24,256]{2,0,1:T(4,128)S(1)} %bitcast.185), channel_id=1, source_target_pairs={{1,9},{3,10},{5,11},{7,12},{9,13},{11,14},{13,15},{15,16},{17,17},... | collective-permute-start | bytes 294920 | tf_op jit(solution)/shard_map/ppermute | solution.py:192
  113.5 1.6 %collective-permute-start.15 = (f32[4,24,256]{2,0,1:T(4,128)S(1)}, f32[4,24,256]{2,0,1:T(4,128)S(1)}, u32[]{:S(2)}, u32[]{:S(2)}) collective-permute-start(f32[4,24,256]{2,0,1:T(4,128)S(1)} %bitcast.186), channel_id=1, source_target_pairs={{0,9},{2,10},{4,11},{6,12},{8,13},{10,14},{12,15},{14,16},{16,17},... | collective-permute-start | bytes 294920 | tf_op jit(solution)/shard_map/ppermute | solution.py:192
  115.3 9.7 %collective-permute-start.20 = (f32[8,24,256]{2,0,1:T(8,128)S(1)}, f32[8,24,256]{2,0,1:T(8,128)S(1)}, u32[]{:S(2)}, u32[]{:S(2)}) collective-permute-start(f32[8,24,256]{2,0,1:T(8,128)S(1)} %fusion.53), channel_id=1, source_target_pairs={{0,8},{1,9},{2,10},{3,11},{4,12},{5,13},{6,14},{7,15},{8,16},{9,17... | collective-permute-start | bytes 589832 | tf_op jit(solution)/shard_map/ppermute | solution.py:19
  122.5 10.2 %collective-permute-start.19 = (f32[8,24,256]{2,0,1:T(8,128)S(1)}, f32[8,24,256]{2,0,1:T(8,128)S(1)}, u32[]{:S(2)}, u32[]{:S(2)}) collective-permute-start(f32[8,24,256]{2,0,1:T(8,128)S(1)} %fusion.53), channel_id=1, source_target_pairs={{8,0},{9,1},{10,2},{11,3},{12,4},{13,5},{14,6},{15,7},{16,8},{17,9... | collective-permute-start | bytes 589832 | tf_op jit(solution)/shard_map/ppermute | solution.py:19
  132.7 6.7 %collective-permute-start.21 = (f32[8,24,256]{2,0,1:T(8,128)S(1)}, f32[8,24,256]{2,0,1:T(8,128)S(1)}, u32[]{:S(2)}, u32[]{:S(2)}) collective-permute-start(f32[8,24,256]{2,0,1:T(8,128)S(1)} %select_select_fusion.2), channel_id=1, source_target_pairs={{7,0},{0,1},{1,2},{2,3},{3,4},{4,5},{5,6},{6,7},{15,8},{8,9},{9,10... | collective-permute-start | bytes 589832 | tf_op jit(solution)/shard_map/ppermute | solution.py:65
  139.4 7.4 %collective-permute-start.22 = (f32[8,24,256]{2,0,1:T(8,128)S(1)}, f32[8,24,256]{2,0,1:T(8,128)S(1)}, u32[]{:S(2)}, u32[]{:S(2)}) collective-permute-start(f32[8,24,256]{2,0,1:T(8,128)S(1)} %broadcast_select_fusion.1), channel_id=1, source_target_pairs={{6,0},{7,1},{0,2},{1,3},{2,4},{3,5},{4,6},{5,7},{14,8},{15,9},{8,1... | collective-permute-start | bytes 589832 | tf_op jit(solution)/shard_map/ppermute | solution.py:65
  146.8 8.1 %collective-permute-start.23 = (f32[8,24,256]{2,0,1:T(8,128)S(1)}, f32[8,24,256]{2,0,1:T(8,128)S(1)}, u32[]{:S(2)}, u32[]{:S(2)}) collective-permute-start(f32[8,24,256]{2,0,1:T(8,128)S(1)} %broadcast_select_fusion.2), channel_id=1, source_target_pairs={{4,0},{5,1},{6,2},{7,3},{0,4},{1,5},{2,6},{3,7},{12,8},{13,9},{14,... | collective-permute-start | bytes 589832 | tf_op jit(solution)/shard_map/ppermute | solution.py:65
  (15 other events, 78.8 us)

commit v12 on v11

--- a/solution.py
+++ b/solution.py
@@ -137,7 +137,8 @@
     bit3 = ((q >> 3) & 1) == 1
     low3 = q & (center - 1)
     slab_pos = tile_index % center
-    block = rotate(block, [(1, low == 1), (2, low == 2), (3, low == 3)], center, tiles)
+    block = rotate(block, [(1, (low & 1) == 1)], center, tiles)
+    block = rotate(block, [(2, (low & 2) == 2)], center, tiles)
     block = rotate(block, [(4, bit2)], center, tiles)
     carry = (slab_pos + low3 >= center).astype(jnp.int32)
     slab_shift = bit3.astype(jnp.int32) + carry - 1

time: 162 us -> 165 us (1.019)
  the two profiles are of different devices: /device:TPU:1 before, /device:TPU:8 now
where the time goes in v12:
time: 165 us; the launch traced here: 164 us
  waiting for transfers between devices  74.5 us (45%)
  starting transfers between devices  49.7 us (30%)
  local copies, waits for them, and re-layouts  20.7 us (13%)
  other arithmetic  8.53 us (5%)
  between operations  7.87 us (5%)
  matrix products  2.44 us (1%)
    ppermute x6, waiting for transfers between devices, rotate(): out = jnp.where(predicate, lax.ppermute(value, 'tile', pairs), out)  32.9 us
    ppermute x8, starting transfers between devices, shift_from(): return lax.ppermute(value, axis, pairs)  27.8 us
    ppermute x8, waiting for transfers between devices, shift_from(): return lax.ppermute(value, axis, pairs)  27.6 us
    ppermute x1, waiting for transfers between devices, local(): lax.ppermute(block, 'tile', [(m + center, 2 * m) for m in range(half)])  10.9 us
    ppermute x4, starting transfers between devices, local(): lax.ppermute(means, 'tile', [(2 * m + k, m + center) for m in range(half...  9.5 us
    unnamed x36, local copies, waits for them, and re-layouts  9.06 us
    ppermute x6, starting transfers between devices, rotate(): out = jnp.where(predicate, lax.ppermute(value, 'tile', pairs), out)  6.32 us
    dynamic_update_slice x1, local copies, waits for them, and re-layouts, local(): lax.dynamic_update_slice_in_dim(advanced, merged, col_offset, axis=3)  3.8 us
  transfers between devices with their start and end apart: 23, of which 13 were waited for; matrix products, arithmetic and copies ran while one was open for 5% of the time, Pallas kernels for 0%

profile of v12, /device:TPU:8, one launch (start us, length us, event | category | flops | bytes accessed | tf_op | source)
XLA Modules:
  0.0 163.8 jit_solution(8870701323524116490)
XLA Ops:
  3.4 3.0 %collective-permute-start.2 = (f32[3,3,8,768]{3,2,0,1:T(8,128)S(1)}, f32[3,3,8,768]{3,2,0,1:T(8,128)S(1)}, u32[]{:S(2)}, u32[]{:S(2)}) collective-permute-start(f32[3,3,8,768]{3,2,0,1:T(8,128)S(1)} %get-tuple-element.25), channel_id=1, source_target_pairs={{0,1},{1,2},{2,3},{3,4},{4,5},{5,6},{6,7},{7,8},{8,9},{9,10},{10,1... | collective-permute-start | bytes 663560 | tf_op jit(solution)/shard_map/ppermute | solution.py:19
  7.9 3.0 %collective-permute-start = (f32[2,8,2048]{2,1,0:T(8,128)}, f32[2,8,2048]{2,1,0:T(8,128)S(1)}, u32[]{:S(2)}, u32[]{:S(2)}) collective-permute-start(f32[2,8,2048]{2,1,0:T(8,128)} %get-tuple-element.22), channel_id=1, source_target_pairs={{0,1},{1,2},{2,3},{3,4},{4,5},{5,6},{6,7},{7,8},{8,9},{9,10},{10,1... | collective-permute-start | bytes 393224 | tf_op jit(solution)/shard_map/ppermute | solution.py:19
  10.9 8.2 %collective-permute-start.1 = (f32[2,8,2048]{2,1,0:T(8,128)S(1)}, f32[2,8,2048]{2,1,0:T(8,128)S(1)}, u32[]{:S(2)}, u32[]{:S(2)}) collective-permute-start(f32[2,8,2048]{2,1,0:T(8,128)S(1)} %get-tuple-element.23), channel_id=1, source_target_pairs={{1,0},{2,1},{3,2},{4,3},{5,4},{6,5},{7,6},{8,7},{9,8},{10,9},{11,1... | collective-permute-start | bytes 393224 | tf_op jit(solution)/shard_map/ppermute | solution.py:19
  25.3 2.2 %collective-permute-start.4 = (f32[26,8,256]{2,1,0:T(8,128)S(1)}, f32[26,8,256]{2,1,0:T(8,128)S(1)}, u32[]{:S(2)}, u32[]{:S(2)}) collective-permute-start(f32[26,8,256]{2,1,0:T(8,128)S(1)} %pad_maximum_fusion.15), channel_id=1, source_target_pairs={{1,0},{2,1},{3,2},{4,3},{5,4},{6,5},{7,6},{0,7},{9,8},{10,9},{11,1... | collective-permute-start | bytes 638984 | tf_op jit(solution)/shard_map/ppermute | solution.py:65
  31.1 5.8 %collective-permute-done.5 = f32[26,8,256]{2,1,0:T(8,128)S(1)} collective-permute-done((f32[26,8,256]{2,1,0:T(8,128)S(1)}, f32[26,8,256]{2,1,0:T(8,128)S(1)}, u32[]{:S(2)}, u32[]{:S(2)}) %collective-permute-start.5) | collective-permute-done | bytes 213024 | tf_op jit(solution)/shard_map/ppermute | solution.py:65
  37.0 8.8 %collective-permute-done.6 = f32[26,8,256]{2,1,0:T(8,128)S(1)} collective-permute-done((f32[26,8,256]{2,1,0:T(8,128)S(1)}, f32[26,8,256]{2,1,0:T(8,128)S(1)}, u32[]{:S(2)}, u32[]{:S(2)}) %collective-permute-start.6) | collective-permute-done | bytes 213024 | tf_op jit(solution)/shard_map/ppermute | solution.py:65
  45.9 7.5 %collective-permute-start.8 = (f32[26,8,256]{2,1,0:T(8,128)S(1)}, f32[26,8,256]{2,1,0:T(8,128)S(1)}, u32[]{:S(2)}, u32[]{:S(2)}) collective-permute-start(f32[26,8,256]{2,1,0:T(8,128)S(1)} %broadcast_select_fusion.2), channel_id=1, source_target_pairs={{0,8},{1,9},{2,10},{3,11},{4,12},{5,13},{6,14},{7,15},{8,16},{9,17... | collective-permute-start | bytes 638984 | tf_op jit(solution)/shard_map/ppermute | solution.py:19
  55.3 2.1 %collective-permute-done.8 = f32[26,8,256]{2,1,0:T(8,128)S(1)} collective-permute-done((f32[26,8,256]{2,1,0:T(8,128)S(1)}, f32[26,8,256]{2,1,0:T(8,128)S(1)}, u32[]{:S(2)}, u32[]{:S(2)}) %collective-permute-start.8) | collective-permute-done | bytes 213024 | tf_op jit(solution)/shard_map/ppermute | solution.py:19
  57.4 10.4 %collective-permute-done.7 = f32[26,8,256]{2,1,0:T(8,128)S(1)} collective-permute-done((f32[26,8,256]{2,1,0:T(8,128)S(1)}, f32[26,8,256]{2,1,0:T(8,128)S(1)}, u32[]{:S(2)}, u32[]{:S(2)}) %collective-permute-start.7) | collective-permute-done | bytes 213024 | tf_op jit(solution)/shard_map/ppermute | solution.py:19
  71.2 10.9 %collective-permute-done.10 = f32[26,8,256]{2,1,0:T(8,128)S(1)} collective-permute-done((f32[26,8,256]{2,1,0:T(8,128)S(1)}, f32[26,8,256]{2,1,0:T(8,128)S(1)}, u32[]{:S(2)}, u32[]{:S(2)}) %collective-permute-start.10) | collective-permute-done | bytes 213024 | tf_op jit(solution)/shard_map/ppermute | solution.py:147
  83.4 1.5 collective-permute-start.12
  103.9 4.7 %collective-permute-start.16 = (f32[4,24,256]{2,0,1:T(4,128)S(1)}, f32[4,24,256]{2,0,1:T(4,128)S(1)}, u32[]{:S(2)}, u32[]{:S(2)}) collective-permute-start(f32[4,24,256]{2,0,1:T(4,128)S(1)} %bitcast.184), channel_id=1, source_target_pairs={{0,8},{2,9},{4,10},{6,11},{8,12},{10,13},{12,14},{14,15},{16,16},{... | collective-permute-start | bytes 294920 | tf_op jit(solution)/shard_map/ppermute | solution.py:193
  109.2 3.5 %collective-permute-start.14 = (f32[4,24,256]{2,0,1:T(4,128)S(1)}, f32[4,24,256]{2,0,1:T(4,128)S(1)}, u32[]{:S(2)}, u32[]{:S(2)}) collective-permute-start(f32[4,24,256]{2,0,1:T(4,128)S(1)} %bitcast.186), channel_id=1, source_target_pairs={{0,9},{2,10},{4,11},{6,12},{8,13},{10,14},{12,15},{14,16},{16,17},... | collective-permute-start | bytes 294920 | tf_op jit(solution)/shard_map/ppermute | solution.py:193
  112.8 2.2 %collective-permute-done.14 = f32[4,24,256]{2,0,1:T(4,128)S(1)} collective-permute-done((f32[4,24,256]{2,0,1:T(4,128)S(1)}, f32[4,24,256]{2,0,1:T(4,128)S(1)}, u32[]{:S(2)}, u32[]{:S(2)}) %collective-permute-start.14) | collective-permute-done | bytes 98336 | tf_op jit(solution)/shard_map/ppermute | solution.py:193
  115.1 2.2 %collective-permute-start.19 = (f32[8,24,256]{2,0,1:T(8,128)S(1)}, f32[8,24,256]{2,0,1:T(8,128)S(1)}, u32[]{:S(2)}, u32[]{:S(2)}) collective-permute-start(f32[8,24,256]{2,0,1:T(8,128)S(1)} %fusion.53), channel_id=1, source_target_pairs={{0,8},{1,9},{2,10},{3,11},{4,12},{5,13},{6,14},{7,15},{8,16},{9,17... | collective-permute-start | bytes 589832 | tf_op jit(solution)/shard_map/ppermute | solution.py:19
  118.6 2.1 %collective-permute-done.19 = f32[8,24,256]{2,0,1:T(8,128)S(1)} collective-permute-done((f32[8,24,256]{2,0,1:T(8,128)S(1)}, f32[8,24,256]{2,0,1:T(8,128)S(1)}, u32[]{:S(2)}, u32[]{:S(2)}) %collective-permute-start.19) | collective-permute-done | bytes 196640 | tf_op jit(solution)/shard_map/ppermute | solution.py:19
  120.7 13.0 %collective-permute-done.18 = f32[8,24,256]{2,0,1:T(8,128)S(1)} collective-permute-done((f32[8,24,256]{2,0,1:T(8,128)S(1)}, f32[8,24,256]{2,0,1:T(8,128)S(1)}, u32[]{:S(2)}, u32[]{:S(2)}) %collective-permute-start.18) | collective-permute-done | bytes 196640 | tf_op jit(solution)/shard_map/ppermute | solution.py:19
  133.8 6.3 %collective-permute-done.20 = f32[8,24,256]{2,0,1:T(8,128)S(1)} collective-permute-done((f32[8,24,256]{2,0,1:T(8,128)S(1)}, f32[8,24,256]{2,0,1:T(8,128)S(1)}, u32[]{:S(2)}, u32[]{:S(2)}) %collective-permute-start.20) | collective-permute-done | bytes 196640 | tf_op jit(solution)/shard_map/ppermute | solution.py:65
  140.1 3.3 %collective-permute-start.21 = (f32[8,24,256]{2,0,1:T(8,128)S(1)}, f32[8,24,256]{2,0,1:T(8,128)S(1)}, u32[]{:S(2)}, u32[]{:S(2)}) collective-permute-start(f32[8,24,256]{2,0,1:T(8,128)S(1)} %broadcast_select_fusion.3), channel_id=1, source_target_pairs={{6,0},{7,1},{0,2},{1,3},{2,4},{3,5},{4,6},{5,7},{14,8},{15,9},{8,1... | collective-permute-start | bytes 589832 | tf_op jit(solution)/shard_map/ppermute | solution.py:65
  144.1 5.0 %collective-permute-done.21 = f32[8,24,256]{2,0,1:T(8,128)S(1)} collective-permute-done((f32[8,24,256]{2,0,1:T(8,128)S(1)}, f32[8,24,256]{2,0,1:T(8,128)S(1)}, u32[]{:S(2)}, u32[]{:S(2)}) %collective-permute-start.21) | collective-permute-done | bytes 196640 | tf_op jit(solution)/shard_map/ppermute | solution.py:65
  149.8 1.8 %copy.44 = f32[3,8,1,12,768]{4,2,3,1,0:T(1,128)} copy(f32[3,8,1,12,768]{4,1,3,2,0:T(8,128)S(1)} %slice_bitcast_fusion) | data formatting | bytes 1769472
  151.6 6.1 %collective-permute-done.22 = f32[8,24,256]{2,0,1:T(8,128)S(1)} collective-permute-done((f32[8,24,256]{2,0,1:T(8,128)S(1)}, f32[8,24,256]{2,0,1:T(8,128)S(1)}, u32[]{:S(2)}, u32[]{:S(2)}) %collective-permute-start.22) | collective-permute-done | bytes 196640 | tf_op jit(solution)/shard_map/ppermute | solution.py:65
  157.9 3.8 %dynamic_update_slice.3 = f32[3,8,8,2048]{3,1,2,0:T(8,128)S(1)} dynamic-update-slice(f32[3,8,8,2048]{3,1,2,0:T(8,128)S(1)} %copy-done.1, f32[3,8,8,256]{3,1,2,0:T(8,128)S(1)} %copy_select_fusion, s32[]{:T(128)} %constant.93.clone.1, s32[]{:T(128)} %constant.93.clone.1, s32[]{:T(128)} %constant.93.clone.1, s32[]{:T(128)S(6)} %select_n.165) | dynamic-update-slice | bytes 393220 | tf_op jit(solution)/shard_map/dynamic_update_slice | solution.py:211
  161.7 2.1 %copy.43 = f32[3,8,8,2048]{3,2,1,0:T(8,128)} copy(f32[3,8,8,2048]{3,1,2,0:T(8,128)S(1)} %dynamic_update_slice.3) | data formatting | bytes 3145728
  (141 shorter events, 36.4 us)
Async XLA Ops:
  2.1 23.2 %collective-permute-start.3 = (f32[3,3,8,768]{3,2,0,1:T(8,128)S(1)}, f32[3,3,8,768]{3,2,0,1:T(8,128)S(1)}, u32[]{:S(2)}, u32[]{:S(2)}) collective-permute-start(f32[3,3,8,768]{3,2,0,1:T(8,128)S(1)} %get-tuple-element.24), channel_id=1, source_target_pairs={{1,0},{2,1},{3,2},{4,3},{5,4},{6,5},{7,6},{8,7},{9,8},{10,9},{11,1... | collective-permute-start | bytes 663560 | tf_op jit(solution)/shard_map/ppermute | solution.py:19
  3.4 21.9 %collective-permute-start.2 = (f32[3,3,8,768]{3,2,0,1:T(8,128)S(1)}, f32[3,3,8,768]{3,2,0,1:T(8,128)S(1)}, u32[]{:S(2)}, u32[]{:S(2)}) collective-permute-start(f32[3,3,8,768]{3,2,0,1:T(8,128)S(1)} %get-tuple-element.25), channel_id=1, source_target_pairs={{0,1},{1,2},{2,3},{3,4},{4,5},{5,6},{6,7},{7,8},{8,9},{9,10},{10,1... | collective-permute-start | bytes 663560 | tf_op jit(solution)/shard_map/ppermute | solution.py:19
  7.2 15.1 %copy-start.9 = (s32[8,2048]{1,0:T(8,128)S(1)}, s32[8,2048]{1,0:T(8,128)}, u32[]{:S(2)}) copy-start(s32[8,2048]{1,0:T(8,128)} %param.5) | copy-start | bytes 196612
  7.9 15.5 %collective-permute-start = (f32[2,8,2048]{2,1,0:T(8,128)}, f32[2,8,2048]{2,1,0:T(8,128)S(1)}, u32[]{:S(2)}, u32[]{:S(2)}) collective-permute-start(f32[2,8,2048]{2,1,0:T(8,128)} %get-tuple-element.22), channel_id=1, source_target_pairs={{0,1},{1,2},{2,3},{3,4},{4,5},{5,6},{6,7},{7,8},{8,9},{9,10},{10,1... | collective-permute-start | bytes 393224 | tf_op jit(solution)/shard_map/ppermute | solution.py:19
  10.9 12.5 %collective-permute-start.1 = (f32[2,8,2048]{2,1,0:T(8,128)S(1)}, f32[2,8,2048]{2,1,0:T(8,128)S(1)}, u32[]{:S(2)}, u32[]{:S(2)}) collective-permute-start(f32[2,8,2048]{2,1,0:T(8,128)S(1)} %get-tuple-element.23), channel_id=1, source_target_pairs={{1,0},{2,1},{3,2},{4,3},{5,4},{6,5},{7,6},{8,7},{9,8},{10,9},{11,1... | collective-permute-start | bytes 393224 | tf_op jit(solution)/shard_map/ppermute | solution.py:19
  25.3 5.6 %collective-permute-start.4 = (f32[26,8,256]{2,1,0:T(8,128)S(1)}, f32[26,8,256]{2,1,0:T(8,128)S(1)}, u32[]{:S(2)}, u32[]{:S(2)}) collective-permute-start(f32[26,8,256]{2,1,0:T(8,128)S(1)} %pad_maximum_fusion.15), channel_id=1, source_target_pairs={{1,0},{2,1},{3,2},{4,3},{5,4},{6,5},{7,6},{0,7},{9,8},{10,9},{11,1... | collective-permute-start | bytes 638984 | tf_op jit(solution)/shard_map/ppermute | solution.py:65
  31.0 5.9 %collective-permute-start.5 = (f32[26,8,256]{2,1,0:T(8,128)S(1)}, f32[26,8,256]{2,1,0:T(8,128)S(1)}, u32[]{:S(2)}, u32[]{:S(2)}) collective-permute-start(f32[26,8,256]{2,1,0:T(8,128)S(1)} %broadcast_select_fusion), channel_id=1, source_target_pairs={{2,0},{3,1},{4,2},{5,3},{6,4},{7,5},{0,6},{1,7},{10,8},{11,9},{12,... | collective-permute-start | bytes 638984 | tf_op jit(solution)/shard_map/ppermute | solution.py:65
  36.9 8.9 %collective-permute-start.6 = (f32[26,8,256]{2,1,0:T(8,128)S(1)}, f32[26,8,256]{2,1,0:T(8,128)S(1)}, u32[]{:S(2)}, u32[]{:S(2)}) collective-permute-start(f32[26,8,256]{2,1,0:T(8,128)S(1)} %broadcast_select_fusion.1), channel_id=1, source_target_pairs={{4,0},{5,1},{6,2},{7,3},{0,4},{1,5},{2,6},{3,7},{12,8},{13,9},{14,... | collective-permute-start | bytes 638984 | tf_op jit(solution)/shard_map/ppermute | solution.py:65
  45.9 11.5 %collective-permute-start.8 = (f32[26,8,256]{2,1,0:T(8,128)S(1)}, f32[26,8,256]{2,1,0:T(8,128)S(1)}, u32[]{:S(2)}, u32[]{:S(2)}) collective-permute-start(f32[26,8,256]{2,1,0:T(8,128)S(1)} %broadcast_select_fusion.2), channel_id=1, source_target_pairs={{0,8},{1,9},{2,10},{3,11},{4,12},{5,13},{6,14},{7,15},{8,16},{9,17... | collective-permute-start | bytes 638984 | tf_op jit(solution)/shard_map/ppermute | solution.py:19
  53.4 14.4 %collective-permute-start.7 = (f32[26,8,256]{2,1,0:T(8,128)S(1)}, f32[26,8,256]{2,1,0:T(8,128)S(1)}, u32[]{:S(2)}, u32[]{:S(2)}) collective-permute-start(f32[26,8,256]{2,1,0:T(8,128)S(1)} %broadcast_select_fusion.2), channel_id=1, source_target_pairs={{8,0},{9,1},{10,2},{11,3},{12,4},{13,5},{14,6},{15,7},{16,8},{17,9... | collective-permute-start | bytes 638984 | tf_op jit(solution)/shard_map/ppermute | solution.py:19
  67.8 15.5 %collective-permute-start.11 = (f32[26,8,256]{2,1,0:T(8,128)S(1)}, f32[26,8,256]{2,1,0:T(8,128)S(1)}, u32[]{:S(2)}, u32[]{:S(2)}) collective-permute-start(f32[26,8,256]{2,1,0:T(8,128)S(1)} %select_select_fusion), channel_id=1, source_target_pairs={{9,1},{10,3},{11,5},{12,7},{13,9},{14,11},{15,13},{16,15},{17,17},... | collective-permute-start | bytes 638984 | tf_op jit(solution)/shard_map/ppermute | solution.py:151
  68.5 13.6 %collective-permute-start.10 = (f32[26,8,256]{2,1,0:T(8,128)S(1)}, f32[26,8,256]{2,1,0:T(8,128)S(1)}, u32[]{:S(2)}, u32[]{:S(2)}) collective-permute-start(f32[26,8,256]{2,1,0:T(8,128)S(1)} %select_select_fusion), channel_id=1, source_target_pairs={{8,0},{9,2},{10,4},{11,6},{12,8},{13,10},{14,12},{15,14},{16,16},{... | collective-permute-start | bytes 638984 | tf_op jit(solution)/shard_map/ppermute | solution.py:147
  69.9 15.7 %collective-permute-start.9 = (f32[26,256]{1,0:T(8,128)S(1)}, f32[26,256]{1,0:T(8,128)S(1)}, u32[]{:S(2)}, u32[]{:S(2)}) collective-permute-start(f32[26,256]{1,0:T(8,128)S(1)} %bitcast.187), channel_id=1, source_target_pairs={{7,0},{8,2},{9,4},{10,6},{11,8},{12,10},{13,12},{14,14},{15,16},{1... | collective-permute-start | bytes 79880 | tf_op jit(solution)/shard_map/ppermute | solution.py:148
  82.1 4.5 %collective-permute-start.13 = (f32[26,8,256]{2,1,0:T(8,128)S(1)}, f32[26,8,256]{2,1,0:T(8,128)S(1)}, u32[]{:S(2)}, u32[]{:S(2)}) collective-permute-start(f32[26,8,256]{2,1,0:T(8,128)S(1)} %collective-permute-done.10), channel_id=1, source_target_pairs={{0,1},{2,3},{4,5},{6,7},{8,9},{10,11},{12,13},{14,15},{16,17},{18,... | collective-permute-start | bytes 638984 | tf_op jit(solution)/shard_map/ppermute | solution.py:152
  83.4 3.2 %collective-permute-start.12 = (f32[4,26,256]{2,0,1:T(4,128)S(1)}, f32[4,26,256]{2,0,1:T(4,128)S(1)}, u32[]{:S(2)}, u32[]{:S(2)}) collective-permute-start(f32[4,26,256]{2,0,1:T(4,128)S(1)} %slice_bitcast_fusion.13), channel_id=1, source_target_pairs={{1,0},{3,2},{5,4},{7,6},{9,8},{11,10},{13,12},{15,14},{17,16},{19,... | collective-permute-start | bytes 319496 | tf_op jit(solution)/shard_map/ppermute | solution.py:154
  103.2 9.5 %collective-permute-start.17 = (f32[4,24,256]{2,0,1:T(4,128)S(1)}, f32[4,24,256]{2,0,1:T(4,128)S(1)}, u32[]{:S(2)}, u32[]{:S(2)}) collective-permute-start(f32[4,24,256]{2,0,1:T(4,128)S(1)} %bitcast.183), channel_id=1, source_target_pairs={{1,8},{3,9},{5,10},{7,11},{9,12},{11,13},{13,14},{15,15},{17,16},{... | collective-permute-start | bytes 294920 | tf_op jit(solution)/shard_map/ppermute | solution.py:193
  103.9 8.9 %collective-permute-start.16 = (f32[4,24,256]{2,0,1:T(4,128)S(1)}, f32[4,24,256]{2,0,1:T(4,128)S(1)}, u32[]{:S(2)}, u32[]{:S(2)}) collective-permute-start(f32[4,24,256]{2,0,1:T(4,128)S(1)} %bitcast.184), channel_id=1, source_target_pairs={{0,8},{2,9},{4,10},{6,11},{8,12},{10,13},{12,14},{14,15},{16,16},{... | collective-permute-start | bytes 294920 | tf_op jit(solution)/shard_map/ppermute | solution.py:193
  108.6 4.2 %collective-permute-start.15 = (f32[4,24,256]{2,0,1:T(4,128)S(1)}, f32[4,24,256]{2,0,1:T(4,128)S(1)}, u32[]{:S(2)}, u32[]{:S(2)}) collective-permute-start(f32[4,24,256]{2,0,1:T(4,128)S(1)} %bitcast.185), channel_id=1, source_target_pairs={{1,9},{3,10},{5,11},{7,12},{9,13},{11,14},{13,15},{15,16},{17,17},... | collective-permute-start | bytes 294920 | tf_op jit(solution)/shard_map/ppermute | solution.py:193
  109.2 5.7 %collective-permute-start.14 = (f32[4,24,256]{2,0,1:T(4,128)S(1)}, f32[4,24,256]{2,0,1:T(4,128)S(1)}, u32[]{:S(2)}, u32[]{:S(2)}) collective-permute-start(f32[4,24,256]{2,0,1:T(4,128)S(1)} %bitcast.186), channel_id=1, source_target_pairs={{0,9},{2,10},{4,11},{6,12},{8,13},{10,14},{12,15},{14,16},{16,17},... | collective-permute-start | bytes 294920 | tf_op jit(solution)/shard_map/ppermute | solution.py:193
  115.1 5.6 %collective-permute-start.19 = (f32[8,24,256]{2,0,1:T(8,128)S(1)}, f32[8,24,256]{2,0,1:T(8,128)S(1)}, u32[]{:S(2)}, u32[]{:S(2)}) collective-permute-start(f32[8,24,256]{2,0,1:T(8,128)S(1)} %fusion.53), channel_id=1, source_target_pairs={{0,8},{1,9},{2,10},{3,11},{4,12},{5,13},{6,14},{7,15},{8,16},{9,17... | collective-permute-start | bytes 589832 | tf_op jit(solution)/shard_map/ppermute | solution.py:19
  117.3 16.4 %collective-permute-start.18 = (f32[8,24,256]{2,0,1:T(8,128)S(1)}, f32[8,24,256]{2,0,1:T(8,128)S(1)}, u32[]{:S(2)}, u32[]{:S(2)}) collective-permute-start(f32[8,24,256]{2,0,1:T(8,128)S(1)} %fusion.53), channel_id=1, source_target_pairs={{8,0},{9,1},{10,2},{11,3},{12,4},{13,5},{14,6},{15,7},{16,8},{17,9... | collective-permute-start | bytes 589832 | tf_op jit(solution)/shard_map/ppermute | solution.py:19
  133.8 6.3 %collective-permute-start.20 = (f32[8,24,256]{2,0,1:T(8,128)S(1)}, f32[8,24,256]{2,0,1:T(8,128)S(1)}, u32[]{:S(2)}, u32[]{:S(2)}) collective-permute-start(f32[8,24,256]{2,0,1:T(8,128)S(1)} %select_select_fusion.1), channel_id=1, source_target_pairs={{7,0},{0,1},{1,2},{2,3},{3,4},{4,5},{5,6},{6,7},{15,8},{8,9},{9,10... | collective-permute-start | bytes 589832 | tf_op jit(solution)/shard_map/ppermute | solution.py:65
  140.1 8.9 %collective-permute-start.21 = (f32[8,24,256]{2,0,1:T(8,128)S(1)}, f32[8,24,256]{2,0,1:T(8,128)S(1)}, u32[]{:S(2)}, u32[]{:S(2)}) collective-permute-start(f32[8,24,256]{2,0,1:T(8,128)S(1)} %broadcast_select_fusion.3), channel_id=1, source_target_pairs={{6,0},{7,1},{0,2},{1,3},{2,4},{3,5},{4,6},{5,7},{14,8},{15,9},{8,1... | collective-permute-start | bytes 589832 | tf_op jit(solution)/shard_map/ppermute | solution.py:65
  149.1 8.6 %collective-permute-start.22 = (f32[8,24,256]{2,0,1:T(8,128)S(1)}, f32[8,24,256]{2,0,1:T(8,128)S(1)}, u32[]{:S(2)}, u32[]{:S(2)}) collective-permute-start(f32[8,24,256]{2,0,1:T(8,128)S(1)} %broadcast_select_fusion.4), channel_id=1, source_target_pairs={{4,0},{5,1},{6,2},{7,3},{0,4},{1,5},{2,6},{3,7},{12,8},{13,9},{14,... | collective-permute-start | bytes 589832 | tf_op jit(solution)/shard_map/ppermute | solution.py:65
  (14 other events, 58.4 us)
